TPU v7x, 32 devices: a whole 2x2x4 slice. The times are simulated.
32 devices in a mesh: req: 4 (over y, x), head: 4 (over z), dev: 2 (over core).
Axes of the slice: x: 2, y: 2, z: 4, core: 2. Of those that a mesh axis runs over, the one named last changes fastest.
Arguments:
- tokens: bfloat16 [4, 512, 2304], P('req', 'dev')
- attn_gain: float32 [2304], replicated, may hold values from 0.1 to 1.9
- w_qkv: bfloat16 [2304, 3, 2048], P(None, None, 'head')
- w_out: bfloat16 [2048, 2304], P('head'), may hold values from -0.125 to 0.125
- moe_gain: float32 [2304], replicated, may hold values from 0.1 to 1.9
- routes: int32 [4, 512, 2], P(None, 'dev'), may hold values from 0 to 7, all different within a row; in each aligned block of 256 rows (0 to 255, 256 to 511, ..., all dimensions but the last counted through in order) at most 96 rows name the same one
- route_weight: float32 [4, 512, 2], P(None, 'dev'), may hold values from 0.2 to 1
- w_gate_up: bfloat16 [8, 2, 2304, 5760], P('head', None, None, 'req'), may hold values from -0.125 to 0.125
- w_down: bfloat16 [8, 5760, 2304], P('head', 'req'), may hold values from -0.078125 to 0.078125
- kv_cache: bfloat16 [4, 16, 128, 2, 2048], P('req', None, 'dev', None, 'head'), may hold values from -6 to 6
- lengths: int32 [4], replicated, may hold values from 1 to 2048, as said below
- block_owner: int32 [4, 16], replicated, may hold values from 0 to 3, as said below
- block_slot: int32 [4, 16], replicated, may hold values from 0 to 15, as said below
Outputs:
- layer_out: bfloat16 [4, 2, 256, 2304], P('req', 'dev', 'head')
- page_pool: bfloat16 [64, 128, 2, 2048], P('req', 'dev', None, 'head')
Inputs may be any that keep to these rules, and one draw needn't show every extreme that they name: `routes`: in each aligned block of 256 rows (the rows of one device) no expert is named more than 96 times; the other loads are skewed. `lengths`: each request has a length of 1 or more tokens; some request has exactly 2048. `block_owner`: each holder holds exactly 4 pages of every request. The pairs of block_owner and block_slot are distinct over all pages of all requests.
All inputs are finite; a program needn't handle non-finite values.
Results may differ from a plain program's by a relative error of at most 0.012.
Values may be sent and summed in bfloat16 or wider, within the bound.
No kernel may reach another device: no remote copies, remote signals or barrier semaphores. Data moves between devices by JAX's collectives and lax.ppermute only.
A program may use at most 192 MiB of HBM per device.

v0:
```python
import jax
import jax.numpy as jnp
from jax import lax
from jax.sharding import PartitionSpec as P

EXPERTS = 8
HD = 64


def shifted(block, axis, distance):
    devices = range(lax.axis_size(axis))
    route = [(i - distance, i) for i in devices if i - distance in devices]
    return lax.ppermute(block, axis, route)


def norm_rows(values, gain_vec):
    widened = values.astype(jnp.float32)
    inv_rms = lax.rsqrt(jnp.mean(widened * widened, axis=-1, keepdims=True) + 1e-05)
    return (widened * inv_rms * gain_vec).astype(jnp.bfloat16)


def rotate(values, positions):
    half_dim = values.shape[-1] // 2
    frequency = 10000.0 ** (-jnp.arange(half_dim, dtype=jnp.float32) / half_dim)
    angles = positions[:, None] * frequency[None, :]
    cosine = jnp.cos(angles)[:, None, :]
    sine_part = jnp.sin(angles)[:, None, :]
    front_half = values[..., :half_dim]
    back_half = values[..., half_dim:]
    return jnp.concatenate(
        [front_half * cosine - back_half * sine_part, back_half * cosine + front_half * sine_part],
        axis=-1,
    )


def slot_tables(route_ids, weights, first_expert, experts_here, capacity):
    expert_ids = first_expert + jnp.arange(experts_here, dtype=jnp.int32)
    matches = (route_ids[..., None] == expert_ids).astype(jnp.float32)
    hit_shape = matches.shape
    flat_hits = matches.reshape(hit_shape[:-3] + (hit_shape[-3] * hit_shape[-2], hit_shape[-1]))
    ranking = (jnp.cumsum(flat_hits, axis=-2) - flat_hits).reshape(hit_shape)
    places = (ranking[..., None] == jnp.arange(capacity, dtype=jnp.float32)).astype(
        jnp.float32
    ) * matches[..., None]
    dispatch = jnp.sum(places, axis=-3)
    combine = jnp.sum(places * weights[..., None, None], axis=-3)
    return (dispatch, combine)


def body(
    tokens,
    attn_gain,
    w_qkv,
    w_out,
    moe_gain,
    routes,
    route_weight,
    w_gate_up,
    w_down,
    kv_cache,
    lengths,
    block_owner,
    block_slot,
):
    half_rows = tokens.shape[1]
    model_width = tokens.shape[2]
    dev_index = lax.axis_index("dev")
    req_index = lax.axis_index("req")
    head_index = lax.axis_index("head")
    local_cols = w_qkv.shape[2]
    head_count = local_cols // HD
    normed = norm_rows(tokens[0], attn_gain)
    projected = jnp.dot(
        normed, w_qkv.reshape(model_width, 3 * local_cols), preferred_element_type=jnp.float32
    ).reshape(half_rows, 3, head_count, HD)
    query_pos = dev_index * half_rows + jnp.arange(half_rows, dtype=jnp.int32)
    angles_at = query_pos.astype(jnp.float32)
    queries = rotate(projected[:, 0], angles_at).astype(jnp.bfloat16)
    key_rows = rotate(projected[:, 1], angles_at).astype(jnp.bfloat16)
    values = projected[:, 2].astype(jnp.bfloat16)
    earlier_keys, earlier_values = shifted((key_rows, values), "dev", 1)
    all_keys = jnp.concatenate([earlier_keys, key_rows], axis=0)
    all_values = jnp.concatenate([earlier_values, values], axis=0)
    key_pos = (dev_index - 1) * half_rows + jnp.arange(2 * half_rows, dtype=jnp.int32)
    allowed = (key_pos[None, :] <= query_pos[:, None]) & (key_pos[None, :] >= 0)
    scores = (
        jnp.einsum("qhd,khd->hqk", queries, all_keys, preferred_element_type=jnp.float32) * 0.125
    )
    scores = jnp.where(allowed[None], scores, -1e30)
    row_peak = jnp.max(scores, axis=-1, keepdims=True)
    exp_scores = jnp.exp(scores - row_peak)
    row_total = jnp.sum(exp_scores, axis=-1)
    attended = (
        jnp.einsum(
            "hqk,khd->qhd",
            exp_scores.astype(jnp.bfloat16),
            all_values,
            preferred_element_type=jnp.float32,
        )
        / jnp.transpose(row_total)[:, :, None]
    )
    attended = attended.astype(jnp.bfloat16).reshape(half_rows, local_cols)
    partial_value = jnp.dot(attended, w_out, preferred_element_type=jnp.float32)
    attn_mixed = lax.psum(partial_value.astype(jnp.bfloat16), "head").astype(jnp.float32)
    residual = (tokens[0].astype(jnp.float32) + attn_mixed).astype(jnp.bfloat16)
    moe_in = norm_rows(residual, moe_gain)
    experts_here = w_gate_up.shape[0]
    first_expert = head_index * experts_here
    top_count = routes.shape[2]
    capacity = half_rows * top_count * 3 // (2 * EXPERTS)
    all_rows_here = lax.all_gather(moe_in, "req", axis=0, tiled=True)
    sources = all_rows_here.shape[0] // half_rows
    every_dispatch, every_combine = slot_tables(
        routes, route_weight, first_expert, experts_here, capacity
    )
    picked_all = jnp.einsum(
        "stec,std->sced",
        every_dispatch.astype(jnp.bfloat16),
        all_rows_here.reshape(sources, half_rows, model_width),
        preferred_element_type=jnp.float32,
    )
    picked_all = picked_all.astype(jnp.bfloat16).reshape(
        sources * capacity, experts_here, model_width
    )
    both = jnp.einsum("ned,egdf->gnef", picked_all, w_gate_up, preferred_element_type=jnp.float32)
    hidden_all = (jax.nn.silu(both[0]) * both[1]).astype(jnp.bfloat16)
    source_count = half_rows * lax.axis_size("req") // half_rows
    down_out = jnp.einsum("nef,efd->ned", hidden_all, w_down, preferred_element_type=jnp.float32)
    down_out = down_out.astype(jnp.bfloat16).reshape(
        source_count, capacity, experts_here, model_width
    )
    dispatch_part = every_dispatch.astype(jnp.bfloat16)
    selected = jnp.einsum(
        "stec,sced->sted", dispatch_part, down_out, preferred_element_type=jnp.float32
    )
    expert_back = (
        lax.psum_scatter(
            selected.reshape(half_rows * lax.axis_size("req"), experts_here * model_width).astype(
                jnp.bfloat16
            ),
            "req",
            scatter_dimension=0,
            tiled=True,
        )
        .astype(jnp.float32)
        .reshape(half_rows, experts_here, model_width)
    )
    own_combine = lax.dynamic_index_in_dim(every_combine, req_index, 0, keepdims=False)
    token_weights = jnp.sum(own_combine, axis=-1)
    moe_out = jnp.sum(token_weights[:, :, None] * expert_back, axis=1)
    summed = lax.psum_scatter(
        moe_out.astype(jnp.bfloat16), "head", scatter_dimension=0, tiled=True
    ).astype(jnp.float32)
    rows_out = summed.shape[0]
    kept_rows = lax.dynamic_slice_in_dim(residual, head_index * rows_out, rows_out, 0)
    layer_out = (
        (kept_rows.astype(jnp.float32) + summed)
        .astype(jnp.bfloat16)
        .reshape(1, 1, rows_out, model_width)
    )
    owners_total = lax.axis_size("req")
    block_total = block_owner.shape[1]
    finished_total = block_owner.shape[0]
    per_owner = block_total // owners_total
    block_ids = jnp.arange(block_total, dtype=jnp.int32)
    same_owner = block_owner[:, :, None] == block_owner[:, None, :]
    before_mask = block_ids[None, :] < block_ids[:, None]
    page_rank = jnp.sum((same_owner & before_mask[None]).astype(jnp.int32), axis=2)
    own_owner = lax.dynamic_index_in_dim(block_owner, req_index, 0, keepdims=False)
    own_rank = lax.dynamic_index_in_dim(page_rank, req_index, 0, keepdims=False)
    dest_place = own_owner * per_owner + own_rank
    source_block = jnp.sum(
        jnp.where(dest_place[None, :] == block_ids[:, None], block_ids[None, :], 0), axis=1
    )
    page_half = kv_cache.shape[2]
    page_size = page_half * lax.axis_size("dev")
    token_pos = (
        block_ids[:, None] * page_size
        + dev_index * page_half
        + jnp.arange(page_half, dtype=jnp.int32)[None, :]
    )
    own_length = lax.dynamic_index_in_dim(lengths, req_index, 0, keepdims=False)
    live_cache = jnp.where(
        (token_pos < own_length)[:, :, None, None], kv_cache[0], jnp.zeros((), jnp.bfloat16)
    )
    outgoing = jnp.take(live_cache, source_block, axis=0)
    received = lax.all_to_all(outgoing, "req", split_axis=0, concat_axis=0, tiled=True)
    request_ids = jnp.arange(finished_total, dtype=jnp.int32)
    arrive_place = request_ids[:, None] * per_owner + page_rank
    own_blocks = block_owner == req_index
    slot_match = own_blocks[None] & (block_slot[None] == block_ids[:, None, None])
    gather_place = jnp.sum(jnp.where(slot_match, arrive_place[None], 0), axis=(1, 2))
    page_pool = jnp.take(received, gather_place, axis=0)
    return (layer_out, page_pool)


def solution(mesh):
    return jax.shard_map(
        body,
        mesh=mesh,
        in_specs=(
            P("req", "dev", None),
            P(),
            P(None, None, "head"),
            P("head", None),
            P(),
            P(None, "dev", None),
            P(None, "dev", None),
            P("head", None, None, "req"),
            P("head", "req", None),
            P("req", None, "dev", None, "head"),
            P(),
            P(),
            P(),
        ),
        out_specs=(P("req", "dev", "head", None), P("req", "dev", None, "head")),
        check_vma=False,
    )
```

profile of v0, /device:TPU:0, one launch (start us, length us, event | category | flops | bytes accessed | tf_op | source)
XLA Modules:
  0.0 389.8 jit_solution(5004357111727362680)
XLA Ops:
  7.2 0.0 all-reduce.2.cloned.1.call-start
  7.3 9.9 %copy.47 = bf16[2304,3,512]{0,2,1:T(8,128)(2,1)} copy(bf16[2304,3,512]{2,0,1:T(8,128)(2,1)} %param.17) | data formatting | bytes 14155776 | tf_op args[2]
  17.2 0.3 fusion.11
  17.5 5.2 %fusion.25 = f32[256,3,8,64]{0,3,2,1:T(8,128)S(1)} fusion(bf16[3,8,64,2304]{3,2,1,0:T(8,128)(2,1)} %bitcast.100, bf16[1,256,2304]{2,1,0:T(8,128)(2,1)S(1)} %copy-done.2, f32[2304]{0:T(1024)} %param.16, f32[256]{0:T(256)S(1)} %add_rsqrt_fusion.1), kind=kOutput, calls=%fused_computation.43 | convolution fusion | flops 1814298624 | bytes 9840640 | tf_op jit(solution)/shard_map/dot_general | solution.py:73
  22.7 0.1 slice_bitcast_fusion.3
  22.8 0.2 multiply_cosine_fusion
  23.0 0.2 subtract_convert_fusion.1
  23.2 3.1 collective-permute-start.1
  26.2 2.0 collective-permute-start
  28.3 0.2 compare_and_fusion
  28.4 1.9 fusion.2
  30.3 1.3 fusion.4
  31.6 2.1 fusion.32
  33.8 1.8 convolution_convert_fusion.1
  35.6 0.0 all-reduce.2.cloned.1.call-update
  35.6 0.0 all-gather.2.cloned.1.call-start
  35.7 58.1 %all-reduce.2.cloned.1.call-done = bf16[256,2304]{1,0:T(8,128)(2,1)} async-done(((bf16[256,2304]{1,0:T(8,128)(2,1)}), bf16[256,2304]{1,0:T(8,128)(2,1)}) %all-reduce.2.cloned.1.call-update) | async-done | bytes 1179664 | tf_op jit(solution)/shard_map/psum | solution.py:104
  93.8 2.1 fusion.8
  95.9 1.4 fusion.10
  97.3 0.0 all-gather.2.cloned.1.call-update
  97.3 0.2 reduce-scatter.3.cloned.1.call-start
  97.5 0.2 copy.48
  97.7 0.1 copy.49
  97.8 0.1 compare_convert_fusion.1
  97.9 2.4 reduce-window.6
  100.3 0.2 slice_reduce_fusion
  100.5 0.7 reduce-window.9
  101.2 0.1 broadcast_add_fusion
  101.3 0.2 copy.62
  101.5 0.1 bitcast_subtract_fusion
  101.7 0.2 copy.52
  101.9 0.1 compare_convert_fusion
  101.9 1.2 fusion.20
  103.1 50.9 %all-gather.2.cloned.1.call-done = bf16[1024,2304]{1,0:T(8,128)(2,1)} async-done(((bf16[256,2304]{1,0:T(8,128)(2,1)}), bf16[1024,2304]{1,0:T(8,128)(2,1)}) %all-gather.2.cloned.1.call-update) | async-done | bytes 4718608 | tf_op jit(solution)/shard_map/all_gather | solution.py:111
  154.1 3.4 fusion.60
  157.5 0.4 convert_bitcast_fusion.1
  157.9 2.0 copy.54
  159.9 18.4 %convolution_bitcast_fusion = f32[2,384,2,1440]{1,3,0,2:T(8,128)S(1)} fusion(bf16[384,2,2304,1]{2,0,3,1:T(8,128)(2,1)} %bitcast.97, bf16[2,2,2304,1440]{2,3,1,0:T(8,128)(2,1)} %param.22), kind=kOutput, calls=%fused_computation.3 | convolution fusion | flops 10192158720 | bytes 38928384 | tf_op jit(solution)/shard_map/ned,egdf->gnef/dot_general | solution.py:125
  178.3 12.7 %convolution_convert_fusion = bf16[2,384,2304]{2,1,0:T(8,128)(2,1)} fusion(bf16[2,1440,2304]{2,1,0:T(8,128)(2,1)} %param.23, f32[2,384,2,1440]{1,3,0,2:T(8,128)S(1)} %convolution_bitcast_fusion), kind=kOutput, calls=%fused_computation.4 | convolution fusion | flops 5104484352 | bytes 25657344 | tf_op jit(solution)/shard_map/nef,efd->ned/dot_general | solution.py:128
  191.0 8.3 %convert_bitcast_fusion = bf16[4,256,2,2304]{1,3,2,0:T(8,128)(2,1)} fusion(bf16[4,256,2,96]{1,3,2,0:T(8,128)(2,1)S(1)} %get-tuple-element.10, bf16[4,96,2,2304]{3,1,0,2:T(8,128)(2,1)} %bitcast.99), kind=kOutput, calls=%fused_computation.2 | convolution fusion | flops 910688256 | bytes 13369344 | tf_op jit(solution)/shard_map/stec,sced->sted/dot_general | solution.py:133
  199.3 23.9 %copy.57 = bf16[4,256,2,2304]{3,2,1,0:T(2,128)(2,1)} copy(bf16[4,256,2,2304]{1,3,2,0:T(8,128)(2,1)} %convert_bitcast_fusion) | data formatting | bytes 18874368 | tf_op jit(solution)/shard_map/convert_element_type | solution.py:138
  223.2 9.0 %copy.64 = bf16[128,8,2,2304]{3,1,2,0:T(8,128)(2,1)} copy(bf16[128,8,2,2304]{3,2,1,0:T(2,128)(2,1)} %bitcast.96) | data formatting | bytes 18874368
  232.1 0.0 reduce-scatter.3.cloned.1.call-update
  232.2 0.3 reduce-scatter.5.cloned.1.call-start
  232.4 1.1 dynamic-slice_reduce_fusion
  233.6 0.1 copy.53
  233.7 0.6 dynamic_slice.20
  234.3 0.2 convert_reduce_fusion
  234.6 0.1 select_reduce_fusion.2
  234.7 0.7 add_compare_fusion
  235.4 1.7 bitcast_select_fusion
  237.1 2.3 gather_fusion
  239.4 88.0 %reduce-scatter.3.cloned.1.call-done = bf16[256,4608]{1,0:T(8,128)(2,1)} async-done(((bf16[1024,4608]{1,0:T(8,128)(2,1)}), bf16[256,4608]{1,0:T(8,128)(2,1)}) %reduce-scatter.3.cloned.1.call-update) | async-done | bytes 2359312 | tf_op jit(solution)/shard_map/reduce_scatter | solution.py:137
  327.4 5.9 %reshape.283 = f32[256,2,2304]{2,1,0:T(2,128)} reshape(bf16[256,4608]{1,0:T(8,128)(2,1)} %reduce-scatter.3.cloned.1.call-done) | data formatting | bytes 7077888 | tf_op jit(solution)/shard_map/reshape | solution.py:146
  333.3 10.3 %multiply_reduce_fusion = bf16[256,2304]{1,0:T(8,128)(2,1)} fusion(f32[256,2,2304]{2,1,0:T(2,128)} %reshape.283, f32[256,2]{1,0:T(8,128)S(1)} %copy.53), kind=kLoop, calls=%fused_computation.5 | loop fusion | flops 1769472 | bytes 5900288 | tf_op jit(solution)/shard_map/reduce_sum | solution.py:150
  343.6 1.6 broadcast_select_fusion.1
  345.2 4.0 %all-to-all-start = ((bf16[16,64,2,512]{3,1,2,0:T(8,128)(2,1)}), bf16[16,64,2,512]{3,1,2,0:T(8,128)(2,1)S(1)}, u32[]{:S(2)}, u32[]{:S(2)}) async-start(bf16[16,64,2,512]{3,1,2,0:T(8,128)(2,1)} %broadcast_select_fusion.1), calls=%async_computation.2 | async-start | bytes 4194304 | tf_op jit(solution)/shard_map/all_to_all | solution.py:187
  349.3 0.1 broadcast_add_fusion.1
  349.3 0.1 select_reduce_fusion.1
  349.5 24.5 %all-to-all-done = bf16[16,64,2,512]{3,1,2,0:T(8,128)(2,1)S(1)} async-done(((bf16[16,64,2,512]{3,1,2,0:T(8,128)(2,1)}), bf16[16,64,2,512]{3,1,2,0:T(8,128)(2,1)S(1)}, u32[]{:S(2)}, u32[]{:S(2)}) %all-to-all-start) | async-done | bytes 2097184 | tf_op jit(solution)/shard_map/all_to_all | solution.py:187
  374.0 2.0 gather_fusion.1
  376.0 2.0 broadcast_select_fusion
  378.0 3.5 copy.59
  381.5 1.7 fusion.44
  (45 shorter events, 0.2 us)
Async XLA Ops:
  7.2 26.6 %copy-start = (bf16[512,2304]{1,0:T(8,128)(2,1)S(1)}, bf16[512,2304]{1,0:T(8,128)(2,1)}, u32[]{:S(2)}) copy-start(bf16[512,2304]{1,0:T(8,128)(2,1)} %param.18) | copy-start | bytes 7077892
  7.2 86.6 %all-reduce.2.cloned.1.call-start = ((), (), s32[]{:S(2)}) async-start(), calls=%async_computation.3 | async-start | bytes 2359296 | tf_op jit(solution)/shard_map/psum | solution.py:104
  7.3 9.9 %copy-start.2 = (bf16[1,256,2304]{2,1,0:T(8,128)(2,1)S(1)}, bf16[1,256,2304]{2,1,0:T(8,128)(2,1)}, u32[]{:S(2)}) copy-start(bf16[1,256,2304]{2,1,0:T(8,128)(2,1)} %param.15) | copy-start | bytes 3538948
  23.2 5.3 %collective-permute-start.1 = (bf16[256,8,64]{0,2,1:T(8,128)(2,1)S(1)}, bf16[256,8,64]{0,2,1:T(8,128)(2,1)}, u32[]{:S(2)}, u32[]{:S(2)}) collective-permute-start(bf16[256,8,64]{0,2,1:T(8,128)(2,1)S(1)} %pad_maximum_fusion), channel_id=1, source_target_pairs={{0,1},{2,3},{4,5},{6,7},{8,9},{10,11},{12,13},{14,15},{16,17},{18,... | collective-permute-start | bytes 786440 | tf_op jit(solution)/shard_map/ppermute | solution.py:13
  26.2 5.4 %collective-permute-start = (bf16[256,8,64]{0,2,1:T(8,128)(2,1)S(1)}, bf16[256,8,64]{0,2,1:T(8,128)(2,1)}, u32[]{:S(2)}, u32[]{:S(2)}) collective-permute-start(bf16[256,8,64]{0,2,1:T(8,128)(2,1)S(1)} %fusion.45), channel_id=1, source_target_pairs={{0,1},{2,3},{4,5},{6,7},{8,9},{10,11},{12,13},{14,15},{16,17},{18,... | collective-permute-start | bytes 786440 | tf_op jit(solution)/shard_map/ppermute | solution.py:13
  35.6 60.3 %copy-start.6 = (f32[2304]{0:T(1024)S(1)}, f32[2304]{0:T(1024)}, u32[]{:S(2)}) copy-start(f32[2304]{0:T(1024)} %param.19) | copy-start | bytes 27652
  35.6 118.5 %all-gather.2.cloned.1.call-start = ((), (), s32[]{:S(2)}) async-start(), calls=%async_computation.4 | async-start | bytes 5898240 | tf_op jit(solution)/shard_map/all_gather | solution.py:111
  95.9 1.6 copy-start.4
  97.3 4.7 %copy-start.7 = (f32[4,256,2]{1,2,0:T(2,128)S(1)}, f32[4,256,2]{1,2,0:T(2,128)}, u32[]{:S(2)}) copy-start(f32[4,256,2]{1,2,0:T(2,128)} %param.21) | copy-start | bytes 24580
  97.3 230.1 %reduce-scatter.3.cloned.1.call-start = ((), (), s32[]{:S(2)}) async-start(), calls=%async_computation.5 | async-start | bytes 11796480 | tf_op jit(solution)/shard_map/reduce_scatter | solution.py:137
  232.1 1.6 copy-start.9
  232.1 2.2 copy-start.5
  232.1 3.3 copy-start.3
  232.2 149.4 %reduce-scatter.5.cloned.1.call-start = ((), (), s32[]{:S(2)}) async-start(), calls=%async_computation.6 | async-start | bytes 1474560 | tf_op jit(solution)/shard_map/reduce_scatter | solution.py:151
  345.2 4.1 %copy-start.8 = (s32[4,16]{1,0:T(4,128)S(1)}, s32[4,16]{1,0:T(4,128)}, u32[]{:S(2)}) copy-start(s32[4,16]{1,0:T(4,128)} %param.27) | copy-start | bytes 772
  345.2 28.8 %all-to-all-start = ((bf16[16,64,2,512]{3,1,2,0:T(8,128)(2,1)}), bf16[16,64,2,512]{3,1,2,0:T(8,128)(2,1)S(1)}, u32[]{:S(2)}, u32[]{:S(2)}) async-start(bf16[16,64,2,512]{3,1,2,0:T(8,128)(2,1)} %broadcast_select_fusion.1), calls=%async_computation.2 | async-start | bytes 4194304 | tf_op jit(solution)/shard_map/all_to_all | solution.py:187
  376.0 7.2 %copy-start.1 = (bf16[512,2304]{1,0:T(8,128)(2,1)S(1)}, bf16[512,2304]{1,0:T(8,128)(2,1)}, u32[]{:S(2)}) copy-start(bf16[512,2304]{1,0:T(8,128)(2,1)} %param.18) | copy-start | bytes 7077892
Sparse Core Ops, SparseCore 0:
  35.7 57.9 all-reduce.1
  97.4 56.6 all-gather.1
  232.3 95.0 reduce-scatter.2
  343.8 29.1 reduce-scatter.4
where the time goes:
time: 391 us; the launch traced here: 390 us
  waiting for transfers between devices  222 us (57%)
  local copies, waits for them, and re-layouts  60.1 us (15%)
  matrix products  53.9 us (14%)
  other arithmetic  30.5 us (8%)
  between operations  14.1 us (4%)
  starting transfers between devices  9.62 us (2%)
    reduce_scatter x1, waiting for transfers between devices, body(): lax.psum_scatter(selected.reshape(half_rows * lax.axis_size('req'), exper...  88 us
    psum x1, waiting for transfers between devices, body(): lax.psum(partial_value.astype(jnp.bfloat16), 'head').astype(jnp.float32)  58.1 us
    all_gather x1, waiting for transfers between devices, body(): all_rows_here = lax.all_gather(moe_in, 'req', axis=0, tiled=True)  50.9 us
    all_to_all x1, waiting for transfers between devices, body(): lax.all_to_all(outgoing, 'req', split_axis=0, concat_axis=0, tiled=True)  24.5 us
    convert_element_type x1, local copies, waits for them, and re-layouts, body(): selected.reshape(half_rows * lax.axis_size('req'), experts_here * model_w...  23.9 us
    unnamed x24, local copies, waits for them, and re-layouts  22.6 us
    dot_general x1, matrix products, body(): jnp.einsum('ned,egdf->gnef', picked_all, w_gate_up, preferred_element_typ...  18.4 us
    dot_general x1, matrix products, body(): jnp.einsum('nef,efd->ned', hidden_all, w_down, preferred_element_type=jnp...  12.7 us
  transfers between devices with their start and end apart: 7, of which 4 were waited for; matrix products, arithmetic and copies ran while one was open for 6% of the time, Pallas kernels for 0%

commit v1 on v0

--- a/solution.py
+++ b/solution.py
@@ -129,25 +129,17 @@
     down_out = down_out.astype(jnp.bfloat16).reshape(
         source_count, capacity, experts_here, model_width
     )
-    dispatch_part = every_dispatch.astype(jnp.bfloat16)
-    selected = jnp.einsum(
-        "stec,sced->sted", dispatch_part, down_out, preferred_element_type=jnp.float32
-    )
-    expert_back = (
-        lax.psum_scatter(
-            selected.reshape(half_rows * lax.axis_size("req"), experts_here * model_width).astype(
-                jnp.bfloat16
-            ),
-            "req",
-            scatter_dimension=0,
-            tiled=True,
-        )
-        .astype(jnp.float32)
-        .reshape(half_rows, experts_here, model_width)
-    )
+    expert_back = lax.psum_scatter(down_out, "req", scatter_dimension=0, tiled=True)[0]
+    own_dispatch = lax.dynamic_index_in_dim(every_dispatch, req_index, 0, keepdims=False)
     own_combine = lax.dynamic_index_in_dim(every_combine, req_index, 0, keepdims=False)
     token_weights = jnp.sum(own_combine, axis=-1)
-    moe_out = jnp.sum(token_weights[:, :, None] * expert_back, axis=1)
+    selected = jnp.einsum(
+        "tec,ced->ted",
+        own_dispatch.astype(jnp.bfloat16),
+        expert_back,
+        preferred_element_type=jnp.float32,
+    )
+    moe_out = jnp.sum(token_weights[:, :, None] * selected, axis=1)
     summed = lax.psum_scatter(
         moe_out.astype(jnp.bfloat16), "head", scatter_dimension=0, tiled=True
     ).astype(jnp.float32)

time: 391 us -> 295 us (0.75)
  waiting for transfers between devices: 222 us -> 174 us
  local copies, waits for them, and re-layouts: 60.1 us -> 29.9 us
  matrix products: 53.9 us -> 44.8 us
  other arithmetic: 30.5 us -> 22.4 us
    reduce_scatter x1 -> x0, waiting for transfers between devices: 88 us -> none  [body(): lax.psum_scatter(selected.reshape(half_rows * lax.axis_size('req'), exper...]
    unnamed x4 -> x5, waiting for transfers between devices: 0.07 us -> 40.1 us
    convert_element_type x1 -> x0, local copies, waits for them, and re-layouts: 23.9 us -> none  [body(): selected.reshape(half_rows * lax.axis_size('req'), experts_here * model_w...]
    reduce_sum x2 -> x1, other arithmetic: 11.5 us -> 1.17 us  [slot_tables(): dispatch = jnp.sum(places, axis=-3)]
    unnamed x24 -> x33, local copies, waits for them, and re-layouts: 22.6 us -> 17 us
    dot_general x1, matrix products: 8.27 us -> 3.27 us  [body(): jnp.einsum('tec,ced->ted', own_dispatch.astype(jnp.bfloat16), expert_back...]
    reshape x1, local copies, waits for them, and re-layouts: 5.92 us -> 1.99 us  [body(): down_out.astype(jnp.bfloat16)]
  transfers between devices with their start and end apart: 7 -> 7, of which waited for: 4 -> 4; matrix products, arithmetic and copies ran while one was open for 6% -> 9% of each run, Pallas kernels for 0% -> 0%
where the time goes in v1:
time: 295 us; the launch traced here: 294 us
  waiting for transfers between devices  174 us (59%)
  matrix products  44.8 us (15%)
  local copies, waits for them, and re-layouts  29.9 us (10%)
  other arithmetic  22.4 us (8%)
  between operations  14 us (5%)
  starting transfers between devices  9.34 us (3%)
    psum x1, waiting for transfers between devices, body(): lax.psum(partial_value.astype(jnp.bfloat16), 'head').astype(jnp.float32)  58.1 us
    all_gather x1, waiting for transfers between devices, body(): all_rows_here = lax.all_gather(moe_in, 'req', axis=0, tiled=True)  51 us
    unnamed x5, waiting for transfers between devices  40.1 us
    all_to_all x1, waiting for transfers between devices, body(): lax.all_to_all(outgoing, 'req', split_axis=0, concat_axis=0, tiled=True)  24.6 us
    dot_general x1, matrix products, body(): jnp.einsum('ned,egdf->gnef', picked_all, w_gate_up, preferred_element_typ...  17.8 us
    unnamed x33, local copies, waits for them, and re-layouts  17 us
    dot_general x1, matrix products, body(): jnp.einsum('nef,efd->ned', hidden_all, w_down, preferred_element_type=jnp...  8.91 us
  transfers between devices with their start and end apart: 7, of which 4 were waited for; matrix products, arithmetic and copies ran while one was open for 9% of the time, Pallas kernels for 0%

profile of v1, /device:TPU:0, one launch (start us, length us, event | category | flops | bytes accessed | tf_op | source)
XLA Modules:
  0.0 294.3 jit_solution(4278821264607326831)
XLA Ops:
  7.2 0.0 all-reduce.3.cloned.1.call-start
  7.3 9.9 %copy.59 = bf16[2304,3,512]{0,2,1:T(8,128)(2,1)} copy(bf16[2304,3,512]{2,0,1:T(8,128)(2,1)} %param.17) | data formatting | bytes 14155776 | tf_op args[2]
  17.1 0.3 fusion.11
  17.5 5.2 %fusion.26 = f32[256,3,8,64]{0,3,2,1:T(8,128)S(1)} fusion(bf16[3,8,64,2304]{3,2,1,0:T(8,128)(2,1)} %bitcast.104, bf16[1,256,2304]{2,1,0:T(8,128)(2,1)S(1)} %copy-done.3, f32[2304]{0:T(1024)S(1)} %copy-done.13, f32[256]{0:T(256)S(1)} %add_rsqrt_fusion.1), kind=kOutput, calls=%fused_computation.43 | convolution fusion | flops 1814298624 | bytes 9840640 | tf_op jit(solution)/shard_map/dot_general | solution.py:73
  22.7 1.1 copy-done.5
  23.8 1.1 slice_bitcast_fusion.3
  24.9 0.2 multiply_cosine_fusion
  25.1 2.1 subtract_convert_fusion.1
  27.1 0.6 copy-done.6
  27.8 0.7 pad_maximum_fusion
  28.5 3.0 %collective-permute-start.1 = (bf16[256,8,64]{0,2,1:T(8,128)(2,1)}, bf16[256,8,64]{0,2,1:T(8,128)(2,1)}, u32[]{:S(2)}, u32[]{:S(2)}) collective-permute-start(bf16[256,8,64]{0,2,1:T(8,128)(2,1)} %pad_maximum_fusion), channel_id=1, source_target_pairs={{0,1},{2,3},{4,5},{6,7},{8,9},{10,11},{12,13},{14,15},{16,17},{18,... | collective-permute-start | bytes 786440 | tf_op jit(solution)/shard_map/ppermute | solution.py:13
  31.6 1.8 fusion.47
  33.3 2.0 collective-permute-start
  35.3 0.2 compare_and_fusion
  35.5 2.1 fusion.3
  37.6 1.3 fusion.4
  39.0 2.2 fusion.33
  41.2 1.8 convolution_convert_fusion.1
  43.0 0.0 all-gather.2.cloned.1.call-start
  43.1 58.1 %all-reduce.3.cloned.1.call-done = bf16[256,2304]{1,0:T(8,128)(2,1)} async-done(((bf16[256,2304]{1,0:T(8,128)(2,1)}), bf16[256,2304]{1,0:T(8,128)(2,1)}) %all-reduce.3.cloned.1.call-update) | async-done | bytes 1179664 | tf_op jit(solution)/shard_map/psum | solution.py:104
  101.2 1.8 fusion.8
  103.0 1.0 copy-done.2
  104.0 1.3 fusion.10
  105.4 0.2 reduce-scatter.7.cloned.1.call-start
  105.6 0.2 copy.60
  105.8 0.1 copy.61
  105.9 0.1 compare_convert_fusion.1
  106.0 2.4 reduce-window.6
  108.4 0.2 slice_reduce_fusion
  108.6 0.7 reduce-window.9
  109.3 0.1 broadcast_add_fusion
  109.4 0.2 copy.73
  109.6 0.1 bitcast_subtract_fusion
  109.8 0.2 copy.64
  110.0 0.1 compare_convert_fusion
  110.0 1.2 select_reduce_fusion
  111.2 51.0 %all-gather.2.cloned.1.call-done = bf16[1024,2304]{1,0:T(8,128)(2,1)} async-done(((bf16[256,2304]{1,0:T(8,128)(2,1)}), bf16[1024,2304]{1,0:T(8,128)(2,1)}) %all-gather.2.cloned.1.call-update) | async-done | bytes 4718608 | tf_op jit(solution)/shard_map/all_gather | solution.py:111
  162.2 3.4 %fusion.65 = f32[4,2304,192]{1,2,0:S(1)} fusion(bf16[4,256,192]{1,2,0:T(8,128)(2,1)S(1)} %bitcast.110, bf16[4,256,2304]{2,1,0:T(8,128)(2,1)} %bitcast.105), kind=kOutput, calls=%fused_computation.120 | convolution fusion | flops 905969664 | bytes 12189696
  165.6 0.4 convert_bitcast_fusion
  166.0 0.2 copy.65
  166.2 17.8 %convolution_bitcast_fusion = f32[2,384,2,1440]{1,3,0,2:T(8,128)S(1)} fusion(bf16[384,2,2304,1]{2,0,3,1:T(8,128)(2,1)S(1)} %bitcast.102, bf16[2,2,2304,1440]{2,3,1,0:T(8,128)(2,1)} %param.22), kind=kOutput, calls=%fused_computation.2 | convolution fusion | flops 10192158720 | bytes 38928384 | tf_op jit(solution)/shard_map/ned,egdf->gnef/dot_general | solution.py:125
  184.0 8.9 %convolution_convert_fusion = bf16[2,384,2304]{2,1,0:T(8,128)(2,1)S(1)} fusion(bf16[2,1440,2304]{2,1,0:T(8,128)(2,1)} %param.23, f32[2,384,2,1440]{1,3,0,2:T(8,128)S(1)} %convolution_bitcast_fusion), kind=kOutput, calls=%fused_computation.3 | convolution fusion | flops 5104484352 | bytes 25657344 | tf_op jit(solution)/shard_map/nef,efd->ned/dot_general | solution.py:128
  192.9 2.0 copy.67
  194.9 0.0 reduce-scatter.5.cloned.1.call-start
  195.0 0.6 copy-done.14
  195.6 0.6 dynamic_slice.24
  196.2 0.2 convert_reduce_fusion
  196.4 0.1 select_reduce_fusion.2
  196.5 0.7 add_compare_fusion
  197.3 1.7 bitcast_select_fusion
  198.9 2.3 gather_fusion
  201.2 1.1 dynamic-slice_reduce_fusion
  202.2 40.1 %reduce-scatter.7.cloned.1.call-done = bf16[1,96,2,2304]{3,1,2,0:T(8,128)(2,1)} async-done(((bf16[4,96,2,2304]{3,1,2,0:T(8,128)(2,1)}), bf16[1,96,2,2304]{3,1,2,0:T(8,128)(2,1)}) %reduce-scatter.7.cloned.1.call-update) | async-done | bytes 884752
  242.3 3.3 %fusion.20 = bf16[256,2304]{0,1:T(8,128)(2,1)} fusion(f32[256,2]{0,1:T(2,128)S(1)} %dynamic-slice_reduce_fusion, bf16[1,96,2,2304]{3,1,2,0:T(8,128)(2,1)} %reduce-scatter.7.cloned.1.call-done, bf16[4,256,2,96]{1,3,2,0:T(8,128)(2,1)S(1)} %get-tuple-element.11, s32[]{:T(128)S(6)} %select_n.38), kind=kOutput, calls=%fused_computation.38 | convolution fusion | flops 228261888 | bytes 2164740 | tf_op jit(solution)/shard_map/tec,ced->ted/dot_general | solution.py:136
  245.6 2.4 copy.68
  248.0 1.6 broadcast_select_fusion.1
  249.6 4.0 %all-to-all-start = ((bf16[16,64,2,512]{3,1,2,0:T(8,128)(2,1)}), bf16[16,64,2,512]{3,1,2,0:T(8,128)(2,1)S(1)}, u32[]{:S(2)}, u32[]{:S(2)}) async-start(bf16[16,64,2,512]{3,1,2,0:T(8,128)(2,1)} %broadcast_select_fusion.1), calls=%async_computation.1 | async-start | bytes 4194304 | tf_op jit(solution)/shard_map/all_to_all | solution.py:179
  253.6 0.1 broadcast_add_fusion.1
  253.6 0.1 select_reduce_fusion.1
  253.8 24.6 %all-to-all-done = bf16[16,64,2,512]{3,1,2,0:T(8,128)(2,1)S(1)} async-done(((bf16[16,64,2,512]{3,1,2,0:T(8,128)(2,1)}), bf16[16,64,2,512]{3,1,2,0:T(8,128)(2,1)S(1)}, u32[]{:S(2)}, u32[]{:S(2)}) %all-to-all-start) | async-done | bytes 2097184 | tf_op jit(solution)/shard_map/all_to_all | solution.py:179
  278.4 2.0 gather_fusion.1
  280.4 2.0 broadcast_select_fusion
  282.4 3.5 %copy.70 = bf16[16,64,2,512]{3,2,1,0:T(2,128)(2,1)} copy(bf16[16,64,2,512]{3,1,2,0:T(8,128)(2,1)S(1)} %broadcast_select_fusion) | data formatting | bytes 4194304
  285.9 1.8 fusion.46
  (52 shorter events, 0.3 us)
Async XLA Ops:
  7.2 34.0 %copy-start = (bf16[512,2304]{1,0:T(8,128)(2,1)S(1)}, bf16[512,2304]{1,0:T(8,128)(2,1)}, u32[]{:S(2)}) copy-start(bf16[512,2304]{1,0:T(8,128)(2,1)} %param.18) | copy-start | bytes 7077892
  7.2 94.0 %all-reduce.3.cloned.1.call-start = ((), (), s32[]{:S(2)}) async-start(), calls=%async_computation.3 | async-start | bytes 2359296 | tf_op jit(solution)/shard_map/psum | solution.py:104
  7.2 9.9 %copy-start.3 = (bf16[1,256,2304]{2,1,0:T(8,128)(2,1)S(1)}, bf16[1,256,2304]{2,1,0:T(8,128)(2,1)}, u32[]{:S(2)}) copy-start(bf16[1,256,2304]{2,1,0:T(8,128)(2,1)} %param.15) | copy-start | bytes 3538948
  7.3 10.2 %copy-start.13 = (f32[2304]{0:T(1024)S(1)}, f32[2304]{0:T(1024)}, u32[]{:S(2)}) copy-start(f32[2304]{0:T(1024)} %param.16) | copy-start | bytes 27652
  22.7 1.1 copy-start.5
  27.1 0.6 copy-start.6
  27.1 1.4 copy-start.7
  28.5 7.0 %collective-permute-start.1 = (bf16[256,8,64]{0,2,1:T(8,128)(2,1)}, bf16[256,8,64]{0,2,1:T(8,128)(2,1)}, u32[]{:S(2)}, u32[]{:S(2)}) collective-permute-start(bf16[256,8,64]{0,2,1:T(8,128)(2,1)} %pad_maximum_fusion), channel_id=1, source_target_pairs={{0,1},{2,3},{4,5},{6,7},{8,9},{10,11},{12,13},{14,15},{16,17},{18,... | collective-permute-start | bytes 786440 | tf_op jit(solution)/shard_map/ppermute | solution.py:13
  33.3 5.6 %collective-permute-start = (bf16[256,8,64]{0,2,1:T(8,128)(2,1)}, bf16[256,8,64]{0,2,1:T(8,128)(2,1)}, u32[]{:S(2)}, u32[]{:S(2)}) collective-permute-start(bf16[256,8,64]{0,2,1:T(8,128)(2,1)} %fusion.47), channel_id=1, source_target_pairs={{0,1},{2,3},{4,5},{6,7},{8,9},{10,11},{12,13},{14,15},{16,17},{18,... | collective-permute-start | bytes 786440 | tf_op jit(solution)/shard_map/ppermute | solution.py:13
  43.0 61.0 %copy-start.10 = (f32[2304]{0:T(1024)S(1)}, f32[2304]{0:T(1024)}, u32[]{:S(2)}) copy-start(f32[2304]{0:T(1024)} %param.19) | copy-start | bytes 27652
  43.0 119.1 %all-gather.2.cloned.1.call-start = ((), (), s32[]{:S(2)}) async-start(), calls=%async_computation.4 | async-start | bytes 5898240 | tf_op jit(solution)/shard_map/all_gather | solution.py:111
  103.0 1.1 copy-start.2
  103.0 2.7 copy-start.8
  105.4 4.7 %copy-start.11 = (f32[4,256,2]{1,2,0:T(2,128)S(1)}, f32[4,256,2]{1,2,0:T(2,128)}, u32[]{:S(2)}) copy-start(f32[4,256,2]{1,2,0:T(2,128)} %param.21) | copy-start | bytes 24580
  105.4 136.9 %reduce-scatter.7.cloned.1.call-start = ((), (), s32[]{:S(2)}) async-start(), calls=%async_computation.6 | async-start | bytes 4423680
  194.9 0.7 copy-start.14
  194.9 1.3 copy-start.9
  194.9 2.3 copy-start.4
  194.9 91.0 %reduce-scatter.5.cloned.1.call-start = ((), (), s32[]{:S(2)}) async-start(), calls=%async_computation.5 | async-start | bytes 1474560 | tf_op jit(solution)/shard_map/reduce_scatter | solution.py:143
  249.6 4.1 %copy-start.12 = (s32[4,16]{1,0:T(4,128)S(1)}, s32[4,16]{1,0:T(4,128)}, u32[]{:S(2)}) copy-start(s32[4,16]{1,0:T(4,128)} %param.27) | copy-start | bytes 772
  249.6 28.9 %all-to-all-start = ((bf16[16,64,2,512]{3,1,2,0:T(8,128)(2,1)}), bf16[16,64,2,512]{3,1,2,0:T(8,128)(2,1)S(1)}, u32[]{:S(2)}, u32[]{:S(2)}) async-start(bf16[16,64,2,512]{3,1,2,0:T(8,128)(2,1)} %broadcast_select_fusion.1), calls=%async_computation.1 | async-start | bytes 4194304 | tf_op jit(solution)/shard_map/all_to_all | solution.py:179
  280.4 7.3 %copy-start.1 = (bf16[512,2304]{1,0:T(8,128)(2,1)S(1)}, bf16[512,2304]{1,0:T(8,128)(2,1)}, u32[]{:S(2)}) copy-start(bf16[512,2304]{1,0:T(8,128)(2,1)} %param.18) | copy-start | bytes 7077892
Sparse Core Ops, SparseCore 0:
  43.2 57.9 all-reduce.2
  105.5 56.6 all-gather.1
  195.1 47.2 reduce-scatter.6
  248.1 29.2 reduce-scatter.4

commit v2 on v1

--- a/solution.py
+++ b/solution.py
@@ -45,6 +45,45 @@
     dispatch = jnp.sum(places, axis=-3)
     combine = jnp.sum(places * weights[..., None, None], axis=-3)
     return (dispatch, combine)
+
+
+def hand_over_pages(kv_cache, lengths, block_owner, block_slot):
+    dev_index = lax.axis_index("dev")
+    req_index = lax.axis_index("req")
+    owners_total = lax.axis_size("req")
+    block_total = block_owner.shape[1]
+    finished_total = block_owner.shape[0]
+    per_owner = block_total // owners_total
+    block_ids = jnp.arange(block_total, dtype=jnp.int32)
+    same_owner = block_owner[:, :, None] == block_owner[:, None, :]
+    before_mask = block_ids[None, :] < block_ids[:, None]
+    page_rank = jnp.sum((same_owner & before_mask[None]).astype(jnp.int32), axis=2)
+    own_owner = lax.dynamic_index_in_dim(block_owner, req_index, 0, keepdims=False)
+    own_rank = lax.dynamic_index_in_dim(page_rank, req_index, 0, keepdims=False)
+    dest_place = own_owner * per_owner + own_rank
+    source_block = jnp.sum(
+        jnp.where(dest_place[None, :] == block_ids[:, None], block_ids[None, :], 0), axis=1
+    )
+    page_half = kv_cache.shape[2]
+    page_size = page_half * lax.axis_size("dev")
+    token_pos = (
+        block_ids[:, None] * page_size
+        + dev_index * page_half
+        + jnp.arange(page_half, dtype=jnp.int32)[None, :]
+    )
+    own_length = lax.dynamic_index_in_dim(lengths, req_index, 0, keepdims=False)
+    live_cache = jnp.where(
+        (token_pos < own_length)[:, :, None, None], kv_cache[0], jnp.zeros((), jnp.bfloat16)
+    )
+    outgoing = jnp.take(live_cache, source_block, axis=0)
+    received = lax.all_to_all(outgoing, "req", split_axis=0, concat_axis=0, tiled=True)
+    request_ids = jnp.arange(finished_total, dtype=jnp.int32)
+    arrive_place = request_ids[:, None] * per_owner + page_rank
+    own_blocks = block_owner == req_index
+    slot_match = own_blocks[None] & (block_slot[None] == block_ids[:, None, None])
+    gather_place = jnp.sum(jnp.where(slot_match, arrive_place[None], 0), axis=(1, 2))
+    page_pool = jnp.take(received, gather_place, axis=0)
+    return page_pool
 
 
 def body(
@@ -101,6 +140,8 @@
     )
     attended = attended.astype(jnp.bfloat16).reshape(half_rows, local_cols)
     partial_value = jnp.dot(attended, w_out, preferred_element_type=jnp.float32)
+    page_pool = hand_over_pages(kv_cache, lengths, block_owner, block_slot)
+    partial_value, page_pool = lax.optimization_barrier((partial_value, page_pool))
     attn_mixed = lax.psum(partial_value.astype(jnp.bfloat16), "head").astype(jnp.float32)
     residual = (tokens[0].astype(jnp.float32) + attn_mixed).astype(jnp.bfloat16)
     moe_in = norm_rows(residual, moe_gain)
@@ -150,39 +191,6 @@
         .astype(jnp.bfloat16)
         .reshape(1, 1, rows_out, model_width)
     )
-    owners_total = lax.axis_size("req")
-    block_total = block_owner.shape[1]
-    finished_total = block_owner.shape[0]
-    per_owner = block_total // owners_total
-    block_ids = jnp.arange(block_total, dtype=jnp.int32)
-    same_owner = block_owner[:, :, None] == block_owner[:, None, :]
-    before_mask = block_ids[None, :] < block_ids[:, None]
-    page_rank = jnp.sum((same_owner & before_mask[None]).astype(jnp.int32), axis=2)
-    own_owner = lax.dynamic_index_in_dim(block_owner, req_index, 0, keepdims=False)
-    own_rank = lax.dynamic_index_in_dim(page_rank, req_index, 0, keepdims=False)
-    dest_place = own_owner * per_owner + own_rank
-    source_block = jnp.sum(
-        jnp.where(dest_place[None, :] == block_ids[:, None], block_ids[None, :], 0), axis=1
-    )
-    page_half = kv_cache.shape[2]
-    page_size = page_half * lax.axis_size("dev")
-    token_pos = (
-        block_ids[:, None] * page_size
-        + dev_index * page_half
-        + jnp.arange(page_half, dtype=jnp.int32)[None, :]
-    )
-    own_length = lax.dynamic_index_in_dim(lengths, req_index, 0, keepdims=False)
-    live_cache = jnp.where(
-        (token_pos < own_length)[:, :, None, None], kv_cache[0], jnp.zeros((), jnp.bfloat16)
-    )
-    outgoing = jnp.take(live_cache, source_block, axis=0)
-    received = lax.all_to_all(outgoing, "req", split_axis=0, concat_axis=0, tiled=True)
-    request_ids = jnp.arange(finished_total, dtype=jnp.int32)
-    arrive_place = request_ids[:, None] * per_owner + page_rank
-    own_blocks = block_owner == req_index
-    slot_match = own_blocks[None] & (block_slot[None] == block_ids[:, None, None])
-    gather_place = jnp.sum(jnp.where(slot_match, arrive_place[None], 0), axis=(1, 2))
-    page_pool = jnp.take(received, gather_place, axis=0)
     return (layer_out, page_pool)
 
 

time: 295 us -> 303 us (1.027)
  waiting for transfers between devices: 174 us -> 179 us
  other arithmetic: 22.4 us -> 26.8 us
    all_to_all x1, waiting for transfers between devices: 24.6 us -> 0.01 us  [hand_over_pages(): lax.all_to_all(outgoing, 'req', split_axis=0, concat_axis=0, tiled=True)]
    reduce_scatter x1, waiting for transfers between devices: 0.01 us -> 24.1 us  [body(): lax.psum_scatter(moe_out.astype(jnp.bfloat16), 'head', scatter_dimension=...]
    unnamed x5, waiting for transfers between devices: 40.1 us -> 46.2 us
    unnamed x33 -> x25, local copies, waits for them, and re-layouts: 17 us -> 16.2 us
  transfers between devices with their start and end apart: 7 -> 7, of which waited for: 4 -> 4; matrix products, arithmetic and copies ran while one was open for 9% -> 13% of each run, Pallas kernels for 0% -> 0%
where the time goes in v2:
time: 303 us
  waiting for transfers between devices  179 us (59%)
  matrix products  43.6 us (14%)
  local copies, waits for them, and re-layouts  28.5 us (9%)
  other arithmetic  26.8 us (9%)
  between operations  14 us (5%)
  starting transfers between devices  10.2 us (3%)
    psum x1, waiting for transfers between devices, body(): lax.psum(partial_value.astype(jnp.bfloat16), 'head').astype(jnp.float32)  58.2 us
    all_gather x1, waiting for transfers between devices, body(): all_rows_here = lax.all_gather(moe_in, 'req', axis=0, tiled=True)  50.9 us
    unnamed x5, waiting for transfers between devices  46.2 us
    reduce_scatter x1, waiting for transfers between devices, body(): lax.psum_scatter(moe_out.astype(jnp.bfloat16), 'head', scatter_dimension=...  24.1 us
    dot_general x1, matrix products, body(): jnp.einsum('ned,egdf->gnef', picked_all, w_gate_up, preferred_element_typ...  17.8 us
    unnamed x25, local copies, waits for them, and re-layouts  16.2 us
    dot_general x1, matrix products, body(): jnp.einsum('nef,efd->ned', hidden_all, w_down, preferred_element_type=jnp...  8.91 us
  transfers between devices with their start and end apart: 7, of which 4 were waited for; matrix products, arithmetic and copies ran while one was open for 13% of the time, Pallas kernels for 0%

profile of v2, /device:TPU:0, one launch (start us, length us, event | category | flops | bytes accessed | tf_op | source)
XLA Modules:
  0.0 302.5 jit_solution(10670408887446175535)
XLA Ops:
  7.2 1.1 convert_reduce_fusion
  8.3 0.7 fusion.57
  9.0 0.1 select_reduce_fusion.2
  9.1 1.2 dynamic_slice.21
  10.4 0.7 add_compare_fusion
  11.1 3.2 %bitcast_select_fusion = bf16[16,64,2,512]{3,1,2,0:T(8,128)(2,1)} fusion(bf16[1,16,64,2,512]{4,3,2,1,0:T(2,128)(2,1)} %param.24, pred[16,64]{1,0:T(8,128)(4,1)S(1)} %add_compare_fusion), kind=kLoop, calls=%fused_computation.30 | loop fusion | flops 1048576 | bytes 4195328 | tf_op jit(solution)/shard_map/jit(_where)/select_n | solution.py:75
  14.3 3.6 %gather_fusion = bf16[16,64,2,512]{3,1,2,0:T(8,128)(2,1)} fusion(bf16[16,64,2,512]{3,1,2,0:T(8,128)(2,1)} %bitcast_select_fusion, s32[1024]{0:T(1024)S(1)} %pad_clamp_fusion.1), kind=kCustom, calls=%fused_computation.clone | custom fusion | bytes 4194368 | tf_op jit(solution)/shard_map/jit(_take)/gather | solution.py:78
  18.0 3.2 %broadcast_select_fusion.1 = bf16[16,64,2,512]{3,1,2,0:T(8,128)(2,1)} fusion(bf16[16,64,2,512]{3,1,2,0:T(8,128)(2,1)} %gather_fusion, pred[16]{0:T(512)(128)(4,1)S(1)} %compare_and_fusion.2), kind=kLoop, calls=%fused_computation.33 | loop fusion | flops 1048576 | bytes 4194320 | tf_op jit(solution)/shard_map/jit(_take)/select_n | solution.py:78
  21.1 5.3 %all-to-all-start = ((bf16[16,64,2,512]{3,1,2,0:T(8,128)(2,1)}), bf16[16,64,2,512]{3,1,2,0:T(8,128)(2,1)}, u32[]{:S(2)}, u32[]{:S(2)}) async-start(bf16[16,64,2,512]{3,1,2,0:T(8,128)(2,1)} %broadcast_select_fusion.1), calls=%async_computation | async-start | bytes 4194304 | tf_op jit(solution)/shard_map/all_to_all | solution.py:79
  26.4 0.3 fusion.11
  26.8 9.7 %copy.59 = bf16[2304,3,512]{0,2,1:T(8,128)(2,1)} copy(bf16[2304,3,512]{2,0,1:T(8,128)(2,1)} %param.17) | data formatting | bytes 14155776 | tf_op args[2]
  36.5 5.2 %fusion.26 = f32[256,3,8,64]{0,3,2,1:T(8,128)S(1)} fusion(bf16[3,8,64,2304]{3,2,1,0:T(8,128)(2,1)} %bitcast.104, bf16[1,256,2304]{2,1,0:T(8,128)(2,1)S(1)} %copy-done.3, f32[2304]{0:T(1024)} %param.16, f32[256]{0:T(256)S(1)} %add_rsqrt_fusion.1), kind=kOutput, calls=%fused_computation.42 | convolution fusion | flops 1814298624 | bytes 9840640 | tf_op jit(solution)/shard_map/dot_general | solution.py:112
  41.7 0.1 slice_bitcast_fusion.3
  41.8 0.2 multiply_cosine_fusion
  42.0 0.9 subtract_convert_fusion.1
  42.9 0.8 pad_maximum_fusion
  43.6 2.4 collective-permute-start.1
  46.0 0.7 fusion.47
  46.8 2.0 collective-permute-start
  48.8 0.5 iota_multiply_fusion
  49.3 0.7 broadcast_add_fusion.1
  50.0 0.1 select_reduce_fusion.1
  50.2 0.2 compare_and_fusion
  50.4 2.1 fusion.3
  52.5 1.3 fusion.4
  53.8 2.2 fusion.33
  56.1 1.8 fusion.65
  57.9 2.3 gather_fusion.1
  60.2 1.6 broadcast_select_fusion
  61.8 0.0 all-reduce.3.cloned.1.call-update
  61.8 0.0 all-gather.2.cloned.1.call-start
  61.9 58.2 %all-reduce.3.cloned.1.call-done = bf16[256,2304]{1,0:T(8,128)(2,1)} async-done(((bf16[256,2304]{1,0:T(8,128)(2,1)}), bf16[256,2304]{1,0:T(8,128)(2,1)}) %all-reduce.3.cloned.1.call-update) | async-done | bytes 1179664 | tf_op jit(solution)/shard_map/psum | solution.py:145
  120.1 1.8 fusion.8
  121.9 1.0 copy-done.2
  122.9 1.3 fusion.10
  124.2 0.0 all-gather.2.cloned.1.call-update
  124.2 0.2 reduce-scatter.7.cloned.1.call-start
  124.5 0.2 copy.61
  124.7 0.1 copy.62
  124.8 0.1 compare_convert_fusion.1
  124.9 2.4 reduce-window.6
  127.3 0.2 slice_reduce_fusion
  127.4 0.7 reduce-window.9
  128.2 0.1 broadcast_add_fusion
  128.2 0.2 copy.73
  128.5 0.1 bitcast_subtract_fusion
  128.6 0.2 copy.65
  128.8 0.1 compare_convert_fusion
  128.9 1.2 select_reduce_fusion
  130.1 50.9 %all-gather.2.cloned.1.call-done = bf16[1024,2304]{1,0:T(8,128)(2,1)} async-done(((bf16[256,2304]{1,0:T(8,128)(2,1)}), bf16[1024,2304]{1,0:T(8,128)(2,1)}) %all-gather.2.cloned.1.call-update) | async-done | bytes 4718608 | tf_op jit(solution)/shard_map/all_gather | solution.py:152
  181.0 3.4 %fusion.66 = f32[4,2304,192]{1,2,0:S(1)} fusion(bf16[4,256,192]{1,2,0:T(8,128)(2,1)S(1)} %bitcast.110, bf16[4,256,2304]{2,1,0:T(8,128)(2,1)} %bitcast.105), kind=kOutput, calls=%fused_computation.120 | convolution fusion | flops 905969664 | bytes 12189696
  184.4 0.4 convert_bitcast_fusion
  184.8 0.2 copy.66
  185.0 17.8 %convolution_bitcast_fusion = f32[2,384,2,1440]{1,3,0,2:T(8,128)S(1)} fusion(bf16[384,2,2304,1]{2,0,3,1:T(8,128)(2,1)S(1)} %bitcast.102, bf16[2,2,2304,1440]{2,3,1,0:T(8,128)(2,1)} %param.22), kind=kOutput, calls=%fused_computation.2 | convolution fusion | flops 10192158720 | bytes 38928384 | tf_op jit(solution)/shard_map/ned,egdf->gnef/dot_general | solution.py:166
  202.8 8.9 %convolution_convert_fusion = bf16[2,384,2304]{2,1,0:T(8,128)(2,1)S(1)} fusion(bf16[2,1440,2304]{2,1,0:T(8,128)(2,1)} %param.23, f32[2,384,2,1440]{1,3,0,2:T(8,128)S(1)} %convolution_bitcast_fusion), kind=kOutput, calls=%fused_computation.3 | convolution fusion | flops 5104484352 | bytes 25657344 | tf_op jit(solution)/shard_map/nef,efd->ned/dot_general | solution.py:169
  211.7 2.0 copy.68
  213.8 0.3 reduce-scatter.5.cloned.1.call-start
  214.0 1.0 dynamic-slice_reduce_fusion
  215.0 46.1 %reduce-scatter.7.cloned.1.call-done = bf16[1,96,2,2304]{3,1,2,0:T(8,128)(2,1)} async-done(((bf16[4,96,2,2304]{3,1,2,0:T(8,128)(2,1)}), bf16[1,96,2,2304]{3,1,2,0:T(8,128)(2,1)}) %reduce-scatter.7.cloned.1.call-update) | async-done | bytes 884752
  261.1 2.1 fusion.20
  263.2 1.5 copy.69
  264.8 5.2 %copy.70 = bf16[16,64,2,512]{3,2,1,0:T(2,128)(2,1)} copy(bf16[16,64,2,512]{3,1,2,0:T(8,128)(2,1)} %broadcast_select_fusion) | data formatting | bytes 4194304
  270.0 24.1 %reduce-scatter.5.cloned.1.call-done = bf16[64,2304]{1,0:T(8,128)(2,1)} async-done(((bf16[256,2304]{1,0:T(8,128)(2,1)}), bf16[64,2304]{1,0:T(8,128)(2,1)}) %reduce-scatter.5.cloned.1.call-update) | async-done | bytes 294928 | tf_op jit(solution)/shard_map/reduce_scatter | solution.py:184
  294.1 1.8 fusion.46
  (44 shorter events, 0.2 us)
Async XLA Ops:
  7.2 48.9 %copy-start = (bf16[512,2304]{1,0:T(8,128)(2,1)S(1)}, bf16[512,2304]{1,0:T(8,128)(2,1)}, u32[]{:S(2)}) copy-start(bf16[512,2304]{1,0:T(8,128)(2,1)} %param.18) | copy-start | bytes 7077892
  21.1 5.3 %copy-start.3 = (bf16[1,256,2304]{2,1,0:T(8,128)(2,1)S(1)}, bf16[1,256,2304]{2,1,0:T(8,128)(2,1)}, u32[]{:S(2)}) copy-start(bf16[1,256,2304]{2,1,0:T(8,128)(2,1)} %param.15) | copy-start | bytes 3538948
  21.1 36.8 %all-to-all-start = ((bf16[16,64,2,512]{3,1,2,0:T(8,128)(2,1)}), bf16[16,64,2,512]{3,1,2,0:T(8,128)(2,1)}, u32[]{:S(2)}, u32[]{:S(2)}) async-start(bf16[16,64,2,512]{3,1,2,0:T(8,128)(2,1)} %broadcast_select_fusion.1), calls=%async_computation | async-start | bytes 4194304 | tf_op jit(solution)/shard_map/all_to_all | solution.py:79
  26.4 93.6 %all-reduce.3.cloned.1.call-start = ((), (), s32[]{:S(2)}) async-start(), calls=%async_computation.3 | async-start | bytes 2359296 | tf_op jit(solution)/shard_map/psum | solution.py:145
  41.7 7.1 %copy-start.7 = (s32[4,16]{1,0:T(4,128)S(1)}, s32[4,16]{1,0:T(4,128)}, u32[]{:S(2)}) copy-start(s32[4,16]{1,0:T(4,128)} %param.26) | copy-start | bytes 772
  41.7 8.3 %copy-start.10 = (s32[4,16]{1,0:T(4,128)S(1)}, s32[4,16]{1,0:T(4,128)}, u32[]{:S(2)}) copy-start(s32[4,16]{1,0:T(4,128)} %param.27) | copy-start | bytes 772
  42.9 3.9 %copy-start.4 = (bf16[256,8,32]{0,2,1:T(8,128)(2,1)}, bf16[256,8,32]{0,2,1:T(8,128)(2,1)S(1)}, u32[]{:S(2)}) copy-start(bf16[256,8,32]{0,2,1:T(8,128)(2,1)S(1)} %get-tuple-element.25) | copy-start | bytes 393220
  42.9 5.9 %copy-start.5 = (bf16[256,8,32]{0,2,1:T(8,128)(2,1)}, bf16[256,8,32]{0,2,1:T(8,128)(2,1)S(1)}, u32[]{:S(2)}) copy-start(bf16[256,8,32]{0,2,1:T(8,128)(2,1)S(1)} %get-tuple-element.26) | copy-start | bytes 393220
  43.6 6.7 %collective-permute-start.1 = (bf16[256,8,64]{0,2,1:T(8,128)(2,1)}, bf16[256,8,64]{0,2,1:T(8,128)(2,1)}, u32[]{:S(2)}, u32[]{:S(2)}) collective-permute-start(bf16[256,8,64]{0,2,1:T(8,128)(2,1)} %pad_maximum_fusion), channel_id=1, source_target_pairs={{0,1},{2,3},{4,5},{6,7},{8,9},{10,11},{12,13},{14,15},{16,17},{18,... | collective-permute-start | bytes 786440 | tf_op jit(solution)/shard_map/ppermute | solution.py:13
  46.8 7.1 %collective-permute-start = (bf16[256,8,64]{0,2,1:T(8,128)(2,1)}, bf16[256,8,64]{0,2,1:T(8,128)(2,1)}, u32[]{:S(2)}, u32[]{:S(2)}) collective-permute-start(bf16[256,8,64]{0,2,1:T(8,128)(2,1)} %fusion.47), channel_id=1, source_target_pairs={{0,1},{2,3},{4,5},{6,7},{8,9},{10,11},{12,13},{14,15},{16,17},{18,... | collective-permute-start | bytes 786440 | tf_op jit(solution)/shard_map/ppermute | solution.py:13
  61.8 61.1 %copy-start.8 = (f32[2304]{0:T(1024)S(1)}, f32[2304]{0:T(1024)}, u32[]{:S(2)}) copy-start(f32[2304]{0:T(1024)} %param.19) | copy-start | bytes 27652
  61.8 119.2 %all-gather.2.cloned.1.call-start = ((), (), s32[]{:S(2)}) async-start(), calls=%async_computation.4 | async-start | bytes 5898240 | tf_op jit(solution)/shard_map/all_gather | solution.py:152
  121.9 1.0 copy-start.2
  121.9 2.6 copy-start.6
  124.2 4.7 %copy-start.9 = (f32[4,256,2]{1,2,0:T(2,128)S(1)}, f32[4,256,2]{1,2,0:T(2,128)}, u32[]{:S(2)}) copy-start(f32[4,256,2]{1,2,0:T(2,128)} %param.21) | copy-start | bytes 24580
  124.2 136.9 %reduce-scatter.7.cloned.1.call-start = ((), (), s32[]{:S(2)}) async-start(), calls=%async_computation.6 | async-start | bytes 4423680
  213.8 80.4 %reduce-scatter.5.cloned.1.call-start = ((), (), s32[]{:S(2)}) async-start(), calls=%async_computation.5 | async-start | bytes 1474560 | tf_op jit(solution)/shard_map/reduce_scatter | solution.py:184
  264.8 31.2 %copy-start.1 = (bf16[512,2304]{1,0:T(8,128)(2,1)S(1)}, bf16[512,2304]{1,0:T(8,128)(2,1)}, u32[]{:S(2)}) copy-start(bf16[512,2304]{1,0:T(8,128)(2,1)} %param.18) | copy-start | bytes 7077892
Sparse Core Ops, SparseCore 0:
  62.0 58.0 all-reduce.2
  124.4 56.6 all-gather.1
  213.9 47.2 reduce-scatter.6
  264.9 29.1 reduce-scatter.4

commit v3 on v1

--- a/solution.py
+++ b/solution.py
@@ -101,14 +101,18 @@
     )
     attended = attended.astype(jnp.bfloat16).reshape(half_rows, local_cols)
     partial_value = jnp.dot(attended, w_out, preferred_element_type=jnp.float32)
-    attn_mixed = lax.psum(partial_value.astype(jnp.bfloat16), "head").astype(jnp.float32)
-    residual = (tokens[0].astype(jnp.float32) + attn_mixed).astype(jnp.bfloat16)
-    moe_in = norm_rows(residual, moe_gain)
+    attn_mixed = lax.psum_scatter(
+        partial_value.astype(jnp.bfloat16), "head", scatter_dimension=0, tiled=True
+    ).astype(jnp.float32)
+    rows_out = attn_mixed.shape[0]
+    own_tokens = lax.dynamic_slice_in_dim(tokens[0], head_index * rows_out, rows_out, 0)
+    kept_rows = (own_tokens.astype(jnp.float32) + attn_mixed).astype(jnp.bfloat16)
+    moe_in = norm_rows(kept_rows, moe_gain)
     experts_here = w_gate_up.shape[0]
     first_expert = head_index * experts_here
     top_count = routes.shape[2]
     capacity = half_rows * top_count * 3 // (2 * EXPERTS)
-    all_rows_here = lax.all_gather(moe_in, "req", axis=0, tiled=True)
+    all_rows_here = lax.all_gather(moe_in, ("req", "head"), axis=0, tiled=True)
     sources = all_rows_here.shape[0] // half_rows
     every_dispatch, every_combine = slot_tables(
         routes, route_weight, first_expert, experts_here, capacity
@@ -143,8 +147,6 @@
     summed = lax.psum_scatter(
         moe_out.astype(jnp.bfloat16), "head", scatter_dimension=0, tiled=True
     ).astype(jnp.float32)
-    rows_out = summed.shape[0]
-    kept_rows = lax.dynamic_slice_in_dim(residual, head_index * rows_out, rows_out, 0)
     layer_out = (
         (kept_rows.astype(jnp.float32) + summed)
         .astype(jnp.bfloat16)

time: 295 us -> 283 us (0.959)
  waiting for transfers between devices: 174 us -> 169 us
  other arithmetic: 22.4 us -> 19.3 us
    psum x1 -> x0, waiting for transfers between devices: 58.1 us -> none  [body(): lax.psum(partial_value.astype(jnp.bfloat16), 'head').astype(jnp.float32)]
    reduce_scatter x0 -> x1, waiting for transfers between devices: none -> 31.4 us  [body(): lax.psum_scatter(partial_value.astype(jnp.bfloat16), 'head', scatter_dime...]
    all_gather x1, waiting for transfers between devices: 51 us -> 74.6 us  [body(): all_rows_here = lax.all_gather(moe_in, ('req', 'head'), axis=0, tiled=True)]
    unnamed x33 -> x29, local copies, waits for them, and re-layouts: 17 us -> 15.9 us
where the time goes in v3:
time: 283 us; the launch traced here: 282 us
  waiting for transfers between devices  169 us (60%)
  matrix products  43.7 us (15%)
  local copies, waits for them, and re-layouts  27.5 us (10%)
  other arithmetic  19.3 us (7%)
  between operations  14.1 us (5%)
  starting transfers between devices  8.54 us (3%)
    all_gather x1, waiting for transfers between devices, body(): all_rows_here = lax.all_gather(moe_in, ('req', 'head'), axis=0, tiled=True)  74.6 us
    unnamed x5, waiting for transfers between devices  38.6 us
    reduce_scatter x1, waiting for transfers between devices, body(): lax.psum_scatter(partial_value.astype(jnp.bfloat16), 'head', scatter_dime...  31.4 us
    all_to_all x1, waiting for transfers between devices, body(): lax.all_to_all(outgoing, 'req', split_axis=0, concat_axis=0, tiled=True)  24.7 us
    dot_general x1, matrix products, body(): jnp.einsum('ned,egdf->gnef', picked_all, w_gate_up, preferred_element_typ...  17.8 us
    unnamed x29, local copies, waits for them, and re-layouts  15.9 us
    dot_general x1, matrix products, body(): jnp.einsum('nef,efd->ned', hidden_all, w_down, preferred_element_type=jnp...  8.91 us
  transfers between devices with their start and end apart: 7, of which 4 were waited for; matrix products, arithmetic and copies ran while one was open for 9% of the time, Pallas kernels for 0%

profile of v3, /device:TPU:0, one launch (start us, length us, event | category | flops | bytes accessed | tf_op | source)
XLA Modules:
  0.0 282.3 jit_solution(15806705674773563939)
XLA Ops:
  7.2 0.0 reduce-scatter.6.cloned.1.call-start
  7.3 9.9 %copy.59 = bf16[2304,3,512]{0,2,1:T(8,128)(2,1)} copy(bf16[2304,3,512]{2,0,1:T(8,128)(2,1)} %param.17) | data formatting | bytes 14155776 | tf_op args[2]
  17.1 0.3 fusion.6
  17.5 5.2 %fusion.20 = f32[256,3,8,64]{0,3,2,1:T(8,128)S(1)} fusion(bf16[3,8,64,2304]{3,2,1,0:T(8,128)(2,1)} %bitcast.97, bf16[1,256,2304]{2,1,0:T(8,128)(2,1)S(1)} %copy-done.3, f32[2304]{0:T(1024)S(1)} %copy-done.11, f32[256]{0:T(256)S(1)} %add_rsqrt_fusion), kind=kOutput, calls=%fused_computation.35 | convolution fusion | flops 1814298624 | bytes 9840640 | tf_op jit(solution)/shard_map/dot_general | solution.py:73
  22.7 1.1 copy-done.4
  23.8 0.1 slice_bitcast_fusion.3
  23.9 0.2 multiply_cosine_fusion
  24.1 0.9 subtract_convert_fusion.1
  25.0 0.6 copy-done.5
  25.6 3.1 %collective-permute-start.1 = (bf16[256,8,64]{0,2,1:T(8,128)(2,1)S(1)}, bf16[256,8,64]{0,2,1:T(8,128)(2,1)}, u32[]{:S(2)}, u32[]{:S(2)}) collective-permute-start(bf16[256,8,64]{0,2,1:T(8,128)(2,1)S(1)} %pad_maximum_fusion), channel_id=1, source_target_pairs={{0,1},{2,3},{4,5},{6,7},{8,9},{10,11},{12,13},{14,15},{16,17},{18,... | collective-permute-start | bytes 786440 | tf_op jit(solution)/shard_map/ppermute | solution.py:13
  28.7 1.1 fusion.46
  29.8 1.3 collective-permute-start
  31.1 0.2 compare_and_fusion
  31.3 2.1 fusion.3
  33.4 1.3 fusion.4
  34.7 1.2 fusion.27
  35.9 1.8 convolution_convert_fusion.1
  37.7 0.0 reduce-scatter.6.cloned.1.call-update
  37.8 0.0 all-gather.2.cloned.1.call-start
  37.8 31.4 %reduce-scatter.6.cloned.1.call-done = bf16[64,2304]{1,0:T(8,128)(2,1)} async-done(((bf16[256,2304]{1,0:T(8,128)(2,1)}), bf16[64,2304]{1,0:T(8,128)(2,1)}) %reduce-scatter.6.cloned.1.call-update) | async-done | bytes 294928 | tf_op jit(solution)/shard_map/reduce_scatter | solution.py:104
  69.2 1.3 fusion.31
  70.5 0.9 fusion.33
  71.3 0.0 all-gather.2.cloned.1.call-update
  71.3 0.2 reduce-scatter.10.cloned.1.call-start
  71.6 0.2 copy.60
  71.8 0.1 copy.61
  71.9 0.1 compare_convert_fusion.1
  72.0 2.4 reduce-window.6
  74.4 0.2 slice_reduce_fusion
  74.5 0.7 reduce-window.9
  75.2 0.1 broadcast_add_fusion
  75.3 0.2 copy.73
  75.6 0.1 bitcast_subtract_fusion
  75.7 0.2 copy.64
  75.9 0.1 compare_convert_fusion
  76.0 1.2 select_reduce_fusion
  77.1 74.6 %all-gather.2.cloned.1.call-done = bf16[1024,2304]{1,0:T(8,128)(2,1)} async-done(((bf16[64,2304]{1,0:T(8,128)(2,1)}), bf16[1024,2304]{1,0:T(8,128)(2,1)}) %all-gather.2.cloned.1.call-update) | async-done | bytes 4718608 | tf_op jit(solution)/shard_map/all_gather | solution.py:115
  151.7 3.4 %fusion.64 = f32[4,2304,192]{1,2,0:S(1)} fusion(bf16[4,256,192]{1,2,0:T(8,128)(2,1)S(1)} %bitcast.103, bf16[4,256,2304]{2,1,0:T(8,128)(2,1)} %bitcast.98), kind=kOutput, calls=%fused_computation.120 | convolution fusion | flops 905969664 | bytes 12189696
  155.2 0.4 convert_bitcast_fusion
  155.5 0.2 copy.65
  155.8 17.8 %convolution_bitcast_fusion = f32[2,384,2,1440]{1,3,0,2:T(8,128)S(1)} fusion(bf16[384,2,2304,1]{2,0,3,1:T(8,128)(2,1)S(1)} %bitcast.95, bf16[2,2,2304,1440]{2,3,1,0:T(8,128)(2,1)} %param.22), kind=kOutput, calls=%fused_computation.2 | convolution fusion | flops 10192158720 | bytes 38928384 | tf_op jit(solution)/shard_map/ned,egdf->gnef/dot_general | solution.py:129
  173.6 8.9 %convolution_convert_fusion = bf16[2,384,2304]{2,1,0:T(8,128)(2,1)S(1)} fusion(bf16[2,1440,2304]{2,1,0:T(8,128)(2,1)} %param.23, f32[2,384,2,1440]{1,3,0,2:T(8,128)S(1)} %convolution_bitcast_fusion), kind=kOutput, calls=%fused_computation.3 | convolution fusion | flops 5104484352 | bytes 25657344 | tf_op jit(solution)/shard_map/nef,efd->ned/dot_general | solution.py:132
  182.5 2.0 copy.67
  184.5 0.0 reduce-scatter.8.cloned.1.call-start
  184.6 0.6 copy-done.12
  185.1 0.6 dynamic_slice.24
  185.7 0.2 convert_reduce_fusion
  186.0 0.1 select_reduce_fusion.2
  186.1 0.7 add_compare_fusion
  186.8 1.7 bitcast_select_fusion
  188.5 2.5 gather_fusion
  191.0 1.0 dynamic-slice_reduce_fusion
  192.0 38.5 %reduce-scatter.10.cloned.1.call-done = bf16[1,96,2,2304]{3,1,2,0:T(8,128)(2,1)} async-done(((bf16[4,96,2,2304]{3,1,2,0:T(8,128)(2,1)}), bf16[1,96,2,2304]{3,1,2,0:T(8,128)(2,1)}) %reduce-scatter.10.cloned.1.call-update) | async-done | bytes 884752
  230.5 3.3 %fusion.14 = bf16[256,2304]{0,1:T(8,128)(2,1)} fusion(f32[256,2]{0,1:T(2,128)S(1)} %dynamic-slice_reduce_fusion, bf16[1,96,2,2304]{3,1,2,0:T(8,128)(2,1)} %reduce-scatter.10.cloned.1.call-done, bf16[4,256,2,96]{1,3,2,0:T(8,128)(2,1)S(1)} %get-tuple-element.11, s32[]{:T(128)S(6)} %select_n.38), kind=kOutput, calls=%fused_computation.30 | convolution fusion | flops 228261888 | bytes 2164740 | tf_op jit(solution)/shard_map/tec,ced->ted/dot_general | solution.py:140
  233.8 2.4 copy.68
  236.2 1.6 broadcast_select_fusion.1
  237.8 3.8 %all-to-all-start = ((bf16[16,64,2,512]{3,1,2,0:T(8,128)(2,1)}), bf16[16,64,2,512]{3,1,2,0:T(8,128)(2,1)S(1)}, u32[]{:S(2)}, u32[]{:S(2)}) async-start(bf16[16,64,2,512]{3,1,2,0:T(8,128)(2,1)} %broadcast_select_fusion.1), calls=%async_computation.2 | async-start | bytes 4194304 | tf_op jit(solution)/shard_map/all_to_all | solution.py:181
  241.6 0.1 broadcast_add_fusion.1
  241.7 0.1 select_reduce_fusion.1
  241.9 24.7 %all-to-all-done = bf16[16,64,2,512]{3,1,2,0:T(8,128)(2,1)S(1)} async-done(((bf16[16,64,2,512]{3,1,2,0:T(8,128)(2,1)}), bf16[16,64,2,512]{3,1,2,0:T(8,128)(2,1)S(1)}, u32[]{:S(2)}, u32[]{:S(2)}) %all-to-all-start) | async-done | bytes 2097184 | tf_op jit(solution)/shard_map/all_to_all | solution.py:181
  266.5 2.0 gather_fusion.1
  268.5 2.0 broadcast_select_fusion
  270.5 3.5 %copy.70 = bf16[16,64,2,512]{3,2,1,0:T(2,128)(2,1)} copy(bf16[16,64,2,512]{3,1,2,0:T(8,128)(2,1)S(1)} %broadcast_select_fusion) | data formatting | bytes 4194304
  274.0 1.7 fusion.45
  (48 shorter events, 0.2 us)
Async XLA Ops:
  7.2 28.7 %copy-start = (bf16[512,2304]{1,0:T(8,128)(2,1)S(1)}, bf16[512,2304]{1,0:T(8,128)(2,1)}, u32[]{:S(2)}) copy-start(bf16[512,2304]{1,0:T(8,128)(2,1)} %param.18) | copy-start | bytes 7077892
  7.2 62.0 %reduce-scatter.6.cloned.1.call-start = ((), (), s32[]{:S(2)}) async-start(), calls=%async_computation.4 | async-start | bytes 1474560 | tf_op jit(solution)/shard_map/reduce_scatter | solution.py:104
  7.2 9.9 %copy-start.3 = (bf16[1,256,2304]{2,1,0:T(8,128)(2,1)S(1)}, bf16[1,256,2304]{2,1,0:T(8,128)(2,1)}, u32[]{:S(2)}) copy-start(bf16[1,256,2304]{2,1,0:T(8,128)(2,1)} %param.15) | copy-start | bytes 3538948
  7.3 10.2 %copy-start.11 = (f32[2304]{0:T(1024)S(1)}, f32[2304]{0:T(1024)}, u32[]{:S(2)}) copy-start(f32[2304]{0:T(1024)} %param.16) | copy-start | bytes 27652
  22.7 1.1 copy-start.4
  25.0 0.7 copy-start.5
  25.6 5.7 %collective-permute-start.1 = (bf16[256,8,64]{0,2,1:T(8,128)(2,1)S(1)}, bf16[256,8,64]{0,2,1:T(8,128)(2,1)}, u32[]{:S(2)}, u32[]{:S(2)}) collective-permute-start(bf16[256,8,64]{0,2,1:T(8,128)(2,1)S(1)} %pad_maximum_fusion), channel_id=1, source_target_pairs={{0,1},{2,3},{4,5},{6,7},{8,9},{10,11},{12,13},{14,15},{16,17},{18,... | collective-permute-start | bytes 786440 | tf_op jit(solution)/shard_map/ppermute | solution.py:13
  29.8 4.9 %collective-permute-start = (bf16[256,8,64]{0,2,1:T(8,128)(2,1)S(1)}, bf16[256,8,64]{0,2,1:T(8,128)(2,1)S(1)}, u32[]{:S(2)}, u32[]{:S(2)}) collective-permute-start(bf16[256,8,64]{0,2,1:T(8,128)(2,1)S(1)} %fusion.46), channel_id=1, source_target_pairs={{0,1},{2,3},{4,5},{6,7},{8,9},{10,11},{12,13},{14,15},{16,17},{18,... | collective-permute-start | bytes 786440 | tf_op jit(solution)/shard_map/ppermute | solution.py:13
  35.9 34.6 %copy-start.8 = (f32[2304]{0:T(1024)S(1)}, f32[2304]{0:T(1024)}, u32[]{:S(2)}) copy-start(f32[2304]{0:T(1024)} %param.19) | copy-start | bytes 27652
  35.9 35.7 %copy-start.6 = (s32[4,256,2]{1,2,0:T(2,128)S(1)}, s32[4,256,2]{1,2,0:T(2,128)}, u32[]{:S(2)}) copy-start(s32[4,256,2]{1,2,0:T(2,128)} %param.20) | copy-start | bytes 24580
  37.7 38.2 %copy-start.9 = (f32[4,256,2]{1,2,0:T(2,128)S(1)}, f32[4,256,2]{1,2,0:T(2,128)}, u32[]{:S(2)}) copy-start(f32[4,256,2]{1,2,0:T(2,128)} %param.21) | copy-start | bytes 24580
  37.8 114.0 %all-gather.2.cloned.1.call-start = ((), (), s32[]{:S(2)}) async-start(), calls=%async_computation.5 | async-start | bytes 5013504 | tf_op jit(solution)/shard_map/all_gather | solution.py:115
  71.3 159.2 %reduce-scatter.10.cloned.1.call-start = ((), (), s32[]{:S(2)}) async-start(), calls=%async_computation.7 | async-start | bytes 4423680
  184.5 0.7 copy-start.12
  184.5 1.3 copy-start.7
  184.5 2.3 copy-start.2
  184.5 89.5 %reduce-scatter.8.cloned.1.call-start = ((), (), s32[]{:S(2)}) async-start(), calls=%async_computation.6 | async-start | bytes 1474560 | tf_op jit(solution)/shard_map/reduce_scatter | solution.py:147
  236.2 5.5 %copy-start.10 = (s32[4,16]{1,0:T(4,128)S(1)}, s32[4,16]{1,0:T(4,128)}, u32[]{:S(2)}) copy-start(s32[4,16]{1,0:T(4,128)} %param.27) | copy-start | bytes 772
  237.8 28.7 %all-to-all-start = ((bf16[16,64,2,512]{3,1,2,0:T(8,128)(2,1)}), bf16[16,64,2,512]{3,1,2,0:T(8,128)(2,1)S(1)}, u32[]{:S(2)}, u32[]{:S(2)}) async-start(bf16[16,64,2,512]{3,1,2,0:T(8,128)(2,1)} %broadcast_select_fusion.1), calls=%async_computation.2 | async-start | bytes 4194304 | tf_op jit(solution)/shard_map/all_to_all | solution.py:181
  268.5 7.2 %copy-start.1 = (bf16[512,2304]{1,0:T(8,128)(2,1)S(1)}, bf16[512,2304]{1,0:T(8,128)(2,1)}, u32[]{:S(2)}) copy-start(bf16[512,2304]{1,0:T(8,128)(2,1)} %param.18) | copy-start | bytes 7077892
Sparse Core Ops, SparseCore 0:
  37.9 31.2 reduce-scatter.5
  72.5 79.1 all-gather.1
  184.6 45.8 reduce-scatter.9
  236.3 29.1 reduce-scatter.7

commit v4 on v3

--- a/solution.py
+++ b/solution.py
@@ -126,14 +126,21 @@
     picked_all = picked_all.astype(jnp.bfloat16).reshape(
         sources * capacity, experts_here, model_width
     )
-    both = jnp.einsum("ned,egdf->gnef", picked_all, w_gate_up, preferred_element_type=jnp.float32)
-    hidden_all = (jax.nn.silu(both[0]) * both[1]).astype(jnp.bfloat16)
     source_count = half_rows * lax.axis_size("req") // half_rows
-    down_out = jnp.einsum("nef,efd->ned", hidden_all, w_down, preferred_element_type=jnp.float32)
-    down_out = down_out.astype(jnp.bfloat16).reshape(
-        source_count, capacity, experts_here, model_width
-    )
-    expert_back = lax.psum_scatter(down_out, "req", scatter_dimension=0, tiled=True)[0]
+    picked_all = picked_all.reshape(source_count, capacity, experts_here, model_width)
+    back_parts = []
+    for expert in range(experts_here):
+        rows_e = picked_all[:, :, expert].reshape(source_count * capacity, model_width)
+        both = jnp.einsum(
+            "nd,gdf->gnf", rows_e, w_gate_up[expert], preferred_element_type=jnp.float32
+        )
+        hidden_e = (jax.nn.silu(both[0]) * both[1]).astype(jnp.bfloat16)
+        down_e = jnp.dot(hidden_e, w_down[expert], preferred_element_type=jnp.float32)
+        down_e = down_e.astype(jnp.bfloat16).reshape(source_count, capacity, model_width)
+        back_parts.append(
+            lax.psum_scatter(down_e, "req", scatter_dimension=0, tiled=True)[0]
+        )
+    expert_back = jnp.stack(back_parts, axis=1)
     own_dispatch = lax.dynamic_index_in_dim(every_dispatch, req_index, 0, keepdims=False)
     own_combine = lax.dynamic_index_in_dim(every_combine, req_index, 0, keepdims=False)
     token_weights = jnp.sum(own_combine, axis=-1)

time: 283 us -> 290 us (1.025)
  matrix products: 43.7 us -> 49 us
  waiting for transfers between devices: 169 us -> 173 us
    dot_general x2 -> x4, matrix products: 26.7 us -> 32 us  [the longest x2 20.1 us: body(): jnp.einsum('nd,gdf->gnf', rows_e, w_gate_up[expert], preferred_element_ty...]
    unnamed x5 -> x7, waiting for transfers between devices: 38.6 us -> 42.5 us
    unnamed x29 -> x37, local copies, waits for them, and re-layouts: 15.9 us -> 15.4 us
  transfers between devices with their start and end apart: 7 -> 8, of which waited for: 4 -> 5; matrix products, arithmetic and copies ran while one was open for 9% -> 15% of each run, Pallas kernels for 0% -> 0%
where the time goes in v4:
time: 290 us; the launch traced here: 289 us
  waiting for transfers between devices  173 us (60%)
  matrix products  49 us (17%)
  local copies, waits for them, and re-layouts  24.7 us (9%)
  other arithmetic  19.3 us (7%)
  between operations  14.2 us (5%)
  starting transfers between devices  8.71 us (3%)
    all_gather x1, waiting for transfers between devices, body(): all_rows_here = lax.all_gather(moe_in, ('req', 'head'), axis=0, tiled=True)  74.6 us
    unnamed x7, waiting for transfers between devices  42.5 us
    reduce_scatter x1, waiting for transfers between devices, body(): lax.psum_scatter(partial_value.astype(jnp.bfloat16), 'head', scatter_dime...  31.4 us
    all_to_all x1, waiting for transfers between devices, body(): lax.all_to_all(outgoing, 'req', split_axis=0, concat_axis=0, tiled=True)  24.8 us
    dot_general x2, matrix products, body(): jnp.einsum('nd,gdf->gnf', rows_e, w_gate_up[expert], preferred_element_ty...  20.1 us
    unnamed x37, local copies, waits for them, and re-layouts  15.4 us
    dot_general x2, matrix products, body(): jnp.dot(hidden_e, w_down[expert], preferred_element_type=jnp.float32)  11.9 us
  transfers between devices with their start and end apart: 8, of which 5 were waited for; matrix products, arithmetic and copies ran while one was open for 15% of the time, Pallas kernels for 0%

profile of v4, /device:TPU:0, one launch (start us, length us, event | category | flops | bytes accessed | tf_op | source)
XLA Modules:
  0.0 289.2 jit_solution(5739601841685427996)
XLA Ops:
  7.2 0.0 reduce-scatter.9.cloned.1.call-start
  7.3 9.9 %copy.48 = bf16[2304,3,512]{0,2,1:T(8,128)(2,1)} copy(bf16[2304,3,512]{2,0,1:T(8,128)(2,1)} %param.17) | data formatting | bytes 14155776 | tf_op args[2]
  17.1 0.3 fusion.28
  17.5 5.2 %fusion.42 = f32[256,3,8,64]{0,3,2,1:T(8,128)S(1)} fusion(bf16[3,8,64,2304]{3,2,1,0:T(8,128)(2,1)} %bitcast.108, bf16[1,256,2304]{2,1,0:T(8,128)(2,1)S(1)} %copy-done.3, f32[2304]{0:T(1024)S(1)} %copy-done.11, f32[256]{0:T(256)S(1)} %add_rsqrt_fusion), kind=kOutput, calls=%fused_computation.48 | convolution fusion | flops 1814298624 | bytes 9840640 | tf_op jit(solution)/shard_map/dot_general | solution.py:73
  22.7 1.1 copy-done.4
  23.8 0.1 slice_bitcast_fusion.1
  23.9 0.2 multiply_cosine_fusion
  24.1 0.9 subtract_convert_fusion.1
  25.0 0.6 copy-done.5
  25.6 3.1 %collective-permute-start.1 = (bf16[256,8,64]{0,2,1:T(8,128)(2,1)S(1)}, bf16[256,8,64]{0,2,1:T(8,128)(2,1)}, u32[]{:S(2)}, u32[]{:S(2)}) collective-permute-start(bf16[256,8,64]{0,2,1:T(8,128)(2,1)S(1)} %pad_maximum_fusion), channel_id=1, source_target_pairs={{0,1},{2,3},{4,5},{6,7},{8,9},{10,11},{12,13},{14,15},{16,17},{18,... | collective-permute-start | bytes 786440 | tf_op jit(solution)/shard_map/ppermute | solution.py:13
  28.7 1.1 fusion.74
  29.8 1.3 collective-permute-start
  31.1 0.2 compare_and_fusion
  31.3 2.1 fusion.25
  33.4 1.3 fusion.26
  34.7 1.2 fusion.53
  35.9 1.8 convolution_convert_fusion
  37.8 0.0 all-gather.2.cloned.1.call-start
  37.8 31.4 %reduce-scatter.9.cloned.1.call-done = bf16[64,2304]{1,0:T(8,128)(2,1)} async-done(((bf16[256,2304]{1,0:T(8,128)(2,1)}), bf16[64,2304]{1,0:T(8,128)(2,1)}) %reduce-scatter.9.cloned.1.call-update) | async-done | bytes 294928 | tf_op jit(solution)/shard_map/reduce_scatter | solution.py:104
  69.2 1.3 fusion.59
  70.5 0.9 fusion.61
  71.3 0.2 reduce-scatter.15.cloned.1.call-start
  71.6 0.2 copy.49
  71.8 0.1 copy.50
  71.9 0.1 compare_convert_fusion.1
  71.9 2.4 reduce-window.6
  74.4 0.2 slice_reduce_fusion
  74.5 0.7 reduce-window.9
  75.2 0.1 broadcast_add_fusion
  75.3 0.2 copy.58
  75.6 0.1 bitcast_subtract_fusion
  75.7 0.2 copy.53
  75.9 0.1 compare_convert_fusion
  76.0 1.2 select_reduce_fusion
  77.1 74.6 %all-gather.2.cloned.1.call-done = bf16[1024,2304]{1,0:T(8,128)(2,1)} async-done(((bf16[64,2304]{1,0:T(8,128)(2,1)}), bf16[1024,2304]{1,0:T(8,128)(2,1)}) %all-gather.2.cloned.1.call-update) | async-done | bytes 4718608 | tf_op jit(solution)/shard_map/all_gather | solution.py:115
  151.7 3.4 %fusion.95 = f32[4,2304,192]{1,2,0:S(1)} fusion(bf16[4,256,192]{1,2,0:T(8,128)(2,1)S(1)} %bitcast.117, bf16[4,256,2304]{2,1,0:T(8,128)(2,1)} %bitcast.109), kind=kOutput, calls=%fused_computation.140 | convolution fusion | flops 905969664 | bytes 12189696
  155.2 0.4 convert_bitcast_fusion
  155.6 0.2 fusion.94
  155.8 10.4 %fusion.22 = f32[2,384,1440]{1,2,0:T(8,128)S(1)} fusion(bf16[384,2304,1]{1,0,2:T(8,128)(2,1)S(1)} %bitcast.114, bf16[2,2,2304,1440]{2,3,1,0:T(8,128)(2,1)} %param.22), kind=kOutput, calls=%fused_computation.22 | convolution fusion | flops 5096079360 | bytes 19464192 | tf_op jit(solution)/shard_map/nd,gdf->gnf/dot_general | solution.py:134
  166.3 4.3 %fusion.16 = bf16[384,2304]{1,0:T(8,128)(2,1)} fusion(bf16[2,1440,2304]{2,1,0:T(8,128)(2,1)S(1)} %bitcast.122, f32[2,384,1440]{1,2,0:T(8,128)S(1)} %fusion.22), kind=kOutput, calls=%fused_computation.17 | convolution fusion | flops 2552242176 | bytes 12828672 | tf_op jit(solution)/shard_map/dot_general | solution.py:138
  170.7 0.0 reduce-scatter.13.cloned.1.call-start
  170.7 9.7 %fusion.19 = f32[2,384,1440]{1,2,0:T(8,128)S(1)} fusion(bf16[384,2304,1]{1,0,2:T(8,128)(2,1)S(1)} %bitcast.113, bf16[2,2,2304,1440]{2,3,1,0:T(8,128)(2,1)} %param.22), kind=kOutput, calls=%fused_computation.21 | convolution fusion | flops 5096079360 | bytes 19464192 | tf_op jit(solution)/shard_map/nd,gdf->gnf/dot_general | solution.py:134
  180.5 7.5 %fusion.13 = bf16[384,2304]{1,0:T(8,128)(2,1)} fusion(bf16[2,1440,2304]{2,1,0:T(8,128)(2,1)} %param.23, f32[2,384,1440]{1,2,0:T(8,128)S(1)} %fusion.19), kind=kOutput, calls=%fused_computation.16 | convolution fusion | flops 2552242176 | bytes 12828672 | tf_op jit(solution)/shard_map/dot_general | solution.py:138
  188.0 0.3 reduce-scatter.11.cloned.1.call-start
  188.3 0.6 dynamic_slice.24
  188.9 0.2 convert_reduce_fusion
  189.1 0.1 select_reduce_fusion.2
  189.3 0.7 add_compare_fusion
  190.0 1.7 bitcast_select_fusion
  191.7 2.3 gather_fusion
  193.9 1.0 dynamic-slice_reduce_fusion
  194.9 7.0 %reduce-scatter.15.cloned.1.call-done = bf16[1,96,2304]{2,1,0:T(8,128)(2,1)} async-done(((bf16[4,96,2304]{2,1,0:T(8,128)(2,1)}), bf16[1,96,2304]{2,1,0:T(8,128)(2,1)}) %reduce-scatter.15.cloned.1.call-update) | async-done | bytes 442384
  201.9 35.4 %reduce-scatter.13.cloned.1.call-done = bf16[1,96,2304]{2,1,0:T(8,128)(2,1)} async-done(((bf16[4,96,2304]{2,1,0:T(8,128)(2,1)}), bf16[1,96,2304]{2,1,0:T(8,128)(2,1)}) %reduce-scatter.13.cloned.1.call-update) | async-done | bytes 442384
  237.3 3.3 %fusion.36 = bf16[256,2304]{0,1:T(8,128)(2,1)} fusion(f32[256,2]{0,1:T(2,128)S(1)} %dynamic-slice_reduce_fusion, bf16[96,1,2304]{2,0,1:T(8,128)(2,1)} %bitcast.123, bf16[96,1,2304]{2,0,1:T(8,128)(2,1)} %bitcast.124, bf16[4,256,2,96]{1,3,2,0:T(8,128)(2,1)S(1)} %get-tuple-element.11, s32[]{:T(128)S(6)} %select_n.38), kind=kOutput, calls=%fused_computation.43 | convolution fusion | flops 228704256 | bytes 2164740 | tf_op jit(solution)/shard_map/tec,ced->ted/dot_general | solution.py:147
  240.6 2.4 copy.54
  243.0 1.6 broadcast_select_fusion.1
  244.6 3.7 %all-to-all-start = ((bf16[16,64,2,512]{3,1,2,0:T(8,128)(2,1)}), bf16[16,64,2,512]{3,1,2,0:T(8,128)(2,1)S(1)}, u32[]{:S(2)}, u32[]{:S(2)}) async-start(bf16[16,64,2,512]{3,1,2,0:T(8,128)(2,1)} %broadcast_select_fusion.1), calls=%async_computation.2 | async-start | bytes 4194304 | tf_op jit(solution)/shard_map/all_to_all | solution.py:188
  248.4 0.1 broadcast_add_fusion.1
  248.4 0.1 select_reduce_fusion.1
  248.6 24.8 %all-to-all-done = bf16[16,64,2,512]{3,1,2,0:T(8,128)(2,1)S(1)} async-done(((bf16[16,64,2,512]{3,1,2,0:T(8,128)(2,1)}), bf16[16,64,2,512]{3,1,2,0:T(8,128)(2,1)S(1)}, u32[]{:S(2)}, u32[]{:S(2)}) %all-to-all-start) | async-done | bytes 2097184 | tf_op jit(solution)/shard_map/all_to_all | solution.py:188
  273.4 2.0 gather_fusion.1
  275.4 2.0 broadcast_select_fusion
  277.4 3.5 %copy.56 = bf16[16,64,2,512]{3,2,1,0:T(2,128)(2,1)} copy(bf16[16,64,2,512]{3,1,2,0:T(8,128)(2,1)S(1)} %broadcast_select_fusion) | data formatting | bytes 4194304
  280.9 1.7 fusion.73
  (61 shorter events, 0.3 us)
Async XLA Ops:
  7.2 28.7 %copy-start = (bf16[512,2304]{1,0:T(8,128)(2,1)S(1)}, bf16[512,2304]{1,0:T(8,128)(2,1)}, u32[]{:S(2)}) copy-start(bf16[512,2304]{1,0:T(8,128)(2,1)} %param.18) | copy-start | bytes 7077892
  7.2 62.0 %reduce-scatter.9.cloned.1.call-start = ((), (), s32[]{:S(2)}) async-start(), calls=%async_computation.5 | async-start | bytes 1474560 | tf_op jit(solution)/shard_map/reduce_scatter | solution.py:104
  7.2 9.9 %copy-start.3 = (bf16[1,256,2304]{2,1,0:T(8,128)(2,1)S(1)}, bf16[1,256,2304]{2,1,0:T(8,128)(2,1)}, u32[]{:S(2)}) copy-start(bf16[1,256,2304]{2,1,0:T(8,128)(2,1)} %param.15) | copy-start | bytes 3538948
  7.3 10.2 %copy-start.11 = (f32[2304]{0:T(1024)S(1)}, f32[2304]{0:T(1024)}, u32[]{:S(2)}) copy-start(f32[2304]{0:T(1024)} %param.16) | copy-start | bytes 27652
  22.7 1.1 copy-start.4
  25.0 0.7 copy-start.5
  25.6 5.7 %collective-permute-start.1 = (bf16[256,8,64]{0,2,1:T(8,128)(2,1)S(1)}, bf16[256,8,64]{0,2,1:T(8,128)(2,1)}, u32[]{:S(2)}, u32[]{:S(2)}) collective-permute-start(bf16[256,8,64]{0,2,1:T(8,128)(2,1)S(1)} %pad_maximum_fusion), channel_id=1, source_target_pairs={{0,1},{2,3},{4,5},{6,7},{8,9},{10,11},{12,13},{14,15},{16,17},{18,... | collective-permute-start | bytes 786440 | tf_op jit(solution)/shard_map/ppermute | solution.py:13
  29.8 4.9 %collective-permute-start = (bf16[256,8,64]{0,2,1:T(8,128)(2,1)S(1)}, bf16[256,8,64]{0,2,1:T(8,128)(2,1)S(1)}, u32[]{:S(2)}, u32[]{:S(2)}) collective-permute-start(bf16[256,8,64]{0,2,1:T(8,128)(2,1)S(1)} %fusion.74), channel_id=1, source_target_pairs={{0,1},{2,3},{4,5},{6,7},{8,9},{10,11},{12,13},{14,15},{16,17},{18,... | collective-permute-start | bytes 786440 | tf_op jit(solution)/shard_map/ppermute | solution.py:13
  35.9 34.6 %copy-start.8 = (f32[2304]{0:T(1024)S(1)}, f32[2304]{0:T(1024)}, u32[]{:S(2)}) copy-start(f32[2304]{0:T(1024)} %param.19) | copy-start | bytes 27652
  37.7 33.8 %copy-start.6 = (s32[4,256,2]{1,2,0:T(2,128)S(1)}, s32[4,256,2]{1,2,0:T(2,128)}, u32[]{:S(2)}) copy-start(s32[4,256,2]{1,2,0:T(2,128)} %param.20) | copy-start | bytes 24580
  37.8 114.0 %all-gather.2.cloned.1.call-start = ((), (), s32[]{:S(2)}) async-start(), calls=%async_computation.6 | async-start | bytes 5013504 | tf_op jit(solution)/shard_map/all_gather | solution.py:115
  70.4 5.6 %copy-start.9 = (f32[4,256,2]{1,2,0:T(2,128)S(1)}, f32[4,256,2]{1,2,0:T(2,128)}, u32[]{:S(2)}) copy-start(f32[4,256,2]{1,2,0:T(2,128)} %param.21) | copy-start | bytes 24580
  71.3 130.6 %reduce-scatter.15.cloned.1.call-start = ((), (), s32[]{:S(2)}) async-start(), calls=%async_computation.9 | async-start | bytes 2211840
  155.5 10.7 %slice-start = ((s8[13271040]{0:T(1024)(128)(4,1)}), s8[688128]{0:T(1024)(128)(4,1)S(1)}, s32[]{:S(2)}) async-start(s8[13271040]{0:T(1024)(128)(4,1)} %bitcast.121), calls=%async_computation.10 | async-start | bytes 1376256
  155.8 10.5 %slice-start.1 = ((s8[13271040]{0:T(1024)(128)(4,1)}), s8[4194304]{0:T(1024)(128)(4,1)S(1)}, s32[]{:S(2)}) async-start(s8[13271040]{0:T(1024)(128)(4,1)} %bitcast.121), calls=%async_computation.11 | async-start | bytes 8388608
  155.8 10.5 %slice-start.2 = ((s8[13271040]{0:T(1024)(128)(4,1)}), s8[4194304]{0:T(1024)(128)(4,1)S(1)}, s32[]{:S(2)}) async-start(s8[13271040]{0:T(1024)(128)(4,1)} %bitcast.121), calls=%async_computation.12 | async-start | bytes 8388608
  155.8 10.5 %slice-start.3 = ((s8[13271040]{0:T(1024)(128)(4,1)}), s8[4194304]{0:T(1024)(128)(4,1)S(1)}, s32[]{:S(2)}) async-start(s8[13271040]{0:T(1024)(128)(4,1)} %bitcast.121), calls=%async_computation.13 | async-start | bytes 8388608
  170.7 66.7 %reduce-scatter.13.cloned.1.call-start = ((), (), s32[]{:S(2)}) async-start(), calls=%async_computation.8 | async-start | bytes 2211840
  180.4 7.9 %copy-start.12 = (s32[4]{0:T(128)S(1)}, s32[4]{0:T(128)}, u32[]{:S(2)}) copy-start(s32[4]{0:T(128)} %param.25) | copy-start | bytes 52
  180.4 8.5 %copy-start.7 = (s32[4,16]{1,0:T(4,128)S(1)}, s32[4,16]{1,0:T(4,128)}, u32[]{:S(2)}) copy-start(s32[4,16]{1,0:T(4,128)} %param.26) | copy-start | bytes 772
  180.5 9.6 %copy-start.2 = (bf16[1,16,64,2,512]{4,3,2,1,0:T(2,128)(2,1)S(1)}, bf16[1,16,64,2,512]{4,3,2,1,0:T(2,128)(2,1)}, u32[]{:S(2)}) copy-start(bf16[1,16,64,2,512]{4,3,2,1,0:T(2,128)(2,1)} %param.24) | copy-start | bytes 6291460
  188.0 92.9 %reduce-scatter.11.cloned.1.call-start = ((), (), s32[]{:S(2)}) async-start(), calls=%async_computation.7 | async-start | bytes 1474560 | tf_op jit(solution)/shard_map/reduce_scatter | solution.py:154
  244.6 3.8 %copy-start.10 = (s32[4,16]{1,0:T(4,128)S(1)}, s32[4,16]{1,0:T(4,128)}, u32[]{:S(2)}) copy-start(s32[4,16]{1,0:T(4,128)} %param.27) | copy-start | bytes 772
  244.6 28.8 %all-to-all-start = ((bf16[16,64,2,512]{3,1,2,0:T(8,128)(2,1)}), bf16[16,64,2,512]{3,1,2,0:T(8,128)(2,1)S(1)}, u32[]{:S(2)}, u32[]{:S(2)}) async-start(bf16[16,64,2,512]{3,1,2,0:T(8,128)(2,1)} %broadcast_select_fusion.1), calls=%async_computation.2 | async-start | bytes 4194304 | tf_op jit(solution)/shard_map/all_to_all | solution.py:188
  275.4 7.2 %copy-start.1 = (bf16[512,2304]{1,0:T(8,128)(2,1)S(1)}, bf16[512,2304]{1,0:T(8,128)(2,1)}, u32[]{:S(2)}) copy-start(bf16[512,2304]{1,0:T(8,128)(2,1)} %param.18) | copy-start | bytes 7077892
Sparse Core Ops, SparseCore 0:
  37.9 31.2 reduce-scatter.8
  72.5 79.1 all-gather.1
  170.8 31.1 reduce-scatter.14
  204.8 32.4 reduce-scatter.12
  243.1 29.1 reduce-scatter.10

commit v5 on v1

--- a/solution.py
+++ b/solution.py
@@ -108,20 +108,20 @@
     first_expert = head_index * experts_here
     top_count = routes.shape[2]
     capacity = half_rows * top_count * 3 // (2 * EXPERTS)
-    all_rows_here = lax.all_gather(moe_in, "req", axis=0, tiled=True)
-    sources = all_rows_here.shape[0] // half_rows
-    every_dispatch, every_combine = slot_tables(
-        routes, route_weight, first_expert, experts_here, capacity
-    )
-    picked_all = jnp.einsum(
-        "stec,std->sced",
-        every_dispatch.astype(jnp.bfloat16),
-        all_rows_here.reshape(sources, half_rows, model_width),
+    own_routes = lax.dynamic_index_in_dim(routes, req_index, 0, keepdims=True)
+    own_weights = lax.dynamic_index_in_dim(route_weight, req_index, 0, keepdims=True)
+    own_dispatch, own_combine = slot_tables(
+        own_routes, own_weights, first_expert, experts_here, capacity
+    )
+    own_dispatch = own_dispatch[0]
+    own_combine = own_combine[0]
+    picked_own = jnp.einsum(
+        "tec,td->ced",
+        own_dispatch.astype(jnp.bfloat16),
+        moe_in,
         preferred_element_type=jnp.float32,
-    )
-    picked_all = picked_all.astype(jnp.bfloat16).reshape(
-        sources * capacity, experts_here, model_width
-    )
+    ).astype(jnp.bfloat16)
+    picked_all = lax.all_gather(picked_own, "req", axis=0, tiled=True)
     both = jnp.einsum("ned,egdf->gnef", picked_all, w_gate_up, preferred_element_type=jnp.float32)
     hidden_all = (jax.nn.silu(both[0]) * both[1]).astype(jnp.bfloat16)
     source_count = half_rows * lax.axis_size("req") // half_rows
@@ -130,8 +130,6 @@
         source_count, capacity, experts_here, model_width
     )
     expert_back = lax.psum_scatter(down_out, "req", scatter_dimension=0, tiled=True)[0]
-    own_dispatch = lax.dynamic_index_in_dim(every_dispatch, req_index, 0, keepdims=False)
-    own_combine = lax.dynamic_index_in_dim(every_combine, req_index, 0, keepdims=False)
     token_weights = jnp.sum(own_combine, axis=-1)
     selected = jnp.einsum(
         "tec,ced->ted",

time: 295 us -> 282 us (0.956)
  other arithmetic: 22.4 us -> 15.1 us
  waiting for transfers between devices: 174 us -> 168 us
    all_gather x1, waiting for transfers between devices: 51 us -> 46.7 us  [body(): picked_all = lax.all_gather(picked_own, 'req', axis=0, tiled=True)]
    dot_general x1, matrix products: 8.91 us -> 12.8 us  [body(): jnp.einsum('nef,efd->ned', hidden_all, w_down, preferred_element_type=jnp...]
    another operation x4 -> x3, other arithmetic: 5.28 us -> 1.65 us
    unnamed x33 -> x26, local copies, waits for them, and re-layouts: 17 us -> 15.8 us
  transfers between devices with their start and end apart: 7 -> 7, of which waited for: 4 -> 4; matrix products, arithmetic and copies ran while one was open for 9% -> 8% of each run, Pallas kernels for 0% -> 0%
where the time goes in v5:
time: 282 us; the launch traced here: 281 us
  waiting for transfers between devices  168 us (60%)
  matrix products  45.3 us (16%)
  local copies, waits for them, and re-layouts  29.7 us (11%)
  other arithmetic  15.1 us (5%)
  between operations  14.1 us (5%)
  starting transfers between devices  8.45 us (3%)
    psum x1, waiting for transfers between devices, body(): lax.psum(partial_value.astype(jnp.bfloat16), 'head').astype(jnp.float32)  55.7 us
    all_gather x1, waiting for transfers between devices, body(): picked_all = lax.all_gather(picked_own, 'req', axis=0, tiled=True)  46.7 us
    unnamed x5, waiting for transfers between devices  41.2 us
    all_to_all x1, waiting for transfers between devices, body(): lax.all_to_all(outgoing, 'req', split_axis=0, concat_axis=0, tiled=True)  24.9 us
    dot_general x1, matrix products, body(): jnp.einsum('ned,egdf->gnef', picked_all, w_gate_up, preferred_element_typ...  18.4 us
    unnamed x26, local copies, waits for them, and re-layouts  15.8 us
    dot_general x1, matrix products, body(): jnp.einsum('nef,efd->ned', hidden_all, w_down, preferred_element_type=jnp...  12.8 us
  transfers between devices with their start and end apart: 7, of which 4 were waited for; matrix products, arithmetic and copies ran while one was open for 8% of the time, Pallas kernels for 0%

profile of v5, /device:TPU:0, one launch (start us, length us, event | category | flops | bytes accessed | tf_op | source)
XLA Modules:
  0.0 281.0 jit_solution(15314882941472941911)
XLA Ops:
  7.2 0.0 all-reduce.3.cloned.1.call-start
  7.3 9.9 %copy.45 = bf16[2304,3,512]{0,2,1:T(8,128)(2,1)} copy(bf16[2304,3,512]{2,0,1:T(8,128)(2,1)} %param.17) | data formatting | bytes 14155776 | tf_op args[2]
  17.1 0.3 fusion.12
  17.5 5.2 %fusion.26 = f32[256,3,8,64]{0,3,2,1:T(8,128)S(1)} fusion(bf16[3,8,64,2304]{3,2,1,0:T(8,128)(2,1)} %bitcast.102, bf16[1,256,2304]{2,1,0:T(8,128)(2,1)S(1)} %copy-done.2, f32[2304]{0:T(1024)} %param.16, f32[256]{0:T(256)S(1)} %add_rsqrt_fusion.1), kind=kOutput, calls=%fused_computation.39 | convolution fusion | flops 1814298624 | bytes 9840640 | tf_op jit(solution)/shard_map/dot_general | solution.py:73
  22.7 1.1 copy-done.5
  23.8 0.1 slice_bitcast_fusion.3
  23.9 0.2 multiply_cosine_fusion
  24.1 0.9 subtract_convert_fusion.1
  25.0 0.6 copy-done.6
  25.6 3.1 %collective-permute-start.1 = (bf16[256,8,64]{0,2,1:T(8,128)(2,1)S(1)}, bf16[256,8,64]{0,2,1:T(8,128)(2,1)}, u32[]{:S(2)}, u32[]{:S(2)}) collective-permute-start(bf16[256,8,64]{0,2,1:T(8,128)(2,1)S(1)} %pad_maximum_fusion), channel_id=1, source_target_pairs={{0,1},{2,3},{4,5},{6,7},{8,9},{10,11},{12,13},{14,15},{16,17},{18,... | collective-permute-start | bytes 786440 | tf_op jit(solution)/shard_map/ppermute | solution.py:13
  28.7 1.1 fusion.52
  29.8 1.3 collective-permute-start
  31.2 0.1 copy.46
  31.3 0.1 eq.108
  31.5 0.2 compare_and_fusion
  31.6 2.1 fusion.3
  33.7 1.3 fusion.5
  35.0 1.2 fusion.37
  36.2 1.8 convolution_convert_fusion.1
  38.1 0.0 all-reduce.3.cloned.1.call-update
  38.1 0.0 all-gather.2.cloned.1.call-start
  38.2 0.1 fusion.58
  38.3 0.6 reduce-window.6
  38.9 0.2 slice_reduce_fusion
  39.0 0.2 reduce-window.9
  39.2 0.1 broadcast.322
  39.3 0.1 fusion.57
  39.4 0.2 eq.112
  39.6 0.1 copy.47
  39.7 0.7 dynamic-slice_bitcast_fusion
  40.4 0.1 compare_convert_fusion
  40.5 0.1 fusion.50
  40.6 55.7 %all-reduce.3.cloned.1.call-done = bf16[256,2304]{1,0:T(8,128)(2,1)} async-done(((bf16[256,2304]{1,0:T(8,128)(2,1)}), bf16[256,2304]{1,0:T(8,128)(2,1)}) %all-reduce.3.cloned.1.call-update) | async-done | bytes 1179664 | tf_op jit(solution)/shard_map/psum | solution.py:104
  96.2 1.8 fusion.9
  98.0 0.5 fusion.28
  98.6 1.0 convert_bitcast_fusion.1
  99.6 0.0 all-gather.2.cloned.1.call-update
  99.6 0.2 reduce-scatter.7.cloned.1.call-start
  99.8 46.7 %all-gather.2.cloned.1.call-done = bf16[384,2,2304]{2,0,1:T(8,128)(2,1)} async-done(((bf16[96,2,2304]{2,0,1:T(8,128)(2,1)}), bf16[384,2,2304]{2,0,1:T(8,128)(2,1)}) %all-gather.2.cloned.1.call-update) | async-done | bytes 3538960 | tf_op jit(solution)/shard_map/all_gather | solution.py:124
  146.5 18.4 %convolution_bitcast_fusion = f32[2,384,2,1440]{1,3,0,2:T(8,128)S(1)} fusion(bf16[2,2,2304,1440]{2,3,1,0:T(8,128)(2,1)} %param.22, bf16[384,2,2304]{2,0,1:T(8,128)(2,1)} %all-gather.2.cloned.1.call-done), kind=kOutput, calls=%fused_computation.2 | convolution fusion | flops 10192158720 | bytes 38928384 | tf_op jit(solution)/shard_map/ned,egdf->gnef/dot_general | solution.py:125
  165.0 12.8 %convolution_convert_fusion = bf16[2,384,2304]{2,1,0:T(8,128)(2,1)} fusion(bf16[2,1440,2304]{2,1,0:T(8,128)(2,1)} %param.23, f32[2,384,2,1440]{1,3,0,2:T(8,128)S(1)} %convolution_bitcast_fusion), kind=kOutput, calls=%fused_computation.3 | convolution fusion | flops 5104484352 | bytes 25657344 | tf_op jit(solution)/shard_map/nef,efd->ned/dot_general | solution.py:128
  177.7 4.0 %copy.49 = bf16[4,96,2,2304]{3,1,2,0:T(8,128)(2,1)} copy(bf16[4,96,2,2304]{3,1,0,2:T(8,128)(2,1)} %bitcast.104) | data formatting | bytes 7077888 | tf_op jit(solution)/shard_map/reshape | solution.py:129
  181.7 0.0 reduce-scatter.7.cloned.1.call-update
  181.7 0.0 reduce-scatter.5.cloned.1.call-start
  181.8 0.6 copy-done.11
  182.4 0.6 dynamic_slice.25
  183.0 0.2 convert_reduce_fusion
  183.2 0.1 select_reduce_fusion.2
  183.3 0.7 add_compare_fusion
  184.1 1.7 bitcast_select_fusion
  185.7 2.3 gather_fusion
  188.0 41.1 %reduce-scatter.7.cloned.1.call-done = bf16[1,96,2,2304]{3,1,2,0:T(8,128)(2,1)} async-done(((bf16[4,96,2,2304]{3,1,2,0:T(8,128)(2,1)}), bf16[1,96,2,2304]{3,1,2,0:T(8,128)(2,1)}) %reduce-scatter.7.cloned.1.call-update) | async-done | bytes 884752
  229.1 3.3 %fusion.21 = bf16[256,2304]{0,1:T(8,128)(2,1)} fusion(bf16[256,2,96]{0,2,1:T(8,128)(2,1)S(1)} %get-tuple-element.12, f32[256,2]{0,1:T(2,128)S(1)} %get-tuple-element.11, bf16[1,96,2,2304]{3,1,2,0:T(8,128)(2,1)} %reduce-scatter.7.cloned.1.call-done), kind=kOutput, calls=%fused_computation.36 | convolution fusion | flops 228261888 | bytes 2164736 | tf_op jit(solution)/shard_map/tec,ced->ted/dot_general | solution.py:134
  232.4 2.4 copy.50
  234.8 0.0 reduce-scatter.5.cloned.1.call-update
  234.8 1.6 broadcast_select_fusion.1
  236.4 3.7 %all-to-all-start = ((bf16[16,64,2,512]{3,1,2,0:T(8,128)(2,1)}), bf16[16,64,2,512]{3,1,2,0:T(8,128)(2,1)S(1)}, u32[]{:S(2)}, u32[]{:S(2)}) async-start(bf16[16,64,2,512]{3,1,2,0:T(8,128)(2,1)} %broadcast_select_fusion.1), calls=%async_computation.1 | async-start | bytes 4194304 | tf_op jit(solution)/shard_map/all_to_all | solution.py:177
  240.2 0.1 broadcast_add_fusion
  240.2 0.1 select_reduce_fusion.1
  240.4 24.9 %all-to-all-done = bf16[16,64,2,512]{3,1,2,0:T(8,128)(2,1)S(1)} async-done(((bf16[16,64,2,512]{3,1,2,0:T(8,128)(2,1)}), bf16[16,64,2,512]{3,1,2,0:T(8,128)(2,1)S(1)}, u32[]{:S(2)}, u32[]{:S(2)}) %all-to-all-start) | async-done | bytes 2097184 | tf_op jit(solution)/shard_map/all_to_all | solution.py:177
  265.2 2.0 gather_fusion.1
  267.2 2.0 broadcast_select_fusion
  269.3 3.5 %copy.52 = bf16[16,64,2,512]{3,2,1,0:T(2,128)(2,1)} copy(bf16[16,64,2,512]{3,1,2,0:T(8,128)(2,1)S(1)} %broadcast_select_fusion) | data formatting | bytes 4194304
  272.7 1.7 fusion.51
  (50 shorter events, 0.3 us)
Async XLA Ops:
  7.2 29.1 %copy-start = (bf16[512,2304]{1,0:T(8,128)(2,1)S(1)}, bf16[512,2304]{1,0:T(8,128)(2,1)}, u32[]{:S(2)}) copy-start(bf16[512,2304]{1,0:T(8,128)(2,1)} %param.18) | copy-start | bytes 7077892
  7.2 89.1 %all-reduce.3.cloned.1.call-start = ((), (), s32[]{:S(2)}) async-start(), calls=%async_computation.3 | async-start | bytes 2359296 | tf_op jit(solution)/shard_map/psum | solution.py:104
  7.2 9.9 %copy-start.2 = (bf16[1,256,2304]{2,1,0:T(8,128)(2,1)S(1)}, bf16[1,256,2304]{2,1,0:T(8,128)(2,1)}, u32[]{:S(2)}) copy-start(bf16[1,256,2304]{2,1,0:T(8,128)(2,1)} %param.15) | copy-start | bytes 3538948
  22.7 1.1 copy-start.5
  23.8 7.3 %copy-start.9 = (s32[4,256,2]{1,2,0:T(2,128)S(1)}, s32[4,256,2]{1,2,0:T(2,128)}, u32[]{:S(2)}) copy-start(s32[4,256,2]{1,2,0:T(2,128)} %param.20) | copy-start | bytes 24580
  25.0 0.7 copy-start.6
  25.6 6.0 %collective-permute-start.1 = (bf16[256,8,64]{0,2,1:T(8,128)(2,1)S(1)}, bf16[256,8,64]{0,2,1:T(8,128)(2,1)}, u32[]{:S(2)}, u32[]{:S(2)}) collective-permute-start(bf16[256,8,64]{0,2,1:T(8,128)(2,1)S(1)} %pad_maximum_fusion), channel_id=1, source_target_pairs={{0,1},{2,3},{4,5},{6,7},{8,9},{10,11},{12,13},{14,15},{16,17},{18,... | collective-permute-start | bytes 786440 | tf_op jit(solution)/shard_map/ppermute | solution.py:13
  29.8 5.2 %collective-permute-start = (bf16[256,8,64]{0,2,1:T(8,128)(2,1)S(1)}, bf16[256,8,64]{0,2,1:T(8,128)(2,1)S(1)}, u32[]{:S(2)}, u32[]{:S(2)}) collective-permute-start(bf16[256,8,64]{0,2,1:T(8,128)(2,1)S(1)} %fusion.52), channel_id=1, source_target_pairs={{0,1},{2,3},{4,5},{6,7},{8,9},{10,11},{12,13},{14,15},{16,17},{18,... | collective-permute-start | bytes 786440 | tf_op jit(solution)/shard_map/ppermute | solution.py:13
  38.1 58.2 %copy-start.3 = (bf16[1,256,2304]{2,1,0:T(8,128)(2,1)S(1)}, bf16[1,256,2304]{2,1,0:T(8,128)(2,1)}, u32[]{:S(2)}) copy-start(bf16[1,256,2304]{2,1,0:T(8,128)(2,1)} %param.15) | copy-start | bytes 3538948
  38.1 59.9 %copy-start.8 = (f32[2304]{0:T(1024)S(1)}, f32[2304]{0:T(1024)}, u32[]{:S(2)}) copy-start(f32[2304]{0:T(1024)} %param.19) | copy-start | bytes 27652
  38.1 108.4 %all-gather.2.cloned.1.call-start = ((), (), s32[]{:S(2)}) async-start(), calls=%async_computation.4 | async-start | bytes 4423680 | tf_op jit(solution)/shard_map/all_gather | solution.py:124
  99.6 129.5 %reduce-scatter.7.cloned.1.call-start = ((), (), s32[]{:S(2)}) async-start(), calls=%async_computation.6 | async-start | bytes 4423680
  181.7 0.7 copy-start.11
  181.7 1.3 copy-start.7
  181.7 2.3 copy-start.4
  181.7 91.0 %reduce-scatter.5.cloned.1.call-start = ((), (), s32[]{:S(2)}) async-start(), calls=%async_computation.5 | async-start | bytes 1474560 | tf_op jit(solution)/shard_map/reduce_scatter | solution.py:141
  236.4 3.8 %copy-start.10 = (s32[4,16]{1,0:T(4,128)S(1)}, s32[4,16]{1,0:T(4,128)}, u32[]{:S(2)}) copy-start(s32[4,16]{1,0:T(4,128)} %param.27) | copy-start | bytes 772
  236.4 28.9 %all-to-all-start = ((bf16[16,64,2,512]{3,1,2,0:T(8,128)(2,1)}), bf16[16,64,2,512]{3,1,2,0:T(8,128)(2,1)S(1)}, u32[]{:S(2)}, u32[]{:S(2)}) async-start(bf16[16,64,2,512]{3,1,2,0:T(8,128)(2,1)} %broadcast_select_fusion.1), calls=%async_computation.1 | async-start | bytes 4194304 | tf_op jit(solution)/shard_map/all_to_all | solution.py:177
  267.2 7.2 %copy-start.1 = (bf16[512,2304]{1,0:T(8,128)(2,1)S(1)}, bf16[512,2304]{1,0:T(8,128)(2,1)}, u32[]{:S(2)}) copy-start(bf16[512,2304]{1,0:T(8,128)(2,1)} %param.18) | copy-start | bytes 7077892
Sparse Core Ops, SparseCore 0:
  38.2 57.9 all-reduce.2
  99.7 46.7 all-gather.1
  181.9 47.2 reduce-scatter.6
  234.9 29.1 reduce-scatter.4

commit v6 on v5

--- a/solution.py
+++ b/solution.py
@@ -121,21 +121,40 @@
         moe_in,
         preferred_element_type=jnp.float32,
     ).astype(jnp.bfloat16)
-    picked_all = lax.all_gather(picked_own, "req", axis=0, tiled=True)
-    both = jnp.einsum("ned,egdf->gnef", picked_all, w_gate_up, preferred_element_type=jnp.float32)
-    hidden_all = (jax.nn.silu(both[0]) * both[1]).astype(jnp.bfloat16)
-    source_count = half_rows * lax.axis_size("req") // half_rows
-    down_out = jnp.einsum("nef,efd->ned", hidden_all, w_down, preferred_element_type=jnp.float32)
-    down_out = down_out.astype(jnp.bfloat16).reshape(
-        source_count, capacity, experts_here, model_width
-    )
-    expert_back = lax.psum_scatter(down_out, "req", scatter_dimension=0, tiled=True)[0]
+    req_total = lax.axis_size("req")
+
+    def partner_move(block, step):
+        return lax.ppermute(block, "req", [(i, i ^ step) for i in range(req_total)])
+
+    def experts_on(rows):
+        groups = rows.shape[0]
+        flat = rows.reshape(groups * capacity, experts_here, model_width)
+        both = jnp.einsum("ned,egdf->gnef", flat, w_gate_up, preferred_element_type=jnp.float32)
+        hidden = (jax.nn.silu(both[0]) * both[1]).astype(jnp.bfloat16)
+        down = jnp.einsum("nef,efd->ned", hidden, w_down, preferred_element_type=jnp.float32)
+        return down.astype(jnp.bfloat16).reshape(groups, capacity, experts_here, model_width)
+
+    arrived = {0: picked_own}
+    for step in range(1, req_total):
+        if step == 3:
+            arrived[step] = partner_move(arrived[1], 2)
+        else:
+            arrived[step] = partner_move(picked_own, step)
+    plan = [[0], [1, 2]] + ([list(range(3, req_total))] if req_total > 3 else [])
+    plan = [[k for k in group if k < req_total] for group in plan]
+    returned = []
+    for group in plan:
+        if not group:
+            continue
+        outs = experts_on(jnp.stack([arrived[k] for k in group], axis=0))
+        for slot_index, step in enumerate(group):
+            part = outs[slot_index]
+            returned.append(part if step == 0 else partner_move(part, step))
     token_weights = jnp.sum(own_combine, axis=-1)
-    selected = jnp.einsum(
-        "tec,ced->ted",
-        own_dispatch.astype(jnp.bfloat16),
-        expert_back,
-        preferred_element_type=jnp.float32,
+    dispatch_bf = own_dispatch.astype(jnp.bfloat16)
+    selected = sum(
+        jnp.einsum("tec,ced->ted", dispatch_bf, part, preferred_element_type=jnp.float32)
+        for part in returned
     )
     moe_out = jnp.sum(token_weights[:, :, None] * selected, axis=1)
     summed = lax.psum_scatter(

time: 282 us -> 257 us (0.911)
  waiting for transfers between devices: 168 us -> 90.2 us
  matrix products: 45.3 us -> 91.8 us
  starting transfers between devices: 8.45 us -> 16.1 us
  local copies, waits for them, and re-layouts: 29.7 us -> 26.8 us
    all_gather x1 -> x0, waiting for transfers between devices: 46.7 us -> none  [body(): picked_all = lax.all_gather(picked_own, 'req', axis=0, tiled=True)]
    dot_general x3 -> x9, matrix products: 34.4 us -> 80.2 us  [the longest x3 43 us: experts_on(): jnp.einsum('ned,egdf->gnef', flat, w_gate_up, preferred_element_type=jnp....]
    unnamed x5 -> x2, waiting for transfers between devices: 41.2 us -> 0.03 us
    ppermute x0 -> x6, waiting for transfers between devices: none -> 19.5 us  [partner_move(): return lax.ppermute(block, 'req', [(i, i ^ step) for i in range(req_total)])]
    ppermute x0 -> x6, starting transfers between devices: none -> 7 us  [partner_move(): return lax.ppermute(block, 'req', [(i, i ^ step) for i in range(req_total)])]
    all_to_all x1, waiting for transfers between devices: 24.9 us -> 19.9 us  [body(): lax.all_to_all(outgoing, 'req', split_axis=0, concat_axis=0, tiled=True)]
    psum x1, waiting for transfers between devices: 55.7 us -> 50.8 us  [body(): lax.psum(partial_value.astype(jnp.bfloat16), 'head').astype(jnp.float32)]
    reshape x2 -> x1, local copies, waits for them, and re-layouts: 4 us -> 0.02 us  [the longest x1 3.98 us: body(): down_out.astype(jnp.bfloat16)]
  transfers between devices with their start and end apart: 7 -> 11, of which waited for: 4 -> 6; matrix products, arithmetic and copies ran while one was open for 8% -> 33% of each run, Pallas kernels for 0% -> 0%
where the time goes in v6:
time: 257 us; the launch traced here: 256 us
  matrix products  91.8 us (36%)
  waiting for transfers between devices  90.2 us (35%)
  local copies, waits for them, and re-layouts  26.8 us (10%)
  other arithmetic  16.6 us (6%)
  starting transfers between devices  16.1 us (6%)
  between operations  14.4 us (6%)
    psum x1, waiting for transfers between devices, body(): lax.psum(partial_value.astype(jnp.bfloat16), 'head').astype(jnp.float32)  50.8 us
    dot_general x3, matrix products, experts_on(): jnp.einsum('ned,egdf->gnef', flat, w_gate_up, preferred_element_type=jnp....  43 us
    all_to_all x1, waiting for transfers between devices, body(): lax.all_to_all(outgoing, 'req', split_axis=0, concat_axis=0, tiled=True)  19.9 us
    ppermute x6, waiting for transfers between devices, partner_move(): return lax.ppermute(block, 'req', [(i, i ^ step) for i in range(req_total)])  19.5 us
    dot_general x4, matrix products, body(): jnp.einsum('tec,ced->ted', dispatch_bf, part, preferred_element_type=jnp....  19.1 us
    dot_general x2, matrix products, experts_on(): jnp.einsum('nef,efd->ned', hidden, w_down, preferred_element_type=jnp.flo...  18.1 us
    unnamed x28, local copies, waits for them, and re-layouts  14 us
    ppermute x6, starting transfers between devices, partner_move(): return lax.ppermute(block, 'req', [(i, i ^ step) for i in range(req_total)])  7 us
  transfers between devices with their start and end apart: 11, of which 6 were waited for; matrix products, arithmetic and copies ran while one was open for 33% of the time, Pallas kernels for 0%

profile of v6, /device:TPU:0, one launch (start us, length us, event | category | flops | bytes accessed | tf_op | source)
XLA Modules:
  0.0 255.9 jit_solution(12898580117031378000)
XLA Ops:
  7.3 9.9 %copy.52 = bf16[2304,3,512]{0,2,1:T(8,128)(2,1)} copy(bf16[2304,3,512]{2,0,1:T(8,128)(2,1)} %param.17) | data formatting | bytes 14155776 | tf_op args[2]
  17.2 0.3 fusion.19
  17.5 5.2 %fusion.35 = f32[256,3,8,64]{0,3,2,1:T(8,128)S(1)} fusion(bf16[3,8,64,2304]{3,2,1,0:T(8,128)(2,1)} %bitcast.157, bf16[1,256,2304]{2,1,0:T(8,128)(2,1)S(1)} %copy-done.4, f32[2304]{0:T(1024)} %param.16, f32[256]{0:T(256)S(1)} %add_rsqrt_fusion.1), kind=kOutput, calls=%fused_computation.51 | convolution fusion | flops 1814298624 | bytes 9840640 | tf_op jit(solution)/shard_map/dot_general | solution.py:73
  22.8 0.2 multiply_cosine_fusion
  23.0 0.2 subtract_convert_fusion.1
  23.2 3.1 %collective-permute-start.1 = (bf16[256,8,64]{0,2,1:T(8,128)(2,1)S(1)}, bf16[256,8,64]{0,2,1:T(8,128)(2,1)}, u32[]{:S(2)}, u32[]{:S(2)}) collective-permute-start(bf16[256,8,64]{0,2,1:T(8,128)(2,1)S(1)} %pad_maximum_fusion.1), channel_id=1, source_target_pairs={{0,1},{2,3},{4,5},{6,7},{8,9},{10,11},{12,13},{14,15},{16,17},{18,... | collective-permute-start | bytes 786440 | tf_op jit(solution)/shard_map/ppermute | solution.py:13
  26.3 2.0 collective-permute-start
  28.3 0.7 constant_dynamic-slice_fusion.2
  28.9 0.1 copy.53
  29.1 0.1 eq.108
  29.3 0.6 reduce-window.6
  29.9 0.2 slice_reduce_fusion
  30.1 0.2 reduce-window.9
  30.4 0.2 convert_reduce_fusion
  30.6 0.1 select_reduce_fusion.2
  30.8 0.5 copy-done.11
  31.4 0.2 compare_and_fusion
  31.6 1.9 fusion.6
  33.5 1.3 fusion.9
  34.8 2.2 fusion.51
  37.0 1.9 convolution_convert_fusion.1
  38.8 0.2 reduce-scatter.2.cloned.1.call-start
  39.1 0.2 eq.112
  39.4 0.6 dynamic_slice.25
  40.0 0.7 add_compare_fusion
  40.7 1.9 bitcast_select_fusion
  42.7 2.0 gather_fusion
  44.7 0.7 fusion.113
  45.4 0.7 dynamic-slice_bitcast_fusion
  46.2 50.8 %all-reduce.2.cloned.1.call-done = bf16[256,2304]{1,0:T(8,128)(2,1)} async-done(((bf16[256,2304]{1,0:T(8,128)(2,1)}), bf16[256,2304]{1,0:T(8,128)(2,1)}) %all-reduce.2.cloned.1.call-update) | async-done | bytes 1179664 | tf_op jit(solution)/shard_map/psum | solution.py:104
  97.0 2.1 fusion.16
  99.1 0.5 fusion.37
  99.7 1.0 convert_bitcast_fusion.1
  100.7 1.5 collective-permute-start.2
  102.1 1.5 collective-permute-start.3
  103.6 14.2 %convolution_bitcast_fusion.1 = f32[2,96,2,1440]{3,1,0,2:T(8,128)} fusion(bf16[2,2,2304,1440]{2,3,1,0:T(8,128)(2,1)} %param.22, f32[2304,2,96]{0,2,1:T(8,128)S(1)} %bitcast.156), kind=kOutput, calls=%fused_computation.23 | convolution fusion | flops 2548482048 | bytes 30523392 | tf_op jit(solution)/shard_map/ned,egdf->gnef/dot_general | solution.py:132
  117.8 4.7 %collective-permute-done.2 = bf16[96,2,2304]{2,0,1:T(8,128)(2,1)} collective-permute-done((bf16[96,2,2304]{2,0,1:T(8,128)(2,1)}, bf16[96,2,2304]{2,0,1:T(8,128)(2,1)}, u32[]{:S(2)}, u32[]{:S(2)}) %collective-permute-start.2) | collective-permute-done | bytes 884768 | tf_op jit(solution)/shard_map/ppermute | solution.py:127
  122.6 1.2 collective-permute-done.3
  123.8 1.6 pad_maximum_fusion
  125.4 1.4 copy.56
  126.8 14.8 %convolution_bitcast_fusion = f32[2,192,2,1440]{3,1,0,2:T(8,128)} fusion(bf16[192,2,2304,1]{2,0,3,1:T(8,128)(2,1)} %bitcast.159, bf16[2,2,2304,1440]{2,3,1,0:T(8,128)(2,1)} %param.22), kind=kOutput, calls=%fused_computation.14 | convolution fusion | flops 5096079360 | bytes 32735232 | tf_op jit(solution)/shard_map/ned,egdf->gnef/dot_general | solution.py:132
  141.6 1.5 collective-permute-start.6
  143.1 9.1 %fusion.5 = bf16[192,2,2304]{2,0,1:T(8,128)(2,1)S(1)} fusion(bf16[2,1440,2304]{2,1,0:T(8,128)(2,1)} %param.23, f32[2,192,2,1440]{3,1,0,2:T(8,128)} %convolution_bitcast_fusion), kind=kOutput, calls=%fused_computation.12 | convolution fusion | flops 2552242176 | bytes 19464192 | tf_op jit(solution)/shard_map/nef,efd->ned/dot_general | solution.py:134
  152.2 1.3 fusion.94
  153.5 0.6 collective-permute-start.4
  154.1 0.6 collective-permute-start.5
  154.6 9.9 %collective-permute-done.6 = bf16[96,2,2304]{2,0,1:T(8,128)(2,1)} collective-permute-done((bf16[96,2,2304]{2,0,1:T(8,128)(2,1)}, bf16[96,2,2304]{2,0,1:T(8,128)(2,1)}, u32[]{:S(2)}, u32[]{:S(2)}) %collective-permute-start.6) | collective-permute-done | bytes 884768 | tf_op jit(solution)/shard_map/ppermute | solution.py:127
  164.5 13.9 %fusion.11 = f32[2,96,2,1440]{3,1,2,0:T(8,128)} fusion(bf16[2,2,2304,1440]{2,3,1,0:T(8,128)(2,1)} %param.22, bf16[96,2,2304]{2,0,1:T(8,128)(2,1)} %collective-permute-done.6), kind=kOutput, calls=%fused_computation.22 | convolution fusion | flops 2548039680 | bytes 29638656 | tf_op jit(solution)/shard_map/ned,egdf->gnef/dot_general | solution.py:132
  178.4 8.9 %fusion.8 = bf16[96,2,2304]{2,0,1:T(8,128)(2,1)} fusion(bf16[2,1440,2304]{2,1,0:T(8,128)(2,1)} %param.23, f32[2,96,2,1440]{3,1,2,0:T(8,128)} %fusion.11), kind=kOutput, calls=%fused_computation.19 | convolution fusion | flops 1276121088 | bytes 16367616 | tf_op jit(solution)/shard_map/nef,efd->ned/dot_general | solution.py:134
  187.4 1.5 collective-permute-start.7
  188.8 9.8 %fusion.29 = f32[2,2304,256]{2,1,0:T(8,128)} fusion(bf16[256,2,96]{0,2,1:T(8,128)(2,1)} %copy-done.5, bf16[2,1440,2304]{2,1,0:T(8,128)(2,1)} %param.23, f32[2,96,2,1440]{3,1,0,2:T(8,128)S(1)} %copy-done.3), kind=kOutput, calls=%fused_computation.47 | convolution fusion | flops 1502613504 | bytes 20299776 | tf_op jit(solution)/shard_map/tec,ced->ted/dot_general | solution.py:156
  198.7 3.5 %convolution_add_fusion.1 = f32[2,2304,256]{2,1,0:T(8,128)S(1)} fusion(f32[2,2304,256]{2,1,0:T(8,128)} %fusion.29, bf16[96,2,2304]{2,0,1:T(8,128)(2,1)} %collective-permute-done.4, bf16[256,2,96]{0,2,1:T(8,128)(2,1)} %copy-done.5), kind=kOutput, calls=%fused_computation.6 | convolution fusion | flops 227672064 | bytes 10420224 | tf_op jit(solution)/shard_map/tec,ced->ted/dot_general | solution.py:156
  202.2 3.7 %collective-permute-done.7 = bf16[96,2,2304]{2,0,1:T(8,128)(2,1)} collective-permute-done((bf16[96,2,2304]{2,0,1:T(8,128)(2,1)}, bf16[96,2,2304]{2,0,1:T(8,128)(2,1)}, u32[]{:S(2)}, u32[]{:S(2)}) %collective-permute-start.7) | collective-permute-done | bytes 884768 | tf_op jit(solution)/shard_map/ppermute | solution.py:127
  205.9 2.0 fusion.95
  207.9 3.8 %fusion.28 = bf16[256,2304]{0,1:T(8,128)(2,1)} fusion(f32[2,2304,256]{2,1,0:T(8,128)S(1)} %fusion.95, f32[2,2304,256]{2,1,0:T(8,128)S(1)} %convolution_add_fusion.1, bf16[96,2,2304]{2,0,1:T(8,128)(2,1)} %collective-permute-done.5, bf16[256,2,96]{0,2,1:T(8,128)(2,1)S(1)} %copy-done.6, f32[256,2]{0,1:T(2,128)S(1)} %get-tuple-element.11), kind=kOutput, calls=%fused_computation.46 | convolution fusion | flops 230621184 | bytes 11601920 | tf_op jit(solution)/shard_map/tec,ced->ted/dot_general | solution.py:156
  211.7 2.5 copy.59
  214.3 1.6 broadcast_select_fusion.1
  215.9 3.8 %all-to-all-start = ((bf16[16,64,2,512]{3,1,2,0:T(8,128)(2,1)}), bf16[16,64,2,512]{3,1,2,0:T(8,128)(2,1)S(1)}, u32[]{:S(2)}, u32[]{:S(2)}) async-start(bf16[16,64,2,512]{3,1,2,0:T(8,128)(2,1)} %broadcast_select_fusion.1), calls=%async_computation.1 | async-start | bytes 4194304 | tf_op jit(solution)/shard_map/all_to_all | solution.py:196
  219.8 0.1 select_reduce_fusion.1
  219.9 19.9 %all-to-all-done = bf16[16,64,2,512]{3,1,2,0:T(8,128)(2,1)S(1)} async-done(((bf16[16,64,2,512]{3,1,2,0:T(8,128)(2,1)}), bf16[16,64,2,512]{3,1,2,0:T(8,128)(2,1)S(1)}, u32[]{:S(2)}, u32[]{:S(2)}) %all-to-all-start) | async-done | bytes 2097184 | tf_op jit(solution)/shard_map/all_to_all | solution.py:196
  239.8 2.0 gather_fusion.1
  241.8 2.0 broadcast_select_fusion
  243.8 3.5 %copy.61 = bf16[16,64,2,512]{3,2,1,0:T(2,128)(2,1)} copy(bf16[16,64,2,512]{3,1,2,0:T(8,128)(2,1)S(1)} %broadcast_select_fusion) | data formatting | bytes 4194304
  247.3 1.7 fusion.73
  (66 shorter events, 1.0 us)
Async XLA Ops:
  7.2 29.8 %copy-start = (bf16[512,2304]{1,0:T(8,128)(2,1)S(1)}, bf16[512,2304]{1,0:T(8,128)(2,1)}, u32[]{:S(2)}) copy-start(bf16[512,2304]{1,0:T(8,128)(2,1)} %param.18) | copy-start | bytes 7077892
  7.2 89.8 %all-reduce.2.cloned.1.call-start = ((), (), s32[]{:S(2)}) async-start(), calls=%async_computation.2 | async-start | bytes 2359296 | tf_op jit(solution)/shard_map/psum | solution.py:104
  7.3 9.9 %copy-start.4 = (bf16[1,256,2304]{2,1,0:T(8,128)(2,1)S(1)}, bf16[1,256,2304]{2,1,0:T(8,128)(2,1)}, u32[]{:S(2)}) copy-start(bf16[1,256,2304]{2,1,0:T(8,128)(2,1)} %param.15) | copy-start | bytes 3538948
  22.7 7.7 %copy-start.7 = (s32[4,16]{1,0:T(4,128)S(1)}, s32[4,16]{1,0:T(4,128)}, u32[]{:S(2)}) copy-start(s32[4,16]{1,0:T(4,128)} %param.26) | copy-start | bytes 772
  23.2 8.4 %collective-permute-start.1 = (bf16[256,8,64]{0,2,1:T(8,128)(2,1)S(1)}, bf16[256,8,64]{0,2,1:T(8,128)(2,1)}, u32[]{:S(2)}, u32[]{:S(2)}) collective-permute-start(bf16[256,8,64]{0,2,1:T(8,128)(2,1)S(1)} %pad_maximum_fusion.1), channel_id=1, source_target_pairs={{0,1},{2,3},{4,5},{6,7},{8,9},{10,11},{12,13},{14,15},{16,17},{18,... | collective-permute-start | bytes 786440 | tf_op jit(solution)/shard_map/ppermute | solution.py:13
  26.3 8.5 %collective-permute-start = (bf16[256,8,64]{0,2,1:T(8,128)(2,1)S(1)}, bf16[256,8,64]{0,2,1:T(8,128)(2,1)}, u32[]{:S(2)}, u32[]{:S(2)}) collective-permute-start(bf16[256,8,64]{0,2,1:T(8,128)(2,1)S(1)} %fusion.74), channel_id=1, source_target_pairs={{0,1},{2,3},{4,5},{6,7},{8,9},{10,11},{12,13},{14,15},{16,17},{18,... | collective-permute-start | bytes 786440 | tf_op jit(solution)/shard_map/ppermute | solution.py:13
  30.8 0.6 copy-start.11
  36.9 2.5 copy-start.10
  38.8 208.5 %reduce-scatter.2.cloned.1.call-start = ((), (), s32[]{:S(2)}) async-start(), calls=%async_computation.3 | async-start | bytes 1474560 | tf_op jit(solution)/shard_map/reduce_scatter | solution.py:160
  44.7 54.5 %copy-start.8 = (f32[2304]{0:T(1024)S(1)}, f32[2304]{0:T(1024)}, u32[]{:S(2)}) copy-start(f32[2304]{0:T(1024)} %param.19) | copy-start | bytes 27652
  46.2 53.5 %copy-start.5 = (bf16[256,2,96]{0,2,1:T(8,128)(2,1)}, bf16[256,2,96]{0,2,1:T(8,128)(2,1)S(1)}, u32[]{:S(2)}) copy-start(bf16[256,2,96]{0,2,1:T(8,128)(2,1)S(1)} %get-tuple-element.12) | copy-start | bytes 294916
  100.7 21.9 %collective-permute-start.2 = (bf16[96,2,2304]{2,0,1:T(8,128)(2,1)}, bf16[96,2,2304]{2,0,1:T(8,128)(2,1)}, u32[]{:S(2)}, u32[]{:S(2)}) collective-permute-start(bf16[96,2,2304]{2,0,1:T(8,128)(2,1)} %convert_bitcast_fusion.1), channel_id=1, source_target_pairs={{0,8},{8,0},{16,24},{24,16},{1,9},{9,1},{17,25},{25,17},{2,10},{10... | collective-permute-start | bytes 2654216 | tf_op jit(solution)/shard_map/ppermute | solution.py:127
  102.1 21.6 %collective-permute-start.3 = (bf16[96,2,2304]{2,0,1:T(8,128)(2,1)}, bf16[96,2,2304]{2,0,1:T(8,128)(2,1)}, u32[]{:S(2)}, u32[]{:S(2)}) collective-permute-start(bf16[96,2,2304]{2,0,1:T(8,128)(2,1)} %convert_bitcast_fusion.1), channel_id=1, source_target_pairs={{0,16},{8,24},{16,0},{24,8},{1,17},{9,25},{17,1},{25,9},{2,18},{10... | collective-permute-start | bytes 2654216 | tf_op jit(solution)/shard_map/ppermute | solution.py:127
  141.6 22.9 %collective-permute-start.6 = (bf16[96,2,2304]{2,0,1:T(8,128)(2,1)}, bf16[96,2,2304]{2,0,1:T(8,128)(2,1)}, u32[]{:S(2)}, u32[]{:S(2)}) collective-permute-start(bf16[96,2,2304]{2,0,1:T(8,128)(2,1)} %collective-permute-done.2), channel_id=1, source_target_pairs={{0,16},{8,24},{16,0},{24,8},{1,17},{9,25},{17,1},{25,9},{2,18},{10... | collective-permute-start | bytes 2654216 | tf_op jit(solution)/shard_map/ppermute | solution.py:127
  153.5 45.1 %collective-permute-start.4 = (bf16[96,2,2304]{2,0,1:T(8,128)(2,1)}, bf16[96,2,2304]{2,0,1:T(8,128)(2,1)}, u32[]{:S(2)}, u32[]{:S(2)}) collective-permute-start(bf16[96,2,2304]{2,0,1:T(8,128)(2,1)} %get-tuple-element.16), channel_id=1, source_target_pairs={{0,8},{8,0},{16,24},{24,16},{1,9},{9,1},{17,25},{25,17},{2,10},{10... | collective-permute-start | bytes 2654216 | tf_op jit(solution)/shard_map/ppermute | solution.py:127
  154.1 53.8 %collective-permute-start.5 = (bf16[96,2,2304]{2,0,1:T(8,128)(2,1)}, bf16[96,2,2304]{2,0,1:T(8,128)(2,1)}, u32[]{:S(2)}, u32[]{:S(2)}) collective-permute-start(bf16[96,2,2304]{2,0,1:T(8,128)(2,1)} %get-tuple-element.15), channel_id=1, source_target_pairs={{0,16},{8,24},{16,0},{24,8},{1,17},{9,25},{17,1},{25,9},{2,18},{10... | collective-permute-start | bytes 2654216 | tf_op jit(solution)/shard_map/ppermute | solution.py:127
  178.4 10.4 %copy-start.3 = (f32[2,96,2,1440]{3,1,0,2:T(8,128)S(1)}, f32[2,96,2,1440]{3,1,0,2:T(8,128)}, u32[]{:S(2)}) copy-start(f32[2,96,2,1440]{3,1,0,2:T(8,128)} %convolution_bitcast_fusion.1) | copy-start | bytes 6635524
  187.4 18.6 %collective-permute-start.7 = (bf16[96,2,2304]{2,0,1:T(8,128)(2,1)}, bf16[96,2,2304]{2,0,1:T(8,128)(2,1)}, u32[]{:S(2)}, u32[]{:S(2)}) collective-permute-start(bf16[96,2,2304]{2,0,1:T(8,128)(2,1)} %fusion.8), channel_id=1, source_target_pairs={{0,24},{8,16},{16,8},{24,0},{1,25},{9,17},{17,9},{25,1},{2,26},{10... | collective-permute-start | bytes 2654216 | tf_op jit(solution)/shard_map/ppermute | solution.py:127
  198.7 7.3 %copy-start.6 = (bf16[256,2,96]{0,2,1:T(8,128)(2,1)S(1)}, bf16[256,2,96]{0,2,1:T(8,128)(2,1)}, u32[]{:S(2)}) copy-start(bf16[256,2,96]{0,2,1:T(8,128)(2,1)} %copy-done.5) | copy-start | bytes 294916
  211.7 2.5 copy-start.12
  211.7 2.6 %copy-start.2 = (bf16[16,64,2,512]{3,1,2,0:T(8,128)(2,1)S(1)}, bf16[16,64,2,512]{3,1,2,0:T(8,128)(2,1)}, u32[]{:S(2)}) copy-start(bf16[16,64,2,512]{3,1,2,0:T(8,128)(2,1)} %gather_fusion) | copy-start | bytes 6291460
  215.9 3.9 %copy-start.9 = (s32[4,16]{1,0:T(4,128)S(1)}, s32[4,16]{1,0:T(4,128)}, u32[]{:S(2)}) copy-start(s32[4,16]{1,0:T(4,128)} %param.27) | copy-start | bytes 772
  215.9 23.9 %all-to-all-start = ((bf16[16,64,2,512]{3,1,2,0:T(8,128)(2,1)}), bf16[16,64,2,512]{3,1,2,0:T(8,128)(2,1)S(1)}, u32[]{:S(2)}, u32[]{:S(2)}) async-start(bf16[16,64,2,512]{3,1,2,0:T(8,128)(2,1)} %broadcast_select_fusion.1), calls=%async_computation.1 | async-start | bytes 4194304 | tf_op jit(solution)/shard_map/all_to_all | solution.py:196
  241.8 7.2 %copy-start.1 = (bf16[512,2304]{1,0:T(8,128)(2,1)S(1)}, bf16[512,2304]{1,0:T(8,128)(2,1)}, u32[]{:S(2)}) copy-start(bf16[512,2304]{1,0:T(8,128)(2,1)} %param.18) | copy-start | bytes 7077892
Sparse Core Ops, SparseCore 0:
  39.0 57.9 all-reduce.1
  214.4 27.7 reduce-scatter.1

commit v7 on v6

--- a/solution.py
+++ b/solution.py
@@ -140,7 +140,7 @@
             arrived[step] = partner_move(arrived[1], 2)
         else:
             arrived[step] = partner_move(picked_own, step)
-    plan = [[0], [1, 2]] + ([list(range(3, req_total))] if req_total > 3 else [])
+    plan = [[0, 1, 2]] + ([list(range(3, req_total))] if req_total > 3 else [])
     plan = [[k for k in group if k < req_total] for group in plan]
     returned = []
     for group in plan:

time: 257 us -> 273 us (1.062)
  waiting for transfers between devices: 90.2 us -> 131 us
  matrix products: 91.8 us -> 69.7 us
  other arithmetic: 16.6 us -> 13.8 us
    ppermute x6, waiting for transfers between devices: 19.5 us -> 51 us  [partner_move(): return lax.ppermute(block, 'req', [(i, i ^ step) for i in range(req_total)])]
    dot_general x3 -> x2, matrix products: 43 us -> 30.1 us  [experts_on(): jnp.einsum('ned,egdf->gnef', flat, w_gate_up, preferred_element_type=jnp....]
    dot_general x4, matrix products: 19.1 us -> 8.08 us  [body(): jnp.einsum('tec,ced->ted', dispatch_bf, part, preferred_element_type=jnp....]
    all_to_all x1, waiting for transfers between devices: 19.9 us -> 25 us  [body(): lax.all_to_all(outgoing, 'req', split_axis=0, concat_axis=0, tiled=True)]
    psum x1, waiting for transfers between devices: 50.8 us -> 55 us  [body(): lax.psum(partial_value.astype(jnp.bfloat16), 'head').astype(jnp.float32)]
    unnamed x28 -> x22, local copies, waits for them, and re-layouts: 14 us -> 14.9 us
  transfers between devices with their start and end apart: 11 -> 11, of which waited for: 6 -> 7; matrix products, arithmetic and copies ran while one was open for 33% -> 23% of each run, Pallas kernels for 0% -> 0%
where the time goes in v7:
time: 273 us; the launch traced here: 272 us
  waiting for transfers between devices  131 us (48%)
  matrix products  69.7 us (26%)
  local copies, waits for them, and re-layouts  26.7 us (10%)
  starting transfers between devices  16.2 us (6%)
  between operations  14.4 us (5%)
  other arithmetic  13.8 us (5%)
    psum x1, waiting for transfers between devices, body(): lax.psum(partial_value.astype(jnp.bfloat16), 'head').astype(jnp.float32)  55 us
    ppermute x6, waiting for transfers between devices, partner_move(): return lax.ppermute(block, 'req', [(i, i ^ step) for i in range(req_total)])  51 us
    dot_general x2, matrix products, experts_on(): jnp.einsum('ned,egdf->gnef', flat, w_gate_up, preferred_element_type=jnp....  30.1 us
    all_to_all x1, waiting for transfers between devices, body(): lax.all_to_all(outgoing, 'req', split_axis=0, concat_axis=0, tiled=True)  25 us
    dot_general x2, matrix products, experts_on(): jnp.einsum('nef,efd->ned', hidden, w_down, preferred_element_type=jnp.flo...  19.9 us
    unnamed x22, local copies, waits for them, and re-layouts  14.9 us
    dot_general x4, matrix products, body(): jnp.einsum('tec,ced->ted', dispatch_bf, part, preferred_element_type=jnp....  8.08 us
    ppermute x6, starting transfers between devices, partner_move(): return lax.ppermute(block, 'req', [(i, i ^ step) for i in range(req_total)])  7.17 us
  transfers between devices with their start and end apart: 11, of which 7 were waited for; matrix products, arithmetic and copies ran while one was open for 23% of the time, Pallas kernels for 0%

profile of v7, /device:TPU:0, one launch (start us, length us, event | category | flops | bytes accessed | tf_op | source)
XLA Modules:
  0.0 271.9 jit_solution(14377215154579655694)
XLA Ops:
  7.3 9.9 %copy.48 = bf16[2304,3,512]{0,2,1:T(8,128)(2,1)} copy(bf16[2304,3,512]{2,0,1:T(8,128)(2,1)} %param.17) | data formatting | bytes 14155776 | tf_op args[2]
  17.2 0.3 fusion.15
  17.5 5.2 %fusion.29 = f32[256,3,8,64]{0,3,2,1:T(8,128)S(1)} fusion(bf16[3,8,64,2304]{3,2,1,0:T(8,128)(2,1)} %bitcast.134, bf16[1,256,2304]{2,1,0:T(8,128)(2,1)S(1)} %copy-done.2, f32[2304]{0:T(1024)} %param.16, f32[256]{0:T(256)S(1)} %add_rsqrt_fusion.1), kind=kOutput, calls=%fused_computation.46 | convolution fusion | flops 1814298624 | bytes 9840640 | tf_op jit(solution)/shard_map/dot_general | solution.py:73
  22.8 0.2 multiply_cosine_fusion
  23.0 0.2 subtract_convert_fusion.1
  23.2 3.1 %collective-permute-start.1 = (bf16[256,8,64]{0,2,1:T(8,128)(2,1)S(1)}, bf16[256,8,64]{0,2,1:T(8,128)(2,1)}, u32[]{:S(2)}, u32[]{:S(2)}) collective-permute-start(bf16[256,8,64]{0,2,1:T(8,128)(2,1)S(1)} %pad_maximum_fusion.1), channel_id=1, source_target_pairs={{0,1},{2,3},{4,5},{6,7},{8,9},{10,11},{12,13},{14,15},{16,17},{18,... | collective-permute-start | bytes 786440 | tf_op jit(solution)/shard_map/ppermute | solution.py:13
  26.2 2.0 collective-permute-start
  28.2 0.7 constant_dynamic-slice_fusion.2
  28.9 0.1 copy.49
  29.1 0.1 eq.108
  29.3 0.6 reduce-window.6
  29.9 0.2 slice_reduce_fusion
  30.1 0.2 reduce-window.9
  30.4 0.2 compare_and_fusion
  30.6 1.9 fusion.4
  32.4 1.3 fusion.8
  33.8 2.2 fusion.42
  35.9 1.8 convolution_convert_fusion.1
  37.8 0.2 reduce-scatter.2.cloned.1.call-start
  38.1 0.2 eq.112
  38.4 0.6 dynamic_slice.25
  39.0 0.2 convert_reduce_fusion
  39.3 0.7 fusion.97
  40.0 0.7 dynamic-slice_bitcast_fusion
  40.6 0.1 select_reduce_fusion.2
  40.9 55.0 %all-reduce.2.cloned.1.call-done = bf16[256,2304]{1,0:T(8,128)(2,1)} async-done(((bf16[256,2304]{1,0:T(8,128)(2,1)}), bf16[256,2304]{1,0:T(8,128)(2,1)}) %all-reduce.2.cloned.1.call-update) | async-done | bytes 1179664 | tf_op jit(solution)/shard_map/psum | solution.py:104
  96.0 1.8 fusion.12
  97.8 0.5 fusion.31
  98.3 0.1 convert_bitcast_fusion.1
  98.4 1.5 collective-permute-start.2
  100.0 1.5 collective-permute-start.3
  101.4 0.7 add_compare_fusion
  102.2 1.7 bitcast_select_fusion
  103.8 16.3 %collective-permute-done.2 = bf16[96,2,2304]{2,0,1:T(8,128)(2,1)S(1)} collective-permute-done((bf16[96,2,2304]{2,0,1:T(8,128)(2,1)S(1)}, bf16[96,2,2304]{2,0,1:T(8,128)(2,1)S(1)}, u32[]{:S(2)}, u32[]{:S(2)}) %collective-permute-start.2) | collective-permute-done | bytes 884768 | tf_op jit(solution)/shard_map/ppermute | solution.py:127
  120.1 1.2 collective-permute-done.3
  121.3 0.3 pad_maximum_fusion
  121.6 0.2 copy.51
  121.7 15.9 %convolution_bitcast_fusion = f32[2,288,2,1440]{3,1,0,2:T(8,128)} fusion(bf16[288,2,2304,1]{2,0,3,1:T(8,128)(2,1)S(1)} %bitcast.137, bf16[2,2,2304,1440]{2,3,1,0:T(8,128)(2,1)} %param.22), kind=kOutput, calls=%fused_computation.8 | convolution fusion | flops 7644119040 | bytes 35831808 | tf_op jit(solution)/shard_map/ned,egdf->gnef/dot_general | solution.py:132
  137.6 1.5 collective-permute-start.6
  139.1 11.2 %fusion.3 = bf16[288,2,2304]{2,0,1:T(8,128)(2,1)S(1)} fusion(bf16[2,1440,2304]{2,1,0:T(8,128)(2,1)} %param.23, f32[2,288,2,1440]{3,1,0,2:T(8,128)} %convolution_bitcast_fusion), kind=kOutput, calls=%fused_computation.9 | convolution fusion | flops 3828363264 | bytes 22560768 | tf_op jit(solution)/shard_map/nef,efd->ned/dot_general | solution.py:134
  150.3 1.5 copy-done.4
  151.8 1.4 fusion.79
  153.2 0.6 collective-permute-start.4
  153.7 4.3 %collective-permute-done.6 = bf16[96,2,2304]{2,0,1:T(8,128)(2,1)S(1)} collective-permute-done((bf16[96,2,2304]{2,0,1:T(8,128)(2,1)S(1)}, bf16[96,2,2304]{2,0,1:T(8,128)(2,1)S(1)}, u32[]{:S(2)}, u32[]{:S(2)}) %collective-permute-start.6) | collective-permute-done | bytes 884768 | tf_op jit(solution)/shard_map/ppermute | solution.py:127
  158.0 14.2 %convolution_bitcast_fusion.1 = f32[2,96,2,1440]{3,1,0,2:T(8,128)} fusion(bf16[2,2,2304,1440]{2,3,1,0:T(8,128)(2,1)} %param.22, bf16[96,2,2304]{2,0,1:T(8,128)(2,1)S(1)} %collective-permute-done.6), kind=kOutput, calls=%fused_computation.22 | convolution fusion | flops 2548039680 | bytes 29638656 | tf_op jit(solution)/shard_map/ned,egdf->gnef/dot_general | solution.py:132
  172.3 8.8 %fusion.5 = bf16[96,2,2304]{2,0,1:T(8,128)(2,1)} fusion(bf16[2,1440,2304]{2,1,0:T(8,128)(2,1)} %param.23, f32[2,96,2,1440]{3,1,0,2:T(8,128)} %convolution_bitcast_fusion.1), kind=kOutput, calls=%fused_computation.15 | convolution fusion | flops 1276121088 | bytes 16367616 | tf_op jit(solution)/shard_map/nef,efd->ned/dot_general | solution.py:134
  181.0 1.5 collective-permute-start.7
  182.6 2.3 gather_fusion
  184.8 0.6 collective-permute-start.5
  185.5 2.0 fusion.45
  187.5 2.0 convolution_add_fusion.1
  189.5 12.4 %collective-permute-done.7 = bf16[96,2,2304]{2,0,1:T(8,128)(2,1)} collective-permute-done((bf16[96,2,2304]{2,0,1:T(8,128)(2,1)}, bf16[96,2,2304]{2,0,1:T(8,128)(2,1)}, u32[]{:S(2)}, u32[]{:S(2)}) %collective-permute-start.7) | collective-permute-done | bytes 884768 | tf_op jit(solution)/shard_map/ppermute | solution.py:127
  201.9 2.0 fusion.80
  203.9 16.8 %collective-permute-done.5 = bf16[96,2,2304]{2,0,1:T(8,128)(2,1)S(1)} collective-permute-done((bf16[96,2,2304]{2,0,1:T(8,128)(2,1)}, bf16[96,2,2304]{2,0,1:T(8,128)(2,1)S(1)}, u32[]{:S(2)}, u32[]{:S(2)}) %collective-permute-start.5) | collective-permute-done | bytes 884768 | tf_op jit(solution)/shard_map/ppermute | solution.py:127
  220.6 2.1 fusion.22
  222.7 2.4 copy.54
  225.1 1.6 broadcast_select_fusion.1
  226.7 3.8 %all-to-all-start = ((bf16[16,64,2,512]{3,1,2,0:T(8,128)(2,1)}), bf16[16,64,2,512]{3,1,2,0:T(8,128)(2,1)S(1)}, u32[]{:S(2)}, u32[]{:S(2)}) async-start(bf16[16,64,2,512]{3,1,2,0:T(8,128)(2,1)} %broadcast_select_fusion.1), calls=%async_computation.1 | async-start | bytes 4194304 | tf_op jit(solution)/shard_map/all_to_all | solution.py:196
  230.6 0.1 select_reduce_fusion.1
  230.8 25.0 %all-to-all-done = bf16[16,64,2,512]{3,1,2,0:T(8,128)(2,1)S(1)} async-done(((bf16[16,64,2,512]{3,1,2,0:T(8,128)(2,1)}), bf16[16,64,2,512]{3,1,2,0:T(8,128)(2,1)S(1)}, u32[]{:S(2)}, u32[]{:S(2)}) %all-to-all-start) | async-done | bytes 2097184 | tf_op jit(solution)/shard_map/all_to_all | solution.py:196
  255.8 2.0 gather_fusion.1
  257.8 2.0 broadcast_select_fusion
  259.8 3.5 %copy.56 = bf16[16,64,2,512]{3,2,1,0:T(2,128)(2,1)} copy(bf16[16,64,2,512]{3,1,2,0:T(8,128)(2,1)S(1)} %broadcast_select_fusion) | data formatting | bytes 4194304
  263.3 1.7 fusion.60
  (59 shorter events, 1.0 us)
Async XLA Ops:
  7.2 28.7 %copy-start = (bf16[512,2304]{1,0:T(8,128)(2,1)S(1)}, bf16[512,2304]{1,0:T(8,128)(2,1)}, u32[]{:S(2)}) copy-start(bf16[512,2304]{1,0:T(8,128)(2,1)} %param.18) | copy-start | bytes 7077892
  7.2 88.8 %all-reduce.2.cloned.1.call-start = ((), (), s32[]{:S(2)}) async-start(), calls=%async_computation.2 | async-start | bytes 2359296 | tf_op jit(solution)/shard_map/psum | solution.py:104
  7.3 9.9 %copy-start.2 = (bf16[1,256,2304]{2,1,0:T(8,128)(2,1)S(1)}, bf16[1,256,2304]{2,1,0:T(8,128)(2,1)}, u32[]{:S(2)}) copy-start(bf16[1,256,2304]{2,1,0:T(8,128)(2,1)} %param.15) | copy-start | bytes 3538948
  23.2 7.4 %collective-permute-start.1 = (bf16[256,8,64]{0,2,1:T(8,128)(2,1)S(1)}, bf16[256,8,64]{0,2,1:T(8,128)(2,1)}, u32[]{:S(2)}, u32[]{:S(2)}) collective-permute-start(bf16[256,8,64]{0,2,1:T(8,128)(2,1)S(1)} %pad_maximum_fusion.1), channel_id=1, source_target_pairs={{0,1},{2,3},{4,5},{6,7},{8,9},{10,11},{12,13},{14,15},{16,17},{18,... | collective-permute-start | bytes 786440 | tf_op jit(solution)/shard_map/ppermute | solution.py:13
  26.2 7.5 %collective-permute-start = (bf16[256,8,64]{0,2,1:T(8,128)(2,1)S(1)}, bf16[256,8,64]{0,2,1:T(8,128)(2,1)}, u32[]{:S(2)}, u32[]{:S(2)}) collective-permute-start(bf16[256,8,64]{0,2,1:T(8,128)(2,1)S(1)} %fusion.61), channel_id=1, source_target_pairs={{0,1},{2,3},{4,5},{6,7},{8,9},{10,11},{12,13},{14,15},{16,17},{18,... | collective-permute-start | bytes 786440 | tf_op jit(solution)/shard_map/ppermute | solution.py:13
  35.9 2.5 copy-start.9
  35.9 3.1 %copy-start.6 = (s32[4,16]{1,0:T(4,128)S(1)}, s32[4,16]{1,0:T(4,128)}, u32[]{:S(2)}) copy-start(s32[4,16]{1,0:T(4,128)} %param.26) | copy-start | bytes 772
  37.8 58.2 %copy-start.3 = (bf16[1,256,2304]{2,1,0:T(8,128)(2,1)S(1)}, bf16[1,256,2304]{2,1,0:T(8,128)(2,1)}, u32[]{:S(2)}) copy-start(bf16[1,256,2304]{2,1,0:T(8,128)(2,1)} %param.15) | copy-start | bytes 3538948
  37.8 60.0 %copy-start.7 = (f32[2304]{0:T(1024)S(1)}, f32[2304]{0:T(1024)}, u32[]{:S(2)}) copy-start(f32[2304]{0:T(1024)} %param.19) | copy-start | bytes 27652
  37.8 225.5 %reduce-scatter.2.cloned.1.call-start = ((), (), s32[]{:S(2)}) async-start(), calls=%async_computation.3 | async-start | bytes 1474560 | tf_op jit(solution)/shard_map/reduce_scatter | solution.py:160
  98.3 3.9 %copy-start.5 = (bf16[1,16,64,2,512]{4,3,2,1,0:T(2,128)(2,1)S(1)}, bf16[1,16,64,2,512]{4,3,2,1,0:T(2,128)(2,1)}, u32[]{:S(2)}) copy-start(bf16[1,16,64,2,512]{4,3,2,1,0:T(2,128)(2,1)} %param.24) | copy-start | bytes 6291460
  98.4 21.7 %collective-permute-start.2 = (bf16[96,2,2304]{2,0,1:T(8,128)(2,1)S(1)}, bf16[96,2,2304]{2,0,1:T(8,128)(2,1)S(1)}, u32[]{:S(2)}, u32[]{:S(2)}) collective-permute-start(bf16[96,2,2304]{2,0,1:T(8,128)(2,1)S(1)} %get-tuple-element.18), channel_id=1, source_target_pairs={{0,8},{8,0},{16,24},{24,16},{1,9},{9,1},{17,25},{25,17},{2,10},{10... | collective-permute-start | bytes 2654216 | tf_op jit(solution)/shard_map/ppermute | solution.py:127
  100.0 21.3 %collective-permute-start.3 = (bf16[96,2,2304]{2,0,1:T(8,128)(2,1)S(1)}, bf16[96,2,2304]{2,0,1:T(8,128)(2,1)S(1)}, u32[]{:S(2)}, u32[]{:S(2)}) collective-permute-start(bf16[96,2,2304]{2,0,1:T(8,128)(2,1)S(1)} %get-tuple-element.18), channel_id=1, source_target_pairs={{0,16},{8,24},{16,0},{24,8},{1,17},{9,25},{17,1},{25,9},{2,18},{10... | collective-permute-start | bytes 2654216 | tf_op jit(solution)/shard_map/ppermute | solution.py:127
  137.6 20.4 %collective-permute-start.6 = (bf16[96,2,2304]{2,0,1:T(8,128)(2,1)S(1)}, bf16[96,2,2304]{2,0,1:T(8,128)(2,1)S(1)}, u32[]{:S(2)}, u32[]{:S(2)}) collective-permute-start(bf16[96,2,2304]{2,0,1:T(8,128)(2,1)S(1)} %collective-permute-done.2), channel_id=1, source_target_pairs={{0,16},{8,24},{16,0},{24,8},{1,17},{9,25},{17,1},{25,9},{2,18},{10... | collective-permute-start | bytes 2654216 | tf_op jit(solution)/shard_map/ppermute | solution.py:127
  150.2 1.5 copy-start.4
  153.2 34.3 %collective-permute-start.4 = (bf16[96,2,2304]{2,0,1:T(8,128)(2,1)}, bf16[96,2,2304]{2,0,1:T(8,128)(2,1)}, u32[]{:S(2)}, u32[]{:S(2)}) collective-permute-start(bf16[96,2,2304]{2,0,1:T(8,128)(2,1)} %get-tuple-element.16), channel_id=1, source_target_pairs={{0,8},{8,0},{16,24},{24,16},{1,9},{9,1},{17,25},{25,17},{2,10},{10... | collective-permute-start | bytes 2654216 | tf_op jit(solution)/shard_map/ppermute | solution.py:127
  181.0 20.8 %collective-permute-start.7 = (bf16[96,2,2304]{2,0,1:T(8,128)(2,1)}, bf16[96,2,2304]{2,0,1:T(8,128)(2,1)}, u32[]{:S(2)}, u32[]{:S(2)}) collective-permute-start(bf16[96,2,2304]{2,0,1:T(8,128)(2,1)} %fusion.5), channel_id=1, source_target_pairs={{0,24},{8,16},{16,8},{24,0},{1,25},{9,17},{17,9},{25,1},{2,26},{10... | collective-permute-start | bytes 2654216 | tf_op jit(solution)/shard_map/ppermute | solution.py:127
  184.8 35.8 %collective-permute-start.5 = (bf16[96,2,2304]{2,0,1:T(8,128)(2,1)}, bf16[96,2,2304]{2,0,1:T(8,128)(2,1)S(1)}, u32[]{:S(2)}, u32[]{:S(2)}) collective-permute-start(bf16[96,2,2304]{2,0,1:T(8,128)(2,1)} %get-tuple-element.15), channel_id=1, source_target_pairs={{0,16},{8,24},{16,0},{24,8},{1,17},{9,25},{17,1},{25,9},{2,18},{10... | collective-permute-start | bytes 2654216 | tf_op jit(solution)/shard_map/ppermute | solution.py:127
  226.7 3.9 %copy-start.8 = (s32[4,16]{1,0:T(4,128)S(1)}, s32[4,16]{1,0:T(4,128)}, u32[]{:S(2)}) copy-start(s32[4,16]{1,0:T(4,128)} %param.27) | copy-start | bytes 772
  226.7 29.0 %all-to-all-start = ((bf16[16,64,2,512]{3,1,2,0:T(8,128)(2,1)}), bf16[16,64,2,512]{3,1,2,0:T(8,128)(2,1)S(1)}, u32[]{:S(2)}, u32[]{:S(2)}) async-start(bf16[16,64,2,512]{3,1,2,0:T(8,128)(2,1)} %broadcast_select_fusion.1), calls=%async_computation.1 | async-start | bytes 4194304 | tf_op jit(solution)/shard_map/all_to_all | solution.py:196
  257.8 7.2 %copy-start.1 = (bf16[512,2304]{1,0:T(8,128)(2,1)S(1)}, bf16[512,2304]{1,0:T(8,128)(2,1)}, u32[]{:S(2)}) copy-start(bf16[512,2304]{1,0:T(8,128)(2,1)} %param.18) | copy-start | bytes 7077892
Sparse Core Ops, SparseCore 0:
  37.9 57.9 all-reduce.1
  225.2 27.7 reduce-scatter.1

commit v8 on v6

--- a/solution.py
+++ b/solution.py
@@ -122,24 +122,34 @@
         preferred_element_type=jnp.float32,
     ).astype(jnp.bfloat16)
     req_total = lax.axis_size("req")
+    dev_total = lax.axis_size("dev")
+    split = dev_total > 1 and experts_here % dev_total == 0
+    per_core = experts_here // dev_total if split else experts_here
+    if split:
+        first_here = dev_index * per_core
+        gate_up_here = lax.dynamic_slice_in_dim(w_gate_up, first_here, per_core, 0)
+        down_here = lax.dynamic_slice_in_dim(w_down, first_here, per_core, 0)
+        rows_here = lax.all_to_all(picked_own, "dev", split_axis=1, concat_axis=0, tiled=True)
+    else:
+        gate_up_here, down_here, rows_here = w_gate_up, w_down, picked_own
 
     def partner_move(block, step):
         return lax.ppermute(block, "req", [(i, i ^ step) for i in range(req_total)])
 
     def experts_on(rows):
         groups = rows.shape[0]
-        flat = rows.reshape(groups * capacity, experts_here, model_width)
-        both = jnp.einsum("ned,egdf->gnef", flat, w_gate_up, preferred_element_type=jnp.float32)
+        flat = rows.reshape(groups * rows.shape[1], per_core, model_width)
+        both = jnp.einsum("ned,egdf->gnef", flat, gate_up_here, preferred_element_type=jnp.float32)
         hidden = (jax.nn.silu(both[0]) * both[1]).astype(jnp.bfloat16)
-        down = jnp.einsum("nef,efd->ned", hidden, w_down, preferred_element_type=jnp.float32)
-        return down.astype(jnp.bfloat16).reshape(groups, capacity, experts_here, model_width)
-
-    arrived = {0: picked_own}
+        down = jnp.einsum("nef,efd->ned", hidden, down_here, preferred_element_type=jnp.float32)
+        return down.astype(jnp.bfloat16).reshape(rows.shape)
+
+    arrived = {0: rows_here}
     for step in range(1, req_total):
         if step == 3:
             arrived[step] = partner_move(arrived[1], 2)
         else:
-            arrived[step] = partner_move(picked_own, step)
+            arrived[step] = partner_move(rows_here, step)
     plan = [[0], [1, 2]] + ([list(range(3, req_total))] if req_total > 3 else [])
     plan = [[k for k in group if k < req_total] for group in plan]
     returned = []
@@ -149,7 +159,10 @@
         outs = experts_on(jnp.stack([arrived[k] for k in group], axis=0))
         for slot_index, step in enumerate(group):
             part = outs[slot_index]
-            returned.append(part if step == 0 else partner_move(part, step))
+            part = part if step == 0 else partner_move(part, step)
+            if split:
+                part = lax.all_to_all(part, "dev", split_axis=0, concat_axis=1, tiled=True)
+            returned.append(part)
     token_weights = jnp.sum(own_combine, axis=-1)
     dispatch_bf = own_dispatch.astype(jnp.bfloat16)
     selected = sum(

time: 257 us -> 313 us (1.22)
  matrix products: 91.8 us -> 55.9 us
  blocking collectives: 0 us -> 31.1 us
  local copies, waits for them, and re-layouts: 26.8 us -> 52.6 us
  waiting for transfers between devices: 90.2 us -> 113 us
  other arithmetic: 16.6 us -> 27.7 us
    all_to_all x0 -> x5, blocking collectives: none -> 31.1 us  [the longest x4 25.8 us: body(): part = lax.all_to_all(part, 'dev', split_axis=0, concat_axis=1, tiled=True)]
    dot_general x5 -> x6, matrix products: 61 us -> 33.2 us  [the longest x3 25.9 us: experts_on(): jnp.einsum('ned,egdf->gnef', flat, gate_up_here, preferred_element_type=j...]
    unnamed x28 -> x54, local copies, waits for them, and re-layouts: 14 us -> 40.4 us
    ppermute x6, waiting for transfers between devices: 19.5 us -> 32.2 us  [partner_move(): return lax.ppermute(block, 'req', [(i, i ^ step) for i in range(req_total)])]
    ppermute x0 -> x3, other arithmetic: none -> 9.36 us  [partner_move(): return lax.ppermute(block, 'req', [(i, i ^ step) for i in range(req_total)])]
    dot_general x4, matrix products: 19.1 us -> 11.2 us  [body(): jnp.einsum('tec,ced->ted', dispatch_bf, part, preferred_element_type=jnp....]
    all_to_all x1, waiting for transfers between devices: 19.9 us -> 25.1 us  [body(): lax.all_to_all(outgoing, 'req', split_axis=0, concat_axis=0, tiled=True)]
    psum x1, waiting for transfers between devices: 50.8 us -> 55.2 us  [body(): lax.psum(partial_value.astype(jnp.bfloat16), 'head').astype(jnp.float32)]
  transfers between devices with their start and end apart: 11 -> 11, of which waited for: 6 -> 5; matrix products, arithmetic and copies ran while one was open for 33% -> 22% of each run, Pallas kernels for 0% -> 0%
where the time goes in v8:
time: 313 us; the launch traced here: 311 us
  waiting for transfers between devices  113 us (36%)
  matrix products  55.9 us (18%)
  local copies, waits for them, and re-layouts  52.6 us (17%)
  blocking collectives  31.1 us (10%)
  other arithmetic  27.7 us (9%)
  starting transfers between devices  16.9 us (5%)
  between operations  14.5 us (5%)
    psum x1, waiting for transfers between devices, body(): lax.psum(partial_value.astype(jnp.bfloat16), 'head').astype(jnp.float32)  55.2 us
    unnamed x54, local copies, waits for them, and re-layouts  40.4 us
    ppermute x6, waiting for transfers between devices, partner_move(): return lax.ppermute(block, 'req', [(i, i ^ step) for i in range(req_total)])  32.2 us
    dot_general x3, matrix products, experts_on(): jnp.einsum('ned,egdf->gnef', flat, gate_up_here, preferred_element_type=j...  25.9 us
    all_to_all x4, blocking collectives, body(): part = lax.all_to_all(part, 'dev', split_axis=0, concat_axis=1, tiled=True)  25.8 us
    all_to_all x1, waiting for transfers between devices, body(): lax.all_to_all(outgoing, 'req', split_axis=0, concat_axis=0, tiled=True)  25.1 us
    dot_general x4, matrix products, body(): jnp.einsum('tec,ced->ted', dispatch_bf, part, preferred_element_type=jnp....  11.2 us
    ppermute x3, other arithmetic, partner_move(): return lax.ppermute(block, 'req', [(i, i ^ step) for i in range(req_total)])  9.36 us
  transfers between devices with their start and end apart: 11, of which 5 were waited for; matrix products, arithmetic and copies ran while one was open for 22% of the time, Pallas kernels for 0%

profile of v8, /device:TPU:0, one launch (start us, length us, event | category | flops | bytes accessed | tf_op | source)
XLA Modules:
  0.0 311.2 jit_solution(5563176906753510006)
XLA Ops:
  7.3 9.9 %copy.53 = bf16[2304,3,512]{0,2,1:T(8,128)(2,1)} copy(bf16[2304,3,512]{2,0,1:T(8,128)(2,1)} %param.17) | data formatting | bytes 14155776 | tf_op args[2]
  17.5 5.2 %fusion.68 = f32[256,3,8,64]{0,3,2,1:T(8,128)S(1)} fusion(bf16[3,8,64,2304]{3,2,1,0:T(8,128)(2,1)} %bitcast.186, bf16[1,256,2304]{2,1,0:T(8,128)(2,1)S(1)} %copy-done.2, f32[2304]{0:T(1024)} %param.16, f32[256]{0:T(256)S(1)} %add_rsqrt_fusion.1), kind=kOutput, calls=%fused_computation.64 | convolution fusion | flops 1814298624 | bytes 9840640 | tf_op jit(solution)/shard_map/dot_general | solution.py:73
  23.2 3.1 collective-permute-start.1
  26.2 2.0 collective-permute-start
  28.2 0.7 constant_dynamic-slice_fusion.2
  30.6 1.9 fusion.35
  32.4 1.3 fusion.42
  33.8 2.2 fusion.83
  35.9 1.8 convolution_convert_fusion
  39.1 0.7 fusion.143
  39.8 0.7 dynamic-slice_bitcast_fusion
  40.7 55.2 %all-reduce.2.cloned.1.call-done = bf16[256,2304]{1,0:T(8,128)(2,1)} async-done(((bf16[256,2304]{1,0:T(8,128)(2,1)}), bf16[256,2304]{1,0:T(8,128)(2,1)}) %all-reduce.2.cloned.1.call-update) | async-done | bytes 1179664 | tf_op jit(solution)/shard_map/psum | solution.py:104
  95.9 1.8 fusion.52
  98.4 5.4 %all_to_all.95 = bf16[96,2,2304]{2,0,1:T(8,128)(2,1)} all-to-all(bf16[96,2,2304]{2,0,1:T(8,128)(2,1)S(1)} %convert_bitcast_fusion.1), channel_id=1, replica_groups=mesh['req'=4,'head'=4,'dev'=2] {'dev'}, dimensions={1} | all-to-all | bytes 1769472 | tf_op jit(solution)/shard_map/all_to_all | solution.py:132
  103.7 1.5 collective-permute-start.2
  105.2 1.5 collective-permute-start.3
  106.7 0.7 add_compare_fusion
  107.4 1.7 bitcast_select_fusion
  109.1 2.3 gather_fusion
  111.3 14.4 %collective-permute-done.2 = bf16[192,1,2304]{2,0,1:T(8,128)(2,1)} collective-permute-done((bf16[192,1,2304]{2,0,1:T(8,128)(2,1)}, bf16[192,1,2304]{2,0,1:T(8,128)(2,1)}, u32[]{:S(2)}, u32[]{:S(2)}) %collective-permute-start.2) | collective-permute-done | bytes 884768 | tf_op jit(solution)/shard_map/ppermute | solution.py:137
  125.8 1.2 collective-permute-done.3
  127.0 1.7 pad_maximum_fusion
  128.8 9.9 %fusion.26 = f32[2,384,1,1440]{1,3,0,2:T(8,128)S(1)} fusion(bf16[384,2304,1]{1,0,2:T(8,128)(2,1)S(1)} %bitcast.193, bf16[2,2,2304,1440]{2,3,1,0:T(8,128)(2,1)} %param.22, s32[]{:T(128)S(6)} %select_n.44), kind=kOutput, calls=%fused_computation.30 | convolution fusion | flops 5096079360 | bytes 19464196 | tf_op jit(solution)/shard_map/ned,egdf->gnef/dot_general | solution.py:142
  138.7 3.0 fusion.23
  141.7 1.4 fusion.127
  143.6 1.5 collective-permute-start.5
  145.7 7.6 %fusion.44 = f32[2,192,1,1440]{3,1,0,2:T(8,128)S(1)} fusion(bf16[192,2304,1]{1,0,2:T(8,128)(2,1)} %bitcast.26, bf16[2,2,2304,1440]{2,3,1,0:T(8,128)(2,1)} %param.22, s32[]{:T(128)S(6)} %select_n.44), kind=kOutput, calls=%fused_computation.38 | convolution fusion | flops 2548039680 | bytes 16367620 | tf_op jit(solution)/shard_map/ned,egdf->gnef/dot_general | solution.py:142
  153.3 2.6 fusion.36
  156.4 3.1 %reduce.7 = bf16[192,2304]{1,0:T(8,128)(2,1)} reduce(bf16[192,1,2304]{2,0,1:T(8,128)(2,1)} %fusion.36, bf16[]{:T(256)} %broadcast.399), dimensions={1}, to_apply=%copy.56.reduce_sub_computation | reduce | bytes 1769474 | tf_op jit(solution)/shard_map/convert_element_type | solution.py:145
  159.5 2.0 reshape.485
  161.5 6.4 %all_to_all.96 = bf16[2,2,110592]{2,1,0:T(2,128)(2,1)} all-to-all(bf16[2,2,110592]{2,1,0:T(2,128)(2,1)} %reshape.485), channel_id=1, replica_groups=mesh['req'=4,'head'=4,'dev'=2] {'dev'}, dimensions={0} | all-to-all | bytes 1769472 | tf_op jit(solution)/shard_map/all_to_all | solution.py:164
  168.0 2.7 reshape.486
  170.7 1.6 copy.64
  172.2 3.0 fusion.128
  175.2 3.1 %reduce.8 = bf16[192,2304]{1,0:T(8,128)(2,1)} reduce(bf16[192,1,2304]{2,0,1:T(8,128)(2,1)} %collective-permute-done.4, bf16[]{:T(256)} %broadcast.399), dimensions={1}, to_apply=%copy.57.reduce_sub_computation | reduce | bytes 1769474 | tf_op jit(solution)/shard_map/ppermute | solution.py:137
  178.3 2.1 reshape.487
  180.4 6.5 %all_to_all.97 = bf16[2,2,110592]{2,1,0:T(2,128)(2,1)} all-to-all(bf16[2,2,110592]{2,1,0:T(2,128)(2,1)} %reshape.487), channel_id=1, replica_groups=mesh['req'=4,'head'=4,'dev'=2] {'dev'}, dimensions={0} | all-to-all | bytes 1769472 | tf_op jit(solution)/shard_map/all_to_all | solution.py:164
  186.9 2.7 reshape.488
  189.6 2.5 copy.65
  192.1 3.1 %reduce.9 = bf16[192,2304]{1,0:T(8,128)(2,1)} reduce(bf16[192,1,2304]{2,0,1:T(8,128)(2,1)} %collective-permute-done.5, bf16[]{:T(256)} %broadcast.399), dimensions={1}, to_apply=%copy.58.reduce_sub_computation | reduce | bytes 1769474 | tf_op jit(solution)/shard_map/ppermute | solution.py:137
  195.2 2.1 reshape.489
  197.3 6.4 %all_to_all.98 = bf16[2,2,110592]{2,1,0:T(2,128)(2,1)} all-to-all(bf16[2,2,110592]{2,1,0:T(2,128)(2,1)} %reshape.489), channel_id=1, replica_groups=mesh['req'=4,'head'=4,'dev'=2] {'dev'}, dimensions={0} | all-to-all | bytes 1769472 | tf_op jit(solution)/shard_map/all_to_all | solution.py:164
  203.7 2.7 reshape.490
  206.4 1.7 copy.66
  208.2 8.4 %fusion.47 = f32[2,192,1,1440]{3,1,0,2:T(8,128)S(1)} fusion(bf16[2,2,2304,1440]{2,3,1,0:T(8,128)(2,1)} %param.22, s32[]{:T(128)S(6)} %select_n.44, bf16[192,1,2304]{2,0,1:T(8,128)(2,1)} %collective-permute-done.6), kind=kOutput, calls=%fused_computation.39 | convolution fusion | flops 2548039680 | bytes 16367620 | tf_op jit(solution)/shard_map/ned,egdf->gnef/dot_general | solution.py:142
  217.2 1.7 fusion.39
  218.9 2.5 collective-permute-start.7
  221.3 0.8 convolution_add_fusion.2
  222.1 3.0 convolution_add_fusion.1
  225.1 16.5 %collective-permute-done.7 = bf16[192,1,2304]{2,0,1:T(8,128)(2,1)} collective-permute-done((bf16[192,1,2304]{2,0,1:T(8,128)(2,1)S(1)}, bf16[192,1,2304]{2,0,1:T(8,128)(2,1)}, u32[]{:S(2)}, u32[]{:S(2)}) %collective-permute-start.7) | collective-permute-done | bytes 884768 | tf_op jit(solution)/shard_map/ppermute | solution.py:137
  241.6 3.1 %reduce.10 = bf16[192,2304]{1,0:T(8,128)(2,1)} reduce(bf16[192,1,2304]{2,0,1:T(8,128)(2,1)} %collective-permute-done.7, bf16[]{:T(256)} %broadcast.399), dimensions={1}, to_apply=%copy.59.reduce_sub_computation | reduce | bytes 1769474 | tf_op jit(solution)/shard_map/ppermute | solution.py:137
  244.7 2.0 reshape.491
  246.8 6.4 %all_to_all.99 = bf16[2,2,110592]{2,1,0:T(2,128)(2,1)} all-to-all(bf16[2,2,110592]{2,1,0:T(2,128)(2,1)} %reshape.491), channel_id=1, replica_groups=mesh['req'=4,'head'=4,'dev'=2] {'dev'}, dimensions={0} | all-to-all | bytes 1769472 | tf_op jit(solution)/shard_map/all_to_all | solution.py:164
  253.2 2.7 reshape.492
  255.9 1.6 copy.67
  257.5 4.5 %fusion.63 = bf16[256,2304]{0,1:T(8,128)(2,1)} fusion(f32[2,2304,256]{2,1,0:T(8,128)} %convolution_add_fusion.1, bf16[96,2,2304]{2,0,1:T(8,128)(2,1)S(1)} %bitcast.191, bf16[256,2,96]{0,2,1:T(8,128)(2,1)S(1)} %get-tuple-element.14, f32[256,2]{0,1:T(2,128)S(1)} %get-tuple-element.13), kind=kOutput, calls=%fused_computation.60 | convolution fusion | flops 229441536 | bytes 6883328 | tf_op jit(solution)/shard_map/tec,ced->ted/dot_general | solution.py:169
  262.0 2.4 copy.60
  264.4 1.6 broadcast_select_fusion.1
  266.0 3.8 %all-to-all-start.5 = ((bf16[16,64,2,512]{3,1,2,0:T(8,128)(2,1)}), bf16[16,64,2,512]{3,1,2,0:T(8,128)(2,1)S(1)}, u32[]{:S(2)}, u32[]{:S(2)}) async-start(bf16[16,64,2,512]{3,1,2,0:T(8,128)(2,1)} %broadcast_select_fusion.1), calls=%async_computation.6 | async-start | bytes 4194304 | tf_op jit(solution)/shard_map/all_to_all | solution.py:209
  270.0 25.1 %all-to-all-done.5 = bf16[16,64,2,512]{3,1,2,0:T(8,128)(2,1)S(1)} async-done(((bf16[16,64,2,512]{3,1,2,0:T(8,128)(2,1)}), bf16[16,64,2,512]{3,1,2,0:T(8,128)(2,1)S(1)}, u32[]{:S(2)}, u32[]{:S(2)}) %all-to-all-start.5) | async-done | bytes 2097184 | tf_op jit(solution)/shard_map/all_to_all | solution.py:209
  295.1 2.0 gather_fusion.1
  297.1 2.0 broadcast_select_fusion
  299.1 3.5 %copy.62 = bf16[16,64,2,512]{3,2,1,0:T(2,128)(2,1)} copy(bf16[16,64,2,512]{3,1,2,0:T(8,128)(2,1)S(1)} %broadcast_select_fusion) | data formatting | bytes 4194304
  302.6 1.7 fusion.101
  (105 shorter events, 7.1 us)
Async XLA Ops:
  7.2 28.7 %copy-start = (bf16[512,2304]{1,0:T(8,128)(2,1)S(1)}, bf16[512,2304]{1,0:T(8,128)(2,1)}, u32[]{:S(2)}) copy-start(bf16[512,2304]{1,0:T(8,128)(2,1)} %param.18) | copy-start | bytes 7077892
  7.2 88.7 %all-reduce.2.cloned.1.call-start = ((), (), s32[]{:S(2)}) async-start(), calls=%async_computation.7 | async-start | bytes 2359296 | tf_op jit(solution)/shard_map/psum | solution.py:104
  7.3 9.9 %copy-start.2 = (bf16[1,256,2304]{2,1,0:T(8,128)(2,1)S(1)}, bf16[1,256,2304]{2,1,0:T(8,128)(2,1)}, u32[]{:S(2)}) copy-start(bf16[1,256,2304]{2,1,0:T(8,128)(2,1)} %param.15) | copy-start | bytes 3538948
  23.2 7.4 %collective-permute-start.1 = (bf16[256,8,64]{0,2,1:T(8,128)(2,1)S(1)}, bf16[256,8,64]{0,2,1:T(8,128)(2,1)}, u32[]{:S(2)}, u32[]{:S(2)}) collective-permute-start(bf16[256,8,64]{0,2,1:T(8,128)(2,1)S(1)} %pad_maximum_fusion.1), channel_id=1, source_target_pairs={{0,1},{2,3},{4,5},{6,7},{8,9},{10,11},{12,13},{14,15},{16,17},{18,... | collective-permute-start | bytes 786440 | tf_op jit(solution)/shard_map/ppermute | solution.py:13
  26.2 7.5 %collective-permute-start = (bf16[256,8,64]{0,2,1:T(8,128)(2,1)S(1)}, bf16[256,8,64]{0,2,1:T(8,128)(2,1)}, u32[]{:S(2)}, u32[]{:S(2)}) collective-permute-start(bf16[256,8,64]{0,2,1:T(8,128)(2,1)S(1)} %fusion.102), channel_id=1, source_target_pairs={{0,1},{2,3},{4,5},{6,7},{8,9},{10,11},{12,13},{14,15},{16,17},{18,... | collective-permute-start | bytes 786440 | tf_op jit(solution)/shard_map/ppermute | solution.py:13
  35.9 2.3 copy-start.9
  35.9 2.9 copy-start.6
  37.8 58.2 %copy-start.3 = (bf16[1,256,2304]{2,1,0:T(8,128)(2,1)S(1)}, bf16[1,256,2304]{2,1,0:T(8,128)(2,1)}, u32[]{:S(2)}) copy-start(bf16[1,256,2304]{2,1,0:T(8,128)(2,1)} %param.15) | copy-start | bytes 3538948
  37.8 59.9 %copy-start.7 = (f32[2304]{0:T(1024)S(1)}, f32[2304]{0:T(1024)}, u32[]{:S(2)}) copy-start(f32[2304]{0:T(1024)} %param.19) | copy-start | bytes 27652
  37.8 264.8 %reduce-scatter.2.cloned.1.call-start = ((), (), s32[]{:S(2)}) async-start(), calls=%async_computation.8 | async-start | bytes 1474560 | tf_op jit(solution)/shard_map/reduce_scatter | solution.py:173
  98.3 9.2 %copy-start.5 = (bf16[1,16,64,2,512]{4,3,2,1,0:T(2,128)(2,1)S(1)}, bf16[1,16,64,2,512]{4,3,2,1,0:T(2,128)(2,1)}, u32[]{:S(2)}) copy-start(bf16[1,16,64,2,512]{4,3,2,1,0:T(2,128)(2,1)} %param.24) | copy-start | bytes 6291460
  103.7 22.1 %collective-permute-start.2 = (bf16[192,1,2304]{2,0,1:T(8,128)(2,1)}, bf16[192,1,2304]{2,0,1:T(8,128)(2,1)}, u32[]{:S(2)}, u32[]{:S(2)}) collective-permute-start(bf16[192,1,2304]{2,0,1:T(8,128)(2,1)} %bitcast.36), channel_id=1, source_target_pairs={{0,8},{8,0},{16,24},{24,16},{1,9},{9,1},{17,25},{25,17},{2,10},{10... | collective-permute-start | bytes 2654216 | tf_op jit(solution)/shard_map/ppermute | solution.py:137
  105.2 21.8 %collective-permute-start.3 = (bf16[192,1,2304]{2,0,1:T(8,128)(2,1)}, bf16[192,1,2304]{2,0,1:T(8,128)(2,1)}, u32[]{:S(2)}, u32[]{:S(2)}) collective-permute-start(bf16[192,1,2304]{2,0,1:T(8,128)(2,1)} %bitcast.36), channel_id=1, source_target_pairs={{0,16},{8,24},{16,0},{24,8},{1,17},{9,25},{17,1},{25,9},{2,18},{10... | collective-permute-start | bytes 2654216 | tf_op jit(solution)/shard_map/ppermute | solution.py:137
  127.0 11.7 %slice-start.2 = ((s8[13271040]{0:T(1024)(128)(4,1)}), s8[4194304]{0:T(1024)(128)(4,1)S(1)}, s32[]{:S(2)}) async-start(s8[13271040]{0:T(1024)(128)(4,1)} %bitcast.197), calls=%async_computation.11 | async-start | bytes 8388608
  128.7 10.0 %slice-start.3 = ((s8[13271040]{0:T(1024)(128)(4,1)}), s8[4194304]{0:T(1024)(128)(4,1)S(1)}, s32[]{:S(2)}) async-start(s8[13271040]{0:T(1024)(128)(4,1)} %bitcast.197), calls=%async_computation.12 | async-start | bytes 8388608
  128.7 10.0 %slice-start.4 = ((s8[13271040]{0:T(1024)(128)(4,1)}), s8[4194304]{0:T(1024)(128)(4,1)S(1)}, s32[]{:S(2)}) async-start(s8[13271040]{0:T(1024)(128)(4,1)} %bitcast.197), calls=%async_computation.13 | async-start | bytes 8388608
  128.8 10.0 %slice-start.5 = ((s8[13271040]{0:T(1024)(128)(4,1)}), s8[688128]{0:T(1024)(128)(4,1)S(1)}, s32[]{:S(2)}) async-start(s8[13271040]{0:T(1024)(128)(4,1)} %bitcast.197), calls=%async_computation.14 | async-start | bytes 1376256
  143.1 32.1 %collective-permute-start.4 = (bf16[192,1,2304]{2,0,1:T(8,128)(2,1)}, bf16[192,1,2304]{2,0,1:T(8,128)(2,1)}, u32[]{:S(2)}, u32[]{:S(2)}) collective-permute-start(bf16[192,1,2304]{2,0,1:T(8,128)(2,1)} %get-tuple-element.18), channel_id=1, source_target_pairs={{0,8},{8,0},{16,24},{24,16},{1,9},{9,1},{17,25},{25,17},{2,10},{10... | collective-permute-start | bytes 2654216 | tf_op jit(solution)/shard_map/ppermute | solution.py:137
  143.6 48.5 %collective-permute-start.5 = (bf16[192,1,2304]{2,0,1:T(8,128)(2,1)}, bf16[192,1,2304]{2,0,1:T(8,128)(2,1)}, u32[]{:S(2)}, u32[]{:S(2)}) collective-permute-start(bf16[192,1,2304]{2,0,1:T(8,128)(2,1)} %get-tuple-element.17), channel_id=1, source_target_pairs={{0,16},{8,24},{16,0},{24,8},{1,17},{9,25},{17,1},{25,9},{2,18},{10... | collective-permute-start | bytes 2654216 | tf_op jit(solution)/shard_map/ppermute | solution.py:137
  145.1 63.1 %collective-permute-start.6 = (bf16[192,1,2304]{2,0,1:T(8,128)(2,1)}, bf16[192,1,2304]{2,0,1:T(8,128)(2,1)}, u32[]{:S(2)}, u32[]{:S(2)}) collective-permute-start(bf16[192,1,2304]{2,0,1:T(8,128)(2,1)} %collective-permute-done.2), channel_id=1, source_target_pairs={{0,16},{8,24},{16,0},{24,8},{1,17},{9,25},{17,1},{25,9},{2,18},{10... | collective-permute-start | bytes 2654216 | tf_op jit(solution)/shard_map/ppermute | solution.py:137
  206.4 10.2 %slice-start.6 = ((s8[13271040]{0:T(1024)(128)(4,1)}), s8[4194304]{0:T(1024)(128)(4,1)S(1)}, s32[]{:S(2)}) async-start(s8[13271040]{0:T(1024)(128)(4,1)} %bitcast.199), calls=%async_computation.15 | async-start | bytes 8388608
  206.4 14.9 %slice-start = ((s8[4718592]{0:T(1024)(128)(4,1)}), s8[4194304]{0:T(1024)(128)(4,1)S(1)}, s32[]{:S(2)}) async-start(s8[4718592]{0:T(1024)(128)(4,1)} %bitcast.184), calls=%async_computation.9 | async-start | bytes 8388608
  208.2 8.4 %slice-start.7 = ((s8[13271040]{0:T(1024)(128)(4,1)}), s8[4194304]{0:T(1024)(128)(4,1)S(1)}, s32[]{:S(2)}) async-start(s8[13271040]{0:T(1024)(128)(4,1)} %bitcast.199), calls=%async_computation.16 | async-start | bytes 8388608
  208.2 8.9 %slice-start.8 = ((s8[13271040]{0:T(1024)(128)(4,1)}), s8[4194304]{0:T(1024)(128)(4,1)S(1)}, s32[]{:S(2)}) async-start(s8[13271040]{0:T(1024)(128)(4,1)} %bitcast.199), calls=%async_computation.17 | async-start | bytes 8388608
  208.2 9.0 %slice-start.9 = ((s8[13271040]{0:T(1024)(128)(4,1)}), s8[688128]{0:T(1024)(128)(4,1)S(1)}, s32[]{:S(2)}) async-start(s8[13271040]{0:T(1024)(128)(4,1)} %bitcast.199), calls=%async_computation.18 | async-start | bytes 1376256
  208.2 13.1 %slice-start.1 = ((s8[4718592]{0:T(1024)(128)(4,1)}), s8[524288]{0:T(1024)(128)(4,1)S(1)}, s32[]{:S(2)}) async-start(s8[4718592]{0:T(1024)(128)(4,1)} %bitcast.184), calls=%async_computation.10 | async-start | bytes 1048576
  217.2 4.2 %copy-start.4 = (bf16[192,1,2304]{2,0,1:T(8,128)(2,1)S(1)}, bf16[192,1,2304]{2,0,1:T(8,128)(2,1)}, u32[]{:S(2)}) copy-start(bf16[192,1,2304]{2,0,1:T(8,128)(2,1)} %copy.65) | copy-start | bytes 2654212
  218.9 22.8 %collective-permute-start.7 = (bf16[192,1,2304]{2,0,1:T(8,128)(2,1)S(1)}, bf16[192,1,2304]{2,0,1:T(8,128)(2,1)}, u32[]{:S(2)}, u32[]{:S(2)}) collective-permute-start(bf16[192,1,2304]{2,0,1:T(8,128)(2,1)S(1)} %fusion.39), channel_id=1, source_target_pairs={{0,24},{8,16},{16,8},{24,0},{1,25},{9,17},{17,9},{25,1},{2,26},{10... | collective-permute-start | bytes 2654216 | tf_op jit(solution)/shard_map/ppermute | solution.py:137
  266.0 3.9 %copy-start.8 = (s32[4,16]{1,0:T(4,128)S(1)}, s32[4,16]{1,0:T(4,128)}, u32[]{:S(2)}) copy-start(s32[4,16]{1,0:T(4,128)} %param.27) | copy-start | bytes 772
  266.0 29.2 %all-to-all-start.5 = ((bf16[16,64,2,512]{3,1,2,0:T(8,128)(2,1)}), bf16[16,64,2,512]{3,1,2,0:T(8,128)(2,1)S(1)}, u32[]{:S(2)}, u32[]{:S(2)}) async-start(bf16[16,64,2,512]{3,1,2,0:T(8,128)(2,1)} %broadcast_select_fusion.1), calls=%async_computation.6 | async-start | bytes 4194304 | tf_op jit(solution)/shard_map/all_to_all | solution.py:209
  297.1 7.2 %copy-start.1 = (bf16[512,2304]{1,0:T(8,128)(2,1)S(1)}, bf16[512,2304]{1,0:T(8,128)(2,1)}, u32[]{:S(2)}) copy-start(bf16[512,2304]{1,0:T(8,128)(2,1)} %param.18) | copy-start | bytes 7077892
Sparse Core Ops, SparseCore 0:
  37.9 57.9 all-reduce.1
  264.5 28.7 reduce-scatter.1

commit v9 on v8

--- a/solution.py
+++ b/solution.py
@@ -123,13 +123,17 @@
     ).astype(jnp.bfloat16)
     req_total = lax.axis_size("req")
     dev_total = lax.axis_size("dev")
-    split = dev_total > 1 and experts_here % dev_total == 0
-    per_core = experts_here // dev_total if split else experts_here
+    split = dev_total == 2 and experts_here % 2 == 0
+    per_core = experts_here // 2 if split else experts_here
+    swap = [(0, 1), (1, 0)]
     if split:
-        first_here = dev_index * per_core
-        gate_up_here = lax.dynamic_slice_in_dim(w_gate_up, first_here, per_core, 0)
-        down_here = lax.dynamic_slice_in_dim(w_down, first_here, per_core, 0)
-        rows_here = lax.all_to_all(picked_own, "dev", split_axis=1, concat_axis=0, tiled=True)
+        mine_first = dev_index * per_core
+        other_first = (1 - dev_index) * per_core
+        gate_up_here = lax.dynamic_slice_in_dim(w_gate_up, mine_first, per_core, 0)
+        down_here = lax.dynamic_slice_in_dim(w_down, mine_first, per_core, 0)
+        mine = lax.dynamic_slice_in_dim(picked_own, mine_first, per_core, 1)
+        theirs = lax.dynamic_slice_in_dim(picked_own, other_first, per_core, 1)
+        rows_here = jnp.concatenate([mine, lax.ppermute(theirs, "dev", swap)], axis=0)
     else:
         gate_up_here, down_here, rows_here = w_gate_up, w_down, picked_own
 
@@ -159,17 +163,32 @@
         outs = experts_on(jnp.stack([arrived[k] for k in group], axis=0))
         for slot_index, step in enumerate(group):
             part = outs[slot_index]
-            part = part if step == 0 else partner_move(part, step)
-            if split:
-                part = lax.all_to_all(part, "dev", split_axis=0, concat_axis=1, tiled=True)
-            returned.append(part)
+            returned.append(part if step == 0 else partner_move(part, step))
     token_weights = jnp.sum(own_combine, axis=-1)
     dispatch_bf = own_dispatch.astype(jnp.bfloat16)
-    selected = sum(
-        jnp.einsum("tec,ced->ted", dispatch_bf, part, preferred_element_type=jnp.float32)
-        for part in returned
-    )
-    moe_out = jnp.sum(token_weights[:, :, None] * selected, axis=1)
+
+    def pick(dispatch_part, parts):
+        return sum(
+            jnp.einsum("tec,ced->ted", dispatch_part, part, preferred_element_type=jnp.float32)
+            for part in parts
+        )
+
+    if split:
+        stacked = jnp.stack(returned, axis=0)
+        kept = stacked[:, :capacity]
+        came = lax.ppermute(stacked[:, capacity:], "dev", swap)
+        moe_out = jnp.sum(
+            lax.dynamic_slice_in_dim(token_weights, mine_first, per_core, 1)[:, :, None]
+            * pick(lax.dynamic_slice_in_dim(dispatch_bf, mine_first, per_core, 1), list(kept)),
+            axis=1,
+        ) + jnp.sum(
+            lax.dynamic_slice_in_dim(token_weights, other_first, per_core, 1)[:, :, None]
+            * pick(lax.dynamic_slice_in_dim(dispatch_bf, other_first, per_core, 1), list(came)),
+            axis=1,
+        )
+    else:
+        selected = pick(dispatch_bf, returned)
+        moe_out = jnp.sum(token_weights[:, :, None] * selected, axis=1)
     summed = lax.psum_scatter(
         moe_out.astype(jnp.bfloat16), "head", scatter_dimension=0, tiled=True
     ).astype(jnp.float32)

time: 313 us -> 262 us (0.84)
  blocking collectives: 31.1 us -> 0 us
  local copies, waits for them, and re-layouts: 52.6 us -> 25 us
  waiting for transfers between devices: 113 us -> 135 us
  other arithmetic: 27.7 us -> 18 us
    all_to_all x5 -> x0, blocking collectives: 31.1 us -> none  [the longest x4 25.8 us: body(): part = lax.all_to_all(part, 'dev', split_axis=0, concat_axis=1, tiled=True)]
    unnamed x54 -> x48, local copies, waits for them, and re-layouts: 40.4 us -> 17.2 us
    ppermute x6, waiting for transfers between devices: 32.2 us -> 52.3 us  [partner_move(): return lax.ppermute(block, 'req', [(i, i ^ step) for i in range(req_total)])]
    ppermute x3 -> x0, other arithmetic: 9.36 us -> none  [partner_move(): return lax.ppermute(block, 'req', [(i, i ^ step) for i in range(req_total)])]
    convert_element_type x1 -> x0, other arithmetic: 3.13 us -> none  [experts_on(): return down.astype(jnp.bfloat16).reshape(rows.shape)]
    dot_general x4 -> x8, matrix products: 11.2 us -> 10.6 us  [pick(): jnp.einsum('tec,ced->ted', dispatch_part, part, preferred_element_type=jn...]
  transfers between devices with their start and end apart: 11 -> 13, of which waited for: 5 -> 7; matrix products, arithmetic and copies ran while one was open for 22% -> 18% of each run, Pallas kernels for 0% -> 0%
where the time goes in v9:
time: 262 us; the launch traced here: 261 us
  waiting for transfers between devices  135 us (52%)
  matrix products  53 us (20%)
  local copies, waits for them, and re-layouts  25 us (10%)
  other arithmetic  18 us (7%)
  starting transfers between devices  15.7 us (6%)
  between operations  14.6 us (6%)
    psum x1, waiting for transfers between devices, body(): lax.psum(partial_value.astype(jnp.bfloat16), 'head').astype(jnp.float32)  55.5 us
    ppermute x6, waiting for transfers between devices, partner_move(): return lax.ppermute(block, 'req', [(i, i ^ step) for i in range(req_total)])  52.3 us
    all_to_all x1, waiting for transfers between devices, body(): lax.all_to_all(outgoing, 'req', split_axis=0, concat_axis=0, tiled=True)  25.5 us
    dot_general x3, matrix products, experts_on(): jnp.einsum('ned,egdf->gnef', flat, gate_up_here, preferred_element_type=j...  24.9 us
    unnamed x48, local copies, waits for them, and re-layouts  17.2 us
    dot_general x8, matrix products, pick(): jnp.einsum('tec,ced->ted', dispatch_part, part, preferred_element_type=jn...  10.6 us
    ppermute x6, starting transfers between devices, partner_move(): return lax.ppermute(block, 'req', [(i, i ^ step) for i in range(req_total)])  7.19 us
    dot_general x3, matrix products, experts_on(): jnp.einsum('nef,efd->ned', hidden, down_here, preferred_element_type=jnp....  6.66 us
  transfers between devices with their start and end apart: 13, of which 7 were waited for; matrix products, arithmetic and copies ran while one was open for 18% of the time, Pallas kernels for 0%

profile of v9, /device:TPU:0, one launch (start us, length us, event | category | flops | bytes accessed | tf_op | source)
XLA Modules:
  0.0 261.4 jit_solution(6859959849794285686)
XLA Ops:
  7.3 10.4 %copy.53 = bf16[2304,3,512]{0,2,1:T(8,128)(2,1)} copy(bf16[2304,3,512]{2,0,1:T(8,128)(2,1)} %param.17) | data formatting | bytes 14155776 | tf_op args[2]
  17.6 0.3 fusion.63
  17.9 5.2 %fusion.75 = f32[256,3,8,64]{0,3,2,1:T(8,128)S(1)} fusion(bf16[3,8,64,2304]{3,2,1,0:T(8,128)(2,1)} %bitcast.213, bf16[1,256,2304]{2,1,0:T(8,128)(2,1)S(1)} %copy-done.2, f32[2304]{0:T(1024)} %param.16, f32[256]{0:T(256)S(1)} %add_rsqrt_fusion.1), kind=kOutput, calls=%fused_computation.74 | convolution fusion | flops 1814298624 | bytes 9840640 | tf_op jit(solution)/shard_map/dot_general | solution.py:73
  23.2 1.1 copy-done.12
  24.4 0.2 multiply_cosine_fusion
  24.6 0.9 subtract_convert_fusion.1
  25.5 0.6 copy-done.13
  26.1 3.1 %collective-permute-start.1 = (bf16[256,8,64]{0,2,1:T(8,128)(2,1)S(1)}, bf16[256,8,64]{0,2,1:T(8,128)(2,1)}, u32[]{:S(2)}, u32[]{:S(2)}) collective-permute-start(bf16[256,8,64]{0,2,1:T(8,128)(2,1)S(1)} %pad_maximum_fusion.5), channel_id=1, source_target_pairs={{0,1},{2,3},{4,5},{6,7},{8,9},{10,11},{12,13},{14,15},{16,17},{18,... | collective-permute-start | bytes 786440 | tf_op jit(solution)/shard_map/ppermute | solution.py:13
  29.2 1.1 fusion.115
  30.3 1.3 collective-permute-start
  32.1 2.1 fusion.43
  34.2 1.3 fusion.50
  35.5 1.2 fusion.90
  36.7 1.8 convolution_convert_fusion
  38.6 0.2 reduce-scatter.2.cloned.1.call-start
  38.9 0.6 reduce-window.6
  40.1 0.2 eq.112
  40.4 0.7 fusion.152
  41.2 55.5 %all-reduce.2.cloned.1.call-done = bf16[256,2304]{1,0:T(8,128)(2,1)} async-done(((bf16[256,2304]{1,0:T(8,128)(2,1)}), bf16[256,2304]{1,0:T(8,128)(2,1)}) %all-reduce.2.cloned.1.call-update) | async-done | bytes 1179664 | tf_op jit(solution)/shard_map/psum | solution.py:104
  96.8 1.8 fusion.60
  98.6 0.5 fusion.77
  99.4 1.7 collective-permute-done.2
  101.1 1.0 pad_maximum_fusion.4
  102.1 1.5 collective-permute-start.3
  103.6 1.5 collective-permute-start.4
  105.0 0.2 convert_reduce_fusion
  105.4 18.6 %collective-permute-done.3 = bf16[192,1,2304]{2,0,1:T(8,128)(2,1)S(1)} collective-permute-done((bf16[192,1,2304]{2,0,1:T(8,128)(2,1)}, bf16[192,1,2304]{2,0,1:T(8,128)(2,1)S(1)}, u32[]{:S(2)}, u32[]{:S(2)}) %collective-permute-start.3) | collective-permute-done | bytes 884768 | tf_op jit(solution)/shard_map/ppermute | solution.py:141
  124.0 1.3 collective-permute-done.4
  125.3 1.5 pad_maximum_fusion.3
  126.8 9.9 %fusion.33 = f32[2,384,1,1440]{1,3,0,2:T(8,128)S(1)} fusion(bf16[384,2304,1]{1,0,2:T(8,128)(2,1)S(1)} %bitcast.222, bf16[2,2,2304,1440]{2,3,1,0:T(8,128)(2,1)} %param.22, s32[]{:T(128)S(6)} %select_n.52), kind=kOutput, calls=%fused_computation.37 | convolution fusion | flops 5096079360 | bytes 19464196 | tf_op jit(solution)/shard_map/ned,egdf->gnef/dot_general | solution.py:146
  136.7 1.5 collective-permute-start.7
  138.3 3.2 %fusion.29 = bf16[384,1,2304]{2,0,1:T(8,128)(2,1)S(1)} fusion(bf16[2,1440,2304]{2,1,0:T(8,128)(2,1)S(1)} %bitcast.230, s32[]{:T(128)S(6)} %select_n.52, f32[2,384,1,1440]{1,3,0,2:T(8,128)S(1)} %fusion.33), kind=kOutput, calls=%fused_computation.34 | convolution fusion | flops 2552242176 | bytes 12828676 | tf_op jit(solution)/shard_map/nef,efd->ned/dot_general | solution.py:148
  141.6 0.6 collective-permute-start.6
  142.2 0.6 collective-permute-start.5
  142.8 16.6 %collective-permute-done.7 = bf16[192,1,2304]{2,0,1:T(8,128)(2,1)S(1)} collective-permute-done((bf16[192,1,2304]{2,0,1:T(8,128)(2,1)S(1)}, bf16[192,1,2304]{2,0,1:T(8,128)(2,1)S(1)}, u32[]{:S(2)}, u32[]{:S(2)}) %collective-permute-start.7) | collective-permute-done | bytes 884768 | tf_op jit(solution)/shard_map/ppermute | solution.py:141
  159.4 7.4 %fusion.55 = f32[2,192,1,1440]{3,1,0,2:T(8,128)S(1)} fusion(bf16[2,2,2304,1440]{2,3,1,0:T(8,128)(2,1)} %param.22, s32[]{:T(128)S(6)} %select_n.52, bf16[192,1,2304]{2,0,1:T(8,128)(2,1)S(1)} %collective-permute-done.7), kind=kOutput, calls=%fused_computation.47 | convolution fusion | flops 2548039680 | bytes 16367620 | tf_op jit(solution)/shard_map/ned,egdf->gnef/dot_general | solution.py:146
  166.8 1.7 fusion.47
  168.5 1.5 collective-permute-start.8
  170.1 7.6 %fusion.52 = f32[2,192,1,1440]{3,1,0,2:T(8,128)S(1)} fusion(bf16[2,2,2304,1440]{2,3,1,0:T(8,128)(2,1)} %param.22, s32[]{:T(128)S(6)} %select_n.52, bf16[96,1,2304]{2,0,1:T(8,128)(2,1)S(1)} %collective-permute-done.2, bf16[96,1,2304]{2,0,1:T(8,128)(2,1)S(1)} %get-tuple-element.17), kind=kOutput, calls=%fused_computation.46 | convolution fusion | flops 2549809152 | bytes 16367620 | tf_op jit(solution)/shard_map/ned,egdf->gnef/dot_general | solution.py:146
  177.7 1.7 fusion.44
  179.4 15.8 %collective-permute-done.6 = bf16[192,1,2304]{2,0,1:T(8,128)(2,1)S(1)} collective-permute-done((bf16[192,1,2304]{2,0,1:T(8,128)(2,1)S(1)}, bf16[192,1,2304]{2,0,1:T(8,128)(2,1)S(1)}, u32[]{:S(2)}, u32[]{:S(2)}) %collective-permute-start.6) | collective-permute-done | bytes 884768 | tf_op jit(solution)/shard_map/ppermute | solution.py:141
  195.3 1.3 pad_maximum_fusion
  196.7 0.3 copy-done.10
  197.1 0.4 copy-done.5
  197.5 0.6 dynamic_slice.57
  198.1 0.7 add_compare_fusion
  198.8 1.7 bitcast_select_fusion
  200.5 2.3 gather_fusion
  202.8 1.6 fusion.112
  204.4 0.5 convolution_add_fusion.2
  205.0 0.6 copy-done.6
  205.6 0.5 fusion.111
  206.1 1.5 fusion.108
  207.7 1.5 fusion.109
  209.2 1.5 fusion.110
  210.7 1.7 fusion.26
  212.4 1.7 fusion.42
  214.2 1.6 broadcast_select_fusion.1
  215.7 3.7 %all-to-all-start = ((bf16[16,64,2,512]{3,1,2,0:T(8,128)(2,1)}), bf16[16,64,2,512]{3,1,2,0:T(8,128)(2,1)S(1)}, u32[]{:S(2)}, u32[]{:S(2)}) async-start(bf16[16,64,2,512]{3,1,2,0:T(8,128)(2,1)} %broadcast_select_fusion.1), calls=%async_computation.1 | async-start | bytes 4194304 | tf_op jit(solution)/shard_map/all_to_all | solution.py:228
  219.7 25.5 %all-to-all-done = bf16[16,64,2,512]{3,1,2,0:T(8,128)(2,1)S(1)} async-done(((bf16[16,64,2,512]{3,1,2,0:T(8,128)(2,1)}), bf16[16,64,2,512]{3,1,2,0:T(8,128)(2,1)S(1)}, u32[]{:S(2)}, u32[]{:S(2)}) %all-to-all-start) | async-done | bytes 2097184 | tf_op jit(solution)/shard_map/all_to_all | solution.py:228
  245.3 2.0 gather_fusion.1
  247.3 2.0 broadcast_select_fusion
  249.3 3.5 %copy.65 = bf16[16,64,2,512]{3,2,1,0:T(2,128)(2,1)} copy(bf16[16,64,2,512]{3,1,2,0:T(8,128)(2,1)S(1)} %broadcast_select_fusion) | data formatting | bytes 4194304
  252.8 1.7 fusion.114
  (98 shorter events, 2.5 us)
Async XLA Ops:
  7.2 29.6 %copy-start = (bf16[512,2304]{1,0:T(8,128)(2,1)S(1)}, bf16[512,2304]{1,0:T(8,128)(2,1)}, u32[]{:S(2)}) copy-start(bf16[512,2304]{1,0:T(8,128)(2,1)} %param.18) | copy-start | bytes 7077892
  7.2 89.6 %all-reduce.2.cloned.1.call-start = ((), (), s32[]{:S(2)}) async-start(), calls=%async_computation.2 | async-start | bytes 2359296 | tf_op jit(solution)/shard_map/psum | solution.py:104
  7.2 10.4 %copy-start.2 = (bf16[1,256,2304]{2,1,0:T(8,128)(2,1)S(1)}, bf16[1,256,2304]{2,1,0:T(8,128)(2,1)}, u32[]{:S(2)}) copy-start(bf16[1,256,2304]{2,1,0:T(8,128)(2,1)} %param.15) | copy-start | bytes 3538948
  23.2 1.1 copy-start.12
  24.3 7.3 %copy-start.16 = (s32[4,256,2]{1,2,0:T(2,128)S(1)}, s32[4,256,2]{1,2,0:T(2,128)}, u32[]{:S(2)}) copy-start(s32[4,256,2]{1,2,0:T(2,128)} %param.20) | copy-start | bytes 24580
  25.5 0.6 copy-start.13
  26.1 6.0 %collective-permute-start.1 = (bf16[256,8,64]{0,2,1:T(8,128)(2,1)S(1)}, bf16[256,8,64]{0,2,1:T(8,128)(2,1)}, u32[]{:S(2)}, u32[]{:S(2)}) collective-permute-start(bf16[256,8,64]{0,2,1:T(8,128)(2,1)S(1)} %pad_maximum_fusion.5), channel_id=1, source_target_pairs={{0,1},{2,3},{4,5},{6,7},{8,9},{10,11},{12,13},{14,15},{16,17},{18,... | collective-permute-start | bytes 786440 | tf_op jit(solution)/shard_map/ppermute | solution.py:13
  30.3 5.2 %collective-permute-start = (bf16[256,8,64]{0,2,1:T(8,128)(2,1)S(1)}, bf16[256,8,64]{0,2,1:T(8,128)(2,1)S(1)}, u32[]{:S(2)}, u32[]{:S(2)}) collective-permute-start(bf16[256,8,64]{0,2,1:T(8,128)(2,1)S(1)} %fusion.115), channel_id=1, source_target_pairs={{0,1},{2,3},{4,5},{6,7},{8,9},{10,11},{12,13},{14,15},{16,17},{18,... | collective-permute-start | bytes 786440 | tf_op jit(solution)/shard_map/ppermute | solution.py:13
  38.6 58.2 %copy-start.3 = (bf16[1,256,2304]{2,1,0:T(8,128)(2,1)S(1)}, bf16[1,256,2304]{2,1,0:T(8,128)(2,1)}, u32[]{:S(2)}) copy-start(bf16[1,256,2304]{2,1,0:T(8,128)(2,1)} %param.15) | copy-start | bytes 3538948
  38.6 60.0 %copy-start.15 = (f32[2304]{0:T(1024)S(1)}, f32[2304]{0:T(1024)}, u32[]{:S(2)}) copy-start(f32[2304]{0:T(1024)} %param.19) | copy-start | bytes 27652
  38.6 214.2 %reduce-scatter.2.cloned.1.call-start = ((), (), s32[]{:S(2)}) async-start(), calls=%async_computation.3 | async-start | bytes 1474560 | tf_op jit(solution)/shard_map/reduce_scatter | solution.py:192
  99.2 5.9 %copy-start.14 = (s32[4,16]{1,0:T(4,128)S(1)}, s32[4,16]{1,0:T(4,128)}, u32[]{:S(2)}) copy-start(s32[4,16]{1,0:T(4,128)} %param.26) | copy-start | bytes 772
  99.3 1.9 collective-permute-start.2
  102.1 21.9 %collective-permute-start.3 = (bf16[192,1,2304]{2,0,1:T(8,128)(2,1)}, bf16[192,1,2304]{2,0,1:T(8,128)(2,1)S(1)}, u32[]{:S(2)}, u32[]{:S(2)}) collective-permute-start(bf16[192,1,2304]{2,0,1:T(8,128)(2,1)} %pad_maximum_fusion.4), channel_id=1, source_target_pairs={{0,8},{8,0},{16,24},{24,16},{1,9},{9,1},{17,25},{25,17},{2,10},{10... | collective-permute-start | bytes 2654216 | tf_op jit(solution)/shard_map/ppermute | solution.py:141
  103.6 21.7 %collective-permute-start.4 = (bf16[192,1,2304]{2,0,1:T(8,128)(2,1)}, bf16[192,1,2304]{2,0,1:T(8,128)(2,1)}, u32[]{:S(2)}, u32[]{:S(2)}) collective-permute-start(bf16[192,1,2304]{2,0,1:T(8,128)(2,1)} %pad_maximum_fusion.4), channel_id=1, source_target_pairs={{0,16},{8,24},{16,0},{24,8},{1,17},{9,25},{17,1},{25,9},{2,18},{10... | collective-permute-start | bytes 2654216 | tf_op jit(solution)/shard_map/ppermute | solution.py:141
  125.3 13.0 %slice-start = ((s8[13271040]{0:T(1024)(128)(4,1)}), s8[4194304]{0:T(1024)(128)(4,1)S(1)}, s32[]{:S(2)}) async-start(s8[13271040]{0:T(1024)(128)(4,1)} %bitcast.229), calls=%async_computation.4 | async-start | bytes 8388608
  126.8 11.5 %slice-start.1 = ((s8[13271040]{0:T(1024)(128)(4,1)}), s8[4194304]{0:T(1024)(128)(4,1)S(1)}, s32[]{:S(2)}) async-start(s8[13271040]{0:T(1024)(128)(4,1)} %bitcast.229), calls=%async_computation.5 | async-start | bytes 8388608
  126.8 11.5 %slice-start.2 = ((s8[13271040]{0:T(1024)(128)(4,1)}), s8[4194304]{0:T(1024)(128)(4,1)S(1)}, s32[]{:S(2)}) async-start(s8[13271040]{0:T(1024)(128)(4,1)} %bitcast.229), calls=%async_computation.6 | async-start | bytes 8388608
  126.8 11.5 %slice-start.3 = ((s8[13271040]{0:T(1024)(128)(4,1)}), s8[688128]{0:T(1024)(128)(4,1)S(1)}, s32[]{:S(2)}) async-start(s8[13271040]{0:T(1024)(128)(4,1)} %bitcast.229), calls=%async_computation.7 | async-start | bytes 1376256
  136.7 22.7 %collective-permute-start.7 = (bf16[192,1,2304]{2,0,1:T(8,128)(2,1)S(1)}, bf16[192,1,2304]{2,0,1:T(8,128)(2,1)S(1)}, u32[]{:S(2)}, u32[]{:S(2)}) collective-permute-start(bf16[192,1,2304]{2,0,1:T(8,128)(2,1)S(1)} %collective-permute-done.3), channel_id=1, source_target_pairs={{0,16},{8,24},{16,0},{24,8},{1,17},{9,25},{17,1},{25,9},{2,18},{10... | collective-permute-start | bytes 2654216 | tf_op jit(solution)/shard_map/ppermute | solution.py:141
  141.6 53.6 %collective-permute-start.6 = (bf16[192,1,2304]{2,0,1:T(8,128)(2,1)S(1)}, bf16[192,1,2304]{2,0,1:T(8,128)(2,1)S(1)}, u32[]{:S(2)}, u32[]{:S(2)}) collective-permute-start(bf16[192,1,2304]{2,0,1:T(8,128)(2,1)S(1)} %get-tuple-element.14), channel_id=1, source_target_pairs={{0,16},{8,24},{16,0},{24,8},{1,17},{9,25},{17,1},{25,9},{2,18},{10... | collective-permute-start | bytes 2654216 | tf_op jit(solution)/shard_map/ppermute | solution.py:141
  142.2 53.0 %collective-permute-start.5 = (bf16[192,1,2304]{2,0,1:T(8,128)(2,1)S(1)}, bf16[192,1,2304]{2,0,1:T(8,128)(2,1)S(1)}, u32[]{:S(2)}, u32[]{:S(2)}) collective-permute-start(bf16[192,1,2304]{2,0,1:T(8,128)(2,1)S(1)} %get-tuple-element.13), channel_id=1, source_target_pairs={{0,8},{8,0},{16,24},{24,16},{1,9},{9,1},{17,25},{25,17},{2,10},{10... | collective-permute-start | bytes 2654216 | tf_op jit(solution)/shard_map/ppermute | solution.py:141
  168.5 26.7 %collective-permute-start.8 = (bf16[192,1,2304]{2,0,1:T(8,128)(2,1)S(1)}, bf16[192,1,2304]{2,0,1:T(8,128)(2,1)S(1)}, u32[]{:S(2)}, u32[]{:S(2)}) collective-permute-start(bf16[192,1,2304]{2,0,1:T(8,128)(2,1)S(1)} %fusion.47), channel_id=1, source_target_pairs={{0,24},{8,16},{16,8},{24,0},{1,25},{9,17},{17,9},{25,1},{2,26},{10... | collective-permute-start | bytes 2654216 | tf_op jit(solution)/shard_map/ppermute | solution.py:141
  179.4 17.2 %copy-start.7 = (bf16[1,192,1,2304]{3,1,2,0:T(8,128)(2,1)}, bf16[1,192,1,2304]{3,1,2,0:T(8,128)(2,1)S(1)}, u32[]{:S(2)}) copy-start(bf16[1,192,1,2304]{3,1,2,0:T(8,128)(2,1)S(1)} %fusion.44) | copy-start | bytes 2654212
  195.3 1.5 copy-start.8
  195.3 1.8 copy-start.10
  195.3 2.2 copy-start.5
  195.3 2.2 copy-start.18
  195.3 3.5 %copy-start.4 = (bf16[1,16,64,2,512]{4,3,2,1,0:T(2,128)(2,1)S(1)}, bf16[1,16,64,2,512]{4,3,2,1,0:T(2,128)(2,1)}, u32[]{:S(2)}) copy-start(bf16[1,16,64,2,512]{4,3,2,1,0:T(2,128)(2,1)} %param.24) | copy-start | bytes 6291460
  197.5 8.6 %collective-permute-start.9 = (bf16[4,96,1,2304]{3,1,2,0:T(8,128)(2,1)}, bf16[4,96,1,2304]{3,1,2,0:T(8,128)(2,1)}, u32[]{:S(2)}, u32[]{:S(2)}) collective-permute-start(bf16[4,96,1,2304]{3,1,2,0:T(8,128)(2,1)} %pad_maximum_fusion), channel_id=1, source_target_pairs={{0,1},{1,0},{2,3},{3,2},{4,5},{5,4},{6,7},{7,6},{8,9},{9,8},{10,11... | collective-permute-start | bytes 5308424 | tf_op jit(solution)/shard_map/ppermute | solution.py:179
  202.8 1.6 copy-start.11
  204.4 1.2 copy-start.6
  210.7 1.7 copy-start.9
  215.7 3.8 %copy-start.17 = (s32[4,16]{1,0:T(4,128)S(1)}, s32[4,16]{1,0:T(4,128)}, u32[]{:S(2)}) copy-start(s32[4,16]{1,0:T(4,128)} %param.27) | copy-start | bytes 772
  215.7 29.5 %all-to-all-start = ((bf16[16,64,2,512]{3,1,2,0:T(8,128)(2,1)}), bf16[16,64,2,512]{3,1,2,0:T(8,128)(2,1)S(1)}, u32[]{:S(2)}, u32[]{:S(2)}) async-start(bf16[16,64,2,512]{3,1,2,0:T(8,128)(2,1)} %broadcast_select_fusion.1), calls=%async_computation.1 | async-start | bytes 4194304 | tf_op jit(solution)/shard_map/all_to_all | solution.py:228
  247.3 7.2 %copy-start.1 = (bf16[512,2304]{1,0:T(8,128)(2,1)S(1)}, bf16[512,2304]{1,0:T(8,128)(2,1)}, u32[]{:S(2)}) copy-start(bf16[512,2304]{1,0:T(8,128)(2,1)} %param.18) | copy-start | bytes 7077892
Sparse Core Ops, SparseCore 0:
  38.7 57.9 all-reduce.1
  214.3 27.9 reduce-scatter.1

commit v10 on v9

--- a/solution.py
+++ b/solution.py
@@ -157,10 +157,15 @@
     plan = [[0], [1, 2]] + ([list(range(3, req_total))] if req_total > 3 else [])
     plan = [[k for k in group if k < req_total] for group in plan]
     returned = []
+    previous = None
     for group in plan:
         if not group:
             continue
-        outs = experts_on(jnp.stack([arrived[k] for k in group], axis=0))
+        inputs = [arrived[k] for k in group]
+        if previous is not None:
+            inputs, previous = lax.optimization_barrier((inputs, previous))
+        outs = experts_on(jnp.stack(inputs, axis=0))
+        previous = outs
         for slot_index, step in enumerate(group):
             part = outs[slot_index]
             returned.append(part if step == 0 else partner_move(part, step))

time: 262 us -> 262 us (level)
  waiting for transfers between devices: 135 us -> 131 us
  matrix products: 53 us -> 56.4 us
    ppermute x6, waiting for transfers between devices: 52.3 us -> 48.3 us  [partner_move(): return lax.ppermute(block, 'req', [(i, i ^ step) for i in range(req_total)])]
    unnamed x48 -> x42, local copies, waits for them, and re-layouts: 17.2 us -> 16.9 us
  transfers between devices with their start and end apart: 13 -> 13, of which waited for: 7 -> 7; matrix products, arithmetic and copies ran while one was open for 18% -> 20% of each run, Pallas kernels for 0% -> 0%
where the time goes in v10:
time: 262 us; the launch traced here: 261 us
  waiting for transfers between devices  131 us (50%)
  matrix products  56.4 us (22%)
  local copies, waits for them, and re-layouts  25.9 us (10%)
  other arithmetic  17.3 us (7%)
  starting transfers between devices  15.6 us (6%)
  between operations  14.6 us (6%)
    psum x1, waiting for transfers between devices, body(): lax.psum(partial_value.astype(jnp.bfloat16), 'head').astype(jnp.float32)  55.5 us
    ppermute x6, waiting for transfers between devices, partner_move(): return lax.ppermute(block, 'req', [(i, i ^ step) for i in range(req_total)])  48.3 us
    all_to_all x1, waiting for transfers between devices, body(): lax.all_to_all(outgoing, 'req', split_axis=0, concat_axis=0, tiled=True)  25.5 us
    dot_general x3, matrix products, experts_on(): jnp.einsum('ned,egdf->gnef', flat, gate_up_here, preferred_element_type=j...  25.5 us
    unnamed x42, local copies, waits for them, and re-layouts  16.9 us
    dot_general x8, matrix products, pick(): jnp.einsum('tec,ced->ted', dispatch_part, part, preferred_element_type=jn...  11.6 us
    dot_general x3, matrix products, experts_on(): jnp.einsum('nef,efd->ned', hidden, down_here, preferred_element_type=jnp....  8.51 us
    ppermute x6, starting transfers between devices, partner_move(): return lax.ppermute(block, 'req', [(i, i ^ step) for i in range(req_total)])  7.12 us
  transfers between devices with their start and end apart: 13, of which 7 were waited for; matrix products, arithmetic and copies ran while one was open for 20% of the time, Pallas kernels for 0%

profile of v10, /device:TPU:0, one launch (start us, length us, event | category | flops | bytes accessed | tf_op | source)
XLA Modules:
  0.0 260.9 jit_solution(7207414019882000613)
XLA Ops:
  7.3 10.4 %copy.53 = bf16[2304,3,512]{0,2,1:T(8,128)(2,1)} copy(bf16[2304,3,512]{2,0,1:T(8,128)(2,1)} %param.17) | data formatting | bytes 14155776 | tf_op args[2]
  17.6 0.3 fusion.63
  17.9 5.2 %fusion.75 = f32[256,3,8,64]{0,3,2,1:T(8,128)S(1)} fusion(bf16[3,8,64,2304]{3,2,1,0:T(8,128)(2,1)} %bitcast.213, bf16[1,256,2304]{2,1,0:T(8,128)(2,1)S(1)} %copy-done.2, f32[2304]{0:T(1024)} %param.16, f32[256]{0:T(256)S(1)} %add_rsqrt_fusion.1), kind=kOutput, calls=%fused_computation.74 | convolution fusion | flops 1814298624 | bytes 9840640 | tf_op jit(solution)/shard_map/dot_general | solution.py:73
  23.2 1.1 copy-done.9
  24.4 0.2 multiply_cosine_fusion
  24.6 0.8 subtract_convert_fusion.1
  25.4 0.6 copy-done.10
  26.1 3.1 %collective-permute-start.1 = (bf16[256,8,64]{0,2,1:T(8,128)(2,1)S(1)}, bf16[256,8,64]{0,2,1:T(8,128)(2,1)}, u32[]{:S(2)}, u32[]{:S(2)}) collective-permute-start(bf16[256,8,64]{0,2,1:T(8,128)(2,1)S(1)} %pad_maximum_fusion.5), channel_id=1, source_target_pairs={{0,1},{2,3},{4,5},{6,7},{8,9},{10,11},{12,13},{14,15},{16,17},{18,... | collective-permute-start | bytes 786440 | tf_op jit(solution)/shard_map/ppermute | solution.py:13
  29.2 1.1 fusion.115
  30.2 1.3 collective-permute-start
  32.1 2.1 fusion.43
  34.2 1.3 fusion.50
  35.5 1.2 fusion.90
  36.7 1.8 convolution_convert_fusion
  38.6 0.2 reduce-scatter.2.cloned.1.call-start
  38.9 0.6 reduce-window.6
  39.7 0.2 reduce-window.9
  40.0 0.2 eq.112
  40.4 0.7 fusion.152
  41.2 55.5 %all-reduce.2.cloned.1.call-done = bf16[256,2304]{1,0:T(8,128)(2,1)} async-done(((bf16[256,2304]{1,0:T(8,128)(2,1)}), bf16[256,2304]{1,0:T(8,128)(2,1)}) %all-reduce.2.cloned.1.call-update) | async-done | bytes 1179664 | tf_op jit(solution)/shard_map/psum | solution.py:104
  96.7 1.8 fusion.60
  98.5 0.5 fusion.77
  99.3 1.7 collective-permute-done.2
  101.2 1.5 collective-permute-start.3
  102.7 1.5 collective-permute-start.4
  104.2 8.1 %fusion.52 = f32[2,192,1,1440]{3,1,0,2:T(8,128)S(1)} fusion(bf16[2,2,2304,1440]{2,3,1,0:T(8,128)(2,1)} %param.22, s32[]{:T(128)S(6)} %select_n.52, bf16[96,1,2304]{2,0,1:T(8,128)(2,1)S(1)} %collective-permute-done.2, bf16[96,1,2304]{2,0,1:T(8,128)(2,1)S(1)} %get-tuple-element.21), kind=kOutput, calls=%fused_computation.46 | convolution fusion | flops 2549809152 | bytes 16367620 | tf_op jit(solution)/shard_map/ned,egdf->gnef/dot_general | solution.py:146
  112.4 2.6 %fusion.44 = bf16[1,192,1,2304]{3,1,2,0:T(8,128)(2,1)} fusion(bf16[2,1440,2304]{2,1,0:T(8,128)(2,1)S(1)} %bitcast.229, s32[]{:T(128)S(6)} %select_n.52, f32[2,192,1,1440]{3,1,0,2:T(8,128)S(1)} %fusion.52), kind=kOutput, calls=%fused_computation.42 | convolution fusion | flops 1276121088 | bytes 9879556 | tf_op jit(solution)/shard_map/nef,efd->ned/dot_general | solution.py:148
  115.0 7.9 %collective-permute-done.3 = bf16[192,1,2304]{2,0,1:T(8,128)(2,1)S(1)} collective-permute-done((bf16[192,1,2304]{2,0,1:T(8,128)(2,1)S(1)}, bf16[192,1,2304]{2,0,1:T(8,128)(2,1)S(1)}, u32[]{:S(2)}, u32[]{:S(2)}) %collective-permute-start.3) | collective-permute-done | bytes 884768 | tf_op jit(solution)/shard_map/ppermute | solution.py:141
  122.9 1.2 collective-permute-done.4
  124.1 0.2 pad_maximum_fusion.3
  124.3 9.7 %fusion.33 = f32[2,384,1,1440]{1,3,0,2:T(8,128)S(1)} fusion(bf16[384,2304,1]{1,0,2:T(8,128)(2,1)S(1)} %bitcast.220, bf16[2,2,2304,1440]{2,3,1,0:T(8,128)(2,1)} %param.22, s32[]{:T(128)S(6)} %select_n.52), kind=kOutput, calls=%fused_computation.37 | convolution fusion | flops 5096079360 | bytes 19464196 | tf_op jit(solution)/shard_map/ned,egdf->gnef/dot_general | solution.py:146
  134.0 1.5 collective-permute-start.7
  135.5 3.2 %fusion.29 = bf16[384,1,2304]{2,0,1:T(8,128)(2,1)S(1)} fusion(bf16[2,1440,2304]{2,1,0:T(8,128)(2,1)S(1)} %bitcast.229, s32[]{:T(128)S(6)} %select_n.52, f32[2,384,1,1440]{1,3,0,2:T(8,128)S(1)} %fusion.33), kind=kOutput, calls=%fused_computation.34 | convolution fusion | flops 2552242176 | bytes 12828676 | tf_op jit(solution)/shard_map/nef,efd->ned/dot_general | solution.py:148
  138.8 1.3 fusion.165
  140.1 0.6 collective-permute-start.6
  140.7 0.6 collective-permute-start.5
  141.2 15.4 %collective-permute-done.7 = bf16[192,1,2304]{2,0,1:T(8,128)(2,1)S(1)} collective-permute-done((bf16[192,1,2304]{2,0,1:T(8,128)(2,1)S(1)}, bf16[192,1,2304]{2,0,1:T(8,128)(2,1)S(1)}, u32[]{:S(2)}, u32[]{:S(2)}) %collective-permute-start.7) | collective-permute-done | bytes 884768 | tf_op jit(solution)/shard_map/ppermute | solution.py:141
  156.7 7.7 %fusion.55 = f32[2,192,1,1440]{3,1,0,2:T(8,128)S(1)} fusion(bf16[2,2,2304,1440]{2,3,1,0:T(8,128)(2,1)} %param.22, s32[]{:T(128)S(6)} %select_n.52, bf16[192,1,2304]{2,0,1:T(8,128)(2,1)S(1)} %collective-permute-done.7), kind=kOutput, calls=%fused_computation.47 | convolution fusion | flops 2548039680 | bytes 16367620 | tf_op jit(solution)/shard_map/ned,egdf->gnef/dot_general | solution.py:146
  164.3 2.6 %fusion.47 = bf16[192,1,2304]{2,0,1:T(8,128)(2,1)} fusion(bf16[2,1440,2304]{2,1,0:T(8,128)(2,1)S(1)} %bitcast.229, s32[]{:T(128)S(6)} %select_n.52, f32[2,192,1,1440]{3,1,0,2:T(8,128)S(1)} %fusion.55), kind=kOutput, calls=%fused_computation.43 | convolution fusion | flops 1276121088 | bytes 9879556 | tf_op jit(solution)/shard_map/nef,efd->ned/dot_general | solution.py:148
  167.0 1.5 collective-permute-start.8
  168.5 0.2 convert_reduce_fusion
  168.8 23.7 %collective-permute-done.6 = bf16[192,1,2304]{2,0,1:T(8,128)(2,1)S(1)} collective-permute-done((bf16[192,1,2304]{2,0,1:T(8,128)(2,1)}, bf16[192,1,2304]{2,0,1:T(8,128)(2,1)S(1)}, u32[]{:S(2)}, u32[]{:S(2)}) %collective-permute-start.6) | collective-permute-done | bytes 884768 | tf_op jit(solution)/shard_map/ppermute | solution.py:141
  192.6 0.9 copy-done.7
  193.4 0.3 copy-done.5
  193.7 2.9 %pad_maximum_fusion = bf16[4,96,1,2304]{3,1,2,0:T(8,128)(2,1)} fusion(bf16[1,192,1,2304]{3,1,2,0:T(8,128)(2,1)} %bitcast.216, bf16[1,192,1,2304]{3,1,2,0:T(8,128)(2,1)} %bitcast.218, bf16[1,192,1,2304]{3,1,2,0:T(8,128)(2,1)} %bitcast.48, bf16[1,192,1,2304]{3,1,2,0:T(8,128)(2,1)} %fusion.44), kind=kLoop, calls=%fused_computation.68 | loop fusion | flops 7077888 | bytes 5308416 | tf_op jit(solution)/shard_map/stack | solution.py:182
  196.7 0.6 dynamic_slice.57
  197.3 0.7 add_compare_fusion
  198.0 1.7 bitcast_select_fusion
  199.6 2.3 gather_fusion
  201.9 1.5 fusion.112
  203.5 1.6 convolution_add_fusion.2
  205.1 0.5 fusion.111
  205.6 1.5 fusion.108
  207.2 1.5 fusion.109
  208.7 1.5 fusion.110
  210.3 1.7 fusion.26
  212.0 1.7 fusion.42
  213.7 1.6 broadcast_select_fusion.1
  215.3 3.7 %all-to-all-start = ((bf16[16,64,2,512]{3,1,2,0:T(8,128)(2,1)}), bf16[16,64,2,512]{3,1,2,0:T(8,128)(2,1)S(1)}, u32[]{:S(2)}, u32[]{:S(2)}) async-start(bf16[16,64,2,512]{3,1,2,0:T(8,128)(2,1)} %broadcast_select_fusion.1), calls=%async_computation.1 | async-start | bytes 4194304 | tf_op jit(solution)/shard_map/all_to_all | solution.py:233
  219.3 25.5 %all-to-all-done = bf16[16,64,2,512]{3,1,2,0:T(8,128)(2,1)S(1)} async-done(((bf16[16,64,2,512]{3,1,2,0:T(8,128)(2,1)}), bf16[16,64,2,512]{3,1,2,0:T(8,128)(2,1)S(1)}, u32[]{:S(2)}, u32[]{:S(2)}) %all-to-all-start) | async-done | bytes 2097184 | tf_op jit(solution)/shard_map/all_to_all | solution.py:233
  244.8 2.0 gather_fusion.1
  246.8 2.0 broadcast_select_fusion
  248.8 3.5 %copy.65 = bf16[16,64,2,512]{3,2,1,0:T(2,128)(2,1)} copy(bf16[16,64,2,512]{3,1,2,0:T(8,128)(2,1)S(1)} %broadcast_select_fusion) | data formatting | bytes 4194304
  252.3 1.7 fusion.114
  (92 shorter events, 2.2 us)
Async XLA Ops:
  7.2 29.5 %copy-start = (bf16[512,2304]{1,0:T(8,128)(2,1)S(1)}, bf16[512,2304]{1,0:T(8,128)(2,1)}, u32[]{:S(2)}) copy-start(bf16[512,2304]{1,0:T(8,128)(2,1)} %param.18) | copy-start | bytes 7077892
  7.2 89.5 %all-reduce.2.cloned.1.call-start = ((), (), s32[]{:S(2)}) async-start(), calls=%async_computation.2 | async-start | bytes 2359296 | tf_op jit(solution)/shard_map/psum | solution.py:104
  7.2 10.4 %copy-start.2 = (bf16[1,256,2304]{2,1,0:T(8,128)(2,1)S(1)}, bf16[1,256,2304]{2,1,0:T(8,128)(2,1)}, u32[]{:S(2)}) copy-start(bf16[1,256,2304]{2,1,0:T(8,128)(2,1)} %param.15) | copy-start | bytes 3538948
  23.2 1.1 copy-start.9
  24.3 7.3 %copy-start.13 = (s32[4,256,2]{1,2,0:T(2,128)S(1)}, s32[4,256,2]{1,2,0:T(2,128)}, u32[]{:S(2)}) copy-start(s32[4,256,2]{1,2,0:T(2,128)} %param.20) | copy-start | bytes 24580
  25.4 0.7 copy-start.10
  26.1 6.0 %collective-permute-start.1 = (bf16[256,8,64]{0,2,1:T(8,128)(2,1)S(1)}, bf16[256,8,64]{0,2,1:T(8,128)(2,1)}, u32[]{:S(2)}, u32[]{:S(2)}) collective-permute-start(bf16[256,8,64]{0,2,1:T(8,128)(2,1)S(1)} %pad_maximum_fusion.5), channel_id=1, source_target_pairs={{0,1},{2,3},{4,5},{6,7},{8,9},{10,11},{12,13},{14,15},{16,17},{18,... | collective-permute-start | bytes 786440 | tf_op jit(solution)/shard_map/ppermute | solution.py:13
  30.2 5.2 %collective-permute-start = (bf16[256,8,64]{0,2,1:T(8,128)(2,1)S(1)}, bf16[256,8,64]{0,2,1:T(8,128)(2,1)S(1)}, u32[]{:S(2)}, u32[]{:S(2)}) collective-permute-start(bf16[256,8,64]{0,2,1:T(8,128)(2,1)S(1)} %fusion.115), channel_id=1, source_target_pairs={{0,1},{2,3},{4,5},{6,7},{8,9},{10,11},{12,13},{14,15},{16,17},{18,... | collective-permute-start | bytes 786440 | tf_op jit(solution)/shard_map/ppermute | solution.py:13
  38.5 58.2 %copy-start.3 = (bf16[1,256,2304]{2,1,0:T(8,128)(2,1)S(1)}, bf16[1,256,2304]{2,1,0:T(8,128)(2,1)}, u32[]{:S(2)}) copy-start(bf16[1,256,2304]{2,1,0:T(8,128)(2,1)} %param.15) | copy-start | bytes 3538948
  38.6 60.0 %copy-start.12 = (f32[2304]{0:T(1024)S(1)}, f32[2304]{0:T(1024)}, u32[]{:S(2)}) copy-start(f32[2304]{0:T(1024)} %param.19) | copy-start | bytes 27652
  38.6 213.7 %reduce-scatter.2.cloned.1.call-start = ((), (), s32[]{:S(2)}) async-start(), calls=%async_computation.3 | async-start | bytes 1474560 | tf_op jit(solution)/shard_map/reduce_scatter | solution.py:197
  99.2 1.9 collective-permute-start.2
  101.1 11.3 %slice-start = ((s8[13271040]{0:T(1024)(128)(4,1)}), s8[4194304]{0:T(1024)(128)(4,1)S(1)}, s32[]{:S(2)}) async-start(s8[13271040]{0:T(1024)(128)(4,1)} %bitcast.228), calls=%async_computation.4 | async-start | bytes 8388608
  101.1 11.2 %slice-start.1 = ((s8[13271040]{0:T(1024)(128)(4,1)}), s8[4194304]{0:T(1024)(128)(4,1)S(1)}, s32[]{:S(2)}) async-start(s8[13271040]{0:T(1024)(128)(4,1)} %bitcast.228), calls=%async_computation.5 | async-start | bytes 8388608
  101.2 11.2 %slice-start.2 = ((s8[13271040]{0:T(1024)(128)(4,1)}), s8[4194304]{0:T(1024)(128)(4,1)S(1)}, s32[]{:S(2)}) async-start(s8[13271040]{0:T(1024)(128)(4,1)} %bitcast.228), calls=%async_computation.6 | async-start | bytes 8388608
  101.2 11.2 %slice-start.3 = ((s8[13271040]{0:T(1024)(128)(4,1)}), s8[688128]{0:T(1024)(128)(4,1)S(1)}, s32[]{:S(2)}) async-start(s8[13271040]{0:T(1024)(128)(4,1)} %bitcast.228), calls=%async_computation.7 | async-start | bytes 1376256
  101.2 21.8 %collective-permute-start.3 = (bf16[192,1,2304]{2,0,1:T(8,128)(2,1)S(1)}, bf16[192,1,2304]{2,0,1:T(8,128)(2,1)S(1)}, u32[]{:S(2)}, u32[]{:S(2)}) collective-permute-start(bf16[192,1,2304]{2,0,1:T(8,128)(2,1)S(1)} %pad_maximum_fusion.4), channel_id=1, source_target_pairs={{0,8},{8,0},{16,24},{24,16},{1,9},{9,1},{17,25},{25,17},{2,10},{10... | collective-permute-start | bytes 2654216 | tf_op jit(solution)/shard_map/ppermute | solution.py:141
  102.7 21.4 %collective-permute-start.4 = (bf16[192,1,2304]{2,0,1:T(8,128)(2,1)S(1)}, bf16[192,1,2304]{2,0,1:T(8,128)(2,1)S(1)}, u32[]{:S(2)}, u32[]{:S(2)}) collective-permute-start(bf16[192,1,2304]{2,0,1:T(8,128)(2,1)S(1)} %pad_maximum_fusion.4), channel_id=1, source_target_pairs={{0,16},{8,24},{16,0},{24,8},{1,17},{9,25},{17,1},{25,9},{2,18},{10... | collective-permute-start | bytes 2654216 | tf_op jit(solution)/shard_map/ppermute | solution.py:141
  134.0 22.7 %collective-permute-start.7 = (bf16[192,1,2304]{2,0,1:T(8,128)(2,1)S(1)}, bf16[192,1,2304]{2,0,1:T(8,128)(2,1)S(1)}, u32[]{:S(2)}, u32[]{:S(2)}) collective-permute-start(bf16[192,1,2304]{2,0,1:T(8,128)(2,1)S(1)} %collective-permute-done.3), channel_id=1, source_target_pairs={{0,16},{8,24},{16,0},{24,8},{1,17},{9,25},{17,1},{25,9},{2,18},{10... | collective-permute-start | bytes 2654216 | tf_op jit(solution)/shard_map/ppermute | solution.py:141
  140.1 52.4 %collective-permute-start.6 = (bf16[192,1,2304]{2,0,1:T(8,128)(2,1)}, bf16[192,1,2304]{2,0,1:T(8,128)(2,1)S(1)}, u32[]{:S(2)}, u32[]{:S(2)}) collective-permute-start(bf16[192,1,2304]{2,0,1:T(8,128)(2,1)} %get-tuple-element.18), channel_id=1, source_target_pairs={{0,16},{8,24},{16,0},{24,8},{1,17},{9,25},{17,1},{25,9},{2,18},{10... | collective-permute-start | bytes 2654216 | tf_op jit(solution)/shard_map/ppermute | solution.py:141
  140.7 51.8 %collective-permute-start.5 = (bf16[192,1,2304]{2,0,1:T(8,128)(2,1)}, bf16[192,1,2304]{2,0,1:T(8,128)(2,1)}, u32[]{:S(2)}, u32[]{:S(2)}) collective-permute-start(bf16[192,1,2304]{2,0,1:T(8,128)(2,1)} %get-tuple-element.17), channel_id=1, source_target_pairs={{0,8},{8,0},{16,24},{24,16},{1,9},{9,1},{17,25},{25,17},{2,10},{10... | collective-permute-start | bytes 2654216 | tf_op jit(solution)/shard_map/ppermute | solution.py:141
  164.3 4.1 %copy-start.11 = (s32[4,16]{1,0:T(4,128)S(1)}, s32[4,16]{1,0:T(4,128)}, u32[]{:S(2)}) copy-start(s32[4,16]{1,0:T(4,128)} %param.26) | copy-start | bytes 772
  167.0 25.6 %collective-permute-start.8 = (bf16[192,1,2304]{2,0,1:T(8,128)(2,1)}, bf16[192,1,2304]{2,0,1:T(8,128)(2,1)S(1)}, u32[]{:S(2)}, u32[]{:S(2)}) collective-permute-start(bf16[192,1,2304]{2,0,1:T(8,128)(2,1)} %fusion.47), channel_id=1, source_target_pairs={{0,24},{8,16},{16,8},{24,0},{1,25},{9,17},{17,9},{25,1},{2,26},{10... | collective-permute-start | bytes 2654216 | tf_op jit(solution)/shard_map/ppermute | solution.py:141
  192.5 0.9 copy-start.7
  192.5 1.2 copy-start.5
  193.7 2.9 %copy-start.15 = (s32[4]{0:T(128)S(1)}, s32[4]{0:T(128)}, u32[]{:S(2)}) copy-start(s32[4]{0:T(128)} %param.25) | copy-start | bytes 52
  193.7 4.2 %copy-start.4 = (bf16[1,16,64,2,512]{4,3,2,1,0:T(2,128)(2,1)S(1)}, bf16[1,16,64,2,512]{4,3,2,1,0:T(2,128)(2,1)}, u32[]{:S(2)}) copy-start(bf16[1,16,64,2,512]{4,3,2,1,0:T(2,128)(2,1)} %param.24) | copy-start | bytes 6291460
  196.6 9.0 %collective-permute-start.9 = (bf16[4,96,1,2304]{3,1,2,0:T(8,128)(2,1)}, bf16[4,96,1,2304]{3,1,2,0:T(8,128)(2,1)}, u32[]{:S(2)}, u32[]{:S(2)}) collective-permute-start(bf16[4,96,1,2304]{3,1,2,0:T(8,128)(2,1)} %pad_maximum_fusion), channel_id=1, source_target_pairs={{0,1},{1,0},{2,3},{3,2},{4,5},{5,4},{6,7},{7,6},{8,9},{9,8},{10,11... | collective-permute-start | bytes 5308424 | tf_op jit(solution)/shard_map/ppermute | solution.py:184
  203.5 1.6 copy-start.6
  210.3 1.7 copy-start.8
  215.3 3.8 %copy-start.14 = (s32[4,16]{1,0:T(4,128)S(1)}, s32[4,16]{1,0:T(4,128)}, u32[]{:S(2)}) copy-start(s32[4,16]{1,0:T(4,128)} %param.27) | copy-start | bytes 772
  215.3 29.5 %all-to-all-start = ((bf16[16,64,2,512]{3,1,2,0:T(8,128)(2,1)}), bf16[16,64,2,512]{3,1,2,0:T(8,128)(2,1)S(1)}, u32[]{:S(2)}, u32[]{:S(2)}) async-start(bf16[16,64,2,512]{3,1,2,0:T(8,128)(2,1)} %broadcast_select_fusion.1), calls=%async_computation.1 | async-start | bytes 4194304 | tf_op jit(solution)/shard_map/all_to_all | solution.py:233
  246.8 7.2 %copy-start.1 = (bf16[512,2304]{1,0:T(8,128)(2,1)S(1)}, bf16[512,2304]{1,0:T(8,128)(2,1)}, u32[]{:S(2)}) copy-start(bf16[512,2304]{1,0:T(8,128)(2,1)} %param.18) | copy-start | bytes 7077892
Sparse Core Ops, SparseCore 0:
  38.7 57.9 all-reduce.1
  213.8 27.9 reduce-scatter.1

commit v11 on v2

--- a/solution.py
+++ b/solution.py
@@ -140,45 +140,64 @@
     )
     attended = attended.astype(jnp.bfloat16).reshape(half_rows, local_cols)
     partial_value = jnp.dot(attended, w_out, preferred_element_type=jnp.float32)
+    reduced_in = partial_value.astype(jnp.bfloat16)
+    attn_mixed = lax.psum(reduced_in, "head").astype(jnp.float32)
+    kv_cache, reduced_in = lax.optimization_barrier((kv_cache, reduced_in))
     page_pool = hand_over_pages(kv_cache, lengths, block_owner, block_slot)
-    partial_value, page_pool = lax.optimization_barrier((partial_value, page_pool))
-    attn_mixed = lax.psum(partial_value.astype(jnp.bfloat16), "head").astype(jnp.float32)
     residual = (tokens[0].astype(jnp.float32) + attn_mixed).astype(jnp.bfloat16)
     moe_in = norm_rows(residual, moe_gain)
     experts_here = w_gate_up.shape[0]
     first_expert = head_index * experts_here
     top_count = routes.shape[2]
     capacity = half_rows * top_count * 3 // (2 * EXPERTS)
-    all_rows_here = lax.all_gather(moe_in, "req", axis=0, tiled=True)
-    sources = all_rows_here.shape[0] // half_rows
-    every_dispatch, every_combine = slot_tables(
-        routes, route_weight, first_expert, experts_here, capacity
-    )
-    picked_all = jnp.einsum(
-        "stec,std->sced",
-        every_dispatch.astype(jnp.bfloat16),
-        all_rows_here.reshape(sources, half_rows, model_width),
+    own_routes = lax.dynamic_index_in_dim(routes, req_index, 0, keepdims=True)
+    own_weights = lax.dynamic_index_in_dim(route_weight, req_index, 0, keepdims=True)
+    own_dispatch, own_combine = slot_tables(
+        own_routes, own_weights, first_expert, experts_here, capacity
+    )
+    own_dispatch = own_dispatch[0]
+    own_combine = own_combine[0]
+    picked_own = jnp.einsum(
+        "tec,td->ced",
+        own_dispatch.astype(jnp.bfloat16),
+        moe_in,
         preferred_element_type=jnp.float32,
-    )
-    picked_all = picked_all.astype(jnp.bfloat16).reshape(
-        sources * capacity, experts_here, model_width
-    )
-    both = jnp.einsum("ned,egdf->gnef", picked_all, w_gate_up, preferred_element_type=jnp.float32)
-    hidden_all = (jax.nn.silu(both[0]) * both[1]).astype(jnp.bfloat16)
-    source_count = half_rows * lax.axis_size("req") // half_rows
-    down_out = jnp.einsum("nef,efd->ned", hidden_all, w_down, preferred_element_type=jnp.float32)
-    down_out = down_out.astype(jnp.bfloat16).reshape(
-        source_count, capacity, experts_here, model_width
-    )
-    expert_back = lax.psum_scatter(down_out, "req", scatter_dimension=0, tiled=True)[0]
-    own_dispatch = lax.dynamic_index_in_dim(every_dispatch, req_index, 0, keepdims=False)
-    own_combine = lax.dynamic_index_in_dim(every_combine, req_index, 0, keepdims=False)
+    ).astype(jnp.bfloat16)
+    picked_own, page_pool = lax.optimization_barrier((picked_own, page_pool))
+    req_total = lax.axis_size("req")
+
+    def partner_move(block, step):
+        return lax.ppermute(block, "req", [(i, i ^ step) for i in range(req_total)])
+
+    def experts_on(rows):
+        groups = rows.shape[0]
+        flat = rows.reshape(groups * capacity, experts_here, model_width)
+        both = jnp.einsum("ned,egdf->gnef", flat, w_gate_up, preferred_element_type=jnp.float32)
+        hidden = (jax.nn.silu(both[0]) * both[1]).astype(jnp.bfloat16)
+        down = jnp.einsum("nef,efd->ned", hidden, w_down, preferred_element_type=jnp.float32)
+        return down.astype(jnp.bfloat16).reshape(groups, capacity, experts_here, model_width)
+
+    arrived = {0: picked_own}
+    for step in range(1, req_total):
+        if step == 3:
+            arrived[step] = partner_move(arrived[1], 2)
+        else:
+            arrived[step] = partner_move(picked_own, step)
+    plan = [[0], [1, 2]] + ([list(range(3, req_total))] if req_total > 3 else [])
+    plan = [[k for k in group if k < req_total] for group in plan]
+    returned = []
+    for group in plan:
+        if not group:
+            continue
+        outs = experts_on(jnp.stack([arrived[k] for k in group], axis=0))
+        for slot_index, step in enumerate(group):
+            part = outs[slot_index]
+            returned.append(part if step == 0 else partner_move(part, step))
     token_weights = jnp.sum(own_combine, axis=-1)
-    selected = jnp.einsum(
-        "tec,ced->ted",
-        own_dispatch.astype(jnp.bfloat16),
-        expert_back,
-        preferred_element_type=jnp.float32,
+    dispatch_bf = own_dispatch.astype(jnp.bfloat16)
+    selected = sum(
+        jnp.einsum("tec,ced->ted", dispatch_bf, part, preferred_element_type=jnp.float32)
+        for part in returned
     )
     moe_out = jnp.sum(token_weights[:, :, None] * selected, axis=1)
     summed = lax.psum_scatter(

time: 303 us -> 262 us (0.86)
  waiting for transfers between devices: 179 us -> 87.6 us
  matrix products: 43.6 us -> 90.4 us
  starting transfers between devices: 10.2 us -> 16.8 us
  other arithmetic: 26.8 us -> 23.5 us
    all_gather x1 -> x0, waiting for transfers between devices: 50.9 us -> none  [body(): all_rows_here = lax.all_gather(moe_in, 'req', axis=0, tiled=True)]
    dot_general x3 -> x9, matrix products: 28.8 us -> 78.7 us  [the longest x3 43.1 us: experts_on(): jnp.einsum('ned,egdf->gnef', flat, w_gate_up, preferred_element_type=jnp....]
    unnamed x5 -> x2, waiting for transfers between devices: 46.2 us -> 0.03 us
    ppermute x0 -> x6, waiting for transfers between devices: none -> 19.4 us  [partner_move(): return lax.ppermute(block, 'req', [(i, i ^ step) for i in range(req_total)])]
    psum x1, waiting for transfers between devices: 58.2 us -> 45.5 us  [body(): attn_mixed = lax.psum(reduced_in, 'head').astype(jnp.float32)]
    ppermute x0 -> x6, starting transfers between devices: none -> 6.99 us  [partner_move(): return lax.ppermute(block, 'req', [(i, i ^ step) for i in range(req_total)])]
    unnamed x25 -> x34, local copies, waits for them, and re-layouts: 16.2 us -> 16.7 us
  transfers between devices with their start and end apart: 7 -> 11, of which waited for: 4 -> 6; matrix products, arithmetic and copies ran while one was open for 13% -> 35% of each run, Pallas kernels for 0% -> 0%
where the time goes in v11:
time: 262 us; the launch traced here: 261 us
  matrix products  90.4 us (35%)
  waiting for transfers between devices  87.6 us (33%)
  local copies, waits for them, and re-layouts  28.2 us (11%)
  other arithmetic  23.5 us (9%)
  starting transfers between devices  16.8 us (6%)
  between operations  14.4 us (5%)
    psum x1, waiting for transfers between devices, body(): attn_mixed = lax.psum(reduced_in, 'head').astype(jnp.float32)  45.5 us
    dot_general x3, matrix products, experts_on(): jnp.einsum('ned,egdf->gnef', flat, w_gate_up, preferred_element_type=jnp....  43.1 us
    reduce_scatter x1, waiting for transfers between devices, body(): lax.psum_scatter(moe_out.astype(jnp.bfloat16), 'head', scatter_dimension=...  22.7 us
    ppermute x6, waiting for transfers between devices, partner_move(): return lax.ppermute(block, 'req', [(i, i ^ step) for i in range(req_total)])  19.4 us
    dot_general x2, matrix products, experts_on(): jnp.einsum('nef,efd->ned', hidden, w_down, preferred_element_type=jnp.flo...  18 us
    dot_general x4, matrix products, body(): jnp.einsum('tec,ced->ted', dispatch_bf, part, preferred_element_type=jnp....  17.6 us
    unnamed x34, local copies, waits for them, and re-layouts  16.7 us
    ppermute x6, starting transfers between devices, partner_move(): return lax.ppermute(block, 'req', [(i, i ^ step) for i in range(req_total)])  6.99 us
  transfers between devices with their start and end apart: 11, of which 6 were waited for; matrix products, arithmetic and copies ran while one was open for 35% of the time, Pallas kernels for 0%

profile of v11, /device:TPU:0, one launch (start us, length us, event | category | flops | bytes accessed | tf_op | source)
XLA Modules:
  0.0 260.8 jit_solution(9458294922728880875)
XLA Ops:
  7.3 9.9 %copy.52 = bf16[2304,3,512]{0,2,1:T(8,128)(2,1)} copy(bf16[2304,3,512]{2,0,1:T(8,128)(2,1)} %param.17) | data formatting | bytes 14155776 | tf_op args[2]
  17.2 0.3 fusion.19
  17.5 5.2 %fusion.35 = f32[256,3,8,64]{0,3,2,1:T(8,128)S(1)} fusion(bf16[3,8,64,2304]{3,2,1,0:T(8,128)(2,1)} %bitcast.155, bf16[1,256,2304]{2,1,0:T(8,128)(2,1)S(1)} %copy-done.3, f32[2304]{0:T(1024)} %param.16, f32[256]{0:T(256)S(1)} %add_rsqrt_fusion.1), kind=kOutput, calls=%fused_computation.51 | convolution fusion | flops 1814298624 | bytes 9840640 | tf_op jit(solution)/shard_map/dot_general | solution.py:112
  22.8 0.2 multiply_cosine_fusion
  23.0 0.8 subtract_convert_fusion.1
  23.8 3.1 %collective-permute-start.1 = (bf16[256,8,64]{0,2,1:T(8,128)(2,1)S(1)}, bf16[256,8,64]{0,2,1:T(8,128)(2,1)}, u32[]{:S(2)}, u32[]{:S(2)}) collective-permute-start(bf16[256,8,64]{0,2,1:T(8,128)(2,1)S(1)} %pad_maximum_fusion.1), channel_id=1, source_target_pairs={{0,1},{2,3},{4,5},{6,7},{8,9},{10,11},{12,13},{14,15},{16,17},{18,... | collective-permute-start | bytes 786440 | tf_op jit(solution)/shard_map/ppermute | solution.py:13
  26.9 2.0 collective-permute-start
  28.9 0.6 iota_add_fusion.1
  29.5 0.2 convert_reduce_fusion
  29.9 0.5 compare_and_fusion.2
  30.8 0.6 reduce-window.6
  31.4 0.2 slice_reduce_fusion
  31.6 0.6 pad_clamp_fusion.1
  32.4 0.6 copy-done.14
  33.0 0.2 reduce-window.9
  33.3 0.2 eq.112
  33.7 0.8 compare_convert_fusion
  34.4 0.7 dynamic-slice_bitcast_fusion
  35.1 0.7 fusion.71
  35.9 1.2 dynamic_slice.25
  37.1 0.8 compare_and_fusion
  37.9 1.9 fusion.6
  39.9 1.3 fusion.9
  41.2 2.2 fusion.51
  43.4 1.9 convolution_convert_fusion.1
  45.3 0.6 add_compare_fusion
  45.9 3.2 %bitcast_select_fusion = bf16[16,64,2,512]{3,1,2,0:T(8,128)(2,1)} fusion(bf16[1,16,64,2,512]{4,3,2,1,0:T(2,128)(2,1)} %param.24, pred[16,64]{1,0:T(8,128)(4,1)S(1)} %add_compare_fusion), kind=kLoop, calls=%fused_computation.41 | loop fusion | flops 1048576 | bytes 4195328 | tf_op jit(solution)/shard_map/jit(_where)/select_n | solution.py:75
  49.2 2.4 gather_fusion
  51.6 1.6 broadcast_select_fusion.1
  53.2 4.5 %all-to-all-start = ((bf16[16,64,2,512]{3,1,2,0:T(8,128)(2,1)}), bf16[16,64,2,512]{3,1,2,0:T(8,128)(2,1)S(1)}, u32[]{:S(2)}, u32[]{:S(2)}) async-start(bf16[16,64,2,512]{3,1,2,0:T(8,128)(2,1)} %broadcast_select_fusion.1), calls=%async_computation | async-start | bytes 4194304 | tf_op jit(solution)/shard_map/all_to_all | solution.py:79
  57.7 0.2 reduce-scatter.2.cloned.1.call-start
  57.9 45.5 %all-reduce.2.cloned.1.call-done = bf16[256,2304]{1,0:T(8,128)(2,1)} async-done(((bf16[256,2304]{1,0:T(8,128)(2,1)}), bf16[256,2304]{1,0:T(8,128)(2,1)}) %all-reduce.2.cloned.1.call-update) | async-done | bytes 1179664 | tf_op jit(solution)/shard_map/psum | solution.py:144
  103.4 2.1 fusion.16
  105.6 0.5 fusion.37
  106.1 1.0 convert_bitcast_fusion.1
  107.1 2.0 gather_fusion.1
  109.1 3.3 %broadcast_select_fusion = bf16[16,64,2,512]{3,1,2,0:T(8,128)(2,1)} fusion(bf16[16,64,2,512]{3,1,2,0:T(8,128)(2,1)} %gather_fusion.1, pred[16]{0:T(512)(128)(4,1)S(1)} %compare_and_fusion.1), kind=kLoop, calls=%fused_computation.43 | loop fusion | flops 1048576 | bytes 4194320 | tf_op jit(solution)/shard_map/jit(_take)/select_n | solution.py:85
  112.5 1.5 collective-permute-start.2
  113.9 1.5 collective-permute-start.3
  115.4 14.3 %convolution_bitcast_fusion.1 = f32[2,96,2,1440]{3,1,0,2:T(8,128)} fusion(bf16[2,2,2304,1440]{2,3,1,0:T(8,128)(2,1)} %param.22, bf16[96,2,2304]{2,0,1:T(8,128)(2,1)S(1)} %copy-done.6), kind=kOutput, calls=%fused_computation.23 | convolution fusion | flops 2548039680 | bytes 29638656 | tf_op jit(solution)/shard_map/ned,egdf->gnef/dot_general | solution.py:175
  129.7 4.5 %collective-permute-done.2 = bf16[96,2,2304]{2,0,1:T(8,128)(2,1)} collective-permute-done((bf16[96,2,2304]{2,0,1:T(8,128)(2,1)S(1)}, bf16[96,2,2304]{2,0,1:T(8,128)(2,1)}, u32[]{:S(2)}, u32[]{:S(2)}) %collective-permute-start.2) | collective-permute-done | bytes 884768 | tf_op jit(solution)/shard_map/ppermute | solution.py:170
  134.2 1.1 collective-permute-done.3
  135.3 0.9 copy-done.7
  136.2 1.6 pad_maximum_fusion
  137.8 1.3 copy.57
  139.1 14.9 %convolution_bitcast_fusion = f32[2,192,2,1440]{3,1,0,2:T(8,128)} fusion(bf16[192,2,2304,1]{2,0,3,1:T(8,128)(2,1)} %bitcast.158, bf16[2,2,2304,1440]{2,3,1,0:T(8,128)(2,1)} %param.22), kind=kOutput, calls=%fused_computation.14 | convolution fusion | flops 5096079360 | bytes 32735232 | tf_op jit(solution)/shard_map/ned,egdf->gnef/dot_general | solution.py:175
  154.0 1.5 collective-permute-start.6
  155.5 9.1 %fusion.5 = bf16[192,2,2304]{2,0,1:T(8,128)(2,1)S(1)} fusion(bf16[2,1440,2304]{2,1,0:T(8,128)(2,1)} %param.23, f32[2,192,2,1440]{3,1,0,2:T(8,128)} %convolution_bitcast_fusion), kind=kOutput, calls=%fused_computation.12 | convolution fusion | flops 2552242176 | bytes 19464192 | tf_op jit(solution)/shard_map/nef,efd->ned/dot_general | solution.py:177
  164.6 1.3 fusion.93
  166.0 0.6 collective-permute-start.4
  166.5 0.6 collective-permute-start.5
  167.1 9.8 %collective-permute-done.6 = bf16[96,2,2304]{2,0,1:T(8,128)(2,1)} collective-permute-done((bf16[96,2,2304]{2,0,1:T(8,128)(2,1)}, bf16[96,2,2304]{2,0,1:T(8,128)(2,1)}, u32[]{:S(2)}, u32[]{:S(2)}) %collective-permute-start.6) | collective-permute-done | bytes 884768 | tf_op jit(solution)/shard_map/ppermute | solution.py:170
  176.9 13.9 %fusion.11 = f32[2,96,2,1440]{3,1,2,0:T(8,128)} fusion(bf16[2,2,2304,1440]{2,3,1,0:T(8,128)(2,1)} %param.22, bf16[96,2,2304]{2,0,1:T(8,128)(2,1)} %collective-permute-done.6), kind=kOutput, calls=%fused_computation.22 | convolution fusion | flops 2548039680 | bytes 29638656 | tf_op jit(solution)/shard_map/ned,egdf->gnef/dot_general | solution.py:175
  190.8 8.9 %fusion.8 = bf16[96,2,2304]{2,0,1:T(8,128)(2,1)} fusion(bf16[2,1440,2304]{2,1,0:T(8,128)(2,1)} %param.23, f32[2,96,2,1440]{3,1,2,0:T(8,128)} %fusion.11), kind=kOutput, calls=%fused_computation.19 | convolution fusion | flops 1276121088 | bytes 16367616 | tf_op jit(solution)/shard_map/nef,efd->ned/dot_general | solution.py:177
  199.7 1.5 collective-permute-start.7
  201.1 9.8 %fusion.29 = f32[2,2304,256]{2,1,0:T(8,128)} fusion(bf16[256,2,96]{0,2,1:T(8,128)(2,1)} %get-tuple-element.18, bf16[2,1440,2304]{2,1,0:T(8,128)(2,1)} %param.23, f32[2,96,2,1440]{3,1,0,2:T(8,128)S(1)} %copy-done.2), kind=kOutput, calls=%fused_computation.47 | convolution fusion | flops 1502613504 | bytes 20299776 | tf_op jit(solution)/shard_map/tec,ced->ted/dot_general | solution.py:199
  211.0 3.5 %convolution_add_fusion.1 = f32[2,2304,256]{2,1,0:T(8,128)S(1)} fusion(f32[2,2304,256]{2,1,0:T(8,128)} %fusion.29, bf16[96,2,2304]{2,0,1:T(8,128)(2,1)} %collective-permute-done.4, bf16[256,2,96]{0,2,1:T(8,128)(2,1)} %get-tuple-element.18), kind=kOutput, calls=%fused_computation.6 | convolution fusion | flops 227672064 | bytes 10420224 | tf_op jit(solution)/shard_map/tec,ced->ted/dot_general | solution.py:199
  214.5 4.0 %collective-permute-done.7 = bf16[96,2,2304]{2,0,1:T(8,128)(2,1)} collective-permute-done((bf16[96,2,2304]{2,0,1:T(8,128)(2,1)}, bf16[96,2,2304]{2,0,1:T(8,128)(2,1)}, u32[]{:S(2)}, u32[]{:S(2)}) %collective-permute-start.7) | collective-permute-done | bytes 884768 | tf_op jit(solution)/shard_map/ppermute | solution.py:170
  218.5 2.0 fusion.94
  220.5 2.3 fusion.28
  222.8 1.5 copy.60
  224.3 5.2 %copy.61 = bf16[16,64,2,512]{3,2,1,0:T(2,128)(2,1)} copy(bf16[16,64,2,512]{3,1,2,0:T(8,128)(2,1)} %broadcast_select_fusion) | data formatting | bytes 4194304
  229.5 22.7 %reduce-scatter.2.cloned.1.call-done = bf16[64,2304]{1,0:T(8,128)(2,1)} async-done(((bf16[256,2304]{1,0:T(8,128)(2,1)}), bf16[64,2304]{1,0:T(8,128)(2,1)}) %reduce-scatter.2.cloned.1.call-update) | async-done | bytes 294928 | tf_op jit(solution)/shard_map/reduce_scatter | solution.py:203
  252.2 1.7 fusion.72
  (72 shorter events, 1.4 us)
Async XLA Ops:
  7.2 36.2 %copy-start = (bf16[512,2304]{1,0:T(8,128)(2,1)S(1)}, bf16[512,2304]{1,0:T(8,128)(2,1)}, u32[]{:S(2)}) copy-start(bf16[512,2304]{1,0:T(8,128)(2,1)} %param.18) | copy-start | bytes 7077892
  7.2 96.2 %all-reduce.2.cloned.1.call-start = ((), (), s32[]{:S(2)}) async-start(), calls=%async_computation.2 | async-start | bytes 2359296 | tf_op jit(solution)/shard_map/psum | solution.py:144
  7.3 9.9 %copy-start.3 = (bf16[1,256,2304]{2,1,0:T(8,128)(2,1)S(1)}, bf16[1,256,2304]{2,1,0:T(8,128)(2,1)}, u32[]{:S(2)}) copy-start(bf16[1,256,2304]{2,1,0:T(8,128)(2,1)} %param.15) | copy-start | bytes 3538948
  22.7 6.8 %copy-start.8 = (s32[4,16]{1,0:T(4,128)S(1)}, s32[4,16]{1,0:T(4,128)}, u32[]{:S(2)}) copy-start(s32[4,16]{1,0:T(4,128)} %param.26) | copy-start | bytes 772
  22.7 7.7 %copy-start.11 = (s32[4,256,2]{1,2,0:T(2,128)S(1)}, s32[4,256,2]{1,2,0:T(2,128)}, u32[]{:S(2)}) copy-start(s32[4,256,2]{1,2,0:T(2,128)} %param.20) | copy-start | bytes 24580
  22.7 9.6 %copy-start.12 = (s32[4,16]{1,0:T(4,128)S(1)}, s32[4,16]{1,0:T(4,128)}, u32[]{:S(2)}) copy-start(s32[4,16]{1,0:T(4,128)} %param.27) | copy-start | bytes 772
  23.8 14.1 %collective-permute-start.1 = (bf16[256,8,64]{0,2,1:T(8,128)(2,1)S(1)}, bf16[256,8,64]{0,2,1:T(8,128)(2,1)}, u32[]{:S(2)}, u32[]{:S(2)}) collective-permute-start(bf16[256,8,64]{0,2,1:T(8,128)(2,1)S(1)} %pad_maximum_fusion.1), channel_id=1, source_target_pairs={{0,1},{2,3},{4,5},{6,7},{8,9},{10,11},{12,13},{14,15},{16,17},{18,... | collective-permute-start | bytes 786440 | tf_op jit(solution)/shard_map/ppermute | solution.py:13
  26.9 14.3 %collective-permute-start = (bf16[256,8,64]{0,2,1:T(8,128)(2,1)S(1)}, bf16[256,8,64]{0,2,1:T(8,128)(2,1)}, u32[]{:S(2)}, u32[]{:S(2)}) collective-permute-start(bf16[256,8,64]{0,2,1:T(8,128)(2,1)S(1)} %fusion.73), channel_id=1, source_target_pairs={{0,1},{2,3},{4,5},{6,7},{8,9},{10,11},{12,13},{14,15},{16,17},{18,... | collective-permute-start | bytes 786440 | tf_op jit(solution)/shard_map/ppermute | solution.py:13
  30.7 2.6 copy-start.10
  32.4 0.6 copy-start.14
  43.4 1.9 copy-start.15
  49.2 2.4 copy-start.13
  53.2 54.0 %all-to-all-start = ((bf16[16,64,2,512]{3,1,2,0:T(8,128)(2,1)}), bf16[16,64,2,512]{3,1,2,0:T(8,128)(2,1)S(1)}, u32[]{:S(2)}, u32[]{:S(2)}) async-start(bf16[16,64,2,512]{3,1,2,0:T(8,128)(2,1)} %broadcast_select_fusion.1), calls=%async_computation | async-start | bytes 4194304 | tf_op jit(solution)/shard_map/all_to_all | solution.py:79
  57.7 47.9 %copy-start.4 = (bf16[256,2,96]{0,2,1:T(8,128)(2,1)S(1)}, bf16[256,2,96]{0,2,1:T(8,128)(2,1)}, u32[]{:S(2)}) copy-start(bf16[256,2,96]{0,2,1:T(8,128)(2,1)} %get-tuple-element.18) | copy-start | bytes 294916
  57.7 47.9 %copy-start.9 = (f32[2304]{0:T(1024)S(1)}, f32[2304]{0:T(1024)}, u32[]{:S(2)}) copy-start(f32[2304]{0:T(1024)} %param.19) | copy-start | bytes 27652
  57.7 194.5 %reduce-scatter.2.cloned.1.call-start = ((), (), s32[]{:S(2)}) async-start(), calls=%async_computation.3 | async-start | bytes 1474560 | tf_op jit(solution)/shard_map/reduce_scatter | solution.py:203
  109.1 3.3 %copy-start.6 = (bf16[96,2,2304]{2,0,1:T(8,128)(2,1)S(1)}, bf16[96,2,2304]{2,0,1:T(8,128)(2,1)}, u32[]{:S(2)}) copy-start(bf16[96,2,2304]{2,0,1:T(8,128)(2,1)} %convert_bitcast_fusion.1) | copy-start | bytes 2654212
  112.5 21.7 %collective-permute-start.2 = (bf16[96,2,2304]{2,0,1:T(8,128)(2,1)S(1)}, bf16[96,2,2304]{2,0,1:T(8,128)(2,1)}, u32[]{:S(2)}, u32[]{:S(2)}) collective-permute-start(bf16[96,2,2304]{2,0,1:T(8,128)(2,1)S(1)} %copy-done.6), channel_id=1, source_target_pairs={{0,8},{8,0},{16,24},{24,16},{1,9},{9,1},{17,25},{25,17},{2,10},{10... | collective-permute-start | bytes 2654216 | tf_op jit(solution)/shard_map/ppermute | solution.py:170
  113.9 21.3 %collective-permute-start.3 = (bf16[96,2,2304]{2,0,1:T(8,128)(2,1)S(1)}, bf16[96,2,2304]{2,0,1:T(8,128)(2,1)S(1)}, u32[]{:S(2)}, u32[]{:S(2)}) collective-permute-start(bf16[96,2,2304]{2,0,1:T(8,128)(2,1)S(1)} %copy-done.6), channel_id=1, source_target_pairs={{0,16},{8,24},{16,0},{24,8},{1,17},{9,25},{17,1},{25,9},{2,18},{10... | collective-permute-start | bytes 2654216 | tf_op jit(solution)/shard_map/ppermute | solution.py:170
  135.3 0.9 copy-start.7
  154.0 22.9 %collective-permute-start.6 = (bf16[96,2,2304]{2,0,1:T(8,128)(2,1)}, bf16[96,2,2304]{2,0,1:T(8,128)(2,1)}, u32[]{:S(2)}, u32[]{:S(2)}) collective-permute-start(bf16[96,2,2304]{2,0,1:T(8,128)(2,1)} %collective-permute-done.2), channel_id=1, source_target_pairs={{0,16},{8,24},{16,0},{24,8},{1,17},{9,25},{17,1},{25,9},{2,18},{10... | collective-permute-start | bytes 2654216 | tf_op jit(solution)/shard_map/ppermute | solution.py:170
  166.0 45.0 %collective-permute-start.4 = (bf16[96,2,2304]{2,0,1:T(8,128)(2,1)}, bf16[96,2,2304]{2,0,1:T(8,128)(2,1)}, u32[]{:S(2)}, u32[]{:S(2)}) collective-permute-start(bf16[96,2,2304]{2,0,1:T(8,128)(2,1)} %get-tuple-element.22), channel_id=1, source_target_pairs={{0,8},{8,0},{16,24},{24,16},{1,9},{9,1},{17,25},{25,17},{2,10},{10... | collective-permute-start | bytes 2654216 | tf_op jit(solution)/shard_map/ppermute | solution.py:170
  166.5 53.9 %collective-permute-start.5 = (bf16[96,2,2304]{2,0,1:T(8,128)(2,1)}, bf16[96,2,2304]{2,0,1:T(8,128)(2,1)}, u32[]{:S(2)}, u32[]{:S(2)}) collective-permute-start(bf16[96,2,2304]{2,0,1:T(8,128)(2,1)} %get-tuple-element.21), channel_id=1, source_target_pairs={{0,16},{8,24},{16,0},{24,8},{1,17},{9,25},{17,1},{25,9},{2,18},{10... | collective-permute-start | bytes 2654216 | tf_op jit(solution)/shard_map/ppermute | solution.py:170
  190.8 10.3 %copy-start.2 = (f32[2,96,2,1440]{3,1,0,2:T(8,128)S(1)}, f32[2,96,2,1440]{3,1,0,2:T(8,128)}, u32[]{:S(2)}) copy-start(f32[2,96,2,1440]{3,1,0,2:T(8,128)} %convolution_bitcast_fusion.1) | copy-start | bytes 6635524
  199.7 18.8 %collective-permute-start.7 = (bf16[96,2,2304]{2,0,1:T(8,128)(2,1)}, bf16[96,2,2304]{2,0,1:T(8,128)(2,1)}, u32[]{:S(2)}, u32[]{:S(2)}) collective-permute-start(bf16[96,2,2304]{2,0,1:T(8,128)(2,1)} %fusion.8), channel_id=1, source_target_pairs={{0,24},{8,16},{16,8},{24,0},{1,25},{9,17},{17,9},{25,1},{2,26},{10... | collective-permute-start | bytes 2654216 | tf_op jit(solution)/shard_map/ppermute | solution.py:170
  211.0 7.5 %copy-start.5 = (bf16[256,2,96]{0,2,1:T(8,128)(2,1)S(1)}, bf16[256,2,96]{0,2,1:T(8,128)(2,1)}, u32[]{:S(2)}) copy-start(bf16[256,2,96]{0,2,1:T(8,128)(2,1)} %get-tuple-element.18) | copy-start | bytes 294916
  224.3 29.7 %copy-start.1 = (bf16[512,2304]{1,0:T(8,128)(2,1)S(1)}, bf16[512,2304]{1,0:T(8,128)(2,1)}, u32[]{:S(2)}) copy-start(bf16[512,2304]{1,0:T(8,128)(2,1)} %param.18) | copy-start | bytes 7077892
Sparse Core Ops, SparseCore 0:
  45.4 57.9 all-reduce.1
  224.4 27.7 reduce-scatter.1

commit v12 on v6

--- a/solution.py
+++ b/solution.py
@@ -192,14 +192,14 @@
     live_cache = jnp.where(
         (token_pos < own_length)[:, :, None, None], kv_cache[0], jnp.zeros((), jnp.bfloat16)
     )
-    outgoing = jnp.take(live_cache, source_block, axis=0)
+    outgoing = jnp.take(live_cache, source_block, axis=0, mode="clip")
     received = lax.all_to_all(outgoing, "req", split_axis=0, concat_axis=0, tiled=True)
     request_ids = jnp.arange(finished_total, dtype=jnp.int32)
     arrive_place = request_ids[:, None] * per_owner + page_rank
     own_blocks = block_owner == req_index
     slot_match = own_blocks[None] & (block_slot[None] == block_ids[:, None, None])
     gather_place = jnp.sum(jnp.where(slot_match, arrive_place[None], 0), axis=(1, 2))
-    page_pool = jnp.take(received, gather_place, axis=0)
+    page_pool = jnp.take(received, gather_place, axis=0, mode="clip")
     return (layer_out, page_pool)
 
 

time: 257 us -> 259 us (level)
  waiting for transfers between devices: 90.2 us -> 95.3 us
  other arithmetic: 16.6 us -> 12.6 us
    psum x1, waiting for transfers between devices: 50.8 us -> 55.6 us  [body(): lax.psum(partial_value.astype(jnp.bfloat16), 'head').astype(jnp.float32)]
    select_n x4 -> x0, other arithmetic: 3.6 us -> none  [the longest x2 2.01 us: body(): page_pool = jnp.take(received, gather_place, axis=0)]
    unnamed x28 -> x24, local copies, waits for them, and re-layouts: 14 us -> 15 us
where the time goes in v12:
time: 259 us; the launch traced here: 258 us
  waiting for transfers between devices  95.3 us (37%)
  matrix products  90.2 us (35%)
  local copies, waits for them, and re-layouts  28.5 us (11%)
  starting transfers between devices  16.9 us (7%)
  between operations  14.3 us (6%)
  other arithmetic  12.6 us (5%)
    psum x1, waiting for transfers between devices, body(): lax.psum(partial_value.astype(jnp.bfloat16), 'head').astype(jnp.float32)  55.6 us
    dot_general x3, matrix products, experts_on(): jnp.einsum('ned,egdf->gnef', flat, w_gate_up, preferred_element_type=jnp....  43.1 us
    all_to_all x1, waiting for transfers between devices, body(): lax.all_to_all(outgoing, 'req', split_axis=0, concat_axis=0, tiled=True)  20 us
    ppermute x6, waiting for transfers between devices, partner_move(): return lax.ppermute(block, 'req', [(i, i ^ step) for i in range(req_total)])  19.5 us
    dot_general x2, matrix products, experts_on(): jnp.einsum('nef,efd->ned', hidden, w_down, preferred_element_type=jnp.flo...  18 us
    dot_general x4, matrix products, body(): jnp.einsum('tec,ced->ted', dispatch_bf, part, preferred_element_type=jnp....  17.6 us
    unnamed x24, local copies, waits for them, and re-layouts  15 us
    ppermute x6, starting transfers between devices, partner_move(): return lax.ppermute(block, 'req', [(i, i ^ step) for i in range(req_total)])  7 us
  transfers between devices with their start and end apart: 11, of which 6 were waited for; matrix products, arithmetic and copies ran while one was open for 33% of the time, Pallas kernels for 0%

profile of v12, /device:TPU:0, one launch (start us, length us, event | category | flops | bytes accessed | tf_op | source)
XLA Modules:
  0.0 257.9 jit_solution(9268190976860715263)
XLA Ops:
  7.3 9.9 %copy.52 = bf16[2304,3,512]{0,2,1:T(8,128)(2,1)} copy(bf16[2304,3,512]{2,0,1:T(8,128)(2,1)} %param.15) | data formatting | bytes 14155776 | tf_op args[2]
  17.2 0.3 fusion.19
  17.5 5.2 %fusion.35 = f32[256,3,8,64]{0,3,2,1:T(8,128)S(1)} fusion(bf16[3,8,64,2304]{3,2,1,0:T(8,128)(2,1)} %bitcast.157, bf16[1,256,2304]{2,1,0:T(8,128)(2,1)S(1)} %copy-done.3, f32[2304]{0:T(1024)} %param.14, f32[256]{0:T(256)S(1)} %add_rsqrt_fusion.1), kind=kOutput, calls=%fused_computation.49 | convolution fusion | flops 1814298624 | bytes 9840640 | tf_op jit(solution)/shard_map/dot_general | solution.py:73
  22.8 0.2 multiply_cosine_fusion
  23.0 0.2 subtract_convert_fusion.1
  23.2 3.1 %collective-permute-start.1 = (bf16[256,8,64]{0,2,1:T(8,128)(2,1)S(1)}, bf16[256,8,64]{0,2,1:T(8,128)(2,1)}, u32[]{:S(2)}, u32[]{:S(2)}) collective-permute-start(bf16[256,8,64]{0,2,1:T(8,128)(2,1)S(1)} %pad_maximum_fusion.1), channel_id=1, source_target_pairs={{0,1},{2,3},{4,5},{6,7},{8,9},{10,11},{12,13},{14,15},{16,17},{18,... | collective-permute-start | bytes 786440 | tf_op jit(solution)/shard_map/ppermute | solution.py:13
  26.2 2.0 collective-permute-start
  28.2 0.7 constant_dynamic-slice_fusion.2
  28.9 0.1 copy.53
  29.1 0.1 eq.108
  29.3 0.6 reduce-window.6
  29.9 0.2 slice_reduce_fusion
  30.1 0.2 reduce-window.9
  30.3 0.2 compare_and_fusion
  30.5 1.9 fusion.6
  32.3 1.3 fusion.9
  33.6 2.2 fusion.51
  35.8 1.8 convolution_convert_fusion.1
  37.7 0.2 reduce-scatter.2.cloned.1.call-start
  38.0 0.1 fusion.79
  38.1 0.2 eq.112
  38.3 0.1 copy.54
  38.4 0.7 fusion.113
  39.1 0.7 dynamic-slice_bitcast_fusion
  39.8 0.2 convert_reduce_fusion
  40.1 0.1 fusion.72
  40.2 55.6 %all-reduce.2.cloned.1.call-done = bf16[256,2304]{1,0:T(8,128)(2,1)} async-done(((bf16[256,2304]{1,0:T(8,128)(2,1)}), bf16[256,2304]{1,0:T(8,128)(2,1)}) %all-reduce.2.cloned.1.call-update) | async-done | bytes 1179664 | tf_op jit(solution)/shard_map/psum | solution.py:104
  95.8 1.8 fusion.16
  97.6 0.5 fusion.37
  98.2 1.0 convert_bitcast_fusion.1
  99.2 1.5 collective-permute-start.2
  100.7 1.5 collective-permute-start.3
  102.1 14.2 %convolution_bitcast_fusion.1 = f32[2,96,2,1440]{3,1,0,2:T(8,128)} fusion(bf16[2,2,2304,1440]{2,3,1,0:T(8,128)(2,1)} %param.20, f32[2304,2,96]{0,2,1:T(8,128)S(1)} %bitcast.156), kind=kOutput, calls=%fused_computation.23 | convolution fusion | flops 2548482048 | bytes 30523392 | tf_op jit(solution)/shard_map/ned,egdf->gnef/dot_general | solution.py:132
  116.4 4.7 %collective-permute-done.2 = bf16[96,2,2304]{2,0,1:T(8,128)(2,1)} collective-permute-done((bf16[96,2,2304]{2,0,1:T(8,128)(2,1)}, bf16[96,2,2304]{2,0,1:T(8,128)(2,1)}, u32[]{:S(2)}, u32[]{:S(2)}) %collective-permute-start.2) | collective-permute-done | bytes 884768 | tf_op jit(solution)/shard_map/ppermute | solution.py:127
  121.1 1.2 collective-permute-done.3
  122.3 1.6 pad_maximum_fusion
  123.9 1.3 copy.56
  125.2 14.9 %convolution_bitcast_fusion = f32[2,192,2,1440]{3,1,0,2:T(8,128)} fusion(bf16[192,2,2304,1]{2,0,3,1:T(8,128)(2,1)} %bitcast.159, bf16[2,2,2304,1440]{2,3,1,0:T(8,128)(2,1)} %param.20), kind=kOutput, calls=%fused_computation.14 | convolution fusion | flops 5096079360 | bytes 32735232 | tf_op jit(solution)/shard_map/ned,egdf->gnef/dot_general | solution.py:132
  140.1 1.5 collective-permute-start.6
  141.6 9.1 %fusion.5 = bf16[192,2,2304]{2,0,1:T(8,128)(2,1)S(1)} fusion(bf16[2,1440,2304]{2,1,0:T(8,128)(2,1)} %param.21, f32[2,192,2,1440]{3,1,0,2:T(8,128)} %convolution_bitcast_fusion), kind=kOutput, calls=%fused_computation.12 | convolution fusion | flops 2552242176 | bytes 19464192 | tf_op jit(solution)/shard_map/nef,efd->ned/dot_general | solution.py:134
  150.8 1.3 fusion.94
  152.1 0.6 collective-permute-start.4
  152.6 0.6 collective-permute-start.5
  153.2 9.9 %collective-permute-done.6 = bf16[96,2,2304]{2,0,1:T(8,128)(2,1)} collective-permute-done((bf16[96,2,2304]{2,0,1:T(8,128)(2,1)}, bf16[96,2,2304]{2,0,1:T(8,128)(2,1)}, u32[]{:S(2)}, u32[]{:S(2)}) %collective-permute-start.6) | collective-permute-done | bytes 884768 | tf_op jit(solution)/shard_map/ppermute | solution.py:127
  163.1 13.9 %fusion.11 = f32[2,96,2,1440]{3,1,2,0:T(8,128)} fusion(bf16[2,2,2304,1440]{2,3,1,0:T(8,128)(2,1)} %param.20, bf16[96,2,2304]{2,0,1:T(8,128)(2,1)} %collective-permute-done.6), kind=kOutput, calls=%fused_computation.22 | convolution fusion | flops 2548039680 | bytes 29638656 | tf_op jit(solution)/shard_map/ned,egdf->gnef/dot_general | solution.py:132
  176.9 8.9 %fusion.8 = bf16[96,2,2304]{2,0,1:T(8,128)(2,1)} fusion(bf16[2,1440,2304]{2,1,0:T(8,128)(2,1)} %param.21, f32[2,96,2,1440]{3,1,2,0:T(8,128)} %fusion.11), kind=kOutput, calls=%fused_computation.19 | convolution fusion | flops 1276121088 | bytes 16367616 | tf_op jit(solution)/shard_map/nef,efd->ned/dot_general | solution.py:134
  185.8 1.5 collective-permute-start.7
  187.3 9.8 %fusion.29 = f32[2,2304,256]{2,1,0:T(8,128)} fusion(bf16[256,2,96]{0,2,1:T(8,128)(2,1)} %copy-done.5, bf16[2,1440,2304]{2,1,0:T(8,128)(2,1)} %param.21, f32[2,96,2,1440]{3,1,0,2:T(8,128)S(1)} %copy-done.2), kind=kOutput, calls=%fused_computation.45 | convolution fusion | flops 1502613504 | bytes 20299776 | tf_op jit(solution)/shard_map/tec,ced->ted/dot_general | solution.py:156
  197.1 3.5 %convolution_add_fusion.1 = f32[2,2304,256]{2,1,0:T(8,128)S(1)} fusion(f32[2,2304,256]{2,1,0:T(8,128)} %fusion.29, bf16[96,2,2304]{2,0,1:T(8,128)(2,1)} %collective-permute-done.4, bf16[256,2,96]{0,2,1:T(8,128)(2,1)} %copy-done.5), kind=kOutput, calls=%fused_computation.6 | convolution fusion | flops 227672064 | bytes 10420224 | tf_op jit(solution)/shard_map/tec,ced->ted/dot_general | solution.py:156
  200.6 3.8 %collective-permute-done.7 = bf16[96,2,2304]{2,0,1:T(8,128)(2,1)} collective-permute-done((bf16[96,2,2304]{2,0,1:T(8,128)(2,1)}, bf16[96,2,2304]{2,0,1:T(8,128)(2,1)}, u32[]{:S(2)}, u32[]{:S(2)}) %collective-permute-start.7) | collective-permute-done | bytes 884768 | tf_op jit(solution)/shard_map/ppermute | solution.py:127
  204.4 2.0 fusion.95
  206.4 2.3 fusion.28
  208.7 1.5 copy.59
  210.3 0.6 dynamic_slice.25
  210.9 0.1 select_reduce_fusion.2
  211.0 0.7 add_compare_fusion
  211.7 1.9 bitcast_select_fusion
  213.6 2.0 gather_fusion
  215.6 4.6 %all-to-all-start = ((bf16[16,64,2,512]{3,1,2,0:T(8,128)(2,1)}), bf16[16,64,2,512]{3,1,2,0:T(8,128)(2,1)}, u32[]{:S(2)}, u32[]{:S(2)}) async-start(bf16[16,64,2,512]{3,1,2,0:T(8,128)(2,1)} %gather_fusion), calls=%async_computation.1 | async-start | bytes 4194304 | tf_op jit(solution)/shard_map/all_to_all | solution.py:196
  220.3 0.1 select_reduce_fusion.1
  220.4 20.0 %all-to-all-done = bf16[16,64,2,512]{3,1,2,0:T(8,128)(2,1)} async-done(((bf16[16,64,2,512]{3,1,2,0:T(8,128)(2,1)}), bf16[16,64,2,512]{3,1,2,0:T(8,128)(2,1)}, u32[]{:S(2)}, u32[]{:S(2)}) %all-to-all-start) | async-done | bytes 2097184 | tf_op jit(solution)/shard_map/all_to_all | solution.py:196
  240.5 3.7 %gather_fusion.1 = bf16[16,64,2,512]{3,1,2,0:T(8,128)(2,1)} fusion(bf16[16,64,2,512]{3,1,2,0:T(8,128)(2,1)} %all-to-all-done, s32[1024]{0:T(1024)S(1)} %pad_clamp_fusion), kind=kCustom, calls=%fused_computation.1 | custom fusion | bytes 4194368 | tf_op jit(solution)/shard_map/jit(_take)/gather | solution.py:202
  244.2 5.1 %copy.61 = bf16[16,64,2,512]{3,2,1,0:T(2,128)(2,1)} copy(bf16[16,64,2,512]{3,1,2,0:T(8,128)(2,1)} %gather_fusion.1) | data formatting | bytes 4194304
  249.3 1.7 fusion.73
  (56 shorter events, 0.7 us)
Async XLA Ops:
  7.2 28.6 %copy-start = (bf16[512,2304]{1,0:T(8,128)(2,1)S(1)}, bf16[512,2304]{1,0:T(8,128)(2,1)}, u32[]{:S(2)}) copy-start(bf16[512,2304]{1,0:T(8,128)(2,1)} %param.16) | copy-start | bytes 7077892
  7.2 88.7 %all-reduce.2.cloned.1.call-start = ((), (), s32[]{:S(2)}) async-start(), calls=%async_computation.2 | async-start | bytes 2359296 | tf_op jit(solution)/shard_map/psum | solution.py:104
  7.3 9.9 %copy-start.3 = (bf16[1,256,2304]{2,1,0:T(8,128)(2,1)S(1)}, bf16[1,256,2304]{2,1,0:T(8,128)(2,1)}, u32[]{:S(2)}) copy-start(bf16[1,256,2304]{2,1,0:T(8,128)(2,1)} %param.13) | copy-start | bytes 3538948
  23.2 7.3 %collective-permute-start.1 = (bf16[256,8,64]{0,2,1:T(8,128)(2,1)S(1)}, bf16[256,8,64]{0,2,1:T(8,128)(2,1)}, u32[]{:S(2)}, u32[]{:S(2)}) collective-permute-start(bf16[256,8,64]{0,2,1:T(8,128)(2,1)S(1)} %pad_maximum_fusion.1), channel_id=1, source_target_pairs={{0,1},{2,3},{4,5},{6,7},{8,9},{10,11},{12,13},{14,15},{16,17},{18,... | collective-permute-start | bytes 786440 | tf_op jit(solution)/shard_map/ppermute | solution.py:13
  26.2 7.4 %collective-permute-start = (bf16[256,8,64]{0,2,1:T(8,128)(2,1)S(1)}, bf16[256,8,64]{0,2,1:T(8,128)(2,1)}, u32[]{:S(2)}, u32[]{:S(2)}) collective-permute-start(bf16[256,8,64]{0,2,1:T(8,128)(2,1)S(1)} %fusion.74), channel_id=1, source_target_pairs={{0,1},{2,3},{4,5},{6,7},{8,9},{10,11},{12,13},{14,15},{16,17},{18,... | collective-permute-start | bytes 786440 | tf_op jit(solution)/shard_map/ppermute | solution.py:13
  35.8 4.0 %copy-start.7 = (s32[4,16]{1,0:T(4,128)S(1)}, s32[4,16]{1,0:T(4,128)}, u32[]{:S(2)}) copy-start(s32[4,16]{1,0:T(4,128)} %param.24) | copy-start | bytes 772
  37.6 58.2 %copy-start.4 = (bf16[1,256,2304]{2,1,0:T(8,128)(2,1)S(1)}, bf16[1,256,2304]{2,1,0:T(8,128)(2,1)}, u32[]{:S(2)}) copy-start(bf16[1,256,2304]{2,1,0:T(8,128)(2,1)} %param.13) | copy-start | bytes 3538948
  37.7 60.0 %copy-start.8 = (f32[2304]{0:T(1024)S(1)}, f32[2304]{0:T(1024)}, u32[]{:S(2)}) copy-start(f32[2304]{0:T(1024)} %param.17) | copy-start | bytes 27652
  37.7 211.6 %reduce-scatter.2.cloned.1.call-start = ((), (), s32[]{:S(2)}) async-start(), calls=%async_computation.3 | async-start | bytes 1474560 | tf_op jit(solution)/shard_map/reduce_scatter | solution.py:160
  40.2 58.0 %copy-start.5 = (bf16[256,2,96]{0,2,1:T(8,128)(2,1)}, bf16[256,2,96]{0,2,1:T(8,128)(2,1)S(1)}, u32[]{:S(2)}) copy-start(bf16[256,2,96]{0,2,1:T(8,128)(2,1)S(1)} %get-tuple-element.11) | copy-start | bytes 294916
  99.2 21.9 %collective-permute-start.2 = (bf16[96,2,2304]{2,0,1:T(8,128)(2,1)}, bf16[96,2,2304]{2,0,1:T(8,128)(2,1)}, u32[]{:S(2)}, u32[]{:S(2)}) collective-permute-start(bf16[96,2,2304]{2,0,1:T(8,128)(2,1)} %convert_bitcast_fusion.1), channel_id=1, source_target_pairs={{0,8},{8,0},{16,24},{24,16},{1,9},{9,1},{17,25},{25,17},{2,10},{10... | collective-permute-start | bytes 2654216 | tf_op jit(solution)/shard_map/ppermute | solution.py:127
  100.7 21.6 %collective-permute-start.3 = (bf16[96,2,2304]{2,0,1:T(8,128)(2,1)}, bf16[96,2,2304]{2,0,1:T(8,128)(2,1)}, u32[]{:S(2)}, u32[]{:S(2)}) collective-permute-start(bf16[96,2,2304]{2,0,1:T(8,128)(2,1)} %convert_bitcast_fusion.1), channel_id=1, source_target_pairs={{0,16},{8,24},{16,0},{24,8},{1,17},{9,25},{17,1},{25,9},{2,18},{10... | collective-permute-start | bytes 2654216 | tf_op jit(solution)/shard_map/ppermute | solution.py:127
  140.1 22.9 %collective-permute-start.6 = (bf16[96,2,2304]{2,0,1:T(8,128)(2,1)}, bf16[96,2,2304]{2,0,1:T(8,128)(2,1)}, u32[]{:S(2)}, u32[]{:S(2)}) collective-permute-start(bf16[96,2,2304]{2,0,1:T(8,128)(2,1)} %collective-permute-done.2), channel_id=1, source_target_pairs={{0,16},{8,24},{16,0},{24,8},{1,17},{9,25},{17,1},{25,9},{2,18},{10... | collective-permute-start | bytes 2654216 | tf_op jit(solution)/shard_map/ppermute | solution.py:127
  152.1 45.0 %collective-permute-start.4 = (bf16[96,2,2304]{2,0,1:T(8,128)(2,1)}, bf16[96,2,2304]{2,0,1:T(8,128)(2,1)}, u32[]{:S(2)}, u32[]{:S(2)}) collective-permute-start(bf16[96,2,2304]{2,0,1:T(8,128)(2,1)} %get-tuple-element.15), channel_id=1, source_target_pairs={{0,8},{8,0},{16,24},{24,16},{1,9},{9,1},{17,25},{25,17},{2,10},{10... | collective-permute-start | bytes 2654216 | tf_op jit(solution)/shard_map/ppermute | solution.py:127
  152.6 53.7 %collective-permute-start.5 = (bf16[96,2,2304]{2,0,1:T(8,128)(2,1)}, bf16[96,2,2304]{2,0,1:T(8,128)(2,1)}, u32[]{:S(2)}, u32[]{:S(2)}) collective-permute-start(bf16[96,2,2304]{2,0,1:T(8,128)(2,1)} %get-tuple-element.14), channel_id=1, source_target_pairs={{0,16},{8,24},{16,0},{24,8},{1,17},{9,25},{17,1},{25,9},{2,18},{10... | collective-permute-start | bytes 2654216 | tf_op jit(solution)/shard_map/ppermute | solution.py:127
  176.9 10.3 %copy-start.2 = (f32[2,96,2,1440]{3,1,0,2:T(8,128)S(1)}, f32[2,96,2,1440]{3,1,0,2:T(8,128)}, u32[]{:S(2)}) copy-start(f32[2,96,2,1440]{3,1,0,2:T(8,128)} %convolution_bitcast_fusion.1) | copy-start | bytes 6635524
  185.8 18.6 %collective-permute-start.7 = (bf16[96,2,2304]{2,0,1:T(8,128)(2,1)}, bf16[96,2,2304]{2,0,1:T(8,128)(2,1)}, u32[]{:S(2)}, u32[]{:S(2)}) collective-permute-start(bf16[96,2,2304]{2,0,1:T(8,128)(2,1)} %fusion.8), channel_id=1, source_target_pairs={{0,24},{8,16},{16,8},{24,0},{1,25},{9,17},{17,9},{25,1},{2,26},{10... | collective-permute-start | bytes 2654216 | tf_op jit(solution)/shard_map/ppermute | solution.py:127
  197.1 7.3 %copy-start.6 = (bf16[256,2,96]{0,2,1:T(8,128)(2,1)S(1)}, bf16[256,2,96]{0,2,1:T(8,128)(2,1)}, u32[]{:S(2)}) copy-start(bf16[256,2,96]{0,2,1:T(8,128)(2,1)} %copy-done.5) | copy-start | bytes 294916
  208.7 1.6 copy-start.10
  215.6 4.7 %copy-start.9 = (s32[4,16]{1,0:T(4,128)S(1)}, s32[4,16]{1,0:T(4,128)}, u32[]{:S(2)}) copy-start(s32[4,16]{1,0:T(4,128)} %param.25) | copy-start | bytes 772
  215.6 24.8 %all-to-all-start = ((bf16[16,64,2,512]{3,1,2,0:T(8,128)(2,1)}), bf16[16,64,2,512]{3,1,2,0:T(8,128)(2,1)}, u32[]{:S(2)}, u32[]{:S(2)}) async-start(bf16[16,64,2,512]{3,1,2,0:T(8,128)(2,1)} %gather_fusion), calls=%async_computation.1 | async-start | bytes 4194304 | tf_op jit(solution)/shard_map/all_to_all | solution.py:196
  240.5 10.5 %copy-start.1 = (bf16[512,2304]{1,0:T(8,128)(2,1)S(1)}, bf16[512,2304]{1,0:T(8,128)(2,1)}, u32[]{:S(2)}) copy-start(bf16[512,2304]{1,0:T(8,128)(2,1)} %param.16) | copy-start | bytes 7077892
Sparse Core Ops, SparseCore 0:
  37.8 58.0 all-reduce.1
  210.4 27.7 reduce-scatter.1

commit v13 on v11

--- a/solution.py
+++ b/solution.py
@@ -47,7 +47,7 @@
     return (dispatch, combine)
 
 
-def hand_over_pages(kv_cache, lengths, block_owner, block_slot):
+def pages_out(kv_cache, lengths, block_owner, block_slot):
     dev_index = lax.axis_index("dev")
     req_index = lax.axis_index("req")
     owners_total = lax.axis_size("req")
@@ -75,14 +75,26 @@
     live_cache = jnp.where(
         (token_pos < own_length)[:, :, None, None], kv_cache[0], jnp.zeros((), jnp.bfloat16)
     )
-    outgoing = jnp.take(live_cache, source_block, axis=0)
+    outgoing = jnp.take(live_cache, source_block, axis=0, mode="clip")
+    return outgoing
+
+
+def pages_in(outgoing, block_owner, block_slot):
+    req_index = lax.axis_index("req")
+    block_total = block_owner.shape[1]
+    finished_total = block_owner.shape[0]
+    per_owner = block_total // lax.axis_size("req")
+    block_ids = jnp.arange(block_total, dtype=jnp.int32)
+    same_owner = block_owner[:, :, None] == block_owner[:, None, :]
+    before_mask = block_ids[None, :] < block_ids[:, None]
+    page_rank = jnp.sum((same_owner & before_mask[None]).astype(jnp.int32), axis=2)
     received = lax.all_to_all(outgoing, "req", split_axis=0, concat_axis=0, tiled=True)
     request_ids = jnp.arange(finished_total, dtype=jnp.int32)
     arrive_place = request_ids[:, None] * per_owner + page_rank
     own_blocks = block_owner == req_index
     slot_match = own_blocks[None] & (block_slot[None] == block_ids[:, None, None])
     gather_place = jnp.sum(jnp.where(slot_match, arrive_place[None], 0), axis=(1, 2))
-    page_pool = jnp.take(received, gather_place, axis=0)
+    page_pool = jnp.take(received, gather_place, axis=0, mode="clip")
     return page_pool
 
 
@@ -140,12 +152,11 @@
     )
     attended = attended.astype(jnp.bfloat16).reshape(half_rows, local_cols)
     partial_value = jnp.dot(attended, w_out, preferred_element_type=jnp.float32)
-    reduced_in = partial_value.astype(jnp.bfloat16)
-    attn_mixed = lax.psum(reduced_in, "head").astype(jnp.float32)
-    kv_cache, reduced_in = lax.optimization_barrier((kv_cache, reduced_in))
-    page_pool = hand_over_pages(kv_cache, lengths, block_owner, block_slot)
+    attn_mixed = lax.psum(partial_value.astype(jnp.bfloat16), "head").astype(jnp.float32)
     residual = (tokens[0].astype(jnp.float32) + attn_mixed).astype(jnp.bfloat16)
     moe_in = norm_rows(residual, moe_gain)
+    outgoing = pages_out(kv_cache, lengths, block_owner, block_slot)
+    moe_in, outgoing = lax.optimization_barrier((moe_in, outgoing))
     experts_here = w_gate_up.shape[0]
     first_expert = head_index * experts_here
     top_count = routes.shape[2]
@@ -163,7 +174,6 @@
         moe_in,
         preferred_element_type=jnp.float32,
     ).astype(jnp.bfloat16)
-    picked_own, page_pool = lax.optimization_barrier((picked_own, page_pool))
     req_total = lax.axis_size("req")
 
     def partner_move(block, step):
@@ -210,6 +220,7 @@
         .astype(jnp.bfloat16)
         .reshape(1, 1, rows_out, model_width)
     )
+    page_pool = pages_in(outgoing, block_owner, block_slot)
     return (layer_out, page_pool)
 
 

time: 262 us -> 256 us (0.977)
  other arithmetic: 23.5 us -> 14.6 us
  waiting for transfers between devices: 87.6 us -> 90.4 us
    reduce_scatter x1, waiting for transfers between devices: 22.7 us -> 0.01 us  [body(): lax.psum_scatter(moe_out.astype(jnp.bfloat16), 'head', scatter_dimension=...]
    all_to_all x1, waiting for transfers between devices: 0.01 us -> 20 us  [pages_in(): lax.all_to_all(outgoing, 'req', split_axis=0, concat_axis=0, tiled=True)]
    select_n x5 -> x1, other arithmetic: 8.18 us -> 1.93 us  [pages_out(): jnp.where((token_pos < own_length)[:, :, None, None], kv_cache[0], jnp.ze...]
    psum x1, waiting for transfers between devices: 45.5 us -> 50.8 us  [body(): lax.psum(partial_value.astype(jnp.bfloat16), 'head').astype(jnp.float32)]
    unnamed x34 -> x22, local copies, waits for them, and re-layouts: 16.7 us -> 15 us
  transfers between devices with their start and end apart: 11 -> 11, of which waited for: 6 -> 6; matrix products, arithmetic and copies ran while one was open for 35% -> 34% of each run, Pallas kernels for 0% -> 0%
where the time goes in v13:
time: 256 us; the launch traced here: 255 us
  waiting for transfers between devices  90.4 us (35%)
  matrix products  90.2 us (35%)
  local copies, waits for them, and re-layouts  28.6 us (11%)
  starting transfers between devices  16.8 us (7%)
  other arithmetic  14.6 us (6%)
  between operations  14.3 us (6%)
    psum x1, waiting for transfers between devices, body(): lax.psum(partial_value.astype(jnp.bfloat16), 'head').astype(jnp.float32)  50.8 us
    dot_general x3, matrix products, experts_on(): jnp.einsum('ned,egdf->gnef', flat, w_gate_up, preferred_element_type=jnp....  43 us
    all_to_all x1, waiting for transfers between devices, pages_in(): lax.all_to_all(outgoing, 'req', split_axis=0, concat_axis=0, tiled=True)  20 us
    ppermute x6, waiting for transfers between devices, partner_move(): return lax.ppermute(block, 'req', [(i, i ^ step) for i in range(req_total)])  19.5 us
    dot_general x2, matrix products, experts_on(): jnp.einsum('nef,efd->ned', hidden, w_down, preferred_element_type=jnp.flo...  18.1 us
    dot_general x4, matrix products, body(): jnp.einsum('tec,ced->ted', dispatch_bf, part, preferred_element_type=jnp....  17.6 us
    unnamed x22, local copies, waits for them, and re-layouts  15 us
    ppermute x6, starting transfers between devices, partner_move(): return lax.ppermute(block, 'req', [(i, i ^ step) for i in range(req_total)])  7 us
  transfers between devices with their start and end apart: 11, of which 6 were waited for; matrix products, arithmetic and copies ran while one was open for 34% of the time, Pallas kernels for 0%

profile of v13, /device:TPU:0, one launch (start us, length us, event | category | flops | bytes accessed | tf_op | source)
XLA Modules:
  0.0 254.9 jit_solution(18271362010034193198)
XLA Ops:
  7.3 9.9 %copy.52 = bf16[2304,3,512]{0,2,1:T(8,128)(2,1)} copy(bf16[2304,3,512]{2,0,1:T(8,128)(2,1)} %param.15) | data formatting | bytes 14155776 | tf_op args[2]
  17.2 0.3 fusion.19
  17.5 5.2 %fusion.35 = f32[256,3,8,64]{0,3,2,1:T(8,128)S(1)} fusion(bf16[3,8,64,2304]{3,2,1,0:T(8,128)(2,1)} %bitcast.158, bf16[1,256,2304]{2,1,0:T(8,128)(2,1)S(1)} %copy-done.3, f32[2304]{0:T(1024)} %param.14, f32[256]{0:T(256)S(1)} %add_rsqrt_fusion.1), kind=kOutput, calls=%fused_computation.49 | convolution fusion | flops 1814298624 | bytes 9840640 | tf_op jit(solution)/shard_map/dot_general | solution.py:124
  22.8 0.2 multiply_cosine_fusion
  23.0 0.2 subtract_convert_fusion.1
  23.2 3.1 %collective-permute-start.1 = (bf16[256,8,64]{0,2,1:T(8,128)(2,1)S(1)}, bf16[256,8,64]{0,2,1:T(8,128)(2,1)}, u32[]{:S(2)}, u32[]{:S(2)}) collective-permute-start(bf16[256,8,64]{0,2,1:T(8,128)(2,1)S(1)} %pad_maximum_fusion.1), channel_id=1, source_target_pairs={{0,1},{2,3},{4,5},{6,7},{8,9},{10,11},{12,13},{14,15},{16,17},{18,... | collective-permute-start | bytes 786440 | tf_op jit(solution)/shard_map/ppermute | solution.py:13
  26.3 2.0 collective-permute-start
  28.3 0.6 iota_add_fusion.1
  28.8 0.7 constant_dynamic-slice_fusion.2
  29.5 0.1 copy.53
  29.7 0.1 eq.115
  29.9 0.6 reduce-window.6
  30.5 0.2 slice_reduce_fusion
  30.7 0.2 convert_reduce_fusion
  30.9 0.1 select_reduce_fusion.2
  31.1 0.2 reduce-window.9
  31.4 0.8 compare_and_fusion
  32.3 1.9 fusion.6
  34.1 1.3 fusion.9
  35.4 2.2 fusion.47
  37.6 1.9 convolution_convert_fusion.1
  39.5 0.2 reduce-scatter.2.cloned.1.call-start
  39.8 0.6 dynamic_slice.25
  40.3 0.2 eq.119
  40.6 0.1 copy.54
  40.7 0.7 add_compare_fusion
  41.4 1.9 bitcast_select_fusion
  43.3 2.0 gather_fusion
  45.3 0.7 fusion.111
  46.0 0.7 dynamic-slice_bitcast_fusion
  46.9 50.8 %all-reduce.2.cloned.1.call-done = bf16[256,2304]{1,0:T(8,128)(2,1)} async-done(((bf16[256,2304]{1,0:T(8,128)(2,1)}), bf16[256,2304]{1,0:T(8,128)(2,1)}) %all-reduce.2.cloned.1.call-update) | async-done | bytes 1179664 | tf_op jit(solution)/shard_map/psum | solution.py:155
  97.7 2.1 fusion.16
  99.8 0.3 fusion.18
  100.2 0.4 fusion.92
  100.6 1.0 convert_bitcast_fusion.1
  101.6 1.5 collective-permute-start.2
  103.1 1.5 collective-permute-start.3
  104.6 14.2 %convolution_bitcast_fusion.1 = f32[2,96,2,1440]{3,1,0,2:T(8,128)} fusion(bf16[2,2,2304,1440]{2,3,1,0:T(8,128)(2,1)} %param.20, f32[2304,2,96]{0,2,1:T(8,128)S(1)} %bitcast.157), kind=kOutput, calls=%fused_computation.23 | convolution fusion | flops 2548482048 | bytes 30523392 | tf_op jit(solution)/shard_map/ned,egdf->gnef/dot_general | solution.py:185
  118.8 4.7 %collective-permute-done.2 = bf16[96,2,2304]{2,0,1:T(8,128)(2,1)} collective-permute-done((bf16[96,2,2304]{2,0,1:T(8,128)(2,1)}, bf16[96,2,2304]{2,0,1:T(8,128)(2,1)}, u32[]{:S(2)}, u32[]{:S(2)}) %collective-permute-start.2) | collective-permute-done | bytes 884768 | tf_op jit(solution)/shard_map/ppermute | solution.py:180
  123.5 1.2 collective-permute-done.3
  124.7 1.6 pad_maximum_fusion
  126.3 1.4 copy.57
  127.7 14.8 %convolution_bitcast_fusion = f32[2,192,2,1440]{3,1,0,2:T(8,128)} fusion(bf16[192,2,2304,1]{2,0,3,1:T(8,128)(2,1)} %bitcast.160, bf16[2,2,2304,1440]{2,3,1,0:T(8,128)(2,1)} %param.20), kind=kOutput, calls=%fused_computation.14 | convolution fusion | flops 5096079360 | bytes 32735232 | tf_op jit(solution)/shard_map/ned,egdf->gnef/dot_general | solution.py:185
  142.6 1.5 collective-permute-start.6
  144.0 9.1 %fusion.5 = bf16[192,2,2304]{2,0,1:T(8,128)(2,1)S(1)} fusion(bf16[2,1440,2304]{2,1,0:T(8,128)(2,1)} %param.21, f32[2,192,2,1440]{3,1,0,2:T(8,128)} %convolution_bitcast_fusion), kind=kOutput, calls=%fused_computation.12 | convolution fusion | flops 2552242176 | bytes 19464192 | tf_op jit(solution)/shard_map/nef,efd->ned/dot_general | solution.py:187
  153.2 1.3 fusion.90
  154.5 0.6 collective-permute-start.4
  155.1 0.5 collective-permute-start.5
  155.6 9.9 %collective-permute-done.6 = bf16[96,2,2304]{2,0,1:T(8,128)(2,1)} collective-permute-done((bf16[96,2,2304]{2,0,1:T(8,128)(2,1)}, bf16[96,2,2304]{2,0,1:T(8,128)(2,1)}, u32[]{:S(2)}, u32[]{:S(2)}) %collective-permute-start.6) | collective-permute-done | bytes 884768 | tf_op jit(solution)/shard_map/ppermute | solution.py:180
  165.5 13.9 %fusion.11 = f32[2,96,2,1440]{3,1,2,0:T(8,128)} fusion(bf16[2,2,2304,1440]{2,3,1,0:T(8,128)(2,1)} %param.20, bf16[96,2,2304]{2,0,1:T(8,128)(2,1)} %collective-permute-done.6), kind=kOutput, calls=%fused_computation.22 | convolution fusion | flops 2548039680 | bytes 29638656 | tf_op jit(solution)/shard_map/ned,egdf->gnef/dot_general | solution.py:185
  179.4 9.0 %fusion.8 = bf16[96,2,2304]{2,0,1:T(8,128)(2,1)} fusion(bf16[2,1440,2304]{2,1,0:T(8,128)(2,1)} %param.21, f32[2,96,2,1440]{3,1,2,0:T(8,128)} %fusion.11), kind=kOutput, calls=%fused_computation.19 | convolution fusion | flops 1276121088 | bytes 16367616 | tf_op jit(solution)/shard_map/nef,efd->ned/dot_general | solution.py:187
  188.3 1.5 collective-permute-start.7
  189.8 9.8 %fusion.29 = f32[2,2304,256]{2,1,0:T(8,128)} fusion(bf16[256,2,96]{0,2,1:T(8,128)(2,1)} %copy-done.4, bf16[2,1440,2304]{2,1,0:T(8,128)(2,1)} %param.21, f32[2,96,2,1440]{3,1,0,2:T(8,128)S(1)} %copy-done.2), kind=kOutput, calls=%fused_computation.45 | convolution fusion | flops 1502613504 | bytes 20299776 | tf_op jit(solution)/shard_map/tec,ced->ted/dot_general | solution.py:209
  199.6 3.5 %convolution_add_fusion.1 = f32[2,2304,256]{2,1,0:T(8,128)S(1)} fusion(f32[2,2304,256]{2,1,0:T(8,128)} %fusion.29, bf16[96,2,2304]{2,0,1:T(8,128)(2,1)} %collective-permute-done.4, bf16[256,2,96]{0,2,1:T(8,128)(2,1)} %copy-done.4), kind=kOutput, calls=%fused_computation.6 | convolution fusion | flops 227672064 | bytes 10420224 | tf_op jit(solution)/shard_map/tec,ced->ted/dot_general | solution.py:209
  203.1 3.8 %collective-permute-done.7 = bf16[96,2,2304]{2,0,1:T(8,128)(2,1)} collective-permute-done((bf16[96,2,2304]{2,0,1:T(8,128)(2,1)}, bf16[96,2,2304]{2,0,1:T(8,128)(2,1)}, u32[]{:S(2)}, u32[]{:S(2)}) %collective-permute-start.7) | collective-permute-done | bytes 884768 | tf_op jit(solution)/shard_map/ppermute | solution.py:180
  206.9 2.0 fusion.91
  208.9 2.3 fusion.28
  211.2 1.5 copy.60
  212.8 4.5 %all-to-all-start = ((bf16[16,64,2,512]{3,1,2,0:T(8,128)(2,1)}), bf16[16,64,2,512]{3,1,2,0:T(8,128)(2,1)}, u32[]{:S(2)}, u32[]{:S(2)}) async-start(bf16[16,64,2,512]{3,1,2,0:T(8,128)(2,1)} %gather_fusion), calls=%async_computation.1 | async-start | bytes 4194304 | tf_op jit(solution)/shard_map/all_to_all | solution.py:91
  217.3 0.1 select_reduce_fusion.1
  217.5 20.0 %all-to-all-done = bf16[16,64,2,512]{3,1,2,0:T(8,128)(2,1)} async-done(((bf16[16,64,2,512]{3,1,2,0:T(8,128)(2,1)}), bf16[16,64,2,512]{3,1,2,0:T(8,128)(2,1)}, u32[]{:S(2)}, u32[]{:S(2)}) %all-to-all-start) | async-done | bytes 2097184 | tf_op jit(solution)/shard_map/all_to_all | solution.py:91
  237.5 3.7 %gather_fusion.1 = bf16[16,64,2,512]{3,1,2,0:T(8,128)(2,1)} fusion(bf16[16,64,2,512]{3,1,2,0:T(8,128)(2,1)} %all-to-all-done, s32[1024]{0:T(1024)S(1)} %pad_clamp_fusion), kind=kCustom, calls=%fused_computation.1 | custom fusion | bytes 4194368 | tf_op jit(solution)/shard_map/jit(_take)/gather | solution.py:97
  241.2 5.1 %copy.61 = bf16[16,64,2,512]{3,2,1,0:T(2,128)(2,1)} copy(bf16[16,64,2,512]{3,1,2,0:T(8,128)(2,1)} %gather_fusion.1) | data formatting | bytes 4194304
  246.3 1.7 fusion.69
  (55 shorter events, 0.9 us)
Async XLA Ops:
  7.2 30.4 %copy-start = (bf16[512,2304]{1,0:T(8,128)(2,1)S(1)}, bf16[512,2304]{1,0:T(8,128)(2,1)}, u32[]{:S(2)}) copy-start(bf16[512,2304]{1,0:T(8,128)(2,1)} %param.16) | copy-start | bytes 7077892
  7.2 90.5 %all-reduce.2.cloned.1.call-start = ((), (), s32[]{:S(2)}) async-start(), calls=%async_computation.2 | async-start | bytes 2359296 | tf_op jit(solution)/shard_map/psum | solution.py:155
  7.3 9.9 %copy-start.3 = (bf16[1,256,2304]{2,1,0:T(8,128)(2,1)S(1)}, bf16[1,256,2304]{2,1,0:T(8,128)(2,1)}, u32[]{:S(2)}) copy-start(bf16[1,256,2304]{2,1,0:T(8,128)(2,1)} %param.13) | copy-start | bytes 3538948
  22.7 8.0 %copy-start.6 = (s32[4,16]{1,0:T(4,128)S(1)}, s32[4,16]{1,0:T(4,128)}, u32[]{:S(2)}) copy-start(s32[4,16]{1,0:T(4,128)} %param.24) | copy-start | bytes 772
  23.2 9.1 %collective-permute-start.1 = (bf16[256,8,64]{0,2,1:T(8,128)(2,1)S(1)}, bf16[256,8,64]{0,2,1:T(8,128)(2,1)}, u32[]{:S(2)}, u32[]{:S(2)}) collective-permute-start(bf16[256,8,64]{0,2,1:T(8,128)(2,1)S(1)} %pad_maximum_fusion.1), channel_id=1, source_target_pairs={{0,1},{2,3},{4,5},{6,7},{8,9},{10,11},{12,13},{14,15},{16,17},{18,... | collective-permute-start | bytes 786440 | tf_op jit(solution)/shard_map/ppermute | solution.py:13
  26.3 9.2 %collective-permute-start = (bf16[256,8,64]{0,2,1:T(8,128)(2,1)S(1)}, bf16[256,8,64]{0,2,1:T(8,128)(2,1)}, u32[]{:S(2)}, u32[]{:S(2)}) collective-permute-start(bf16[256,8,64]{0,2,1:T(8,128)(2,1)S(1)} %fusion.70), channel_id=1, source_target_pairs={{0,1},{2,3},{4,5},{6,7},{8,9},{10,11},{12,13},{14,15},{16,17},{18,... | collective-permute-start | bytes 786440 | tf_op jit(solution)/shard_map/ppermute | solution.py:13
  37.6 2.1 copy-start.9
  39.5 206.8 %reduce-scatter.2.cloned.1.call-start = ((), (), s32[]{:S(2)}) async-start(), calls=%async_computation.3 | async-start | bytes 1474560 | tf_op jit(solution)/shard_map/reduce_scatter | solution.py:213
  45.3 54.5 %copy-start.7 = (f32[2304]{0:T(1024)S(1)}, f32[2304]{0:T(1024)}, u32[]{:S(2)}) copy-start(f32[2304]{0:T(1024)} %param.17) | copy-start | bytes 27652
  46.9 53.3 %copy-start.4 = (bf16[256,2,96]{0,2,1:T(8,128)(2,1)}, bf16[256,2,96]{0,2,1:T(8,128)(2,1)S(1)}, u32[]{:S(2)}) copy-start(bf16[256,2,96]{0,2,1:T(8,128)(2,1)S(1)} %get-tuple-element.15) | copy-start | bytes 294916
  101.6 21.9 %collective-permute-start.2 = (bf16[96,2,2304]{2,0,1:T(8,128)(2,1)}, bf16[96,2,2304]{2,0,1:T(8,128)(2,1)}, u32[]{:S(2)}, u32[]{:S(2)}) collective-permute-start(bf16[96,2,2304]{2,0,1:T(8,128)(2,1)} %convert_bitcast_fusion.1), channel_id=1, source_target_pairs={{0,8},{8,0},{16,24},{24,16},{1,9},{9,1},{17,25},{25,17},{2,10},{10... | collective-permute-start | bytes 2654216 | tf_op jit(solution)/shard_map/ppermute | solution.py:180
  103.1 21.6 %collective-permute-start.3 = (bf16[96,2,2304]{2,0,1:T(8,128)(2,1)}, bf16[96,2,2304]{2,0,1:T(8,128)(2,1)}, u32[]{:S(2)}, u32[]{:S(2)}) collective-permute-start(bf16[96,2,2304]{2,0,1:T(8,128)(2,1)} %convert_bitcast_fusion.1), channel_id=1, source_target_pairs={{0,16},{8,24},{16,0},{24,8},{1,17},{9,25},{17,1},{25,9},{2,18},{10... | collective-permute-start | bytes 2654216 | tf_op jit(solution)/shard_map/ppermute | solution.py:180
  142.6 22.9 %collective-permute-start.6 = (bf16[96,2,2304]{2,0,1:T(8,128)(2,1)}, bf16[96,2,2304]{2,0,1:T(8,128)(2,1)}, u32[]{:S(2)}, u32[]{:S(2)}) collective-permute-start(bf16[96,2,2304]{2,0,1:T(8,128)(2,1)} %collective-permute-done.2), channel_id=1, source_target_pairs={{0,16},{8,24},{16,0},{24,8},{1,17},{9,25},{17,1},{25,9},{2,18},{10... | collective-permute-start | bytes 2654216 | tf_op jit(solution)/shard_map/ppermute | solution.py:180
  154.5 45.1 %collective-permute-start.4 = (bf16[96,2,2304]{2,0,1:T(8,128)(2,1)}, bf16[96,2,2304]{2,0,1:T(8,128)(2,1)}, u32[]{:S(2)}, u32[]{:S(2)}) collective-permute-start(bf16[96,2,2304]{2,0,1:T(8,128)(2,1)} %get-tuple-element.19), channel_id=1, source_target_pairs={{0,8},{8,0},{16,24},{24,16},{1,9},{9,1},{17,25},{25,17},{2,10},{10... | collective-permute-start | bytes 2654216 | tf_op jit(solution)/shard_map/ppermute | solution.py:180
  155.1 53.8 %collective-permute-start.5 = (bf16[96,2,2304]{2,0,1:T(8,128)(2,1)}, bf16[96,2,2304]{2,0,1:T(8,128)(2,1)}, u32[]{:S(2)}, u32[]{:S(2)}) collective-permute-start(bf16[96,2,2304]{2,0,1:T(8,128)(2,1)} %get-tuple-element.18), channel_id=1, source_target_pairs={{0,16},{8,24},{16,0},{24,8},{1,17},{9,25},{17,1},{25,9},{2,18},{10... | collective-permute-start | bytes 2654216 | tf_op jit(solution)/shard_map/ppermute | solution.py:180
  179.4 10.4 %copy-start.2 = (f32[2,96,2,1440]{3,1,0,2:T(8,128)S(1)}, f32[2,96,2,1440]{3,1,0,2:T(8,128)}, u32[]{:S(2)}) copy-start(f32[2,96,2,1440]{3,1,0,2:T(8,128)} %convolution_bitcast_fusion.1) | copy-start | bytes 6635524
  188.3 18.6 %collective-permute-start.7 = (bf16[96,2,2304]{2,0,1:T(8,128)(2,1)}, bf16[96,2,2304]{2,0,1:T(8,128)(2,1)}, u32[]{:S(2)}, u32[]{:S(2)}) collective-permute-start(bf16[96,2,2304]{2,0,1:T(8,128)(2,1)} %fusion.8), channel_id=1, source_target_pairs={{0,24},{8,16},{16,8},{24,0},{1,25},{9,17},{17,9},{25,1},{2,26},{10... | collective-permute-start | bytes 2654216 | tf_op jit(solution)/shard_map/ppermute | solution.py:180
  199.6 7.3 %copy-start.5 = (bf16[256,2,96]{0,2,1:T(8,128)(2,1)S(1)}, bf16[256,2,96]{0,2,1:T(8,128)(2,1)}, u32[]{:S(2)}) copy-start(bf16[256,2,96]{0,2,1:T(8,128)(2,1)} %copy-done.4) | copy-start | bytes 294916
  212.8 4.6 %copy-start.8 = (s32[4,16]{1,0:T(4,128)S(1)}, s32[4,16]{1,0:T(4,128)}, u32[]{:S(2)}) copy-start(s32[4,16]{1,0:T(4,128)} %param.25) | copy-start | bytes 772
  212.8 24.7 %all-to-all-start = ((bf16[16,64,2,512]{3,1,2,0:T(8,128)(2,1)}), bf16[16,64,2,512]{3,1,2,0:T(8,128)(2,1)}, u32[]{:S(2)}, u32[]{:S(2)}) async-start(bf16[16,64,2,512]{3,1,2,0:T(8,128)(2,1)} %gather_fusion), calls=%async_computation.1 | async-start | bytes 4194304 | tf_op jit(solution)/shard_map/all_to_all | solution.py:91
  237.5 10.5 %copy-start.1 = (bf16[512,2304]{1,0:T(8,128)(2,1)S(1)}, bf16[512,2304]{1,0:T(8,128)(2,1)}, u32[]{:S(2)}) copy-start(bf16[512,2304]{1,0:T(8,128)(2,1)} %param.16) | copy-start | bytes 7077892
Sparse Core Ops, SparseCore 0:
  39.6 58.0 all-reduce.1
  212.9 27.7 reduce-scatter.1

commit v14 on v13

--- a/solution.py
+++ b/solution.py
@@ -129,7 +129,8 @@
     queries = rotate(projected[:, 0], angles_at).astype(jnp.bfloat16)
     key_rows = rotate(projected[:, 1], angles_at).astype(jnp.bfloat16)
     values = projected[:, 2].astype(jnp.bfloat16)
-    earlier_keys, earlier_values = shifted((key_rows, values), "dev", 1)
+    earlier_both = shifted(jnp.stack([key_rows, values], axis=0), "dev", 1)
+    earlier_keys, earlier_values = earlier_both[0], earlier_both[1]
     all_keys = jnp.concatenate([earlier_keys, key_rows], axis=0)
     all_values = jnp.concatenate([earlier_values, values], axis=0)
     key_pos = (dev_index - 1) * half_rows + jnp.arange(2 * half_rows, dtype=jnp.int32)

time: 256 us -> 255 us (level)
  starting transfers between devices: 16.8 us -> 14.1 us
    ppermute x2 -> x1, starting transfers between devices: 5.06 us -> 2.39 us  [shifted(): return lax.ppermute(block, axis, route)]
    unnamed x22 -> x28, local copies, waits for them, and re-layouts: 15 us -> 15 us
  transfers between devices with their start and end apart: 11 -> 10, of which waited for: 6 -> 6; matrix products, arithmetic and copies ran while one was open for 34% -> 33% of each run, Pallas kernels for 0% -> 0%
where the time goes in v14:
time: 255 us; the launch traced here: 254 us
  waiting for transfers between devices  90.4 us (35%)
  matrix products  89.4 us (35%)
  local copies, waits for them, and re-layouts  29.5 us (12%)
  other arithmetic  16.3 us (6%)
  between operations  14.4 us (6%)
  starting transfers between devices  14.1 us (6%)
    psum x1, waiting for transfers between devices, body(): lax.psum(partial_value.astype(jnp.bfloat16), 'head').astype(jnp.float32)  50.8 us
    dot_general x3, matrix products, experts_on(): jnp.einsum('ned,egdf->gnef', flat, w_gate_up, preferred_element_type=jnp....  43 us
    all_to_all x1, waiting for transfers between devices, pages_in(): lax.all_to_all(outgoing, 'req', split_axis=0, concat_axis=0, tiled=True)  20 us
    ppermute x6, waiting for transfers between devices, partner_move(): return lax.ppermute(block, 'req', [(i, i ^ step) for i in range(req_total)])  19.5 us
    dot_general x2, matrix products, experts_on(): jnp.einsum('nef,efd->ned', hidden, w_down, preferred_element_type=jnp.flo...  18.1 us
    dot_general x4, matrix products, body(): jnp.einsum('tec,ced->ted', dispatch_bf, part, preferred_element_type=jnp....  17.6 us
    unnamed x28, local copies, waits for them, and re-layouts  15 us
    ppermute x6, starting transfers between devices, partner_move(): return lax.ppermute(block, 'req', [(i, i ^ step) for i in range(req_total)])  6.99 us
  transfers between devices with their start and end apart: 10, of which 6 were waited for; matrix products, arithmetic and copies ran while one was open for 33% of the time, Pallas kernels for 0%

profile of v14, /device:TPU:0, one launch (start us, length us, event | category | flops | bytes accessed | tf_op | source)
XLA Modules:
  0.0 254.1 jit_solution(9697305428355369450)
XLA Ops:
  7.3 9.9 %copy.52 = bf16[2304,3,512]{0,2,1:T(8,128)(2,1)} copy(bf16[2304,3,512]{2,0,1:T(8,128)(2,1)} %param.15) | data formatting | bytes 14155776 | tf_op args[2]
  17.1 0.3 fusion.19
  17.5 5.2 %fusion.35 = f32[256,3,8,64]{0,3,2,1:T(8,128)S(1)} fusion(bf16[3,8,64,2304]{3,2,1,0:T(8,128)(2,1)} %bitcast.166, bf16[1,256,2304]{2,1,0:T(8,128)(2,1)S(1)} %copy-done.3, f32[2304]{0:T(1024)} %param.14, f32[256]{0:T(256)S(1)} %add_rsqrt_fusion.1), kind=kOutput, calls=%fused_computation.49 | convolution fusion | flops 1814298624 | bytes 9840640 | tf_op jit(solution)/shard_map/dot_general | solution.py:124
  22.8 0.9 fusion.73
  23.6 0.2 multiply_cosine_fusion
  23.8 0.8 subtract_convert_fusion
  24.7 1.1 pad_maximum_fusion.1
  25.8 2.4 collective-permute-start
  28.2 0.6 iota_add_fusion.1
  28.7 0.7 constant_dynamic-slice_fusion.2
  29.4 0.1 copy.53
  29.6 0.1 eq.115
  29.8 0.6 reduce-window.6
  30.4 0.2 slice_reduce_fusion
  30.6 0.2 convert_reduce_fusion
  30.8 0.1 select_reduce_fusion.2
  31.0 0.2 reduce-window.9
  31.3 0.8 compare_and_fusion
  32.2 2.0 fusion.6
  34.3 1.3 fusion.9
  35.6 1.2 fusion.47
  36.8 1.9 convolution_convert_fusion.1
  38.7 0.2 reduce-scatter.2.cloned.1.call-start
  39.0 0.6 dynamic_slice.25
  39.5 0.2 eq.119
  39.9 0.7 add_compare_fusion
  40.6 1.9 bitcast_select_fusion
  42.5 2.0 gather_fusion
  44.5 0.7 fusion.112
  45.2 0.7 dynamic-slice_bitcast_fusion
  46.1 50.8 %all-reduce.2.cloned.1.call-done = bf16[256,2304]{1,0:T(8,128)(2,1)} async-done(((bf16[256,2304]{1,0:T(8,128)(2,1)}), bf16[256,2304]{1,0:T(8,128)(2,1)}) %all-reduce.2.cloned.1.call-update) | async-done | bytes 1179664 | tf_op jit(solution)/shard_map/psum | solution.py:156
  96.9 2.1 fusion.16
  99.0 0.3 fusion.18
  99.4 0.4 fusion.93
  99.8 1.0 convert_bitcast_fusion.1
  100.8 1.5 collective-permute-start.1
  102.3 1.5 collective-permute-start.2
  103.8 14.2 %convolution_bitcast_fusion.1 = f32[2,96,2,1440]{3,1,0,2:T(8,128)} fusion(bf16[2,2,2304,1440]{2,3,1,0:T(8,128)(2,1)} %param.20, f32[2304,2,96]{0,2,1:T(8,128)S(1)} %bitcast.165), kind=kOutput, calls=%fused_computation.23 | convolution fusion | flops 2548482048 | bytes 30523392 | tf_op jit(solution)/shard_map/ned,egdf->gnef/dot_general | solution.py:186
  118.0 4.7 %collective-permute-done.1 = bf16[96,2,2304]{2,0,1:T(8,128)(2,1)} collective-permute-done((bf16[96,2,2304]{2,0,1:T(8,128)(2,1)}, bf16[96,2,2304]{2,0,1:T(8,128)(2,1)}, u32[]{:S(2)}, u32[]{:S(2)}) %collective-permute-start.1) | collective-permute-done | bytes 884768 | tf_op jit(solution)/shard_map/ppermute | solution.py:181
  122.7 1.2 collective-permute-done.2
  123.9 1.6 pad_maximum_fusion
  125.5 1.4 copy.57
  126.9 14.9 %convolution_bitcast_fusion = f32[2,192,2,1440]{3,1,0,2:T(8,128)} fusion(bf16[192,2,2304,1]{2,0,3,1:T(8,128)(2,1)} %bitcast.168, bf16[2,2,2304,1440]{2,3,1,0:T(8,128)(2,1)} %param.20), kind=kOutput, calls=%fused_computation.14 | convolution fusion | flops 5096079360 | bytes 32735232 | tf_op jit(solution)/shard_map/ned,egdf->gnef/dot_general | solution.py:186
  141.8 1.5 collective-permute-start.5
  143.2 9.1 %fusion.5 = bf16[192,2,2304]{2,0,1:T(8,128)(2,1)S(1)} fusion(bf16[2,1440,2304]{2,1,0:T(8,128)(2,1)} %param.21, f32[2,192,2,1440]{3,1,0,2:T(8,128)} %convolution_bitcast_fusion), kind=kOutput, calls=%fused_computation.12 | convolution fusion | flops 2552242176 | bytes 19464192 | tf_op jit(solution)/shard_map/nef,efd->ned/dot_general | solution.py:188
  152.4 1.3 fusion.91
  153.7 0.6 collective-permute-start.3
  154.3 0.6 collective-permute-start.4
  154.8 9.9 %collective-permute-done.5 = bf16[96,2,2304]{2,0,1:T(8,128)(2,1)} collective-permute-done((bf16[96,2,2304]{2,0,1:T(8,128)(2,1)}, bf16[96,2,2304]{2,0,1:T(8,128)(2,1)}, u32[]{:S(2)}, u32[]{:S(2)}) %collective-permute-start.5) | collective-permute-done | bytes 884768 | tf_op jit(solution)/shard_map/ppermute | solution.py:181
  164.7 13.9 %fusion.11 = f32[2,96,2,1440]{3,1,2,0:T(8,128)} fusion(bf16[2,2,2304,1440]{2,3,1,0:T(8,128)(2,1)} %param.20, bf16[96,2,2304]{2,0,1:T(8,128)(2,1)} %collective-permute-done.5), kind=kOutput, calls=%fused_computation.22 | convolution fusion | flops 2548039680 | bytes 29638656 | tf_op jit(solution)/shard_map/ned,egdf->gnef/dot_general | solution.py:186
  178.6 8.9 %fusion.8 = bf16[96,2,2304]{2,0,1:T(8,128)(2,1)} fusion(bf16[2,1440,2304]{2,1,0:T(8,128)(2,1)} %param.21, f32[2,96,2,1440]{3,1,2,0:T(8,128)} %fusion.11), kind=kOutput, calls=%fused_computation.19 | convolution fusion | flops 1276121088 | bytes 16367616 | tf_op jit(solution)/shard_map/nef,efd->ned/dot_general | solution.py:188
  187.5 1.5 collective-permute-start.6
  189.0 9.8 %fusion.29 = f32[2,2304,256]{2,1,0:T(8,128)} fusion(bf16[256,2,96]{0,2,1:T(8,128)(2,1)} %copy-done.4, bf16[2,1440,2304]{2,1,0:T(8,128)(2,1)} %param.21, f32[2,96,2,1440]{3,1,0,2:T(8,128)S(1)} %copy-done.2), kind=kOutput, calls=%fused_computation.45 | convolution fusion | flops 1502613504 | bytes 20299776 | tf_op jit(solution)/shard_map/tec,ced->ted/dot_general | solution.py:210
  198.8 3.5 %convolution_add_fusion.1 = f32[2,2304,256]{2,1,0:T(8,128)S(1)} fusion(f32[2,2304,256]{2,1,0:T(8,128)} %fusion.29, bf16[96,2,2304]{2,0,1:T(8,128)(2,1)} %collective-permute-done.3, bf16[256,2,96]{0,2,1:T(8,128)(2,1)} %copy-done.4), kind=kOutput, calls=%fused_computation.6 | convolution fusion | flops 227672064 | bytes 10420224 | tf_op jit(solution)/shard_map/tec,ced->ted/dot_general | solution.py:210
  202.3 3.7 %collective-permute-done.6 = bf16[96,2,2304]{2,0,1:T(8,128)(2,1)} collective-permute-done((bf16[96,2,2304]{2,0,1:T(8,128)(2,1)}, bf16[96,2,2304]{2,0,1:T(8,128)(2,1)}, u32[]{:S(2)}, u32[]{:S(2)}) %collective-permute-start.6) | collective-permute-done | bytes 884768 | tf_op jit(solution)/shard_map/ppermute | solution.py:181
  206.1 2.0 fusion.92
  208.1 2.3 fusion.28
  210.4 1.5 copy.60
  212.0 4.5 %all-to-all-start = ((bf16[16,64,2,512]{3,1,2,0:T(8,128)(2,1)}), bf16[16,64,2,512]{3,1,2,0:T(8,128)(2,1)}, u32[]{:S(2)}, u32[]{:S(2)}) async-start(bf16[16,64,2,512]{3,1,2,0:T(8,128)(2,1)} %gather_fusion), calls=%async_computation.1 | async-start | bytes 4194304 | tf_op jit(solution)/shard_map/all_to_all | solution.py:91
  216.5 0.1 select_reduce_fusion.1
  216.7 20.0 %all-to-all-done = bf16[16,64,2,512]{3,1,2,0:T(8,128)(2,1)} async-done(((bf16[16,64,2,512]{3,1,2,0:T(8,128)(2,1)}), bf16[16,64,2,512]{3,1,2,0:T(8,128)(2,1)}, u32[]{:S(2)}, u32[]{:S(2)}) %all-to-all-start) | async-done | bytes 2097184 | tf_op jit(solution)/shard_map/all_to_all | solution.py:91
  236.7 3.7 %gather_fusion.1 = bf16[16,64,2,512]{3,1,2,0:T(8,128)(2,1)} fusion(bf16[16,64,2,512]{3,1,2,0:T(8,128)(2,1)} %all-to-all-done, s32[1024]{0:T(1024)S(1)} %pad_clamp_fusion), kind=kCustom, calls=%fused_computation.1 | custom fusion | bytes 4194368 | tf_op jit(solution)/shard_map/jit(_take)/gather | solution.py:97
  240.4 5.1 %copy.61 = bf16[16,64,2,512]{3,2,1,0:T(2,128)(2,1)} copy(bf16[16,64,2,512]{3,1,2,0:T(8,128)(2,1)} %gather_fusion.1) | data formatting | bytes 4194304
  245.5 1.7 fusion.69
  (60 shorter events, 1.0 us)
Async XLA Ops:
  7.2 29.6 %copy-start = (bf16[512,2304]{1,0:T(8,128)(2,1)S(1)}, bf16[512,2304]{1,0:T(8,128)(2,1)}, u32[]{:S(2)}) copy-start(bf16[512,2304]{1,0:T(8,128)(2,1)} %param.16) | copy-start | bytes 7077892
  7.2 89.7 %all-reduce.2.cloned.1.call-start = ((), (), s32[]{:S(2)}) async-start(), calls=%async_computation.2 | async-start | bytes 2359296 | tf_op jit(solution)/shard_map/psum | solution.py:156
  7.2 9.9 %copy-start.3 = (bf16[1,256,2304]{2,1,0:T(8,128)(2,1)S(1)}, bf16[1,256,2304]{2,1,0:T(8,128)(2,1)}, u32[]{:S(2)}) copy-start(bf16[1,256,2304]{2,1,0:T(8,128)(2,1)} %param.13) | copy-start | bytes 3538948
  22.7 7.9 %copy-start.9 = (s32[4,16]{1,0:T(4,128)S(1)}, s32[4,16]{1,0:T(4,128)}, u32[]{:S(2)}) copy-start(s32[4,16]{1,0:T(4,128)} %param.24) | copy-start | bytes 772
  24.7 3.5 %copy-start.6 = (bf16[256,8,32]{0,2,1:T(8,128)(2,1)}, bf16[256,8,32]{0,2,1:T(8,128)(2,1)S(1)}, u32[]{:S(2)}) copy-start(bf16[256,8,32]{0,2,1:T(8,128)(2,1)S(1)} %get-tuple-element.30) | copy-start | bytes 393220
  24.7 4.1 %copy-start.7 = (bf16[256,8,32]{0,2,1:T(8,128)(2,1)}, bf16[256,8,32]{0,2,1:T(8,128)(2,1)S(1)}, u32[]{:S(2)}) copy-start(bf16[256,8,32]{0,2,1:T(8,128)(2,1)S(1)} %get-tuple-element.31) | copy-start | bytes 393220
  25.8 6.4 %collective-permute-start = (bf16[2,256,8,64]{1,3,2,0:T(8,128)(2,1)S(1)}, bf16[2,256,8,64]{1,3,2,0:T(8,128)(2,1)S(1)}, u32[]{:S(2)}, u32[]{:S(2)}) collective-permute-start(bf16[2,256,8,64]{1,3,2,0:T(8,128)(2,1)S(1)} %pad_maximum_fusion.1), channel_id=1, source_target_pairs={{0,1},{2,3},{4,5},{6,7},{8,9},{10,11},{12,13},{14,15},{16,17},{18,... | collective-permute-start | bytes 1572872 | tf_op jit(solution)/shard_map/ppermute | solution.py:13
  34.3 1.3 copy-start.8
  36.8 2.1 copy-start.12
  38.7 206.8 %reduce-scatter.2.cloned.1.call-start = ((), (), s32[]{:S(2)}) async-start(), calls=%async_computation.3 | async-start | bytes 1474560 | tf_op jit(solution)/shard_map/reduce_scatter | solution.py:214
  44.5 54.5 %copy-start.10 = (f32[2304]{0:T(1024)S(1)}, f32[2304]{0:T(1024)}, u32[]{:S(2)}) copy-start(f32[2304]{0:T(1024)} %param.17) | copy-start | bytes 27652
  46.1 53.3 %copy-start.4 = (bf16[256,2,96]{0,2,1:T(8,128)(2,1)}, bf16[256,2,96]{0,2,1:T(8,128)(2,1)S(1)}, u32[]{:S(2)}) copy-start(bf16[256,2,96]{0,2,1:T(8,128)(2,1)S(1)} %get-tuple-element.15) | copy-start | bytes 294916
  100.8 21.9 %collective-permute-start.1 = (bf16[96,2,2304]{2,0,1:T(8,128)(2,1)}, bf16[96,2,2304]{2,0,1:T(8,128)(2,1)}, u32[]{:S(2)}, u32[]{:S(2)}) collective-permute-start(bf16[96,2,2304]{2,0,1:T(8,128)(2,1)} %convert_bitcast_fusion.1), channel_id=1, source_target_pairs={{0,8},{8,0},{16,24},{24,16},{1,9},{9,1},{17,25},{25,17},{2,10},{10... | collective-permute-start | bytes 2654216 | tf_op jit(solution)/shard_map/ppermute | solution.py:181
  102.3 21.6 %collective-permute-start.2 = (bf16[96,2,2304]{2,0,1:T(8,128)(2,1)}, bf16[96,2,2304]{2,0,1:T(8,128)(2,1)}, u32[]{:S(2)}, u32[]{:S(2)}) collective-permute-start(bf16[96,2,2304]{2,0,1:T(8,128)(2,1)} %convert_bitcast_fusion.1), channel_id=1, source_target_pairs={{0,16},{8,24},{16,0},{24,8},{1,17},{9,25},{17,1},{25,9},{2,18},{10... | collective-permute-start | bytes 2654216 | tf_op jit(solution)/shard_map/ppermute | solution.py:181
  141.8 22.9 %collective-permute-start.5 = (bf16[96,2,2304]{2,0,1:T(8,128)(2,1)}, bf16[96,2,2304]{2,0,1:T(8,128)(2,1)}, u32[]{:S(2)}, u32[]{:S(2)}) collective-permute-start(bf16[96,2,2304]{2,0,1:T(8,128)(2,1)} %collective-permute-done.1), channel_id=1, source_target_pairs={{0,16},{8,24},{16,0},{24,8},{1,17},{9,25},{17,1},{25,9},{2,18},{10... | collective-permute-start | bytes 2654216 | tf_op jit(solution)/shard_map/ppermute | solution.py:181
  153.7 45.1 %collective-permute-start.3 = (bf16[96,2,2304]{2,0,1:T(8,128)(2,1)}, bf16[96,2,2304]{2,0,1:T(8,128)(2,1)}, u32[]{:S(2)}, u32[]{:S(2)}) collective-permute-start(bf16[96,2,2304]{2,0,1:T(8,128)(2,1)} %get-tuple-element.19), channel_id=1, source_target_pairs={{0,8},{8,0},{16,24},{24,16},{1,9},{9,1},{17,25},{25,17},{2,10},{10... | collective-permute-start | bytes 2654216 | tf_op jit(solution)/shard_map/ppermute | solution.py:181
  154.3 53.8 %collective-permute-start.4 = (bf16[96,2,2304]{2,0,1:T(8,128)(2,1)}, bf16[96,2,2304]{2,0,1:T(8,128)(2,1)}, u32[]{:S(2)}, u32[]{:S(2)}) collective-permute-start(bf16[96,2,2304]{2,0,1:T(8,128)(2,1)} %get-tuple-element.18), channel_id=1, source_target_pairs={{0,16},{8,24},{16,0},{24,8},{1,17},{9,25},{17,1},{25,9},{2,18},{10... | collective-permute-start | bytes 2654216 | tf_op jit(solution)/shard_map/ppermute | solution.py:181
  178.6 10.4 %copy-start.2 = (f32[2,96,2,1440]{3,1,0,2:T(8,128)S(1)}, f32[2,96,2,1440]{3,1,0,2:T(8,128)}, u32[]{:S(2)}) copy-start(f32[2,96,2,1440]{3,1,0,2:T(8,128)} %convolution_bitcast_fusion.1) | copy-start | bytes 6635524
  187.5 18.6 %collective-permute-start.6 = (bf16[96,2,2304]{2,0,1:T(8,128)(2,1)}, bf16[96,2,2304]{2,0,1:T(8,128)(2,1)}, u32[]{:S(2)}, u32[]{:S(2)}) collective-permute-start(bf16[96,2,2304]{2,0,1:T(8,128)(2,1)} %fusion.8), channel_id=1, source_target_pairs={{0,24},{8,16},{16,8},{24,0},{1,25},{9,17},{17,9},{25,1},{2,26},{10... | collective-permute-start | bytes 2654216 | tf_op jit(solution)/shard_map/ppermute | solution.py:181
  198.8 7.3 %copy-start.5 = (bf16[256,2,96]{0,2,1:T(8,128)(2,1)S(1)}, bf16[256,2,96]{0,2,1:T(8,128)(2,1)}, u32[]{:S(2)}) copy-start(bf16[256,2,96]{0,2,1:T(8,128)(2,1)} %copy-done.4) | copy-start | bytes 294916
  212.0 4.6 %copy-start.11 = (s32[4,16]{1,0:T(4,128)S(1)}, s32[4,16]{1,0:T(4,128)}, u32[]{:S(2)}) copy-start(s32[4,16]{1,0:T(4,128)} %param.25) | copy-start | bytes 772
  212.0 24.7 %all-to-all-start = ((bf16[16,64,2,512]{3,1,2,0:T(8,128)(2,1)}), bf16[16,64,2,512]{3,1,2,0:T(8,128)(2,1)}, u32[]{:S(2)}, u32[]{:S(2)}) async-start(bf16[16,64,2,512]{3,1,2,0:T(8,128)(2,1)} %gather_fusion), calls=%async_computation.1 | async-start | bytes 4194304 | tf_op jit(solution)/shard_map/all_to_all | solution.py:91
  236.7 10.5 %copy-start.1 = (bf16[512,2304]{1,0:T(8,128)(2,1)S(1)}, bf16[512,2304]{1,0:T(8,128)(2,1)}, u32[]{:S(2)}) copy-start(bf16[512,2304]{1,0:T(8,128)(2,1)} %param.16) | copy-start | bytes 7077892
Sparse Core Ops, SparseCore 0:
  38.8 58.0 all-reduce.1
  212.1 27.7 reduce-scatter.1

commit v15 on v14

--- a/solution.py
+++ b/solution.py
@@ -131,23 +131,32 @@
     values = projected[:, 2].astype(jnp.bfloat16)
     earlier_both = shifted(jnp.stack([key_rows, values], axis=0), "dev", 1)
     earlier_keys, earlier_values = earlier_both[0], earlier_both[1]
-    all_keys = jnp.concatenate([earlier_keys, key_rows], axis=0)
-    all_values = jnp.concatenate([earlier_values, values], axis=0)
     key_pos = (dev_index - 1) * half_rows + jnp.arange(2 * half_rows, dtype=jnp.int32)
     allowed = (key_pos[None, :] <= query_pos[:, None]) & (key_pos[None, :] >= 0)
-    scores = (
-        jnp.einsum("qhd,khd->hqk", queries, all_keys, preferred_element_type=jnp.float32) * 0.125
-    )
+    own_scores = jnp.einsum("qhd,khd->hqk", queries, key_rows, preferred_element_type=jnp.float32)
+    early_scores = jnp.einsum(
+        "qhd,khd->hqk", queries, earlier_keys, preferred_element_type=jnp.float32
+    )
+    scores = jnp.concatenate([early_scores, own_scores], axis=-1) * 0.125
     scores = jnp.where(allowed[None], scores, -1e30)
     row_peak = jnp.max(scores, axis=-1, keepdims=True)
     exp_scores = jnp.exp(scores - row_peak)
     row_total = jnp.sum(exp_scores, axis=-1)
+    probs = exp_scores.astype(jnp.bfloat16)
     attended = (
-        jnp.einsum(
-            "hqk,khd->qhd",
-            exp_scores.astype(jnp.bfloat16),
-            all_values,
-            preferred_element_type=jnp.float32,
+        (
+            jnp.einsum(
+                "hqk,khd->qhd",
+                probs[:, :, :half_rows],
+                earlier_values,
+                preferred_element_type=jnp.float32,
+            )
+            + jnp.einsum(
+                "hqk,khd->qhd",
+                probs[:, :, half_rows:],
+                values,
+                preferred_element_type=jnp.float32,
+            )
         )
         / jnp.transpose(row_total)[:, :, None]
     )

time: 255 us -> 258 us (1.012)
    dot_general x2 -> x4, matrix products: 3.24 us -> 5.54 us  [the longest x1 1.51 us: body(): jnp.einsum('qhd,khd->hqk', queries, key_rows, preferred_element_type=jnp....]
    unnamed x28 -> x36, local copies, waits for them, and re-layouts: 15 us -> 16.7 us
  transfers between devices with their start and end apart: 10 -> 10, of which waited for: 6 -> 6; matrix products, arithmetic and copies ran while one was open for 33% -> 32% of each run, Pallas kernels for 0% -> 0%
where the time goes in v15:
time: 258 us; the launch traced here: 257 us
  matrix products  91.7 us (36%)
  waiting for transfers between devices  91.1 us (35%)
  local copies, waits for them, and re-layouts  29.6 us (11%)
  other arithmetic  15.7 us (6%)
  starting transfers between devices  14.9 us (6%)
  between operations  14.4 us (6%)
    psum x1, waiting for transfers between devices, body(): lax.psum(partial_value.astype(jnp.bfloat16), 'head').astype(jnp.float32)  51.5 us
    dot_general x3, matrix products, experts_on(): jnp.einsum('ned,egdf->gnef', flat, w_gate_up, preferred_element_type=jnp....  43 us
    all_to_all x1, waiting for transfers between devices, pages_in(): lax.all_to_all(outgoing, 'req', split_axis=0, concat_axis=0, tiled=True)  20 us
    ppermute x6, waiting for transfers between devices, partner_move(): return lax.ppermute(block, 'req', [(i, i ^ step) for i in range(req_total)])  19.5 us
    dot_general x2, matrix products, experts_on(): jnp.einsum('nef,efd->ned', hidden, w_down, preferred_element_type=jnp.flo...  18.1 us
    dot_general x4, matrix products, body(): jnp.einsum('tec,ced->ted', dispatch_bf, part, preferred_element_type=jnp....  17.6 us
    unnamed x36, local copies, waits for them, and re-layouts  16.7 us
    ppermute x6, starting transfers between devices, partner_move(): return lax.ppermute(block, 'req', [(i, i ^ step) for i in range(req_total)])  7 us
  transfers between devices with their start and end apart: 10, of which 6 were waited for; matrix products, arithmetic and copies ran while one was open for 32% of the time, Pallas kernels for 0%

profile of v15, /device:TPU:0, one launch (start us, length us, event | category | flops | bytes accessed | tf_op | source)
XLA Modules:
  0.0 257.3 jit_solution(1130883695292412495)
XLA Ops:
  7.2 0.6 multiply_power_fusion
  7.8 9.8 %copy.60 = bf16[2304,3,512]{0,2,1:T(8,128)(2,1)} copy(bf16[2304,3,512]{2,0,1:T(8,128)(2,1)} %param.15) | data formatting | bytes 14155776 | tf_op args[2]
  17.6 0.3 fusion.20
  17.9 5.2 %fusion.36 = f32[256,3,8,64]{0,3,2,1:T(8,128)S(1)} fusion(bf16[3,8,64,2304]{3,2,1,0:T(8,128)(2,1)} %bitcast.169, bf16[1,256,2304]{2,1,0:T(8,128)(2,1)S(1)} %copy-done.3, f32[2304]{0:T(1024)S(1)} %copy-done.15, f32[256]{0:T(256)S(1)} %add_rsqrt_fusion.1), kind=kOutput, calls=%fused_computation.53 | convolution fusion | flops 1814298624 | bytes 9840640 | tf_op jit(solution)/shard_map/dot_general | solution.py:124
  23.2 1.0 copy-done.6
  24.3 0.7 fusion.65
  25.0 0.2 multiply_cosine_fusion
  25.2 0.8 subtract_convert_fusion
  26.0 0.6 copy-done.8
  26.7 1.0 pad_maximum_fusion.1
  27.7 3.2 %collective-permute-start = (bf16[2,256,8,64]{1,3,2,0:T(8,128)(2,1)S(1)}, bf16[2,256,8,64]{1,3,2,0:T(8,128)(2,1)}, u32[]{:S(2)}, u32[]{:S(2)}) collective-permute-start(bf16[2,256,8,64]{1,3,2,0:T(8,128)(2,1)S(1)} %pad_maximum_fusion.1), channel_id=1, source_target_pairs={{0,1},{2,3},{4,5},{6,7},{8,9},{10,11},{12,13},{14,15},{16,17},{18,... | collective-permute-start | bytes 1572872 | tf_op jit(solution)/shard_map/ppermute | solution.py:13
  30.9 0.1 copy.63
  31.0 0.1 eq.115
  31.3 0.6 reduce-window.6
  31.9 0.2 slice_reduce_fusion
  32.1 0.2 convert_reduce_fusion
  32.4 0.2 reduce-window.9
  32.7 1.5 fusion.60
  34.3 0.2 compare_and_fusion
  34.5 1.4 fusion.59
  36.0 1.4 fusion.83
  37.4 1.3 fusion.45
  38.7 1.3 fusion.33
  40.0 1.9 convolution_convert_fusion.1
  41.9 0.2 reduce-scatter.2.cloned.1.call-start
  42.1 0.6 dynamic_slice.25
  42.7 0.2 eq.119
  43.1 0.7 add_compare_fusion
  43.8 1.9 bitcast_select_fusion
  45.7 2.0 gather_fusion
  47.7 0.7 dynamic-slice_bitcast_fusion
  48.6 51.5 %all-reduce.2.cloned.1.call-done = bf16[256,2304]{1,0:T(8,128)(2,1)} async-done(((bf16[256,2304]{1,0:T(8,128)(2,1)}), bf16[256,2304]{1,0:T(8,128)(2,1)}) %all-reduce.2.cloned.1.call-update) | async-done | bytes 1179664 | tf_op jit(solution)/shard_map/psum | solution.py:165
  100.1 2.1 fusion.17
  102.2 0.3 fusion.19
  102.6 0.4 fusion.86
  103.0 1.0 convert_bitcast_fusion.1
  104.0 1.5 collective-permute-start.1
  105.5 1.5 collective-permute-start.2
  106.9 14.2 %convolution_bitcast_fusion.1 = f32[2,96,2,1440]{3,1,0,2:T(8,128)} fusion(bf16[2,2,2304,1440]{2,3,1,0:T(8,128)(2,1)} %param.20, f32[2304,2,96]{0,2,1:T(8,128)S(1)} %bitcast.168), kind=kOutput, calls=%fused_computation.22 | convolution fusion | flops 2548482048 | bytes 30523392 | tf_op jit(solution)/shard_map/ned,egdf->gnef/dot_general | solution.py:195
  121.2 4.7 %collective-permute-done.1 = bf16[96,2,2304]{2,0,1:T(8,128)(2,1)} collective-permute-done((bf16[96,2,2304]{2,0,1:T(8,128)(2,1)}, bf16[96,2,2304]{2,0,1:T(8,128)(2,1)}, u32[]{:S(2)}, u32[]{:S(2)}) %collective-permute-start.1) | collective-permute-done | bytes 884768 | tf_op jit(solution)/shard_map/ppermute | solution.py:190
  125.9 1.2 collective-permute-done.2
  127.1 1.6 pad_maximum_fusion
  128.7 1.4 copy.67
  130.1 14.8 %convolution_bitcast_fusion = f32[2,192,2,1440]{3,1,0,2:T(8,128)} fusion(bf16[192,2,2304,1]{2,0,3,1:T(8,128)(2,1)} %bitcast.171, bf16[2,2,2304,1440]{2,3,1,0:T(8,128)(2,1)} %param.20), kind=kOutput, calls=%fused_computation.16 | convolution fusion | flops 5096079360 | bytes 32735232 | tf_op jit(solution)/shard_map/ned,egdf->gnef/dot_general | solution.py:195
  145.0 1.5 collective-permute-start.5
  146.4 9.1 %fusion.7 = bf16[192,2,2304]{2,0,1:T(8,128)(2,1)S(1)} fusion(bf16[2,1440,2304]{2,1,0:T(8,128)(2,1)} %param.21, f32[2,192,2,1440]{3,1,0,2:T(8,128)} %convolution_bitcast_fusion), kind=kOutput, calls=%fused_computation.14 | convolution fusion | flops 2552242176 | bytes 19464192 | tf_op jit(solution)/shard_map/nef,efd->ned/dot_general | solution.py:197
  155.6 1.3 fusion.84
  156.9 0.6 collective-permute-start.3
  157.4 0.5 collective-permute-start.4
  158.0 9.9 %collective-permute-done.5 = bf16[96,2,2304]{2,0,1:T(8,128)(2,1)} collective-permute-done((bf16[96,2,2304]{2,0,1:T(8,128)(2,1)}, bf16[96,2,2304]{2,0,1:T(8,128)(2,1)}, u32[]{:S(2)}, u32[]{:S(2)}) %collective-permute-start.5) | collective-permute-done | bytes 884768 | tf_op jit(solution)/shard_map/ppermute | solution.py:190
  167.9 13.9 %fusion.10 = f32[2,96,2,1440]{3,1,2,0:T(8,128)} fusion(bf16[2,2,2304,1440]{2,3,1,0:T(8,128)(2,1)} %param.20, bf16[96,2,2304]{2,0,1:T(8,128)(2,1)} %collective-permute-done.5), kind=kOutput, calls=%fused_computation.21 | convolution fusion | flops 2548039680 | bytes 29638656 | tf_op jit(solution)/shard_map/ned,egdf->gnef/dot_general | solution.py:195
  181.7 9.0 %fusion.9 = bf16[96,2,2304]{2,0,1:T(8,128)(2,1)} fusion(bf16[2,1440,2304]{2,1,0:T(8,128)(2,1)} %param.21, f32[2,96,2,1440]{3,1,2,0:T(8,128)} %fusion.10), kind=kOutput, calls=%fused_computation.20 | convolution fusion | flops 1276121088 | bytes 16367616 | tf_op jit(solution)/shard_map/nef,efd->ned/dot_general | solution.py:197
  190.7 1.5 collective-permute-start.6
  192.2 9.8 %fusion.30 = f32[2,2304,256]{2,1,0:T(8,128)} fusion(bf16[256,2,96]{0,2,1:T(8,128)(2,1)} %copy-done.4, bf16[2,1440,2304]{2,1,0:T(8,128)(2,1)} %param.21, f32[2,96,2,1440]{3,1,0,2:T(8,128)S(1)} %copy-done.2), kind=kOutput, calls=%fused_computation.46 | convolution fusion | flops 1502613504 | bytes 20299776 | tf_op jit(solution)/shard_map/tec,ced->ted/dot_general | solution.py:219
  202.0 3.5 %convolution_add_fusion.1 = f32[2,2304,256]{2,1,0:T(8,128)S(1)} fusion(f32[2,2304,256]{2,1,0:T(8,128)} %fusion.30, bf16[96,2,2304]{2,0,1:T(8,128)(2,1)} %collective-permute-done.3, bf16[256,2,96]{0,2,1:T(8,128)(2,1)} %copy-done.4), kind=kOutput, calls=%fused_computation.7 | convolution fusion | flops 227672064 | bytes 10420224 | tf_op jit(solution)/shard_map/tec,ced->ted/dot_general | solution.py:219
  205.5 3.8 %collective-permute-done.6 = bf16[96,2,2304]{2,0,1:T(8,128)(2,1)} collective-permute-done((bf16[96,2,2304]{2,0,1:T(8,128)(2,1)}, bf16[96,2,2304]{2,0,1:T(8,128)(2,1)}, u32[]{:S(2)}, u32[]{:S(2)}) %collective-permute-start.6) | collective-permute-done | bytes 884768 | tf_op jit(solution)/shard_map/ppermute | solution.py:190
  209.3 2.0 fusion.85
  211.3 2.3 fusion.29
  213.6 1.5 copy.70
  215.2 4.5 %all-to-all-start = ((bf16[16,64,2,512]{3,1,2,0:T(8,128)(2,1)}), bf16[16,64,2,512]{3,1,2,0:T(8,128)(2,1)}, u32[]{:S(2)}, u32[]{:S(2)}) async-start(bf16[16,64,2,512]{3,1,2,0:T(8,128)(2,1)} %gather_fusion), calls=%async_computation.1 | async-start | bytes 4194304 | tf_op jit(solution)/shard_map/all_to_all | solution.py:91
  219.8 20.0 %all-to-all-done = bf16[16,64,2,512]{3,1,2,0:T(8,128)(2,1)} async-done(((bf16[16,64,2,512]{3,1,2,0:T(8,128)(2,1)}), bf16[16,64,2,512]{3,1,2,0:T(8,128)(2,1)}, u32[]{:S(2)}, u32[]{:S(2)}) %all-to-all-start) | async-done | bytes 2097184 | tf_op jit(solution)/shard_map/all_to_all | solution.py:91
  239.9 3.7 %gather_fusion.1 = bf16[16,64,2,512]{3,1,2,0:T(8,128)(2,1)} fusion(bf16[16,64,2,512]{3,1,2,0:T(8,128)(2,1)} %all-to-all-done, s32[1024]{0:T(1024)S(1)} %pad_clamp_fusion), kind=kCustom, calls=%fused_computation.1 | custom fusion | bytes 4194368 | tf_op jit(solution)/shard_map/jit(_take)/gather | solution.py:97
  243.6 5.1 %copy.71 = bf16[16,64,2,512]{3,2,1,0:T(2,128)(2,1)} copy(bf16[16,64,2,512]{3,1,2,0:T(8,128)(2,1)} %gather_fusion.1) | data formatting | bytes 4194304
  248.7 1.7 fusion.58
  (69 shorter events, 1.2 us)
Async XLA Ops:
  7.2 32.8 %copy-start = (bf16[512,2304]{1,0:T(8,128)(2,1)S(1)}, bf16[512,2304]{1,0:T(8,128)(2,1)}, u32[]{:S(2)}) copy-start(bf16[512,2304]{1,0:T(8,128)(2,1)} %param.16) | copy-start | bytes 7077892
  7.2 92.9 %all-reduce.2.cloned.1.call-start = ((), (), s32[]{:S(2)}) async-start(), calls=%async_computation.2 | async-start | bytes 2359296 | tf_op jit(solution)/shard_map/psum | solution.py:165
  7.8 9.8 %copy-start.3 = (bf16[1,256,2304]{2,1,0:T(8,128)(2,1)S(1)}, bf16[1,256,2304]{2,1,0:T(8,128)(2,1)}, u32[]{:S(2)}) copy-start(bf16[1,256,2304]{2,1,0:T(8,128)(2,1)} %param.13) | copy-start | bytes 3538948
  7.8 10.2 %copy-start.15 = (f32[2304]{0:T(1024)S(1)}, f32[2304]{0:T(1024)}, u32[]{:S(2)}) copy-start(f32[2304]{0:T(1024)} %param.14) | copy-start | bytes 27652
  23.1 1.1 copy-start.6
  23.1 1.9 copy-start.14
  24.3 6.6 %copy-start.12 = (s32[4,256,2]{1,2,0:T(2,128)S(1)}, s32[4,256,2]{1,2,0:T(2,128)}, u32[]{:S(2)}) copy-start(s32[4,256,2]{1,2,0:T(2,128)} %param.18) | copy-start | bytes 24580
  24.3 7.8 %copy-start.10 = (s32[4,16]{1,0:T(4,128)S(1)}, s32[4,16]{1,0:T(4,128)}, u32[]{:S(2)}) copy-start(s32[4,16]{1,0:T(4,128)} %param.24) | copy-start | bytes 772
  26.0 0.6 copy-start.8
  26.0 1.7 copy-start.9
  26.7 7.9 %copy-start.7 = (bf16[256,8,32]{0,2,1:T(8,128)(2,1)S(1)}, bf16[256,8,32]{0,2,1:T(8,128)(2,1)}, u32[]{:S(2)}) copy-start(bf16[256,8,32]{0,2,1:T(8,128)(2,1)} %get-tuple-element.25) | copy-start | bytes 393220
  27.7 6.8 %collective-permute-start = (bf16[2,256,8,64]{1,3,2,0:T(8,128)(2,1)S(1)}, bf16[2,256,8,64]{1,3,2,0:T(8,128)(2,1)}, u32[]{:S(2)}, u32[]{:S(2)}) collective-permute-start(bf16[2,256,8,64]{1,3,2,0:T(8,128)(2,1)S(1)} %pad_maximum_fusion.1), channel_id=1, source_target_pairs={{0,1},{2,3},{4,5},{6,7},{8,9},{10,11},{12,13},{14,15},{16,17},{18,... | collective-permute-start | bytes 1572872 | tf_op jit(solution)/shard_map/ppermute | solution.py:13
  40.0 2.1 copy-start.16
  41.9 206.8 %reduce-scatter.2.cloned.1.call-start = ((), (), s32[]{:S(2)}) async-start(), calls=%async_computation.3 | async-start | bytes 1474560 | tf_op jit(solution)/shard_map/reduce_scatter | solution.py:223
  47.7 54.5 %copy-start.11 = (f32[2304]{0:T(1024)S(1)}, f32[2304]{0:T(1024)}, u32[]{:S(2)}) copy-start(f32[2304]{0:T(1024)} %param.17) | copy-start | bytes 27652
  48.6 54.0 %copy-start.4 = (bf16[256,2,96]{0,2,1:T(8,128)(2,1)}, bf16[256,2,96]{0,2,1:T(8,128)(2,1)S(1)}, u32[]{:S(2)}) copy-start(bf16[256,2,96]{0,2,1:T(8,128)(2,1)S(1)} %get-tuple-element.15) | copy-start | bytes 294916
  104.0 21.9 %collective-permute-start.1 = (bf16[96,2,2304]{2,0,1:T(8,128)(2,1)}, bf16[96,2,2304]{2,0,1:T(8,128)(2,1)}, u32[]{:S(2)}, u32[]{:S(2)}) collective-permute-start(bf16[96,2,2304]{2,0,1:T(8,128)(2,1)} %convert_bitcast_fusion.1), channel_id=1, source_target_pairs={{0,8},{8,0},{16,24},{24,16},{1,9},{9,1},{17,25},{25,17},{2,10},{10... | collective-permute-start | bytes 2654216 | tf_op jit(solution)/shard_map/ppermute | solution.py:190
  105.5 21.6 %collective-permute-start.2 = (bf16[96,2,2304]{2,0,1:T(8,128)(2,1)}, bf16[96,2,2304]{2,0,1:T(8,128)(2,1)}, u32[]{:S(2)}, u32[]{:S(2)}) collective-permute-start(bf16[96,2,2304]{2,0,1:T(8,128)(2,1)} %convert_bitcast_fusion.1), channel_id=1, source_target_pairs={{0,16},{8,24},{16,0},{24,8},{1,17},{9,25},{17,1},{25,9},{2,18},{10... | collective-permute-start | bytes 2654216 | tf_op jit(solution)/shard_map/ppermute | solution.py:190
  145.0 22.9 %collective-permute-start.5 = (bf16[96,2,2304]{2,0,1:T(8,128)(2,1)}, bf16[96,2,2304]{2,0,1:T(8,128)(2,1)}, u32[]{:S(2)}, u32[]{:S(2)}) collective-permute-start(bf16[96,2,2304]{2,0,1:T(8,128)(2,1)} %collective-permute-done.1), channel_id=1, source_target_pairs={{0,16},{8,24},{16,0},{24,8},{1,17},{9,25},{17,1},{25,9},{2,18},{10... | collective-permute-start | bytes 2654216 | tf_op jit(solution)/shard_map/ppermute | solution.py:190
  156.9 45.1 %collective-permute-start.3 = (bf16[96,2,2304]{2,0,1:T(8,128)(2,1)}, bf16[96,2,2304]{2,0,1:T(8,128)(2,1)}, u32[]{:S(2)}, u32[]{:S(2)}) collective-permute-start(bf16[96,2,2304]{2,0,1:T(8,128)(2,1)} %get-tuple-element.21), channel_id=1, source_target_pairs={{0,8},{8,0},{16,24},{24,16},{1,9},{9,1},{17,25},{25,17},{2,10},{10... | collective-permute-start | bytes 2654216 | tf_op jit(solution)/shard_map/ppermute | solution.py:190
  157.4 53.8 %collective-permute-start.4 = (bf16[96,2,2304]{2,0,1:T(8,128)(2,1)}, bf16[96,2,2304]{2,0,1:T(8,128)(2,1)}, u32[]{:S(2)}, u32[]{:S(2)}) collective-permute-start(bf16[96,2,2304]{2,0,1:T(8,128)(2,1)} %get-tuple-element.20), channel_id=1, source_target_pairs={{0,16},{8,24},{16,0},{24,8},{1,17},{9,25},{17,1},{25,9},{2,18},{10... | collective-permute-start | bytes 2654216 | tf_op jit(solution)/shard_map/ppermute | solution.py:190
  181.7 10.4 %copy-start.2 = (f32[2,96,2,1440]{3,1,0,2:T(8,128)S(1)}, f32[2,96,2,1440]{3,1,0,2:T(8,128)}, u32[]{:S(2)}) copy-start(f32[2,96,2,1440]{3,1,0,2:T(8,128)} %convolution_bitcast_fusion.1) | copy-start | bytes 6635524
  190.7 18.6 %collective-permute-start.6 = (bf16[96,2,2304]{2,0,1:T(8,128)(2,1)}, bf16[96,2,2304]{2,0,1:T(8,128)(2,1)}, u32[]{:S(2)}, u32[]{:S(2)}) collective-permute-start(bf16[96,2,2304]{2,0,1:T(8,128)(2,1)} %fusion.9), channel_id=1, source_target_pairs={{0,24},{8,16},{16,8},{24,0},{1,25},{9,17},{17,9},{25,1},{2,26},{10... | collective-permute-start | bytes 2654216 | tf_op jit(solution)/shard_map/ppermute | solution.py:190
  202.0 7.3 %copy-start.5 = (bf16[256,2,96]{0,2,1:T(8,128)(2,1)S(1)}, bf16[256,2,96]{0,2,1:T(8,128)(2,1)}, u32[]{:S(2)}) copy-start(bf16[256,2,96]{0,2,1:T(8,128)(2,1)} %copy-done.4) | copy-start | bytes 294916
  215.1 4.6 %copy-start.13 = (s32[4,16]{1,0:T(4,128)S(1)}, s32[4,16]{1,0:T(4,128)}, u32[]{:S(2)}) copy-start(s32[4,16]{1,0:T(4,128)} %param.25) | copy-start | bytes 772
  215.2 24.7 %all-to-all-start = ((bf16[16,64,2,512]{3,1,2,0:T(8,128)(2,1)}), bf16[16,64,2,512]{3,1,2,0:T(8,128)(2,1)}, u32[]{:S(2)}, u32[]{:S(2)}) async-start(bf16[16,64,2,512]{3,1,2,0:T(8,128)(2,1)} %gather_fusion), calls=%async_computation.1 | async-start | bytes 4194304 | tf_op jit(solution)/shard_map/all_to_all | solution.py:91
  239.9 10.5 %copy-start.1 = (bf16[512,2304]{1,0:T(8,128)(2,1)S(1)}, bf16[512,2304]{1,0:T(8,128)(2,1)}, u32[]{:S(2)}) copy-start(bf16[512,2304]{1,0:T(8,128)(2,1)} %param.16) | copy-start | bytes 7077892
Sparse Core Ops, SparseCore 0:
  42.0 58.0 all-reduce.1
  215.3 27.7 reduce-scatter.1

commit v16 on v14

--- a/solution.py
+++ b/solution.py
@@ -197,10 +197,15 @@
     plan = [[0], [1, 2]] + ([list(range(3, req_total))] if req_total > 3 else [])
     plan = [[k for k in group if k < req_total] for group in plan]
     returned = []
+    previous = None
     for group in plan:
         if not group:
             continue
-        outs = experts_on(jnp.stack([arrived[k] for k in group], axis=0))
+        inputs = [arrived[k] for k in group]
+        if previous is not None:
+            inputs, previous = lax.optimization_barrier((inputs, previous))
+        outs = experts_on(jnp.stack(inputs, axis=0))
+        previous = outs
         for slot_index, step in enumerate(group):
             part = outs[slot_index]
             returned.append(part if step == 0 else partner_move(part, step))

time: 255 us -> 255 us (level)
  no operation moved by 1% of the time
where the time goes in v16:
time: 255 us; the launch traced here: 254 us
  waiting for transfers between devices  90.4 us (35%)
  matrix products  89.4 us (35%)
  local copies, waits for them, and re-layouts  29.5 us (12%)
  other arithmetic  16.3 us (6%)
  between operations  14.4 us (6%)
  starting transfers between devices  14.1 us (6%)
    psum x1, waiting for transfers between devices, body(): lax.psum(partial_value.astype(jnp.bfloat16), 'head').astype(jnp.float32)  50.8 us
    dot_general x3, matrix products, experts_on(): jnp.einsum('ned,egdf->gnef', flat, w_gate_up, preferred_element_type=jnp....  43 us
    all_to_all x1, waiting for transfers between devices, pages_in(): lax.all_to_all(outgoing, 'req', split_axis=0, concat_axis=0, tiled=True)  20 us
    ppermute x6, waiting for transfers between devices, partner_move(): return lax.ppermute(block, 'req', [(i, i ^ step) for i in range(req_total)])  19.5 us
    dot_general x2, matrix products, experts_on(): jnp.einsum('nef,efd->ned', hidden, w_down, preferred_element_type=jnp.flo...  18.1 us
    dot_general x4, matrix products, body(): jnp.einsum('tec,ced->ted', dispatch_bf, part, preferred_element_type=jnp....  17.6 us
    unnamed x28, local copies, waits for them, and re-layouts  15 us
    ppermute x6, starting transfers between devices, partner_move(): return lax.ppermute(block, 'req', [(i, i ^ step) for i in range(req_total)])  6.99 us
  transfers between devices with their start and end apart: 10, of which 6 were waited for; matrix products, arithmetic and copies ran while one was open for 33% of the time, Pallas kernels for 0%

profile of v16, /device:TPU:0, one launch (start us, length us, event | category | flops | bytes accessed | tf_op | source)
XLA Modules:
  0.0 254.1 jit_solution(9697305428355369450)
XLA Ops:
  7.3 9.9 %copy.52 = bf16[2304,3,512]{0,2,1:T(8,128)(2,1)} copy(bf16[2304,3,512]{2,0,1:T(8,128)(2,1)} %param.15) | data formatting | bytes 14155776 | tf_op args[2]
  17.1 0.3 fusion.19
  17.5 5.2 %fusion.35 = f32[256,3,8,64]{0,3,2,1:T(8,128)S(1)} fusion(bf16[3,8,64,2304]{3,2,1,0:T(8,128)(2,1)} %bitcast.166, bf16[1,256,2304]{2,1,0:T(8,128)(2,1)S(1)} %copy-done.3, f32[2304]{0:T(1024)} %param.14, f32[256]{0:T(256)S(1)} %add_rsqrt_fusion.1), kind=kOutput, calls=%fused_computation.49 | convolution fusion | flops 1814298624 | bytes 9840640 | tf_op jit(solution)/shard_map/dot_general | solution.py:124
  22.8 0.9 fusion.73
  23.6 0.2 multiply_cosine_fusion
  23.8 0.8 subtract_convert_fusion
  24.7 1.1 pad_maximum_fusion.1
  25.8 2.4 collective-permute-start
  28.2 0.6 iota_add_fusion.1
  28.7 0.7 constant_dynamic-slice_fusion.2
  29.4 0.1 copy.53
  29.6 0.1 eq.115
  29.8 0.6 reduce-window.6
  30.4 0.2 slice_reduce_fusion
  30.6 0.2 convert_reduce_fusion
  30.8 0.1 select_reduce_fusion.2
  31.0 0.2 reduce-window.9
  31.3 0.8 compare_and_fusion
  32.2 2.0 fusion.6
  34.3 1.3 fusion.9
  35.6 1.2 fusion.47
  36.8 1.9 convolution_convert_fusion.1
  38.7 0.2 reduce-scatter.2.cloned.1.call-start
  39.0 0.6 dynamic_slice.25
  39.5 0.2 eq.119
  39.9 0.7 add_compare_fusion
  40.6 1.9 bitcast_select_fusion
  42.5 2.0 gather_fusion
  44.5 0.7 fusion.112
  45.2 0.7 dynamic-slice_bitcast_fusion
  46.1 50.8 %all-reduce.2.cloned.1.call-done = bf16[256,2304]{1,0:T(8,128)(2,1)} async-done(((bf16[256,2304]{1,0:T(8,128)(2,1)}), bf16[256,2304]{1,0:T(8,128)(2,1)}) %all-reduce.2.cloned.1.call-update) | async-done | bytes 1179664 | tf_op jit(solution)/shard_map/psum | solution.py:156
  96.9 2.1 fusion.16
  99.0 0.3 fusion.18
  99.4 0.4 fusion.93
  99.8 1.0 convert_bitcast_fusion.1
  100.8 1.5 collective-permute-start.1
  102.3 1.5 collective-permute-start.2
  103.8 14.2 %convolution_bitcast_fusion.1 = f32[2,96,2,1440]{3,1,0,2:T(8,128)} fusion(bf16[2,2,2304,1440]{2,3,1,0:T(8,128)(2,1)} %param.20, f32[2304,2,96]{0,2,1:T(8,128)S(1)} %bitcast.165), kind=kOutput, calls=%fused_computation.23 | convolution fusion | flops 2548482048 | bytes 30523392 | tf_op jit(solution)/shard_map/ned,egdf->gnef/dot_general | solution.py:186
  118.0 4.7 %collective-permute-done.1 = bf16[96,2,2304]{2,0,1:T(8,128)(2,1)} collective-permute-done((bf16[96,2,2304]{2,0,1:T(8,128)(2,1)}, bf16[96,2,2304]{2,0,1:T(8,128)(2,1)}, u32[]{:S(2)}, u32[]{:S(2)}) %collective-permute-start.1) | collective-permute-done | bytes 884768 | tf_op jit(solution)/shard_map/ppermute | solution.py:181
  122.7 1.2 collective-permute-done.2
  123.9 1.6 pad_maximum_fusion
  125.5 1.4 copy.57
  126.9 14.9 %convolution_bitcast_fusion = f32[2,192,2,1440]{3,1,0,2:T(8,128)} fusion(bf16[192,2,2304,1]{2,0,3,1:T(8,128)(2,1)} %bitcast.168, bf16[2,2,2304,1440]{2,3,1,0:T(8,128)(2,1)} %param.20), kind=kOutput, calls=%fused_computation.14 | convolution fusion | flops 5096079360 | bytes 32735232 | tf_op jit(solution)/shard_map/ned,egdf->gnef/dot_general | solution.py:186
  141.8 1.5 collective-permute-start.5
  143.2 9.1 %fusion.5 = bf16[192,2,2304]{2,0,1:T(8,128)(2,1)S(1)} fusion(bf16[2,1440,2304]{2,1,0:T(8,128)(2,1)} %param.21, f32[2,192,2,1440]{3,1,0,2:T(8,128)} %convolution_bitcast_fusion), kind=kOutput, calls=%fused_computation.12 | convolution fusion | flops 2552242176 | bytes 19464192 | tf_op jit(solution)/shard_map/nef,efd->ned/dot_general | solution.py:188
  152.4 1.3 fusion.91
  153.7 0.6 collective-permute-start.3
  154.3 0.6 collective-permute-start.4
  154.8 9.9 %collective-permute-done.5 = bf16[96,2,2304]{2,0,1:T(8,128)(2,1)} collective-permute-done((bf16[96,2,2304]{2,0,1:T(8,128)(2,1)}, bf16[96,2,2304]{2,0,1:T(8,128)(2,1)}, u32[]{:S(2)}, u32[]{:S(2)}) %collective-permute-start.5) | collective-permute-done | bytes 884768 | tf_op jit(solution)/shard_map/ppermute | solution.py:181
  164.7 13.9 %fusion.11 = f32[2,96,2,1440]{3,1,2,0:T(8,128)} fusion(bf16[2,2,2304,1440]{2,3,1,0:T(8,128)(2,1)} %param.20, bf16[96,2,2304]{2,0,1:T(8,128)(2,1)} %collective-permute-done.5), kind=kOutput, calls=%fused_computation.22 | convolution fusion | flops 2548039680 | bytes 29638656 | tf_op jit(solution)/shard_map/ned,egdf->gnef/dot_general | solution.py:186
  178.6 8.9 %fusion.8 = bf16[96,2,2304]{2,0,1:T(8,128)(2,1)} fusion(bf16[2,1440,2304]{2,1,0:T(8,128)(2,1)} %param.21, f32[2,96,2,1440]{3,1,2,0:T(8,128)} %fusion.11), kind=kOutput, calls=%fused_computation.19 | convolution fusion | flops 1276121088 | bytes 16367616 | tf_op jit(solution)/shard_map/nef,efd->ned/dot_general | solution.py:188
  187.5 1.5 collective-permute-start.6
  189.0 9.8 %fusion.29 = f32[2,2304,256]{2,1,0:T(8,128)} fusion(bf16[256,2,96]{0,2,1:T(8,128)(2,1)} %copy-done.4, bf16[2,1440,2304]{2,1,0:T(8,128)(2,1)} %param.21, f32[2,96,2,1440]{3,1,0,2:T(8,128)S(1)} %copy-done.2), kind=kOutput, calls=%fused_computation.45 | convolution fusion | flops 1502613504 | bytes 20299776 | tf_op jit(solution)/shard_map/tec,ced->ted/dot_general | solution.py:215
  198.8 3.5 %convolution_add_fusion.1 = f32[2,2304,256]{2,1,0:T(8,128)S(1)} fusion(f32[2,2304,256]{2,1,0:T(8,128)} %fusion.29, bf16[96,2,2304]{2,0,1:T(8,128)(2,1)} %collective-permute-done.3, bf16[256,2,96]{0,2,1:T(8,128)(2,1)} %copy-done.4), kind=kOutput, calls=%fused_computation.6 | convolution fusion | flops 227672064 | bytes 10420224 | tf_op jit(solution)/shard_map/tec,ced->ted/dot_general | solution.py:215
  202.3 3.7 %collective-permute-done.6 = bf16[96,2,2304]{2,0,1:T(8,128)(2,1)} collective-permute-done((bf16[96,2,2304]{2,0,1:T(8,128)(2,1)}, bf16[96,2,2304]{2,0,1:T(8,128)(2,1)}, u32[]{:S(2)}, u32[]{:S(2)}) %collective-permute-start.6) | collective-permute-done | bytes 884768 | tf_op jit(solution)/shard_map/ppermute | solution.py:181
  206.1 2.0 fusion.92
  208.1 2.3 fusion.28
  210.4 1.5 copy.60
  212.0 4.5 %all-to-all-start = ((bf16[16,64,2,512]{3,1,2,0:T(8,128)(2,1)}), bf16[16,64,2,512]{3,1,2,0:T(8,128)(2,1)}, u32[]{:S(2)}, u32[]{:S(2)}) async-start(bf16[16,64,2,512]{3,1,2,0:T(8,128)(2,1)} %gather_fusion), calls=%async_computation.1 | async-start | bytes 4194304 | tf_op jit(solution)/shard_map/all_to_all | solution.py:91
  216.5 0.1 select_reduce_fusion.1
  216.7 20.0 %all-to-all-done = bf16[16,64,2,512]{3,1,2,0:T(8,128)(2,1)} async-done(((bf16[16,64,2,512]{3,1,2,0:T(8,128)(2,1)}), bf16[16,64,2,512]{3,1,2,0:T(8,128)(2,1)}, u32[]{:S(2)}, u32[]{:S(2)}) %all-to-all-start) | async-done | bytes 2097184 | tf_op jit(solution)/shard_map/all_to_all | solution.py:91
  236.7 3.7 %gather_fusion.1 = bf16[16,64,2,512]{3,1,2,0:T(8,128)(2,1)} fusion(bf16[16,64,2,512]{3,1,2,0:T(8,128)(2,1)} %all-to-all-done, s32[1024]{0:T(1024)S(1)} %pad_clamp_fusion), kind=kCustom, calls=%fused_computation.1 | custom fusion | bytes 4194368 | tf_op jit(solution)/shard_map/jit(_take)/gather | solution.py:97
  240.4 5.1 %copy.61 = bf16[16,64,2,512]{3,2,1,0:T(2,128)(2,1)} copy(bf16[16,64,2,512]{3,1,2,0:T(8,128)(2,1)} %gather_fusion.1) | data formatting | bytes 4194304
  245.5 1.7 fusion.69
  (60 shorter events, 1.0 us)
Async XLA Ops:
  7.2 29.6 %copy-start = (bf16[512,2304]{1,0:T(8,128)(2,1)S(1)}, bf16[512,2304]{1,0:T(8,128)(2,1)}, u32[]{:S(2)}) copy-start(bf16[512,2304]{1,0:T(8,128)(2,1)} %param.16) | copy-start | bytes 7077892
  7.2 89.7 %all-reduce.2.cloned.1.call-start = ((), (), s32[]{:S(2)}) async-start(), calls=%async_computation.2 | async-start | bytes 2359296 | tf_op jit(solution)/shard_map/psum | solution.py:156
  7.2 9.9 %copy-start.3 = (bf16[1,256,2304]{2,1,0:T(8,128)(2,1)S(1)}, bf16[1,256,2304]{2,1,0:T(8,128)(2,1)}, u32[]{:S(2)}) copy-start(bf16[1,256,2304]{2,1,0:T(8,128)(2,1)} %param.13) | copy-start | bytes 3538948
  22.7 7.9 %copy-start.9 = (s32[4,16]{1,0:T(4,128)S(1)}, s32[4,16]{1,0:T(4,128)}, u32[]{:S(2)}) copy-start(s32[4,16]{1,0:T(4,128)} %param.24) | copy-start | bytes 772
  24.7 3.5 %copy-start.6 = (bf16[256,8,32]{0,2,1:T(8,128)(2,1)}, bf16[256,8,32]{0,2,1:T(8,128)(2,1)S(1)}, u32[]{:S(2)}) copy-start(bf16[256,8,32]{0,2,1:T(8,128)(2,1)S(1)} %get-tuple-element.34) | copy-start | bytes 393220
  24.7 4.1 %copy-start.7 = (bf16[256,8,32]{0,2,1:T(8,128)(2,1)}, bf16[256,8,32]{0,2,1:T(8,128)(2,1)S(1)}, u32[]{:S(2)}) copy-start(bf16[256,8,32]{0,2,1:T(8,128)(2,1)S(1)} %get-tuple-element.35) | copy-start | bytes 393220
  25.8 6.4 %collective-permute-start = (bf16[2,256,8,64]{1,3,2,0:T(8,128)(2,1)S(1)}, bf16[2,256,8,64]{1,3,2,0:T(8,128)(2,1)S(1)}, u32[]{:S(2)}, u32[]{:S(2)}) collective-permute-start(bf16[2,256,8,64]{1,3,2,0:T(8,128)(2,1)S(1)} %pad_maximum_fusion.1), channel_id=1, source_target_pairs={{0,1},{2,3},{4,5},{6,7},{8,9},{10,11},{12,13},{14,15},{16,17},{18,... | collective-permute-start | bytes 1572872 | tf_op jit(solution)/shard_map/ppermute | solution.py:13
  34.3 1.3 copy-start.8
  36.8 2.1 copy-start.12
  38.7 206.8 %reduce-scatter.2.cloned.1.call-start = ((), (), s32[]{:S(2)}) async-start(), calls=%async_computation.3 | async-start | bytes 1474560 | tf_op jit(solution)/shard_map/reduce_scatter | solution.py:219
  44.5 54.5 %copy-start.10 = (f32[2304]{0:T(1024)S(1)}, f32[2304]{0:T(1024)}, u32[]{:S(2)}) copy-start(f32[2304]{0:T(1024)} %param.17) | copy-start | bytes 27652
  46.1 53.3 %copy-start.4 = (bf16[256,2,96]{0,2,1:T(8,128)(2,1)}, bf16[256,2,96]{0,2,1:T(8,128)(2,1)S(1)}, u32[]{:S(2)}) copy-start(bf16[256,2,96]{0,2,1:T(8,128)(2,1)S(1)} %get-tuple-element.19) | copy-start | bytes 294916
  100.8 21.9 %collective-permute-start.1 = (bf16[96,2,2304]{2,0,1:T(8,128)(2,1)}, bf16[96,2,2304]{2,0,1:T(8,128)(2,1)}, u32[]{:S(2)}, u32[]{:S(2)}) collective-permute-start(bf16[96,2,2304]{2,0,1:T(8,128)(2,1)} %convert_bitcast_fusion.1), channel_id=1, source_target_pairs={{0,8},{8,0},{16,24},{24,16},{1,9},{9,1},{17,25},{25,17},{2,10},{10... | collective-permute-start | bytes 2654216 | tf_op jit(solution)/shard_map/ppermute | solution.py:181
  102.3 21.6 %collective-permute-start.2 = (bf16[96,2,2304]{2,0,1:T(8,128)(2,1)}, bf16[96,2,2304]{2,0,1:T(8,128)(2,1)}, u32[]{:S(2)}, u32[]{:S(2)}) collective-permute-start(bf16[96,2,2304]{2,0,1:T(8,128)(2,1)} %convert_bitcast_fusion.1), channel_id=1, source_target_pairs={{0,16},{8,24},{16,0},{24,8},{1,17},{9,25},{17,1},{25,9},{2,18},{10... | collective-permute-start | bytes 2654216 | tf_op jit(solution)/shard_map/ppermute | solution.py:181
  141.8 22.9 %collective-permute-start.5 = (bf16[96,2,2304]{2,0,1:T(8,128)(2,1)}, bf16[96,2,2304]{2,0,1:T(8,128)(2,1)}, u32[]{:S(2)}, u32[]{:S(2)}) collective-permute-start(bf16[96,2,2304]{2,0,1:T(8,128)(2,1)} %collective-permute-done.1), channel_id=1, source_target_pairs={{0,16},{8,24},{16,0},{24,8},{1,17},{9,25},{17,1},{25,9},{2,18},{10... | collective-permute-start | bytes 2654216 | tf_op jit(solution)/shard_map/ppermute | solution.py:181
  153.7 45.1 %collective-permute-start.3 = (bf16[96,2,2304]{2,0,1:T(8,128)(2,1)}, bf16[96,2,2304]{2,0,1:T(8,128)(2,1)}, u32[]{:S(2)}, u32[]{:S(2)}) collective-permute-start(bf16[96,2,2304]{2,0,1:T(8,128)(2,1)} %get-tuple-element.23), channel_id=1, source_target_pairs={{0,8},{8,0},{16,24},{24,16},{1,9},{9,1},{17,25},{25,17},{2,10},{10... | collective-permute-start | bytes 2654216 | tf_op jit(solution)/shard_map/ppermute | solution.py:181
  154.3 53.8 %collective-permute-start.4 = (bf16[96,2,2304]{2,0,1:T(8,128)(2,1)}, bf16[96,2,2304]{2,0,1:T(8,128)(2,1)}, u32[]{:S(2)}, u32[]{:S(2)}) collective-permute-start(bf16[96,2,2304]{2,0,1:T(8,128)(2,1)} %get-tuple-element.22), channel_id=1, source_target_pairs={{0,16},{8,24},{16,0},{24,8},{1,17},{9,25},{17,1},{25,9},{2,18},{10... | collective-permute-start | bytes 2654216 | tf_op jit(solution)/shard_map/ppermute | solution.py:181
  178.6 10.4 %copy-start.2 = (f32[2,96,2,1440]{3,1,0,2:T(8,128)S(1)}, f32[2,96,2,1440]{3,1,0,2:T(8,128)}, u32[]{:S(2)}) copy-start(f32[2,96,2,1440]{3,1,0,2:T(8,128)} %convolution_bitcast_fusion.1) | copy-start | bytes 6635524
  187.5 18.6 %collective-permute-start.6 = (bf16[96,2,2304]{2,0,1:T(8,128)(2,1)}, bf16[96,2,2304]{2,0,1:T(8,128)(2,1)}, u32[]{:S(2)}, u32[]{:S(2)}) collective-permute-start(bf16[96,2,2304]{2,0,1:T(8,128)(2,1)} %fusion.8), channel_id=1, source_target_pairs={{0,24},{8,16},{16,8},{24,0},{1,25},{9,17},{17,9},{25,1},{2,26},{10... | collective-permute-start | bytes 2654216 | tf_op jit(solution)/shard_map/ppermute | solution.py:181
  198.8 7.3 %copy-start.5 = (bf16[256,2,96]{0,2,1:T(8,128)(2,1)S(1)}, bf16[256,2,96]{0,2,1:T(8,128)(2,1)}, u32[]{:S(2)}) copy-start(bf16[256,2,96]{0,2,1:T(8,128)(2,1)} %copy-done.4) | copy-start | bytes 294916
  212.0 4.6 %copy-start.11 = (s32[4,16]{1,0:T(4,128)S(1)}, s32[4,16]{1,0:T(4,128)}, u32[]{:S(2)}) copy-start(s32[4,16]{1,0:T(4,128)} %param.25) | copy-start | bytes 772
  212.0 24.7 %all-to-all-start = ((bf16[16,64,2,512]{3,1,2,0:T(8,128)(2,1)}), bf16[16,64,2,512]{3,1,2,0:T(8,128)(2,1)}, u32[]{:S(2)}, u32[]{:S(2)}) async-start(bf16[16,64,2,512]{3,1,2,0:T(8,128)(2,1)} %gather_fusion), calls=%async_computation.1 | async-start | bytes 4194304 | tf_op jit(solution)/shard_map/all_to_all | solution.py:91
  236.7 10.5 %copy-start.1 = (bf16[512,2304]{1,0:T(8,128)(2,1)S(1)}, bf16[512,2304]{1,0:T(8,128)(2,1)}, u32[]{:S(2)}) copy-start(bf16[512,2304]{1,0:T(8,128)(2,1)} %param.16) | copy-start | bytes 7077892
Sparse Core Ops, SparseCore 0:
  38.8 58.0 all-reduce.1
  212.1 27.7 reduce-scatter.1

commit v17 on v14

--- a/solution.py
+++ b/solution.py
@@ -191,7 +191,7 @@
     arrived = {0: picked_own}
     for step in range(1, req_total):
         if step == 3:
-            arrived[step] = partner_move(arrived[1], 2)
+            arrived[step] = partner_move(arrived[2], 1)
         else:
             arrived[step] = partner_move(picked_own, step)
     plan = [[0], [1, 2]] + ([list(range(3, req_total))] if req_total > 3 else [])

time: 255 us -> 255 us (level)
  no operation moved by 1% of the time
where the time goes in v17:
time: 255 us; the launch traced here: 254 us
  waiting for transfers between devices  89.5 us (35%)
  matrix products  89.4 us (35%)
  local copies, waits for them, and re-layouts  29.5 us (12%)
  other arithmetic  16.3 us (6%)
  starting transfers between devices  15 us (6%)
  between operations  14.4 us (6%)
    psum x1, waiting for transfers between devices, body(): lax.psum(partial_value.astype(jnp.bfloat16), 'head').astype(jnp.float32)  50.8 us
    dot_general x3, matrix products, experts_on(): jnp.einsum('ned,egdf->gnef', flat, w_gate_up, preferred_element_type=jnp....  43 us
    all_to_all x1, waiting for transfers between devices, pages_in(): lax.all_to_all(outgoing, 'req', split_axis=0, concat_axis=0, tiled=True)  20 us
    ppermute x6, waiting for transfers between devices, partner_move(): return lax.ppermute(block, 'req', [(i, i ^ step) for i in range(req_total)])  18.6 us
    dot_general x2, matrix products, experts_on(): jnp.einsum('nef,efd->ned', hidden, w_down, preferred_element_type=jnp.flo...  18.1 us
    dot_general x4, matrix products, body(): jnp.einsum('tec,ced->ted', dispatch_bf, part, preferred_element_type=jnp....  17.6 us
    unnamed x28, local copies, waits for them, and re-layouts  15 us
    ppermute x6, starting transfers between devices, partner_move(): return lax.ppermute(block, 'req', [(i, i ^ step) for i in range(req_total)])  7.91 us
  transfers between devices with their start and end apart: 10, of which 6 were waited for; matrix products, arithmetic and copies ran while one was open for 33% of the time, Pallas kernels for 0%

profile of v17, /device:TPU:0, one launch (start us, length us, event | category | flops | bytes accessed | tf_op | source)
XLA Modules:
  0.0 254.1 jit_solution(526379407509241209)
XLA Ops:
  7.3 9.9 %copy.52 = bf16[2304,3,512]{0,2,1:T(8,128)(2,1)} copy(bf16[2304,3,512]{2,0,1:T(8,128)(2,1)} %param.15) | data formatting | bytes 14155776 | tf_op args[2]
  17.1 0.3 fusion.19
  17.5 5.2 %fusion.35 = f32[256,3,8,64]{0,3,2,1:T(8,128)S(1)} fusion(bf16[3,8,64,2304]{3,2,1,0:T(8,128)(2,1)} %bitcast.166, bf16[1,256,2304]{2,1,0:T(8,128)(2,1)S(1)} %copy-done.3, f32[2304]{0:T(1024)} %param.14, f32[256]{0:T(256)S(1)} %add_rsqrt_fusion.1), kind=kOutput, calls=%fused_computation.49 | convolution fusion | flops 1814298624 | bytes 9840640 | tf_op jit(solution)/shard_map/dot_general | solution.py:124
  22.8 0.9 fusion.73
  23.6 0.2 multiply_cosine_fusion
  23.8 0.8 subtract_convert_fusion
  24.7 1.1 pad_maximum_fusion.1
  25.8 2.4 collective-permute-start
  28.2 0.6 iota_add_fusion.1
  28.7 0.7 constant_dynamic-slice_fusion.2
  29.4 0.1 copy.53
  29.6 0.1 eq.115
  29.8 0.6 reduce-window.6
  30.4 0.2 slice_reduce_fusion
  30.6 0.2 convert_reduce_fusion
  30.8 0.1 select_reduce_fusion.2
  31.0 0.2 reduce-window.9
  31.3 0.8 compare_and_fusion
  32.2 2.0 fusion.6
  34.3 1.3 fusion.9
  35.6 1.2 fusion.47
  36.8 1.9 convolution_convert_fusion.1
  38.7 0.2 reduce-scatter.2.cloned.1.call-start
  39.0 0.6 dynamic_slice.25
  39.5 0.2 eq.119
  39.9 0.7 add_compare_fusion
  40.6 1.9 bitcast_select_fusion
  42.5 2.0 gather_fusion
  44.5 0.7 fusion.112
  45.2 0.7 dynamic-slice_bitcast_fusion
  46.1 50.8 %all-reduce.2.cloned.1.call-done = bf16[256,2304]{1,0:T(8,128)(2,1)} async-done(((bf16[256,2304]{1,0:T(8,128)(2,1)}), bf16[256,2304]{1,0:T(8,128)(2,1)}) %all-reduce.2.cloned.1.call-update) | async-done | bytes 1179664 | tf_op jit(solution)/shard_map/psum | solution.py:156
  96.9 2.1 fusion.16
  99.0 0.3 fusion.18
  99.4 0.4 fusion.93
  99.8 1.0 convert_bitcast_fusion.1
  100.8 1.5 collective-permute-start.1
  102.3 1.5 collective-permute-start.2
  103.8 14.2 %convolution_bitcast_fusion.1 = f32[2,96,2,1440]{3,1,0,2:T(8,128)} fusion(bf16[2,2,2304,1440]{2,3,1,0:T(8,128)(2,1)} %param.20, f32[2304,2,96]{0,2,1:T(8,128)S(1)} %bitcast.165), kind=kOutput, calls=%fused_computation.23 | convolution fusion | flops 2548482048 | bytes 30523392 | tf_op jit(solution)/shard_map/ned,egdf->gnef/dot_general | solution.py:186
  118.0 4.7 %collective-permute-done.1 = bf16[96,2,2304]{2,0,1:T(8,128)(2,1)} collective-permute-done((bf16[96,2,2304]{2,0,1:T(8,128)(2,1)}, bf16[96,2,2304]{2,0,1:T(8,128)(2,1)}, u32[]{:S(2)}, u32[]{:S(2)}) %collective-permute-start.1) | collective-permute-done | bytes 884768 | tf_op jit(solution)/shard_map/ppermute | solution.py:181
  122.7 1.2 collective-permute-done.2
  123.9 1.6 pad_maximum_fusion
  125.5 1.4 copy.57
  126.9 14.9 %convolution_bitcast_fusion = f32[2,192,2,1440]{3,1,0,2:T(8,128)} fusion(bf16[192,2,2304,1]{2,0,3,1:T(8,128)(2,1)} %bitcast.168, bf16[2,2,2304,1440]{2,3,1,0:T(8,128)(2,1)} %param.20), kind=kOutput, calls=%fused_computation.14 | convolution fusion | flops 5096079360 | bytes 32735232 | tf_op jit(solution)/shard_map/ned,egdf->gnef/dot_general | solution.py:186
  141.8 0.6 collective-permute-start.5
  142.3 9.1 %fusion.5 = bf16[192,2,2304]{2,0,1:T(8,128)(2,1)S(1)} fusion(bf16[2,1440,2304]{2,1,0:T(8,128)(2,1)} %param.21, f32[2,192,2,1440]{3,1,0,2:T(8,128)} %convolution_bitcast_fusion), kind=kOutput, calls=%fused_computation.12 | convolution fusion | flops 2552242176 | bytes 19464192 | tf_op jit(solution)/shard_map/nef,efd->ned/dot_general | solution.py:188
  151.5 1.3 fusion.91
  152.8 1.5 collective-permute-start.3
  154.3 1.5 collective-permute-start.4
  155.7 9.0 %collective-permute-done.5 = bf16[96,2,2304]{2,0,1:T(8,128)(2,1)} collective-permute-done((bf16[96,2,2304]{2,0,1:T(8,128)(2,1)}, bf16[96,2,2304]{2,0,1:T(8,128)(2,1)}, u32[]{:S(2)}, u32[]{:S(2)}) %collective-permute-start.5) | collective-permute-done | bytes 884768 | tf_op jit(solution)/shard_map/ppermute | solution.py:181
  164.7 13.9 %fusion.11 = f32[2,96,2,1440]{3,1,2,0:T(8,128)} fusion(bf16[2,2,2304,1440]{2,3,1,0:T(8,128)(2,1)} %param.20, bf16[96,2,2304]{2,0,1:T(8,128)(2,1)} %collective-permute-done.5), kind=kOutput, calls=%fused_computation.22 | convolution fusion | flops 2548039680 | bytes 29638656 | tf_op jit(solution)/shard_map/ned,egdf->gnef/dot_general | solution.py:186
  178.6 8.9 %fusion.8 = bf16[96,2,2304]{2,0,1:T(8,128)(2,1)} fusion(bf16[2,1440,2304]{2,1,0:T(8,128)(2,1)} %param.21, f32[2,96,2,1440]{3,1,2,0:T(8,128)} %fusion.11), kind=kOutput, calls=%fused_computation.19 | convolution fusion | flops 1276121088 | bytes 16367616 | tf_op jit(solution)/shard_map/nef,efd->ned/dot_general | solution.py:188
  187.5 1.5 collective-permute-start.6
  189.0 9.8 %fusion.29 = f32[2,2304,256]{2,1,0:T(8,128)} fusion(bf16[256,2,96]{0,2,1:T(8,128)(2,1)} %copy-done.4, bf16[2,1440,2304]{2,1,0:T(8,128)(2,1)} %param.21, f32[2,96,2,1440]{3,1,0,2:T(8,128)S(1)} %copy-done.2), kind=kOutput, calls=%fused_computation.45 | convolution fusion | flops 1502613504 | bytes 20299776 | tf_op jit(solution)/shard_map/tec,ced->ted/dot_general | solution.py:210
  198.8 3.5 %convolution_add_fusion.1 = f32[2,2304,256]{2,1,0:T(8,128)S(1)} fusion(f32[2,2304,256]{2,1,0:T(8,128)} %fusion.29, bf16[96,2,2304]{2,0,1:T(8,128)(2,1)} %collective-permute-done.3, bf16[256,2,96]{0,2,1:T(8,128)(2,1)} %copy-done.4), kind=kOutput, calls=%fused_computation.6 | convolution fusion | flops 227672064 | bytes 10420224 | tf_op jit(solution)/shard_map/tec,ced->ted/dot_general | solution.py:210
  202.3 3.7 %collective-permute-done.6 = bf16[96,2,2304]{2,0,1:T(8,128)(2,1)} collective-permute-done((bf16[96,2,2304]{2,0,1:T(8,128)(2,1)}, bf16[96,2,2304]{2,0,1:T(8,128)(2,1)}, u32[]{:S(2)}, u32[]{:S(2)}) %collective-permute-start.6) | collective-permute-done | bytes 884768 | tf_op jit(solution)/shard_map/ppermute | solution.py:181
  206.1 2.0 fusion.92
  208.1 2.3 fusion.28
  210.4 1.5 copy.60
  212.0 4.5 %all-to-all-start = ((bf16[16,64,2,512]{3,1,2,0:T(8,128)(2,1)}), bf16[16,64,2,512]{3,1,2,0:T(8,128)(2,1)}, u32[]{:S(2)}, u32[]{:S(2)}) async-start(bf16[16,64,2,512]{3,1,2,0:T(8,128)(2,1)} %gather_fusion), calls=%async_computation.1 | async-start | bytes 4194304 | tf_op jit(solution)/shard_map/all_to_all | solution.py:91
  216.5 0.1 select_reduce_fusion.1
  216.7 20.0 %all-to-all-done = bf16[16,64,2,512]{3,1,2,0:T(8,128)(2,1)} async-done(((bf16[16,64,2,512]{3,1,2,0:T(8,128)(2,1)}), bf16[16,64,2,512]{3,1,2,0:T(8,128)(2,1)}, u32[]{:S(2)}, u32[]{:S(2)}) %all-to-all-start) | async-done | bytes 2097184 | tf_op jit(solution)/shard_map/all_to_all | solution.py:91
  236.7 3.7 %gather_fusion.1 = bf16[16,64,2,512]{3,1,2,0:T(8,128)(2,1)} fusion(bf16[16,64,2,512]{3,1,2,0:T(8,128)(2,1)} %all-to-all-done, s32[1024]{0:T(1024)S(1)} %pad_clamp_fusion), kind=kCustom, calls=%fused_computation.1 | custom fusion | bytes 4194368 | tf_op jit(solution)/shard_map/jit(_take)/gather | solution.py:97
  240.4 5.1 %copy.61 = bf16[16,64,2,512]{3,2,1,0:T(2,128)(2,1)} copy(bf16[16,64,2,512]{3,1,2,0:T(8,128)(2,1)} %gather_fusion.1) | data formatting | bytes 4194304
  245.5 1.7 fusion.69
  (60 shorter events, 1.0 us)
Async XLA Ops:
  7.2 29.6 %copy-start = (bf16[512,2304]{1,0:T(8,128)(2,1)S(1)}, bf16[512,2304]{1,0:T(8,128)(2,1)}, u32[]{:S(2)}) copy-start(bf16[512,2304]{1,0:T(8,128)(2,1)} %param.16) | copy-start | bytes 7077892
  7.2 89.7 %all-reduce.2.cloned.1.call-start = ((), (), s32[]{:S(2)}) async-start(), calls=%async_computation.2 | async-start | bytes 2359296 | tf_op jit(solution)/shard_map/psum | solution.py:156
  7.2 9.9 %copy-start.3 = (bf16[1,256,2304]{2,1,0:T(8,128)(2,1)S(1)}, bf16[1,256,2304]{2,1,0:T(8,128)(2,1)}, u32[]{:S(2)}) copy-start(bf16[1,256,2304]{2,1,0:T(8,128)(2,1)} %param.13) | copy-start | bytes 3538948
  22.7 7.9 %copy-start.9 = (s32[4,16]{1,0:T(4,128)S(1)}, s32[4,16]{1,0:T(4,128)}, u32[]{:S(2)}) copy-start(s32[4,16]{1,0:T(4,128)} %param.24) | copy-start | bytes 772
  24.7 3.5 %copy-start.6 = (bf16[256,8,32]{0,2,1:T(8,128)(2,1)}, bf16[256,8,32]{0,2,1:T(8,128)(2,1)S(1)}, u32[]{:S(2)}) copy-start(bf16[256,8,32]{0,2,1:T(8,128)(2,1)S(1)} %get-tuple-element.30) | copy-start | bytes 393220
  24.7 4.1 %copy-start.7 = (bf16[256,8,32]{0,2,1:T(8,128)(2,1)}, bf16[256,8,32]{0,2,1:T(8,128)(2,1)S(1)}, u32[]{:S(2)}) copy-start(bf16[256,8,32]{0,2,1:T(8,128)(2,1)S(1)} %get-tuple-element.31) | copy-start | bytes 393220
  25.8 6.4 %collective-permute-start = (bf16[2,256,8,64]{1,3,2,0:T(8,128)(2,1)S(1)}, bf16[2,256,8,64]{1,3,2,0:T(8,128)(2,1)S(1)}, u32[]{:S(2)}, u32[]{:S(2)}) collective-permute-start(bf16[2,256,8,64]{1,3,2,0:T(8,128)(2,1)S(1)} %pad_maximum_fusion.1), channel_id=1, source_target_pairs={{0,1},{2,3},{4,5},{6,7},{8,9},{10,11},{12,13},{14,15},{16,17},{18,... | collective-permute-start | bytes 1572872 | tf_op jit(solution)/shard_map/ppermute | solution.py:13
  34.3 1.3 copy-start.8
  36.8 2.1 copy-start.12
  38.7 206.8 %reduce-scatter.2.cloned.1.call-start = ((), (), s32[]{:S(2)}) async-start(), calls=%async_computation.3 | async-start | bytes 1474560 | tf_op jit(solution)/shard_map/reduce_scatter | solution.py:214
  44.5 54.5 %copy-start.10 = (f32[2304]{0:T(1024)S(1)}, f32[2304]{0:T(1024)}, u32[]{:S(2)}) copy-start(f32[2304]{0:T(1024)} %param.17) | copy-start | bytes 27652
  46.1 53.3 %copy-start.4 = (bf16[256,2,96]{0,2,1:T(8,128)(2,1)}, bf16[256,2,96]{0,2,1:T(8,128)(2,1)S(1)}, u32[]{:S(2)}) copy-start(bf16[256,2,96]{0,2,1:T(8,128)(2,1)S(1)} %get-tuple-element.15) | copy-start | bytes 294916
  100.8 21.9 %collective-permute-start.1 = (bf16[96,2,2304]{2,0,1:T(8,128)(2,1)}, bf16[96,2,2304]{2,0,1:T(8,128)(2,1)}, u32[]{:S(2)}, u32[]{:S(2)}) collective-permute-start(bf16[96,2,2304]{2,0,1:T(8,128)(2,1)} %convert_bitcast_fusion.1), channel_id=1, source_target_pairs={{0,8},{8,0},{16,24},{24,16},{1,9},{9,1},{17,25},{25,17},{2,10},{10... | collective-permute-start | bytes 2654216 | tf_op jit(solution)/shard_map/ppermute | solution.py:181
  102.3 21.6 %collective-permute-start.2 = (bf16[96,2,2304]{2,0,1:T(8,128)(2,1)}, bf16[96,2,2304]{2,0,1:T(8,128)(2,1)}, u32[]{:S(2)}, u32[]{:S(2)}) collective-permute-start(bf16[96,2,2304]{2,0,1:T(8,128)(2,1)} %convert_bitcast_fusion.1), channel_id=1, source_target_pairs={{0,16},{8,24},{16,0},{24,8},{1,17},{9,25},{17,1},{25,9},{2,18},{10... | collective-permute-start | bytes 2654216 | tf_op jit(solution)/shard_map/ppermute | solution.py:181
  141.8 22.9 %collective-permute-start.5 = (bf16[96,2,2304]{2,0,1:T(8,128)(2,1)}, bf16[96,2,2304]{2,0,1:T(8,128)(2,1)}, u32[]{:S(2)}, u32[]{:S(2)}) collective-permute-start(bf16[96,2,2304]{2,0,1:T(8,128)(2,1)} %collective-permute-done.2), channel_id=1, source_target_pairs={{0,8},{8,0},{16,24},{24,16},{1,9},{9,1},{17,25},{25,17},{2,10},{10... | collective-permute-start | bytes 2654216 | tf_op jit(solution)/shard_map/ppermute | solution.py:181
  152.8 46.0 %collective-permute-start.3 = (bf16[96,2,2304]{2,0,1:T(8,128)(2,1)}, bf16[96,2,2304]{2,0,1:T(8,128)(2,1)}, u32[]{:S(2)}, u32[]{:S(2)}) collective-permute-start(bf16[96,2,2304]{2,0,1:T(8,128)(2,1)} %get-tuple-element.19), channel_id=1, source_target_pairs={{0,8},{8,0},{16,24},{24,16},{1,9},{9,1},{17,25},{25,17},{2,10},{10... | collective-permute-start | bytes 2654216 | tf_op jit(solution)/shard_map/ppermute | solution.py:181
  154.3 53.8 %collective-permute-start.4 = (bf16[96,2,2304]{2,0,1:T(8,128)(2,1)}, bf16[96,2,2304]{2,0,1:T(8,128)(2,1)}, u32[]{:S(2)}, u32[]{:S(2)}) collective-permute-start(bf16[96,2,2304]{2,0,1:T(8,128)(2,1)} %get-tuple-element.18), channel_id=1, source_target_pairs={{0,16},{8,24},{16,0},{24,8},{1,17},{9,25},{17,1},{25,9},{2,18},{10... | collective-permute-start | bytes 2654216 | tf_op jit(solution)/shard_map/ppermute | solution.py:181
  178.6 10.4 %copy-start.2 = (f32[2,96,2,1440]{3,1,0,2:T(8,128)S(1)}, f32[2,96,2,1440]{3,1,0,2:T(8,128)}, u32[]{:S(2)}) copy-start(f32[2,96,2,1440]{3,1,0,2:T(8,128)} %convolution_bitcast_fusion.1) | copy-start | bytes 6635524
  187.5 18.6 %collective-permute-start.6 = (bf16[96,2,2304]{2,0,1:T(8,128)(2,1)}, bf16[96,2,2304]{2,0,1:T(8,128)(2,1)}, u32[]{:S(2)}, u32[]{:S(2)}) collective-permute-start(bf16[96,2,2304]{2,0,1:T(8,128)(2,1)} %fusion.8), channel_id=1, source_target_pairs={{0,24},{8,16},{16,8},{24,0},{1,25},{9,17},{17,9},{25,1},{2,26},{10... | collective-permute-start | bytes 2654216 | tf_op jit(solution)/shard_map/ppermute | solution.py:181
  198.8 7.3 %copy-start.5 = (bf16[256,2,96]{0,2,1:T(8,128)(2,1)S(1)}, bf16[256,2,96]{0,2,1:T(8,128)(2,1)}, u32[]{:S(2)}) copy-start(bf16[256,2,96]{0,2,1:T(8,128)(2,1)} %copy-done.4) | copy-start | bytes 294916
  212.0 4.6 %copy-start.11 = (s32[4,16]{1,0:T(4,128)S(1)}, s32[4,16]{1,0:T(4,128)}, u32[]{:S(2)}) copy-start(s32[4,16]{1,0:T(4,128)} %param.25) | copy-start | bytes 772
  212.0 24.7 %all-to-all-start = ((bf16[16,64,2,512]{3,1,2,0:T(8,128)(2,1)}), bf16[16,64,2,512]{3,1,2,0:T(8,128)(2,1)}, u32[]{:S(2)}, u32[]{:S(2)}) async-start(bf16[16,64,2,512]{3,1,2,0:T(8,128)(2,1)} %gather_fusion), calls=%async_computation.1 | async-start | bytes 4194304 | tf_op jit(solution)/shard_map/all_to_all | solution.py:91
  236.7 10.5 %copy-start.1 = (bf16[512,2304]{1,0:T(8,128)(2,1)S(1)}, bf16[512,2304]{1,0:T(8,128)(2,1)}, u32[]{:S(2)}) copy-start(bf16[512,2304]{1,0:T(8,128)(2,1)} %param.16) | copy-start | bytes 7077892
Sparse Core Ops, SparseCore 0:
  38.8 58.0 all-reduce.1
  212.1 27.7 reduce-scatter.1
